TPU v7x, 128 devices: a whole 4x4x4 slice. The times are simulated.
128 devices in a mesh: tile: 16 (over z_hi, x, core), lag: 8 (over z_lo, y).
Axes of the slice: x: 4, y: 4, z: 4 (z_hi: 2, z_lo: 2; z = z_hi * 2 + z_lo), core: 2. Of those that a mesh axis runs over, the one named last changes fastest.
Arguments:
- history: bfloat16 [16, 128, 384, 512], P('lag', 'tile'), may hold values from -6 to 6
- lag_blocks: bfloat16 [16, 128, 2, 384, 384], P('lag', 'tile'), may hold values from -0.0625 to 0.0625
- self_inverse: bfloat16 [128, 384, 384], P('tile'), may hold values from -0.3125 to 0.3125
- excitation: float32 [128, 384, 512], P('tile'), may hold values from -6 to 6
- pattern: int32 [16, 128, 2], P('lag', 'tile'), may hold values from 0 to 8
- live_counts: int32 [16, 128], P('lag', 'tile'), may hold values from 1 to 2
Outputs:
- traction: bfloat16 [128, 384, 512], P('tile')
- shifted_history: bfloat16 [16, 128, 384, 512], P('lag', 'tile')
All inputs are finite; a program needn't handle non-finite values.
Results may differ from a plain program's by a relative error of at most 0.013.
Values may be sent and summed in bfloat16 or wider, within the bound.
No kernel may reach another device: no remote copies, remote signals or barrier semaphores. Data moves between devices by JAX's collectives and lax.ppermute only.
A program may use at most 128 MiB of HBM per device.

v0:
```python
import jax
import jax.numpy as jnp
from jax import lax
from jax.sharding import PartitionSpec as P

SLOTS = 2
EDGE = 4


def padded(cells, sides, width):
    for axis, dim in sides:
        count = lax.axis_size(axis)
        head = lax.slice_in_dim(cells, 0, width, axis=dim)
        tail = lax.slice_in_dim(cells, cells.shape[dim] - width, cells.shape[dim], axis=dim)
        cells = jnp.concatenate(
            [
                lax.ppermute(tail, axis, [(i, (i + 1) % count) for i in range(count)]),
                cells,
                lax.ppermute(head, axis, [((i + 1) % count, i) for i in range(count)]),
            ],
            axis=dim,
        )
    return cells


def passed_along(array, axis, by):
    length = lax.axis_size(axis)
    pairs = [(i, i + by) for i in range(length) if 0 <= i + by < length]
    return lax.ppermute(array, axis, pairs)


def pick_sources(window, source_index):
    return window[source_index]


def shards(history, lag_blocks, self_inverse, excitation, pattern, live_counts):
    blocks_here = history.shape[1]
    window = padded(history, (("tile", 1),), EDGE)
    positions = jnp.arange(blocks_here, dtype=jnp.int32)
    source_index = positions[None, :, None] + pattern
    sources = jax.vmap(pick_sources)(window, source_index)
    live = jnp.arange(SLOTS, dtype=jnp.int32)[None, None, :] < live_counts[:, :, None]
    sources = sources * live[:, :, :, None, None].astype(sources.dtype)
    partial_field = jnp.einsum(
        "lbsij,lbsjr->bir", lag_blocks, sources, preferred_element_type=jnp.float32
    )
    carried = passed_along(history[-1], "lag", 1)
    field = lax.psum(partial_field.astype(jnp.bfloat16), "lag").astype(jnp.float32)
    residual = (excitation - field).astype(jnp.bfloat16)
    traction = jnp.einsum(
        "bij,bjr->bir", self_inverse, residual, preferred_element_type=jnp.float32
    ).astype(jnp.bfloat16)
    newest = jnp.where(lax.axis_index("lag") == 0, traction, carried)
    shifted_history = jnp.concatenate([newest[None], history[:-1]], axis=0)
    return (traction, shifted_history)


def solution(mesh):
    in_specs = (
        P("lag", "tile", None, None),
        P("lag", "tile", None, None, None),
        P("tile", None, None),
        P("tile", None, None),
        P("lag", "tile", None),
        P("lag", "tile"),
    )
    out_specs = (P("tile", None, None), P("lag", "tile", None, None))
    return jax.shard_map(shards, mesh=mesh, in_specs=in_specs, out_specs=out_specs, check_vma=False)
```

profile of v0, /device:TPU:14, one launch (start us, length us, event | category | flops | bytes accessed | tf_op | source)
XLA Modules:
  0.0 261.7 jit_solution(10920987208944018283)
XLA Ops:
  7.2 0.0 copy-start
  7.2 0.0 copy-start.2
  7.2 0.0 copy-start.3
  7.2 0.0 all-reduce.2.cloned.1.call-start
  7.2 6.2 %fusion.13 = (bf16[2,4,384,512]{3,2,1,0:T(8,128)(2,1)}, bf16[2,4,384,512]{3,2,1,0:T(8,128)(2,1)}) fusion(bf16[2,8,384,512]{3,2,1,0:T(8,128)(2,1)} %param.6), kind=kLoop, calls=%fused_computation.20 | loop fusion | bytes 12582912 | tf_op jit(solution)/shard_map/slice | solution.py:14
  13.5 0.0 collective-permute-start
  13.5 1.7 collective-permute-start.1
  15.2 0.0 copy-done.2
  15.3 0.1 copy.14
  15.3 0.1 reshape.10
  15.4 0.0 copy-done.3
  15.4 0.1 fusion.7
  15.5 35.0 %collective-permute-done = bf16[2,4,384,512]{3,2,1,0:T(8,128)(2,1)} collective-permute-done((bf16[2,4,384,512]{3,2,1,0:T(8,128)(2,1)}, bf16[2,4,384,512]{3,2,1,0:T(8,128)(2,1)}, u32[]{:S(2)}, u32[]{:S(2)}) %collective-permute-start) | collective-permute-done | bytes 3145760 | tf_op jit(solution)/shard_map/ppermute | solution.py:17
  50.5 0.0 collective-permute-done.1
  50.5 10.5 %pad_maximum_fusion = bf16[2,16,384,512]{3,2,1,0:T(8,128)(2,1)} fusion(bf16[2,4,384,512]{3,2,1,0:T(8,128)(2,1)} %collective-permute-done.1, bf16[2,8,384,512]{3,2,1,0:T(8,128)(2,1)} %param.6, bf16[2,4,384,512]{3,2,1,0:T(8,128)(2,1)} %collective-permute-done), kind=kLoop, calls=%fused_computation.1 | loop fusion | flops 12582912 | bytes 25165824 | tf_op jit(solution)/shard_map/concatenate | solution.py:15
  61.0 11.4 %gather_fusion = bf16[32,384,512]{2,1,0:T(8,128)(2,1)} fusion(bf16[2,16,384,512]{3,2,1,0:T(8,128)(2,1)} %pad_maximum_fusion, s32[32]{0:T(128)S(1)} %reshape.10), kind=kCustom, calls=%fused_computation | custom fusion | bytes 25166080 | tf_op jit(solution)/shard_map/vmap()/gather | solution.py:33
  72.4 12.6 %fusion.4 = bf16[8,384,512]{2,1,0:T(8,128)(2,1)} fusion(bf16[2,8,2,384,384]{4,3,2,1,0:T(8,128)(2,1)} %param.7, bf16[2,8,2,384,512]{4,3,2,1,0:T(8,128)(2,1)} %bitcast.24, bf16[2,8,2]{2,1,0:T(8,128)(2,1)S(1)} %fusion.7), kind=kOutput, calls=%fused_computation.9 | convolution fusion | flops 4858576896 | bytes 25165888 | tf_op jit(solution)/shard_map/lbsij,lbsjr->bir/dot_general | solution.py:44
  85.1 0.0 all-reduce.2.cloned.1.call-update
  85.1 6.1 %fusion.12 = (bf16[1,8,384,512]{3,2,1,0:T(8,128)(2,1)}, bf16[1,8,384,512]{3,2,1,0:T(8,128)(2,1)}) fusion(bf16[2,8,384,512]{3,2,1,0:T(8,128)(2,1)} %param.6), kind=kLoop, calls=%fused_computation.19 | loop fusion | bytes 12582912 | tf_op jit(solution)/shard_map/slice | solution.py:47
  91.2 4.7 %copy.22 = bf16[1,8,384,512]{2,3,1,0:T(8,128)(2,1)} copy(bf16[1,8,384,512]{3,2,1,0:T(8,128)(2,1)} %get-tuple-element.6) | data formatting | bytes 6291456
  95.9 3.5 %collective-permute-start.2 = (bf16[8,384,512]{1,2,0:T(8,128)(2,1)}, bf16[8,384,512]{1,2,0:T(8,128)(2,1)}, u32[]{:S(2)}, u32[]{:S(2)}) collective-permute-start(bf16[8,384,512]{1,2,0:T(8,128)(2,1)} %bitcast.25), channel_id=1, source_target_pairs={{0,1},{1,2},{2,3},{3,4},{4,5},{5,6},{6,7},{8,9},{9,10},{10,11},{11... | collective-permute-start | bytes 9437192 | tf_op jit(solution)/shard_map/ppermute | solution.py:29
  99.4 4.8 %copy.23 = bf16[1,8,384,512]{2,3,1,0:T(8,128)(2,1)} copy(bf16[1,8,384,512]{3,2,1,0:T(8,128)(2,1)} %get-tuple-element.7) | data formatting | bytes 6291456
  104.2 123.6 %all-reduce.2.cloned.1.call-done = bf16[8,384,512]{2,1,0:T(8,128)(2,1)} async-done(((bf16[8,384,512]{2,1,0:T(8,128)(2,1)}), bf16[8,384,512]{2,1,0:T(8,128)(2,1)}) %all-reduce.2.cloned.1.call-update) | async-done | bytes 3145744 | tf_op jit(solution)/shard_map/psum | solution.py:48
  227.7 0.0 copy-done
  227.8 7.6 %convert_bitcast_fusion = bf16[8,384,512]{1,2,0:T(8,128)(2,1)} fusion(bf16[8,384,384]{2,1,0:T(8,128)(2,1)S(1)} %copy-done, f32[8,384,512]{2,1,0:T(8,128)} %param.9, bf16[8,384,512]{2,1,0:T(8,128)(2,1)} %all-reduce.2.cloned.1.call-done), kind=kOutput, calls=%fused_computation.11 | convolution fusion | flops 1214251008 | bytes 14942208 | tf_op jit(solution)/shard_map/bij,bjr->bir/dot_general | solution.py:50
  235.4 4.6 %copy.18 = bf16[8,384,512]{2,1,0:T(8,128)(2,1)} copy(bf16[8,384,512]{1,2,0:T(8,128)(2,1)} %convert_bitcast_fusion) | data formatting | bytes 6291456
  240.0 0.0 copy-start.1
  240.0 0.0 collective-permute-done.2
  240.0 2.4 select_bitcast_fusion
  242.4 0.4 copy-done.1
  242.8 3.4 %pad_maximum_fusion.1 = bf16[2,8,384,512]{2,3,1,0:T(8,128)(2,1)} fusion(bf16[1,8,384,512]{2,3,1,0:T(8,128)(2,1)S(1)} %copy-done.1, bf16[1,8,384,512]{2,3,1,0:T(8,128)(2,1)S(1)} %select_bitcast_fusion), kind=kLoop, calls=%fused_computation.4 | loop fusion | flops 3145728 | bytes 12582912 | tf_op jit(solution)/shard_map/concatenate | solution.py:54
  246.2 8.6 %copy.19 = bf16[2,8,384,512]{3,2,1,0:T(8,128)(2,1)} copy(bf16[2,8,384,512]{2,3,1,0:T(8,128)(2,1)} %pad_maximum_fusion.1) | data formatting | bytes 12582912
  (1 shorter events, 0.0 us)
Async XLA Ops:
  7.2 220.6 %copy-start = (bf16[8,384,384]{2,1,0:T(8,128)(2,1)S(1)}, bf16[8,384,384]{2,1,0:T(8,128)(2,1)}, u32[]{:S(2)}) copy-start(bf16[8,384,384]{2,1,0:T(8,128)(2,1)} %param.8) | copy-start | bytes 7077892
  7.2 8.1 %copy-start.2 = (s32[2,8,2]{1,2,0:T(2,128)S(1)}, s32[2,8,2]{1,2,0:T(2,128)}, u32[]{:S(2)}) copy-start(s32[2,8,2]{1,2,0:T(2,128)} %param.10) | copy-start | bytes 388
  7.2 8.2 %copy-start.3 = (s32[2,8]{1,0:T(2,128)S(1)}, s32[2,8]{1,0:T(2,128)}, u32[]{:S(2)}) copy-start(s32[2,8]{1,0:T(2,128)} %param.11) | copy-start | bytes 196
  7.2 220.5 %all-reduce.2.cloned.1.call-start = ((), (), s32[]{:S(2)}) async-start(), calls=%async_computation | async-start | bytes 6291456 | tf_op jit(solution)/shard_map/psum | solution.py:48
  13.5 37.0 %collective-permute-start = (bf16[2,4,384,512]{3,2,1,0:T(8,128)(2,1)}, bf16[2,4,384,512]{3,2,1,0:T(8,128)(2,1)}, u32[]{:S(2)}, u32[]{:S(2)}) collective-permute-start(bf16[2,4,384,512]{3,2,1,0:T(8,128)(2,1)} %get-tuple-element.8), channel_id=1, source_target_pairs={{0,8},{8,16},{16,24},{24,32},{32,40},{40,48},{48,56},{56,64},{64,7... | collective-permute-start | bytes 9437192 | tf_op jit(solution)/shard_map/ppermute | solution.py:17
  13.5 37.0 %collective-permute-start.1 = (bf16[2,4,384,512]{3,2,1,0:T(8,128)(2,1)}, bf16[2,4,384,512]{3,2,1,0:T(8,128)(2,1)}, u32[]{:S(2)}, u32[]{:S(2)}) collective-permute-start(bf16[2,4,384,512]{3,2,1,0:T(8,128)(2,1)} %get-tuple-element.9), channel_id=1, source_target_pairs={{8,0},{16,8},{24,16},{32,24},{40,32},{48,40},{56,48},{64,56},{72,6... | collective-permute-start | bytes 9437192 | tf_op jit(solution)/shard_map/ppermute | solution.py:19
  95.9 144.1 %collective-permute-start.2 = (bf16[8,384,512]{1,2,0:T(8,128)(2,1)}, bf16[8,384,512]{1,2,0:T(8,128)(2,1)}, u32[]{:S(2)}, u32[]{:S(2)}) collective-permute-start(bf16[8,384,512]{1,2,0:T(8,128)(2,1)} %bitcast.25), channel_id=1, source_target_pairs={{0,1},{1,2},{2,3},{3,4},{4,5},{5,6},{6,7},{8,9},{9,10},{10,11},{11... | collective-permute-start | bytes 9437192 | tf_op jit(solution)/shard_map/ppermute | solution.py:29
  240.0 2.8 %copy-start.1 = (bf16[1,8,384,512]{2,3,1,0:T(8,128)(2,1)S(1)}, bf16[1,8,384,512]{2,3,1,0:T(8,128)(2,1)}, u32[]{:S(2)}) copy-start(bf16[1,8,384,512]{2,3,1,0:T(8,128)(2,1)} %copy.23) | copy-start | bytes 9437188
Sparse Core Ops, SparseCore 0:
  85.2 142.4 all-reduce.1
where the time goes:
time: 264 us; the launch traced here: 262 us
  waiting for transfers between devices  159 us (60%)
  local copies, waits for them, and re-layouts  47.1 us (18%)
  matrix products  20.2 us (8%)
  other arithmetic  16.4 us (6%)
  between operations  14.1 us (5%)
  starting transfers between devices  5.26 us (2%)
    psum x1, waiting for transfers between devices, shards(): lax.psum(partial_field.astype(jnp.bfloat16), 'lag').astype(jnp.float32)  124 us
    ppermute x1, waiting for transfers between devices, padded(): lax.ppermute(tail, axis, [(i, (i + 1) % count) for i in range(count)])  35 us
    unnamed x12, local copies, waits for them, and re-layouts  23.2 us
    dot_general x1, matrix products, shards(): jnp.einsum('lbsij,lbsjr->bir', lag_blocks, sources, preferred_element_typ...  12.6 us
    gather x3, local copies, waits for them, and re-layouts, pick_sources(): return window[source_index]  11.6 us
    concatenate x1, other arithmetic, padded(): jnp.concatenate([lax.ppermute(tail, axis, [(i, (i + 1) % count) for i in...  10.5 us
    dot_general x1, matrix products, shards(): jnp.einsum('bij,bjr->bir', self_inverse, residual, preferred_element_type...  7.62 us
    slice x1, local copies, waits for them, and re-layouts, padded(): lax.slice_in_dim(cells, cells.shape[dim] - width, cells.shape[dim], axis=...  6.25 us
  transfers between devices with their start and end apart: 4, of which 2 were waited for; matrix products, arithmetic and copies ran while one was open for 11% of the time, Pallas kernels for 0%

commit v1 on v0

v1 whole, which is shorter than its diff:
```python
import jax
import jax.numpy as jnp
from jax import lax
from jax.experimental import pallas as pl
from jax.experimental.pallas import tpu as pltpu
from jax.sharding import PartitionSpec as P

EDGE = 4


def term_kernel(src_ref, cnt_ref, a_ref, l0, m0, r0, l1, m1, r1, out_ref, acc_ref):
    b = pl.program_id(0)
    l = pl.program_id(1)
    blocks = pl.num_programs(0)

    @pl.when(l == 0)
    def _():
        acc_ref[...] = jnp.zeros_like(acc_ref)

    cnt = cnt_ref[l, b]
    for s, (lf, md, rt) in enumerate(((l0, m0, r0), (l1, m1, r1))):
        w = src_ref[l, b, s]
        live = s < cnt
        for ref, cond in ((lf, w < EDGE), (md, (w >= EDGE) & (w < EDGE + blocks)), (rt, w >= EDGE + blocks)):
            @pl.when(live & cond)
            def _():
                acc_ref[...] += jnp.dot(a_ref[s], ref[...], preferred_element_type=jnp.float32)

    @pl.when(l == pl.num_programs(1) - 1)
    def _():
        out_ref[...] = acc_ref[...].astype(out_ref.dtype)


def lag_partial(history, left, right, lag_blocks, pattern, live_counts):
    lags, blocks, vec, ex = history.shape
    slots = lag_blocks.shape[2]
    window = jnp.arange(blocks, dtype=jnp.int32)[None, :, None] + pattern

    def local_spec(s):
        return pl.BlockSpec((None, None, vec, ex), lambda b, l, src, cnt: (l, jnp.clip(src[l, b, s] - EDGE, 0, blocks - 1), 0, 0))

    def left_spec(s):
        return pl.BlockSpec((None, None, vec, ex), lambda b, l, src, cnt: (l, jnp.clip(src[l, b, s], 0, EDGE - 1), 0, 0))

    def right_spec(s):
        return pl.BlockSpec((None, None, vec, ex), lambda b, l, src, cnt: (l, jnp.clip(src[l, b, s] - EDGE - blocks, 0, EDGE - 1), 0, 0))

    in_specs = [pl.BlockSpec((None, None, slots, vec, vec), lambda b, l, src, cnt: (l, b, 0, 0, 0))]
    operands = [lag_blocks]
    for s in range(slots):
        in_specs += [left_spec(s), local_spec(s), right_spec(s)]
        operands += [left, history, right]
    grid_spec = pltpu.PrefetchScalarGridSpec(
        num_scalar_prefetch=2,
        grid=(blocks, lags),
        in_specs=in_specs,
        out_specs=pl.BlockSpec((None, vec, ex), lambda b, l, src, cnt: (b, 0, 0)),
        scratch_shapes=[pltpu.VMEM((vec, ex), jnp.float32)],
    )
    flops = 2 * lags * blocks * slots * vec * vec * ex
    moved = 2 * (lag_blocks.size + slots * history.size + blocks * vec * ex)
    return pl.pallas_call(
        term_kernel,
        grid_spec=grid_spec,
        out_shape=jax.ShapeDtypeStruct((blocks, vec, ex), jnp.bfloat16),
        cost_estimate=pl.CostEstimate(flops=flops, transcendentals=0, bytes_accessed=moved),
    )(window, live_counts, *operands)


def shifted_by(array, axis, by):
    count = lax.axis_size(axis)
    return lax.ppermute(array, axis, [(i, (i + by) % count) for i in range(count)])


def passed_along(array, axis, by):
    length = lax.axis_size(axis)
    pairs = [(i, i + by) for i in range(length) if 0 <= i + by < length]
    return lax.ppermute(array, axis, pairs)


def shards(history, lag_blocks, self_inverse, excitation, pattern, live_counts):
    blocks_here = history.shape[1]
    carried = passed_along(history[-1], "lag", 1)
    left = shifted_by(history[:, blocks_here - EDGE:], "tile", 1)
    right = shifted_by(history[:, :EDGE], "tile", -1)
    live = jnp.minimum(live_counts, lag_blocks.shape[2])
    partial = lag_partial(history, left, right, lag_blocks, pattern, live)

    n_lag = lax.axis_size("lag")
    me = lax.axis_index("lag")
    field = lax.dynamic_index_in_dim(partial, me, 0, keepdims=False).astype(jnp.float32)
    for k in range(1, n_lag):
        piece = lax.dynamic_index_in_dim(partial, (me + k) % n_lag, 0, keepdims=False)
        field = field + shifted_by(piece, "lag", k).astype(jnp.float32)
    mine = lax.dynamic_index_in_dim(excitation, me, 0, keepdims=False)
    residual = (mine - field).astype(jnp.bfloat16)
    inverse = lax.dynamic_index_in_dim(self_inverse, me, 0, keepdims=False)
    block = jnp.dot(inverse, residual, preferred_element_type=jnp.float32).astype(jnp.bfloat16)

    gathered = [block] + [shifted_by(block, "lag", k) for k in range(1, n_lag)]
    ordered = jnp.stack(gathered[::-1])
    traction = jnp.roll(ordered, me + 1, axis=0)

    newest = jnp.where(me == 0, traction, carried)
    shifted_history = jnp.concatenate([newest[None], history[:-1]], axis=0)
    return (traction, shifted_history)


def solution(mesh):
    in_specs = (
        P("lag", "tile", None, None),
        P("lag", "tile", None, None, None),
        P("tile", None, None),
        P("tile", None, None),
        P("lag", "tile", None),
        P("lag", "tile"),
    )
    out_specs = (P("tile", None, None), P("lag", "tile", None, None))
    return jax.shard_map(shards, mesh=mesh, in_specs=in_specs, out_specs=out_specs, check_vma=False)
```

time: 264 us -> 251 us (0.951)
  local copies, waits for them, and re-layouts: 47.1 us -> 16.5 us
  Pallas kernels: 0 us -> 27.4 us
  starting transfers between devices: 5.26 us -> 23.6 us
  matrix products: 20.2 us -> 2.63 us
  between operations: 14.1 us -> 0.86 us
  waiting for transfers between devices: 159 us -> 168 us
  other arithmetic: 16.4 us -> 8.54 us
    ppermute x2 -> x16, waiting for transfers between devices: 35 us -> 168 us  [shifted_by(): lax.ppermute(array, axis, [(i, (i + by) % count) for i in range(count)])]
    psum x1 -> x0, waiting for transfers between devices: 124 us -> none  [shards(): lax.psum(partial_field.astype(jnp.bfloat16), 'lag').astype(jnp.float32)]
    pallas_call x0 -> x1, Pallas kernels: none -> 27.4 us  [lag_partial(): pl.pallas_call(term_kernel, grid_spec=grid_spec, out_shape=jax.ShapeDtype...]
    unnamed x12 -> x26, local copies, waits for them, and re-layouts: 23.2 us -> 1.29 us
    ppermute x2 -> x16, starting transfers between devices: 1.75 us -> 21.3 us  [shifted_by(): lax.ppermute(array, axis, [(i, (i + by) % count) for i in range(count)])]
    dot_general x2 -> x1, matrix products: 20.2 us -> 2.63 us  [shards(): jnp.dot(inverse, residual, preferred_element_type=jnp.float32)]
    gather x3 -> x0, local copies, waits for them, and re-layouts: 11.6 us -> none  [pick_sources(): return window[source_index]]
    concatenate x1 -> x0, other arithmetic: 10.5 us -> none  [padded(): jnp.concatenate([lax.ppermute(tail, axis, [(i, (i + 1) % count) for i in...]
  transfers between devices with their start and end apart: 4 -> 17, of which waited for: 2 -> 10; matrix products, arithmetic and copies ran while one was open for 11% -> 3% of each run, Pallas kernels for 0% -> 0%
where the time goes in v1:
time: 251 us; the launch traced here: 248 us
  waiting for transfers between devices  168 us (67%)
  Pallas kernels  27.4 us (11%)
  starting transfers between devices  23.6 us (9%)
  local copies, waits for them, and re-layouts  16.5 us (7%)
  other arithmetic  8.54 us (3%)
  matrix products  2.63 us (1%)
    ppermute x16, waiting for transfers between devices, shifted_by(): lax.ppermute(array, axis, [(i, (i + by) % count) for i in range(count)])  168 us
    pallas_call x1, Pallas kernels, lag_partial(): pl.pallas_call(term_kernel, grid_spec=grid_spec, out_shape=jax.ShapeDtype...  27.4 us
    ppermute x16, starting transfers between devices, shifted_by(): lax.ppermute(array, axis, [(i, (i + by) % count) for i in range(count)])  21.3 us
    slice x1, local copies, waits for them, and re-layouts, shards(): right = shifted_by(history[:, :EDGE], 'tile', -1)  6.25 us
    slice x1, local copies, waits for them, and re-layouts, shards(): shifted_history = jnp.concatenate([newest[None], history[:-1]], axis=0)  6.1 us
  transfers between devices with their start and end apart: 17, of which 10 were waited for; matrix products, arithmetic and copies ran while one was open for 3% of the time, Pallas kernels for 0%

profile of v1, /device:TPU:14, one launch (start us, length us, event | category | flops | bytes accessed | tf_op | source)
XLA Modules:
  0.0 247.8 jit_solution(6544004500573716159)
XLA Ops:
  0.6 0.0 copy-start
  0.6 0.0 copy-start.3
  0.7 0.0 copy-start.4
  0.7 6.2 %fusion.15 = (bf16[2,4,384,512]{3,2,1,0:T(8,128)(2,1)}, bf16[2,4,384,512]{3,2,1,0:T(8,128)(2,1)}) fusion(bf16[2,8,384,512]{3,2,1,0:T(8,128)(2,1)} %m1.1), kind=kLoop, calls=%fused_computation.45 | loop fusion | bytes 12582912 | tf_op jit(solution)/shard_map/slice | solution.py:85
  6.9 0.3 collective-permute-start.1
  7.2 0.2 collective-permute-start
  7.4 0.0 copy-done.3
  7.4 0.1 copy.8
  7.5 0.0 copy-done.4
  7.5 0.6 broadcast_minimum_fusion.cnt_ref
  8.1 0.6 iota_add_fusion.src_ref
  8.7 33.6 %collective-permute-done.1.r0.r1 = bf16[2,4,384,512]{3,2,1,0:T(8,128)(2,1)} collective-permute-done((bf16[2,4,384,512]{3,2,1,0:T(8,128)(2,1)}, bf16[2,4,384,512]{3,2,1,0:T(8,128)(2,1)}, u32[]{:S(2)}, u32[]{:S(2)}) %collective-permute-start.1) | collective-permute-done | bytes 3145760 | tf_op jit(solution)/shard_map/ppermute | solution.py:72
  42.3 1.9 collective-permute-done.l0.l1
  44.2 27.4 %shard_map.77 = bf16[8,384,512]{2,1,0:T(8,128)(2,1)} custom-call(s32[2,8,2]{2,1,0:T(8,128)} %iota_add_fusion.src_ref, s32[2,8]{1,0:T(2,128)} %broadcast_minimum_fusion.cnt_ref, bf16[2,8,2,384,384]{4,3,2,1,0:T(8,128)(2,1)} %a_ref.1, bf16[2,4,384,512]{3,2,1,0:T(8,128)(2,1)} %collective-permute-done.l0.l1, bf16[2,8,384,512]{3,2,1,0:T(8,128)(2,1)} %m1.1, ...), custom_call_target="tpu_custom_call" | custom-call | flops 4831838208 | bytes 25165824 | tf_op jit(solution)/shard_map/pallas_call | solution.py:62
  71.6 2.8 %dynamic-slice_bitcast_fusion.6 = (bf16[384,512]{1,0:T(8,128)(2,1)S(1)}, bf16[384,512]{1,0:T(8,128)(2,1)S(1)}, bf16[384,512]{1,0:T(8,128)(2,1)}, bf16[384,512]{1...) fusion(bf16[8,384,512]{2,1,0:T(8,128)(2,1)} %shard_map.77, ...), kind=kLoop, calls=%fused_computation.36 | loop fusion | bytes 5505052 | tf_op jit(solution)/shard_map/jit(dynamic_index_in_dim)/squeeze | solution.py:93
  74.4 1.7 collective-permute-start.2
  76.1 0.4 collective-permute-start.8
  76.4 2.8 %collective-permute-start.7 = (bf16[384,512]{1,0:T(8,128)(2,1)}, bf16[384,512]{1,0:T(8,128)(2,1)}, u32[]{:S(2)}, u32[]{:S(2)}) collective-permute-start(bf16[384,512]{1,0:T(8,128)(2,1)} %get-tuple-element.10), channel_id=1, source_target_pairs={{0,6},{1,7},{2,0},{3,1},{4,2},{5,3},{6,4},{7,5},{8,14},{9,15},{10,... | collective-permute-start | bytes 1179656 | tf_op jit(solution)/shard_map/ppermute | solution.py:72
  79.3 2.2 collective-permute-start.6
  81.4 0.0 collective-permute-start.5
  81.4 2.6 %collective-permute-done.2 = bf16[384,512]{1,0:T(8,128)(2,1)S(1)} collective-permute-done((bf16[384,512]{1,0:T(8,128)(2,1)S(1)}, bf16[384,512]{1,0:T(8,128)(2,1)S(1)}, u32[]{:S(2)}, u32[]{:S(2)}) %collective-permute-start.2) | collective-permute-done | bytes 393248 | tf_op jit(solution)/shard_map/ppermute | solution.py:72
  84.0 3.9 %collective-permute-start.4 = (bf16[384,512]{1,0:T(8,128)(2,1)S(1)}, bf16[384,512]{1,0:T(8,128)(2,1)}, u32[]{:S(2)}, u32[]{:S(2)}) collective-permute-start(bf16[384,512]{1,0:T(8,128)(2,1)S(1)} %get-tuple-element.13), channel_id=1, source_target_pairs={{0,3},{1,4},{2,5},{3,6},{4,7},{5,0},{6,1},{7,2},{8,11},{9,12},{10,... | collective-permute-start | bytes 1179656 | tf_op jit(solution)/shard_map/ppermute | solution.py:72
  87.9 0.0 collective-permute-done.8
  87.9 0.0 copy-start.2
  87.9 0.8 copy-done.2
  88.7 2.7 %collective-permute-start.3 = (bf16[384,512]{1,0:T(8,128)(2,1)S(1)}, bf16[384,512]{1,0:T(8,128)(2,1)}, u32[]{:S(2)}, u32[]{:S(2)}) collective-permute-start(bf16[384,512]{1,0:T(8,128)(2,1)S(1)} %get-tuple-element.14), channel_id=1, source_target_pairs={{0,2},{1,3},{2,4},{3,5},{4,6},{5,7},{6,0},{7,1},{8,10},{9,11},{10,... | collective-permute-start | bytes 1179656 | tf_op jit(solution)/shard_map/ppermute | solution.py:72
  91.4 3.5 %collective-permute-done.7 = bf16[384,512]{1,0:T(8,128)(2,1)} collective-permute-done((bf16[384,512]{1,0:T(8,128)(2,1)}, bf16[384,512]{1,0:T(8,128)(2,1)}, u32[]{:S(2)}, u32[]{:S(2)}) %collective-permute-start.7) | collective-permute-done | bytes 393248 | tf_op jit(solution)/shard_map/ppermute | solution.py:72
  94.8 12.1 %collective-permute-done.6 = bf16[384,512]{1,0:T(8,128)(2,1)} collective-permute-done((bf16[384,512]{1,0:T(8,128)(2,1)}, bf16[384,512]{1,0:T(8,128)(2,1)}, u32[]{:S(2)}, u32[]{:S(2)}) %collective-permute-start.6) | collective-permute-done | bytes 393248 | tf_op jit(solution)/shard_map/ppermute | solution.py:72
  107.0 0.0 collective-permute-done.5
  107.0 0.8 collective-permute-done.4
  107.7 9.9 %collective-permute-done.3 = bf16[384,512]{1,0:T(8,128)(2,1)} collective-permute-done((bf16[384,512]{1,0:T(8,128)(2,1)S(1)}, bf16[384,512]{1,0:T(8,128)(2,1)}, u32[]{:S(2)}, u32[]{:S(2)}) %collective-permute-start.3) | collective-permute-done | bytes 393248 | tf_op jit(solution)/shard_map/ppermute | solution.py:72
  117.6 0.0 copy-done
  117.7 2.6 %convolution_convert_fusion = bf16[384,512]{1,0:T(8,128)(2,1)S(1)} fusion(bf16[384,512]{1,0:T(8,128)(2,1)} %copy-done.2, bf16[384,512]{1,0:T(8,128)(2,1)} %collective-permute-done.7, bf16[384,512]{1,0:T(8,128)(2,1)} %collective-permute-done.6, bf16[384,512]{1,0:T(8,128)(2,1)} %collective-permute-done.5, bf16[384,512]{1,0:T(8,128)(2,1)} %collective-permute-done.4, ...), kind=kOutput, calls=%fused_computation.3 | convolution fusion | flops 154533888 | bytes 4621312 | tf_op jit(solution)/shard_map/dot_general | solution.py:98
  120.3 0.1 collective-permute-start.9
  120.4 1.5 collective-permute-start.10
  121.9 6.1 %fusion.14 = (bf16[1,8,384,512]{3,2,1,0:T(8,128)(2,1)}, bf16[8,384,512]{2,1,0:T(8,128)(2,1)}) fusion(bf16[2,8,384,512]{3,2,1,0:T(8,128)(2,1)} %m1.1), kind=kLoop, calls=%fused_computation.44 | loop fusion | bytes 12582912 | tf_op jit(solution)/shard_map/slice | solution.py:105
  128.0 2.4 collective-permute-start.16
  130.4 2.2 collective-permute-start.15
  132.6 3.2 %collective-permute-start.14 = (bf16[384,512]{1,0:T(8,128)(2,1)S(1)}, bf16[384,512]{1,0:T(8,128)(2,1)S(1)}, u32[]{:S(2)}, u32[]{:S(2)}) collective-permute-start(bf16[384,512]{1,0:T(8,128)(2,1)S(1)} %convolution_convert_fusion), channel_id=1, source_target_pairs={{0,2},{1,3},{2,4},{3,5},{4,6},{5,7},{6,0},{7,1},{8,10},{9,11},{10,... | collective-permute-start | bytes 1179656 | tf_op jit(solution)/shard_map/ppermute | solution.py:72
  135.9 0.0 collective-permute-done.9
  135.9 0.1 collective-permute-start.11
  136.0 5.2 %collective-permute-done.10 = bf16[384,512]{1,0:T(8,128)(2,1)S(1)} collective-permute-done((bf16[384,512]{1,0:T(8,128)(2,1)S(1)}, bf16[384,512]{1,0:T(8,128)(2,1)S(1)}, u32[]{:S(2)}, u32[]{:S(2)}) %collective-permute-start.10) | collective-permute-done | bytes 393248 | tf_op jit(solution)/shard_map/ppermute | solution.py:72
  141.2 0.0 collective-permute-start.12
  141.2 86.0 %collective-permute-done.11 = bf16[384,512]{1,0:T(8,128)(2,1)S(1)} collective-permute-done((bf16[384,512]{1,0:T(8,128)(2,1)S(1)}, bf16[384,512]{1,0:T(8,128)(2,1)S(1)}, u32[]{:S(2)}, u32[]{:S(2)}) %collective-permute-start.11) | collective-permute-done | bytes 393248 | tf_op jit(solution)/shard_map/ppermute | solution.py:72
  227.3 0.0 collective-permute-start.13
  227.3 0.0 collective-permute-done.12
  227.3 12.6 %collective-permute-done.13 = bf16[384,512]{1,0:T(8,128)(2,1)S(1)} collective-permute-done((bf16[384,512]{1,0:T(8,128)(2,1)S(1)}, bf16[384,512]{1,0:T(8,128)(2,1)S(1)}, u32[]{:S(2)}, u32[]{:S(2)}) %collective-permute-start.13) | collective-permute-done | bytes 393248 | tf_op jit(solution)/shard_map/ppermute | solution.py:72
  239.9 0.0 collective-permute-done.14
  240.0 0.0 collective-permute-done.15
  240.4 0.0 copy-start.1
  240.4 0.0 collective-permute-done.16
  240.4 4.1 %select_bitcast_fusion = (bf16[1,8,384,512]{3,2,1,0:T(8,128)(2,1)S(1)}, bf16[8,384,512]{2,1,0:T(8,128)(2,1)}) fusion(bf16[8,384,512]{2,1,0:T(8,128)(2,1)} %collective-permute-done.16, pred[]{:T(512)S(6)} %eq.14, bf16[16,384,512]{2,1,0:T(8,128)(2,1)S(1)} %bitcast_dynamic-update-slice_fusion.1, s32[]{:T(128)S(6)} %select_n.93), kind=kLoop, calls=%fused_computation.1 | loop fusion | flops 1572864 | bytes 12582917 | tf_op jit(solution)/shard_map/broadcast_in_dim | solution.py:105
  244.5 0.0 copy-done.1
  244.5 3.2 %pad_maximum_fusion = bf16[2,8,384,512]{3,2,1,0:T(8,128)(2,1)} fusion(bf16[1,8,384,512]{3,2,1,0:T(8,128)(2,1)S(1)} %copy-done.1, bf16[1,8,384,512]{3,2,1,0:T(8,128)(2,1)S(1)} %get-tuple-element.2), kind=kLoop, calls=%fused_computation | loop fusion | flops 3145728 | bytes 12582912 | tf_op jit(solution)/shard_map/concatenate | solution.py:105
  (16 shorter events, 0.4 us)
Async XLA Ops:
  0.6 117.0 %copy-start = (bf16[8,384,384]{2,1,0:T(8,128)(2,1)S(1)}, bf16[8,384,384]{2,1,0:T(8,128)(2,1)}, u32[]{:S(2)}) copy-start(bf16[8,384,384]{2,1,0:T(8,128)(2,1)} %param.8) | copy-start | bytes 7077892
  0.6 6.8 %copy-start.3 = (s32[2,8,2]{1,2,0:T(2,128)S(1)}, s32[2,8,2]{1,2,0:T(2,128)}, u32[]{:S(2)}) copy-start(s32[2,8,2]{1,2,0:T(2,128)} %param.10) | copy-start | bytes 388
  0.7 6.9 %copy-start.4 = (s32[2,8]{1,0:T(2,128)S(1)}, s32[2,8]{1,0:T(2,128)}, u32[]{:S(2)}) copy-start(s32[2,8]{1,0:T(2,128)} %param.11) | copy-start | bytes 196
  6.9 35.4 %collective-permute-start.1 = (bf16[2,4,384,512]{3,2,1,0:T(8,128)(2,1)}, bf16[2,4,384,512]{3,2,1,0:T(8,128)(2,1)}, u32[]{:S(2)}, u32[]{:S(2)}) collective-permute-start(bf16[2,4,384,512]{3,2,1,0:T(8,128)(2,1)} %get-tuple-element.6), channel_id=1, source_target_pairs={{0,120},{8,0},{16,8},{24,16},{32,24},{40,32},{48,40},{56,48},{64,5... | collective-permute-start | bytes 9437192 | tf_op jit(solution)/shard_map/ppermute | solution.py:72
  7.2 37.0 %collective-permute-start = (bf16[2,4,384,512]{3,2,1,0:T(8,128)(2,1)}, bf16[2,4,384,512]{3,2,1,0:T(8,128)(2,1)}, u32[]{:S(2)}, u32[]{:S(2)}) collective-permute-start(bf16[2,4,384,512]{3,2,1,0:T(8,128)(2,1)} %get-tuple-element.7), channel_id=1, source_target_pairs={{0,8},{8,16},{16,24},{24,32},{32,40},{40,48},{48,56},{56,64},{64,7... | collective-permute-start | bytes 9437192 | tf_op jit(solution)/shard_map/ppermute | solution.py:72
  74.4 9.6 %collective-permute-start.2 = (bf16[384,512]{1,0:T(8,128)(2,1)S(1)}, bf16[384,512]{1,0:T(8,128)(2,1)S(1)}, u32[]{:S(2)}, u32[]{:S(2)}) collective-permute-start(bf16[384,512]{1,0:T(8,128)(2,1)S(1)} %get-tuple-element.8), channel_id=1, source_target_pairs={{0,1},{1,2},{2,3},{3,4},{4,5},{5,6},{6,7},{7,0},{8,9},{9,10},{10,1... | collective-permute-start | bytes 1179656 | tf_op jit(solution)/shard_map/ppermute | solution.py:72
  76.1 11.8 %collective-permute-start.8 = (bf16[384,512]{1,0:T(8,128)(2,1)S(1)}, bf16[384,512]{1,0:T(8,128)(2,1)S(1)}, u32[]{:S(2)}, u32[]{:S(2)}) collective-permute-start(bf16[384,512]{1,0:T(8,128)(2,1)S(1)} %get-tuple-element.9), channel_id=1, source_target_pairs={{0,7},{1,0},{2,1},{3,2},{4,3},{5,4},{6,5},{7,6},{8,15},{9,8},{10,9... | collective-permute-start | bytes 1179656 | tf_op jit(solution)/shard_map/ppermute | solution.py:72
  76.4 18.4 %collective-permute-start.7 = (bf16[384,512]{1,0:T(8,128)(2,1)}, bf16[384,512]{1,0:T(8,128)(2,1)}, u32[]{:S(2)}, u32[]{:S(2)}) collective-permute-start(bf16[384,512]{1,0:T(8,128)(2,1)} %get-tuple-element.10), channel_id=1, source_target_pairs={{0,6},{1,7},{2,0},{3,1},{4,2},{5,3},{6,4},{7,5},{8,14},{9,15},{10,... | collective-permute-start | bytes 1179656 | tf_op jit(solution)/shard_map/ppermute | solution.py:72
  79.3 27.7 %collective-permute-start.6 = (bf16[384,512]{1,0:T(8,128)(2,1)}, bf16[384,512]{1,0:T(8,128)(2,1)}, u32[]{:S(2)}, u32[]{:S(2)}) collective-permute-start(bf16[384,512]{1,0:T(8,128)(2,1)} %get-tuple-element.11), channel_id=1, source_target_pairs={{0,5},{1,6},{2,7},{3,0},{4,1},{5,2},{6,3},{7,4},{8,13},{9,14},{10,... | collective-permute-start | bytes 1179656 | tf_op jit(solution)/shard_map/ppermute | solution.py:72
  81.4 25.5 %collective-permute-start.5 = (bf16[384,512]{1,0:T(8,128)(2,1)}, bf16[384,512]{1,0:T(8,128)(2,1)}, u32[]{:S(2)}, u32[]{:S(2)}) collective-permute-start(bf16[384,512]{1,0:T(8,128)(2,1)} %get-tuple-element.12), channel_id=1, source_target_pairs={{0,4},{1,5},{2,6},{3,7},{4,0},{5,1},{6,2},{7,3},{8,12},{9,13},{10,... | collective-permute-start | bytes 1179656 | tf_op jit(solution)/shard_map/ppermute | solution.py:72
  84.0 23.7 %collective-permute-start.4 = (bf16[384,512]{1,0:T(8,128)(2,1)S(1)}, bf16[384,512]{1,0:T(8,128)(2,1)}, u32[]{:S(2)}, u32[]{:S(2)}) collective-permute-start(bf16[384,512]{1,0:T(8,128)(2,1)S(1)} %get-tuple-element.13), channel_id=1, source_target_pairs={{0,3},{1,4},{2,5},{3,6},{4,7},{5,0},{6,1},{7,2},{8,11},{9,12},{10,... | collective-permute-start | bytes 1179656 | tf_op jit(solution)/shard_map/ppermute | solution.py:72
  87.9 0.8 copy-start.2
  88.7 29.0 %collective-permute-start.3 = (bf16[384,512]{1,0:T(8,128)(2,1)S(1)}, bf16[384,512]{1,0:T(8,128)(2,1)}, u32[]{:S(2)}, u32[]{:S(2)}) collective-permute-start(bf16[384,512]{1,0:T(8,128)(2,1)S(1)} %get-tuple-element.14), channel_id=1, source_target_pairs={{0,2},{1,3},{2,4},{3,5},{4,6},{5,7},{6,0},{7,1},{8,10},{9,11},{10,... | collective-permute-start | bytes 1179656 | tf_op jit(solution)/shard_map/ppermute | solution.py:72
  120.3 15.6 %collective-permute-start.9 = (bf16[384,512]{1,0:T(8,128)(2,1)S(1)}, bf16[384,512]{1,0:T(8,128)(2,1)S(1)}, u32[]{:S(2)}, u32[]{:S(2)}) collective-permute-start(bf16[384,512]{1,0:T(8,128)(2,1)S(1)} %convolution_convert_fusion), channel_id=1, source_target_pairs={{0,7},{1,0},{2,1},{3,2},{4,3},{5,4},{6,5},{7,6},{8,15},{9,8},{10,9... | collective-permute-start | bytes 1179656 | tf_op jit(solution)/shard_map/ppermute | solution.py:72
  120.4 20.8 %collective-permute-start.10 = (bf16[384,512]{1,0:T(8,128)(2,1)S(1)}, bf16[384,512]{1,0:T(8,128)(2,1)S(1)}, u32[]{:S(2)}, u32[]{:S(2)}) collective-permute-start(bf16[384,512]{1,0:T(8,128)(2,1)S(1)} %convolution_convert_fusion), channel_id=1, source_target_pairs={{0,6},{1,7},{2,0},{3,1},{4,2},{5,3},{6,4},{7,5},{8,14},{9,15},{10,... | collective-permute-start | bytes 1179656 | tf_op jit(solution)/shard_map/ppermute | solution.py:72
  128.0 112.4 %collective-permute-start.16 = (bf16[8,384,512]{2,1,0:T(8,128)(2,1)}, bf16[8,384,512]{2,1,0:T(8,128)(2,1)}, u32[]{:S(2)}, u32[]{:S(2)}) collective-permute-start(bf16[8,384,512]{2,1,0:T(8,128)(2,1)} %get-tuple-element.5), channel_id=1, source_target_pairs={{0,1},{1,2},{2,3},{3,4},{4,5},{5,6},{6,7},{8,9},{9,10},{10,11},{11... | collective-permute-start | bytes 9437192 | tf_op jit(solution)/shard_map/ppermute | solution.py:78
  130.4 109.6 %collective-permute-start.15 = (bf16[384,512]{1,0:T(8,128)(2,1)S(1)}, bf16[384,512]{1,0:T(8,128)(2,1)S(1)}, u32[]{:S(2)}, u32[]{:S(2)}) collective-permute-start(bf16[384,512]{1,0:T(8,128)(2,1)S(1)} %convolution_convert_fusion), channel_id=1, source_target_pairs={{0,1},{1,2},{2,3},{3,4},{4,5},{5,6},{6,7},{7,0},{8,9},{9,10},{10,1... | collective-permute-start | bytes 1179656 | tf_op jit(solution)/shard_map/ppermute | solution.py:72
  132.6 107.3 %collective-permute-start.14 = (bf16[384,512]{1,0:T(8,128)(2,1)S(1)}, bf16[384,512]{1,0:T(8,128)(2,1)S(1)}, u32[]{:S(2)}, u32[]{:S(2)}) collective-permute-start(bf16[384,512]{1,0:T(8,128)(2,1)S(1)} %convolution_convert_fusion), channel_id=1, source_target_pairs={{0,2},{1,3},{2,4},{3,5},{4,6},{5,7},{6,0},{7,1},{8,10},{9,11},{10,... | collective-permute-start | bytes 1179656 | tf_op jit(solution)/shard_map/ppermute | solution.py:72
  135.9 91.4 %collective-permute-start.11 = (bf16[384,512]{1,0:T(8,128)(2,1)S(1)}, bf16[384,512]{1,0:T(8,128)(2,1)S(1)}, u32[]{:S(2)}, u32[]{:S(2)}) collective-permute-start(bf16[384,512]{1,0:T(8,128)(2,1)S(1)} %convolution_convert_fusion), channel_id=1, source_target_pairs={{0,5},{1,6},{2,7},{3,0},{4,1},{5,2},{6,3},{7,4},{8,13},{9,14},{10,... | collective-permute-start | bytes 1179656 | tf_op jit(solution)/shard_map/ppermute | solution.py:72
  141.2 86.1 %collective-permute-start.12 = (bf16[384,512]{1,0:T(8,128)(2,1)S(1)}, bf16[384,512]{1,0:T(8,128)(2,1)S(1)}, u32[]{:S(2)}, u32[]{:S(2)}) collective-permute-start(bf16[384,512]{1,0:T(8,128)(2,1)S(1)} %convolution_convert_fusion), channel_id=1, source_target_pairs={{0,4},{1,5},{2,6},{3,7},{4,0},{5,1},{6,2},{7,3},{8,12},{9,13},{10,... | collective-permute-start | bytes 1179656 | tf_op jit(solution)/shard_map/ppermute | solution.py:72
  227.3 12.7 %collective-permute-start.13 = (bf16[384,512]{1,0:T(8,128)(2,1)S(1)}, bf16[384,512]{1,0:T(8,128)(2,1)S(1)}, u32[]{:S(2)}, u32[]{:S(2)}) collective-permute-start(bf16[384,512]{1,0:T(8,128)(2,1)S(1)} %convolution_convert_fusion), channel_id=1, source_target_pairs={{0,3},{1,4},{2,5},{3,6},{4,7},{5,0},{6,1},{7,2},{8,11},{9,12},{10,... | collective-permute-start | bytes 1179656 | tf_op jit(solution)/shard_map/ppermute | solution.py:72
  240.4 4.1 %copy-start.1 = (bf16[1,8,384,512]{3,2,1,0:T(8,128)(2,1)S(1)}, bf16[1,8,384,512]{3,2,1,0:T(8,128)(2,1)}, u32[]{:S(2)}) copy-start(bf16[1,8,384,512]{3,2,1,0:T(8,128)(2,1)} %get-tuple-element.4) | copy-start | bytes 9437188

commit v2 on v1

--- a/solution.py
+++ b/solution.py
@@ -36,14 +36,24 @@
     slots = lag_blocks.shape[2]
     window = jnp.arange(blocks, dtype=jnp.int32)[None, :, None] + pattern
 
+    def used(src, cnt, l, b, s, lo, hi):
+        w = src[l, b, s]
+        return (s < cnt[l, b]) & (w >= lo) & (w < hi), w - lo
+
+    def source_spec(s, lo, hi, count):
+        def index(b, l, src, cnt):
+            on, at = used(src, cnt, l, b, s, lo, hi)
+            return (jnp.where(on, l, 0), jnp.where(on, jnp.clip(at, 0, count - 1), 0), 0, 0)
+        return pl.BlockSpec((None, None, vec, ex), index)
+
     def local_spec(s):
-        return pl.BlockSpec((None, None, vec, ex), lambda b, l, src, cnt: (l, jnp.clip(src[l, b, s] - EDGE, 0, blocks - 1), 0, 0))
+        return source_spec(s, EDGE, EDGE + blocks, blocks)
 
     def left_spec(s):
-        return pl.BlockSpec((None, None, vec, ex), lambda b, l, src, cnt: (l, jnp.clip(src[l, b, s], 0, EDGE - 1), 0, 0))
+        return source_spec(s, 0, EDGE, EDGE)
 
     def right_spec(s):
-        return pl.BlockSpec((None, None, vec, ex), lambda b, l, src, cnt: (l, jnp.clip(src[l, b, s] - EDGE - blocks, 0, EDGE - 1), 0, 0))
+        return source_spec(s, EDGE + blocks, 2 * EDGE + blocks, EDGE)
 
     in_specs = [pl.BlockSpec((None, None, slots, vec, vec), lambda b, l, src, cnt: (l, b, 0, 0, 0))]
     operands = [lag_blocks]
@@ -85,6 +95,7 @@
     right = shifted_by(history[:, :EDGE], "tile", -1)
     live = jnp.minimum(live_counts, lag_blocks.shape[2])
     partial = lag_partial(history, left, right, lag_blocks, pattern, live)
+    partial, carried = lax.optimization_barrier((partial, carried))
 
     n_lag = lax.axis_size("lag")
     me = lax.axis_index("lag")

time: 251 us -> 224 us (0.89); the launches traced: 248 us -> 223 us
  waiting for transfers between devices: 168 us -> 104 us
  starting transfers between devices: 23.6 us -> 73.6 us
  Pallas kernels: 27.4 us -> 19.9 us
    ppermute x16, waiting for transfers between devices: 168 us -> 87.6 us  [shifted_by(): lax.ppermute(array, axis, [(i, (i + by) % count) for i in range(count)])]
    ppermute x16, starting transfers between devices: 21.3 us -> 70.1 us  [shifted_by(): lax.ppermute(array, axis, [(i, (i + by) % count) for i in range(count)])]
    ppermute x1, waiting for transfers between devices: 0.01 us -> 16.1 us  [passed_along(): return lax.ppermute(array, axis, pairs)]
    pallas_call x1, Pallas kernels: 27.4 us -> 19.9 us  [lag_partial(): pl.pallas_call(term_kernel, grid_spec=grid_spec, out_shape=jax.ShapeDtype...]
    slice x1, local copies, waits for them, and re-layouts: 6.1 us -> 3.34 us  [shards(): shifted_history = jnp.concatenate([newest[None], history[:-1]], axis=0)]
  transfers between devices with their start and end apart: 17 -> 17, of which waited for: 10 -> 8; matrix products, arithmetic and copies ran while one was open for 3% -> 2% of each run, Pallas kernels for 0% -> 9%
where the time goes in v2:
time: 224 us; the launch traced here: 223 us
  waiting for transfers between devices  104 us (46%)
  starting transfers between devices  73.6 us (33%)
  Pallas kernels  19.9 us (9%)
  local copies, waits for them, and re-layouts  14.1 us (6%)
  other arithmetic  8.56 us (4%)
  matrix products  2.64 us (1%)
    ppermute x16, waiting for transfers between devices, shifted_by(): lax.ppermute(array, axis, [(i, (i + by) % count) for i in range(count)])  87.6 us
    ppermute x16, starting transfers between devices, shifted_by(): lax.ppermute(array, axis, [(i, (i + by) % count) for i in range(count)])  70.1 us
    pallas_call x1, Pallas kernels, lag_partial(): pl.pallas_call(term_kernel, grid_spec=grid_spec, out_shape=jax.ShapeDtype...  19.9 us
    ppermute x1, waiting for transfers between devices, passed_along(): return lax.ppermute(array, axis, pairs)  16.1 us
    slice x1, local copies, waits for them, and re-layouts, shards(): right = shifted_by(history[:, :EDGE], 'tile', -1)  6.6 us
  transfers between devices with their start and end apart: 17, of which 8 were waited for; matrix products, arithmetic and copies ran while one was open for 2% of the time, Pallas kernels for 9%

profile of v2, /device:TPU:14, one launch (start us, length us, event | category | flops | bytes accessed | tf_op | source)
XLA Modules:
  0.0 223.4 jit_solution(661756564715710915)
XLA Ops:
  0.6 0.0 copy-start
  0.6 0.0 copy-start.1
  0.7 6.6 %fusion.15 = (bf16[2,4,384,512]{3,2,1,0:T(8,128)(2,1)}, bf16[2,4,384,512]{3,2,1,0:T(8,128)(2,1)}) fusion(bf16[2,8,384,512]{3,2,1,0:T(8,128)(2,1)} %m1.1), kind=kLoop, calls=%fused_computation.45 | loop fusion | bytes 12582912 | tf_op jit(solution)/shard_map/slice | solution.py:95
  7.3 0.3 collective-permute-start.1
  7.5 0.0 copy-start.4
  7.5 0.0 copy-start.5
  7.5 0.2 collective-permute-start
  7.8 0.0 copy-done.1
  7.8 3.3 %fusion.14 = (bf16[1,8,384,512]{3,2,1,0:T(8,128)(2,1)}, bf16[8,384,512]{2,1,0:T(8,128)(2,1)}) fusion(bf16[2,8,384,512]{3,2,1,0:T(8,128)(2,1)S(1)} %copy-done.1), kind=kLoop, calls=%fused_computation.44 | loop fusion | bytes 12582912 | tf_op jit(solution)/shard_map/slice | solution.py:116
  11.1 3.5 %collective-permute-start.2 = (bf16[8,384,512]{2,1,0:T(8,128)(2,1)}, bf16[8,384,512]{2,1,0:T(8,128)(2,1)}, u32[]{:S(2)}, u32[]{:S(2)}) collective-permute-start(bf16[8,384,512]{2,1,0:T(8,128)(2,1)} %get-tuple-element.9), channel_id=1, source_target_pairs={{0,1},{1,2},{2,3},{3,4},{4,5},{5,6},{6,7},{8,9},{9,10},{10,11},{11... | collective-permute-start | bytes 9437192 | tf_op jit(solution)/shard_map/ppermute | solution.py:88
  14.7 0.0 copy-done.4
  14.7 0.1 copy.8
  14.8 0.0 copy-done.5
  14.8 0.6 broadcast_minimum_fusion.cnt_ref
  15.4 0.6 iota_add_fusion.src_ref
  16.0 26.6 %collective-permute-done.1.r0.r1 = bf16[2,4,384,512]{3,2,1,0:T(8,128)(2,1)} collective-permute-done((bf16[2,4,384,512]{3,2,1,0:T(8,128)(2,1)}, bf16[2,4,384,512]{3,2,1,0:T(8,128)(2,1)}, u32[]{:S(2)}, u32[]{:S(2)}) %collective-permute-start.1) | collective-permute-done | bytes 3145760 | tf_op jit(solution)/shard_map/ppermute | solution.py:82
  42.6 1.9 collective-permute-done.l0.l1
  44.5 19.9 %shard_map.77 = bf16[8,384,512]{2,1,0:T(8,128)(2,1)} custom-call(s32[2,8,2]{2,1,0:T(8,128)} %iota_add_fusion.src_ref, s32[2,8]{1,0:T(2,128)} %broadcast_minimum_fusion.cnt_ref, bf16[2,8,2,384,384]{4,3,2,1,0:T(8,128)(2,1)} %a_ref.1, bf16[2,4,384,512]{3,2,1,0:T(8,128)(2,1)} %collective-permute-done.l0.l1, bf16[2,8,384,512]{3,2,1,0:T(8,128)(2,1)} %m1.1, ...), custom_call_target="tpu_custom_call" | custom-call | flops 4831838208 | bytes 25165824 | tf_op jit(solution)/shard_map/pallas_call | solution.py:72
  64.5 16.1 %collective-permute-done.2 = bf16[8,384,512]{2,1,0:T(8,128)(2,1)} collective-permute-done((bf16[8,384,512]{2,1,0:T(8,128)(2,1)}, bf16[8,384,512]{2,1,0:T(8,128)(2,1)}, u32[]{:S(2)}, u32[]{:S(2)}) %collective-permute-start.2) | collective-permute-done | bytes 3145760 | tf_op jit(solution)/shard_map/ppermute | solution.py:88
  80.6 2.8 %dynamic-slice_bitcast_fusion.6 = (bf16[384,512]{1,0:T(8,128)(2,1)S(1)}, bf16[384,512]{1,0:T(8,128)(2,1)S(1)}, bf16[384,512]{1,0:T(8,128)(2,1)}, bf16[384,512]{1...) fusion(bf16[8,384,512]{2,1,0:T(8,128)(2,1)} %shard_map.77, ...), kind=kLoop, calls=%fused_computation.36 | loop fusion | bytes 5505052 | tf_op jit(solution)/shard_map/jit(dynamic_index_in_dim)/squeeze | solution.py:104
  83.4 1.6 collective-permute-start.3
  85.0 0.4 collective-permute-start.9
  85.4 3.6 %collective-permute-start.8 = (bf16[384,512]{1,0:T(8,128)(2,1)}, bf16[384,512]{1,0:T(8,128)(2,1)}, u32[]{:S(2)}, u32[]{:S(2)}) collective-permute-start(bf16[384,512]{1,0:T(8,128)(2,1)} %get-tuple-element.14), channel_id=1, source_target_pairs={{0,6},{1,7},{2,0},{3,1},{4,2},{5,3},{6,4},{7,5},{8,14},{9,15},{10,... | collective-permute-start | bytes 1179656 | tf_op jit(solution)/shard_map/ppermute | solution.py:82
  89.1 33.9 %collective-permute-start.7 = (bf16[384,512]{1,0:T(8,128)(2,1)}, bf16[384,512]{1,0:T(8,128)(2,1)}, u32[]{:S(2)}, u32[]{:S(2)}) collective-permute-start(bf16[384,512]{1,0:T(8,128)(2,1)} %get-tuple-element.15), channel_id=1, source_target_pairs={{0,5},{1,6},{2,7},{3,0},{4,1},{5,2},{6,3},{7,4},{8,13},{9,14},{10,... | collective-permute-start | bytes 1179656 | tf_op jit(solution)/shard_map/ppermute | solution.py:82
  123.0 0.0 collective-permute-start.6
  123.0 0.0 collective-permute-done.3
  123.0 14.3 %collective-permute-start.5 = (bf16[384,512]{1,0:T(8,128)(2,1)S(1)}, bf16[384,512]{1,0:T(8,128)(2,1)}, u32[]{:S(2)}, u32[]{:S(2)}) collective-permute-start(bf16[384,512]{1,0:T(8,128)(2,1)S(1)} %get-tuple-element.17), channel_id=1, source_target_pairs={{0,3},{1,4},{2,5},{3,6},{4,7},{5,0},{6,1},{7,2},{8,11},{9,12},{10,... | collective-permute-start | bytes 1179656 | tf_op jit(solution)/shard_map/ppermute | solution.py:82
  137.3 0.0 collective-permute-done.9
  137.3 0.0 copy-start.3
  137.3 0.8 copy-done.3
  138.1 7.5 %collective-permute-start.4 = (bf16[384,512]{1,0:T(8,128)(2,1)S(1)}, bf16[384,512]{1,0:T(8,128)(2,1)}, u32[]{:S(2)}, u32[]{:S(2)}) collective-permute-start(bf16[384,512]{1,0:T(8,128)(2,1)S(1)} %get-tuple-element.18), channel_id=1, source_target_pairs={{0,2},{1,3},{2,4},{3,5},{4,6},{5,7},{6,0},{7,1},{8,10},{9,11},{10,... | collective-permute-start | bytes 1179656 | tf_op jit(solution)/shard_map/ppermute | solution.py:82
  145.6 0.0 collective-permute-done.8
  145.6 1.1 collective-permute-done.7
  146.7 13.2 %collective-permute-done.6 = bf16[384,512]{1,0:T(8,128)(2,1)} collective-permute-done((bf16[384,512]{1,0:T(8,128)(2,1)}, bf16[384,512]{1,0:T(8,128)(2,1)}, u32[]{:S(2)}, u32[]{:S(2)}) %collective-permute-start.6) | collective-permute-done | bytes 393248 | tf_op jit(solution)/shard_map/ppermute | solution.py:82
  159.9 0.0 collective-permute-done.5
  159.9 0.0 collective-permute-done.4
  159.9 0.0 copy-done
  159.9 2.6 %convolution_convert_fusion = bf16[384,512]{1,0:T(8,128)(2,1)S(1)} fusion(bf16[384,512]{1,0:T(8,128)(2,1)} %copy-done.3, bf16[384,512]{1,0:T(8,128)(2,1)} %collective-permute-done.8, bf16[384,512]{1,0:T(8,128)(2,1)} %collective-permute-done.7, bf16[384,512]{1,0:T(8,128)(2,1)} %collective-permute-done.6, bf16[384,512]{1,0:T(8,128)(2,1)} %collective-permute-done.5, ...), kind=kOutput, calls=%fused_computation.3 | convolution fusion | flops 154533888 | bytes 4621312 | tf_op jit(solution)/shard_map/dot_general | solution.py:109
  162.5 0.1 collective-permute-start.10
  162.6 0.4 collective-permute-start.11
  163.1 2.5 %collective-permute-start.16 = (bf16[384,512]{1,0:T(8,128)(2,1)S(1)}, bf16[384,512]{1,0:T(8,128)(2,1)S(1)}, u32[]{:S(2)}, u32[]{:S(2)}) collective-permute-start(bf16[384,512]{1,0:T(8,128)(2,1)S(1)} %convolution_convert_fusion), channel_id=1, source_target_pairs={{0,1},{1,2},{2,3},{3,4},{4,5},{5,6},{6,7},{7,0},{8,9},{9,10},{10,1... | collective-permute-start | bytes 1179656 | tf_op jit(solution)/shard_map/ppermute | solution.py:82
  165.6 4.0 %collective-permute-start.15 = (bf16[384,512]{1,0:T(8,128)(2,1)S(1)}, bf16[384,512]{1,0:T(8,128)(2,1)S(1)}, u32[]{:S(2)}, u32[]{:S(2)}) collective-permute-start(bf16[384,512]{1,0:T(8,128)(2,1)S(1)} %convolution_convert_fusion), channel_id=1, source_target_pairs={{0,2},{1,3},{2,4},{3,5},{4,6},{5,7},{6,0},{7,1},{8,10},{9,11},{10,... | collective-permute-start | bytes 1179656 | tf_op jit(solution)/shard_map/ppermute | solution.py:82
  169.7 0.0 collective-permute-start.14
  169.7 21.8 %collective-permute-done.10 = bf16[384,512]{1,0:T(8,128)(2,1)S(1)} collective-permute-done((bf16[384,512]{1,0:T(8,128)(2,1)S(1)}, bf16[384,512]{1,0:T(8,128)(2,1)S(1)}, u32[]{:S(2)}, u32[]{:S(2)}) %collective-permute-start.10) | collective-permute-done | bytes 393248 | tf_op jit(solution)/shard_map/ppermute | solution.py:82
  191.5 0.0 collective-permute-start.12
  191.5 0.0 collective-permute-done.11
  191.5 1.1 collective-permute-start.13
  192.6 14.6 %collective-permute-done.12 = bf16[384,512]{1,0:T(8,128)(2,1)S(1)} collective-permute-done((bf16[384,512]{1,0:T(8,128)(2,1)S(1)}, bf16[384,512]{1,0:T(8,128)(2,1)S(1)}, u32[]{:S(2)}, u32[]{:S(2)}) %collective-permute-start.12) | collective-permute-done | bytes 393248 | tf_op jit(solution)/shard_map/ppermute | solution.py:82
  207.3 8.3 %collective-permute-done.13 = bf16[384,512]{1,0:T(8,128)(2,1)S(1)} collective-permute-done((bf16[384,512]{1,0:T(8,128)(2,1)S(1)}, bf16[384,512]{1,0:T(8,128)(2,1)S(1)}, u32[]{:S(2)}, u32[]{:S(2)}) %collective-permute-start.13) | collective-permute-done | bytes 393248 | tf_op jit(solution)/shard_map/ppermute | solution.py:82
  215.6 0.0 collective-permute-done.14
  215.6 0.0 collective-permute-done.15
  215.7 0.0 collective-permute-done.16
  216.1 0.0 copy-start.2
  216.1 4.1 %select_bitcast_fusion = (bf16[1,8,384,512]{3,2,1,0:T(8,128)(2,1)S(1)}, bf16[8,384,512]{2,1,0:T(8,128)(2,1)}) fusion(bf16[8,384,512]{2,1,0:T(8,128)(2,1)} %collective-permute-done.2, pred[]{:T(512)S(6)} %eq.14, bf16[16,384,512]{2,1,0:T(8,128)(2,1)S(1)} %bitcast_dynamic-update-slice_fusion.1, s32[]{:T(128)S(6)} %select_n.93), kind=kLoop, calls=%fused_computation.1 | loop fusion | flops 1572864 | bytes 12582917 | tf_op jit(solution)/shard_map/broadcast_in_dim | solution.py:116
  220.2 0.0 copy-done.2
  220.2 3.2 %pad_maximum_fusion = bf16[2,8,384,512]{3,2,1,0:T(8,128)(2,1)} fusion(bf16[1,8,384,512]{3,2,1,0:T(8,128)(2,1)S(1)} %copy-done.2, bf16[1,8,384,512]{3,2,1,0:T(8,128)(2,1)S(1)} %get-tuple-element.6), kind=kLoop, calls=%fused_computation | loop fusion | flops 3145728 | bytes 12582912 | tf_op jit(solution)/shard_map/concatenate | solution.py:116
  (16 shorter events, 0.4 us)
Async XLA Ops:
  0.6 159.3 %copy-start = (bf16[8,384,384]{2,1,0:T(8,128)(2,1)S(1)}, bf16[8,384,384]{2,1,0:T(8,128)(2,1)}, u32[]{:S(2)}) copy-start(bf16[8,384,384]{2,1,0:T(8,128)(2,1)} %param.8) | copy-start | bytes 7077892
  0.6 7.1 %copy-start.1 = (bf16[2,8,384,512]{3,2,1,0:T(8,128)(2,1)S(1)}, bf16[2,8,384,512]{3,2,1,0:T(8,128)(2,1)}, u32[]{:S(2)}) copy-start(bf16[2,8,384,512]{3,2,1,0:T(8,128)(2,1)} %m1.1) | copy-start | bytes 18874372
  7.3 35.4 %collective-permute-start.1 = (bf16[2,4,384,512]{3,2,1,0:T(8,128)(2,1)}, bf16[2,4,384,512]{3,2,1,0:T(8,128)(2,1)}, u32[]{:S(2)}, u32[]{:S(2)}) collective-permute-start(bf16[2,4,384,512]{3,2,1,0:T(8,128)(2,1)} %get-tuple-element.10), channel_id=1, source_target_pairs={{0,120},{8,0},{16,8},{24,16},{32,24},{40,32},{48,40},{56,48},{64,5... | collective-permute-start | bytes 9437192 | tf_op jit(solution)/shard_map/ppermute | solution.py:82
  7.5 7.2 %copy-start.4 = (s32[2,8,2]{1,2,0:T(2,128)S(1)}, s32[2,8,2]{1,2,0:T(2,128)}, u32[]{:S(2)}) copy-start(s32[2,8,2]{1,2,0:T(2,128)} %param.10) | copy-start | bytes 388
  7.5 7.3 %copy-start.5 = (s32[2,8]{1,0:T(2,128)S(1)}, s32[2,8]{1,0:T(2,128)}, u32[]{:S(2)}) copy-start(s32[2,8]{1,0:T(2,128)} %param.11) | copy-start | bytes 196
  7.5 37.0 %collective-permute-start = (bf16[2,4,384,512]{3,2,1,0:T(8,128)(2,1)}, bf16[2,4,384,512]{3,2,1,0:T(8,128)(2,1)}, u32[]{:S(2)}, u32[]{:S(2)}) collective-permute-start(bf16[2,4,384,512]{3,2,1,0:T(8,128)(2,1)} %get-tuple-element.11), channel_id=1, source_target_pairs={{0,8},{8,16},{16,24},{24,32},{32,40},{40,48},{48,56},{56,64},{64,7... | collective-permute-start | bytes 9437192 | tf_op jit(solution)/shard_map/ppermute | solution.py:82
  11.1 69.5 %collective-permute-start.2 = (bf16[8,384,512]{2,1,0:T(8,128)(2,1)}, bf16[8,384,512]{2,1,0:T(8,128)(2,1)}, u32[]{:S(2)}, u32[]{:S(2)}) collective-permute-start(bf16[8,384,512]{2,1,0:T(8,128)(2,1)} %get-tuple-element.9), channel_id=1, source_target_pairs={{0,1},{1,2},{2,3},{3,4},{4,5},{5,6},{6,7},{8,9},{9,10},{10,11},{11... | collective-permute-start | bytes 9437192 | tf_op jit(solution)/shard_map/ppermute | solution.py:88
  83.4 39.6 %collective-permute-start.3 = (bf16[384,512]{1,0:T(8,128)(2,1)S(1)}, bf16[384,512]{1,0:T(8,128)(2,1)S(1)}, u32[]{:S(2)}, u32[]{:S(2)}) collective-permute-start(bf16[384,512]{1,0:T(8,128)(2,1)S(1)} %get-tuple-element.12), channel_id=1, source_target_pairs={{0,1},{1,2},{2,3},{3,4},{4,5},{5,6},{6,7},{7,0},{8,9},{9,10},{10,1... | collective-permute-start | bytes 1179656 | tf_op jit(solution)/shard_map/ppermute | solution.py:82
  85.0 52.4 %collective-permute-start.9 = (bf16[384,512]{1,0:T(8,128)(2,1)S(1)}, bf16[384,512]{1,0:T(8,128)(2,1)S(1)}, u32[]{:S(2)}, u32[]{:S(2)}) collective-permute-start(bf16[384,512]{1,0:T(8,128)(2,1)S(1)} %get-tuple-element.13), channel_id=1, source_target_pairs={{0,7},{1,0},{2,1},{3,2},{4,3},{5,4},{6,5},{7,6},{8,15},{9,8},{10,9... | collective-permute-start | bytes 1179656 | tf_op jit(solution)/shard_map/ppermute | solution.py:82
  85.4 60.2 %collective-permute-start.8 = (bf16[384,512]{1,0:T(8,128)(2,1)}, bf16[384,512]{1,0:T(8,128)(2,1)}, u32[]{:S(2)}, u32[]{:S(2)}) collective-permute-start(bf16[384,512]{1,0:T(8,128)(2,1)} %get-tuple-element.14), channel_id=1, source_target_pairs={{0,6},{1,7},{2,0},{3,1},{4,2},{5,3},{6,4},{7,5},{8,14},{9,15},{10,... | collective-permute-start | bytes 1179656 | tf_op jit(solution)/shard_map/ppermute | solution.py:82
  89.1 57.7 %collective-permute-start.7 = (bf16[384,512]{1,0:T(8,128)(2,1)}, bf16[384,512]{1,0:T(8,128)(2,1)}, u32[]{:S(2)}, u32[]{:S(2)}) collective-permute-start(bf16[384,512]{1,0:T(8,128)(2,1)} %get-tuple-element.15), channel_id=1, source_target_pairs={{0,5},{1,6},{2,7},{3,0},{4,1},{5,2},{6,3},{7,4},{8,13},{9,14},{10,... | collective-permute-start | bytes 1179656 | tf_op jit(solution)/shard_map/ppermute | solution.py:82
  123.0 36.9 %collective-permute-start.6 = (bf16[384,512]{1,0:T(8,128)(2,1)}, bf16[384,512]{1,0:T(8,128)(2,1)}, u32[]{:S(2)}, u32[]{:S(2)}) collective-permute-start(bf16[384,512]{1,0:T(8,128)(2,1)} %get-tuple-element.16), channel_id=1, source_target_pairs={{0,4},{1,5},{2,6},{3,7},{4,0},{5,1},{6,2},{7,3},{8,12},{9,13},{10,... | collective-permute-start | bytes 1179656 | tf_op jit(solution)/shard_map/ppermute | solution.py:82
  123.0 36.9 %collective-permute-start.5 = (bf16[384,512]{1,0:T(8,128)(2,1)S(1)}, bf16[384,512]{1,0:T(8,128)(2,1)}, u32[]{:S(2)}, u32[]{:S(2)}) collective-permute-start(bf16[384,512]{1,0:T(8,128)(2,1)S(1)} %get-tuple-element.17), channel_id=1, source_target_pairs={{0,3},{1,4},{2,5},{3,6},{4,7},{5,0},{6,1},{7,2},{8,11},{9,12},{10,... | collective-permute-start | bytes 1179656 | tf_op jit(solution)/shard_map/ppermute | solution.py:82
  137.3 0.8 copy-start.3
  138.1 21.8 %collective-permute-start.4 = (bf16[384,512]{1,0:T(8,128)(2,1)S(1)}, bf16[384,512]{1,0:T(8,128)(2,1)}, u32[]{:S(2)}, u32[]{:S(2)}) collective-permute-start(bf16[384,512]{1,0:T(8,128)(2,1)S(1)} %get-tuple-element.18), channel_id=1, source_target_pairs={{0,2},{1,3},{2,4},{3,5},{4,6},{5,7},{6,0},{7,1},{8,10},{9,11},{10,... | collective-permute-start | bytes 1179656 | tf_op jit(solution)/shard_map/ppermute | solution.py:82
  162.5 28.9 %collective-permute-start.10 = (bf16[384,512]{1,0:T(8,128)(2,1)S(1)}, bf16[384,512]{1,0:T(8,128)(2,1)S(1)}, u32[]{:S(2)}, u32[]{:S(2)}) collective-permute-start(bf16[384,512]{1,0:T(8,128)(2,1)S(1)} %convolution_convert_fusion), channel_id=1, source_target_pairs={{0,7},{1,0},{2,1},{3,2},{4,3},{5,4},{6,5},{7,6},{8,15},{9,8},{10,9... | collective-permute-start | bytes 1179656 | tf_op jit(solution)/shard_map/ppermute | solution.py:82
  162.6 28.9 %collective-permute-start.11 = (bf16[384,512]{1,0:T(8,128)(2,1)S(1)}, bf16[384,512]{1,0:T(8,128)(2,1)S(1)}, u32[]{:S(2)}, u32[]{:S(2)}) collective-permute-start(bf16[384,512]{1,0:T(8,128)(2,1)S(1)} %convolution_convert_fusion), channel_id=1, source_target_pairs={{0,6},{1,7},{2,0},{3,1},{4,2},{5,3},{6,4},{7,5},{8,14},{9,15},{10,... | collective-permute-start | bytes 1179656 | tf_op jit(solution)/shard_map/ppermute | solution.py:82
  163.1 52.6 %collective-permute-start.16 = (bf16[384,512]{1,0:T(8,128)(2,1)S(1)}, bf16[384,512]{1,0:T(8,128)(2,1)S(1)}, u32[]{:S(2)}, u32[]{:S(2)}) collective-permute-start(bf16[384,512]{1,0:T(8,128)(2,1)S(1)} %convolution_convert_fusion), channel_id=1, source_target_pairs={{0,1},{1,2},{2,3},{3,4},{4,5},{5,6},{6,7},{7,0},{8,9},{9,10},{10,1... | collective-permute-start | bytes 1179656 | tf_op jit(solution)/shard_map/ppermute | solution.py:82
  165.6 50.0 %collective-permute-start.15 = (bf16[384,512]{1,0:T(8,128)(2,1)S(1)}, bf16[384,512]{1,0:T(8,128)(2,1)S(1)}, u32[]{:S(2)}, u32[]{:S(2)}) collective-permute-start(bf16[384,512]{1,0:T(8,128)(2,1)S(1)} %convolution_convert_fusion), channel_id=1, source_target_pairs={{0,2},{1,3},{2,4},{3,5},{4,6},{5,7},{6,0},{7,1},{8,10},{9,11},{10,... | collective-permute-start | bytes 1179656 | tf_op jit(solution)/shard_map/ppermute | solution.py:82
  169.7 45.9 %collective-permute-start.14 = (bf16[384,512]{1,0:T(8,128)(2,1)S(1)}, bf16[384,512]{1,0:T(8,128)(2,1)S(1)}, u32[]{:S(2)}, u32[]{:S(2)}) collective-permute-start(bf16[384,512]{1,0:T(8,128)(2,1)S(1)} %convolution_convert_fusion), channel_id=1, source_target_pairs={{0,3},{1,4},{2,5},{3,6},{4,7},{5,0},{6,1},{7,2},{8,11},{9,12},{10,... | collective-permute-start | bytes 1179656 | tf_op jit(solution)/shard_map/ppermute | solution.py:82
  191.5 15.8 %collective-permute-start.12 = (bf16[384,512]{1,0:T(8,128)(2,1)S(1)}, bf16[384,512]{1,0:T(8,128)(2,1)S(1)}, u32[]{:S(2)}, u32[]{:S(2)}) collective-permute-start(bf16[384,512]{1,0:T(8,128)(2,1)S(1)} %convolution_convert_fusion), channel_id=1, source_target_pairs={{0,5},{1,6},{2,7},{3,0},{4,1},{5,2},{6,3},{7,4},{8,13},{9,14},{10,... | collective-permute-start | bytes 1179656 | tf_op jit(solution)/shard_map/ppermute | solution.py:82
  191.5 24.1 %collective-permute-start.13 = (bf16[384,512]{1,0:T(8,128)(2,1)S(1)}, bf16[384,512]{1,0:T(8,128)(2,1)S(1)}, u32[]{:S(2)}, u32[]{:S(2)}) collective-permute-start(bf16[384,512]{1,0:T(8,128)(2,1)S(1)} %convolution_convert_fusion), channel_id=1, source_target_pairs={{0,4},{1,5},{2,6},{3,7},{4,0},{5,1},{6,2},{7,3},{8,12},{9,13},{10,... | collective-permute-start | bytes 1179656 | tf_op jit(solution)/shard_map/ppermute | solution.py:82
  216.1 4.1 %copy-start.2 = (bf16[1,8,384,512]{3,2,1,0:T(8,128)(2,1)S(1)}, bf16[1,8,384,512]{3,2,1,0:T(8,128)(2,1)}, u32[]{:S(2)}) copy-start(bf16[1,8,384,512]{3,2,1,0:T(8,128)(2,1)} %get-tuple-element.8) | copy-start | bytes 9437188

commit v3 on v2

--- a/solution.py
+++ b/solution.py
@@ -31,8 +31,9 @@
         out_ref[...] = acc_ref[...].astype(out_ref.dtype)
 
 
-def lag_partial(history, left, right, lag_blocks, pattern, live_counts):
-    lags, blocks, vec, ex = history.shape
+def lag_partial(history, left, right, lag_blocks, pattern, live_counts, column):
+    lags, blocks, vec, _ = history.shape
+    ex = left.shape[-1]
     slots = lag_blocks.shape[2]
     window = jnp.arange(blocks, dtype=jnp.int32)[None, :, None] + pattern
 
@@ -40,20 +41,20 @@
         w = src[l, b, s]
         return (s < cnt[l, b]) & (w >= lo) & (w < hi), w - lo
 
-    def source_spec(s, lo, hi, count):
+    def source_spec(s, lo, hi, count, col):
         def index(b, l, src, cnt):
             on, at = used(src, cnt, l, b, s, lo, hi)
-            return (jnp.where(on, l, 0), jnp.where(on, jnp.clip(at, 0, count - 1), 0), 0, 0)
+            return (jnp.where(on, l, 0), jnp.where(on, jnp.clip(at, 0, count - 1), 0), 0, col)
         return pl.BlockSpec((None, None, vec, ex), index)
 
     def local_spec(s):
-        return source_spec(s, EDGE, EDGE + blocks, blocks)
+        return source_spec(s, EDGE, EDGE + blocks, blocks, column)
 
     def left_spec(s):
-        return source_spec(s, 0, EDGE, EDGE)
+        return source_spec(s, 0, EDGE, EDGE, 0)
 
     def right_spec(s):
-        return source_spec(s, EDGE + blocks, 2 * EDGE + blocks, EDGE)
+        return source_spec(s, EDGE + blocks, 2 * EDGE + blocks, EDGE, 0)
 
     in_specs = [pl.BlockSpec((None, None, slots, vec, vec), lambda b, l, src, cnt: (l, b, 0, 0, 0))]
     operands = [lag_blocks]
@@ -68,7 +69,7 @@
         scratch_shapes=[pltpu.VMEM((vec, ex), jnp.float32)],
     )
     flops = 2 * lags * blocks * slots * vec * vec * ex
-    moved = 2 * (lag_blocks.size + slots * history.size + blocks * vec * ex)
+    moved = 2 * (lag_blocks.size + slots * lags * blocks * vec * ex + blocks * vec * ex)
     return pl.pallas_call(
         term_kernel,
         grid_spec=grid_spec,
@@ -88,15 +89,7 @@
     return lax.ppermute(array, axis, pairs)
 
 
-def shards(history, lag_blocks, self_inverse, excitation, pattern, live_counts):
-    blocks_here = history.shape[1]
-    carried = passed_along(history[-1], "lag", 1)
-    left = shifted_by(history[:, blocks_here - EDGE:], "tile", 1)
-    right = shifted_by(history[:, :EDGE], "tile", -1)
-    live = jnp.minimum(live_counts, lag_blocks.shape[2])
-    partial = lag_partial(history, left, right, lag_blocks, pattern, live)
-    partial, carried = lax.optimization_barrier((partial, carried))
-
+def lag_sum(partial, excitation, self_inverse):
     n_lag = lax.axis_size("lag")
     me = lax.axis_index("lag")
     field = lax.dynamic_index_in_dim(partial, me, 0, keepdims=False).astype(jnp.float32)
@@ -107,10 +100,34 @@
     residual = (mine - field).astype(jnp.bfloat16)
     inverse = lax.dynamic_index_in_dim(self_inverse, me, 0, keepdims=False)
     block = jnp.dot(inverse, residual, preferred_element_type=jnp.float32).astype(jnp.bfloat16)
-
     gathered = [block] + [shifted_by(block, "lag", k) for k in range(1, n_lag)]
     ordered = jnp.stack(gathered[::-1])
-    traction = jnp.roll(ordered, me + 1, axis=0)
+    return jnp.roll(ordered, me + 1, axis=0)
+
+
+CHUNKS = 2
+
+
+def shards(history, lag_blocks, self_inverse, excitation, pattern, live_counts):
+    blocks_here = history.shape[1]
+    width = history.shape[-1] // CHUNKS
+    carried = passed_along(history[-1], "lag", 1)
+    live = jnp.minimum(live_counts, lag_blocks.shape[2])
+    me = lax.axis_index("lag")
+    pieces = []
+    for c in range(CHUNKS):
+        cols = slice(c * width, (c + 1) * width)
+        tail = history[:, blocks_here - EDGE:, :, cols]
+        head = history[:, :EDGE, :, cols]
+        if c:
+            tail, head, _, _ = lax.optimization_barrier((tail, head, left, right))
+        left = shifted_by(tail, "tile", 1)
+        right = shifted_by(head, "tile", -1)
+        partial = lag_partial(history, left, right, lag_blocks, pattern, live, c)
+        if c == CHUNKS - 1:
+            partial, carried = lax.optimization_barrier((partial, carried))
+        pieces.append(lag_sum(partial, excitation[..., cols], self_inverse))
+    traction = jnp.concatenate(pieces, axis=-1)
 
     newest = jnp.where(me == 0, traction, carried)
     shifted_history = jnp.concatenate([newest[None], history[:-1]], axis=0)

time: 224 us -> 269 us (1.20)
  local copies, waits for them, and re-layouts: 14.1 us -> 48 us
  Pallas kernels: 19.9 us -> 36.4 us
  waiting for transfers between devices: 104 us -> 88.1 us
  starting transfers between devices: 73.6 us -> 78.4 us
    unnamed x28 -> x29, local copies, waits for them, and re-layouts: 1.29 us -> 27.8 us
    pallas_call x1 -> x2, Pallas kernels: 19.9 us -> 36.4 us  [lag_partial(): pl.pallas_call(term_kernel, grid_spec=grid_spec, out_shape=jax.ShapeDtype...]
    ppermute x1, waiting for transfers between devices: 16.1 us -> 0.01 us  [passed_along(): return lax.ppermute(array, axis, pairs)]
    slice x1 -> x2, local copies, waits for them, and re-layouts: 6.6 us -> 12.4 us  [the longest x1 6.33 us: shards(): head = history[:, :EDGE, :, cols]]
    ppermute x16 -> x32, starting transfers between devices: 70.1 us -> 74.9 us  [shifted_by(): lax.ppermute(array, axis, [(i, (i + by) % count) for i in range(count)])]
    concatenate x0 -> x1, other arithmetic: none -> 2.7 us  [lag_sum(): return jnp.roll(ordered, me + 1, axis=0)]
    ppermute x16 -> x32, waiting for transfers between devices: 87.6 us -> 88.1 us  [shifted_by(): lax.ppermute(array, axis, [(i, (i + by) % count) for i in range(count)])]
  transfers between devices with their start and end apart: 17 -> 33, of which waited for: 8 -> 12; matrix products, arithmetic and copies ran while one was open for 2% -> 12% of each run, Pallas kernels for 9% -> 14%
where the time goes in v3:
time: 269 us; the launch traced here: 266 us
  waiting for transfers between devices  88.1 us (33%)
  starting transfers between devices  78.4 us (29%)
  local copies, waits for them, and re-layouts  48 us (18%)
  Pallas kernels  36.4 us (14%)
  other arithmetic  11.1 us (4%)
  matrix products  3.19 us (1%)
    ppermute x32, waiting for transfers between devices, shifted_by(): lax.ppermute(array, axis, [(i, (i + by) % count) for i in range(count)])  88.1 us
    ppermute x32, starting transfers between devices, shifted_by(): lax.ppermute(array, axis, [(i, (i + by) % count) for i in range(count)])  74.9 us
    pallas_call x2, Pallas kernels, lag_partial(): pl.pallas_call(term_kernel, grid_spec=grid_spec, out_shape=jax.ShapeDtype...  36.4 us
    unnamed x29, local copies, waits for them, and re-layouts  27.8 us
    slice x1, local copies, waits for them, and re-layouts, shards(): head = history[:, :EDGE, :, cols]  6.33 us
    slice x1, local copies, waits for them, and re-layouts, shards(): pieces.append(lag_sum(partial, excitation[..., cols], self_inverse))  6.11 us
  transfers between devices with their start and end apart: 33, of which 12 were waited for; matrix products, arithmetic and copies ran while one was open for 12% of the time, Pallas kernels for 14%

profile of v3, /device:TPU:14, one launch (start us, length us, event | category | flops | bytes accessed | tf_op | source)
XLA Modules:
  0.0 266.2 jit_solution(665170413774543193)
XLA Ops:
  0.7 6.3 %fusion.32 = (bf16[2,4,384,256]{3,2,1,0:T(8,128)(2,1)}, bf16[2,4,384,256]{3,2,1,0:T(8,128)(2,1)}, bf16[2,4,384,256]{3,2,1,0:T(8,128)(2,1)}, bf16[2,4,384,256]{3,2,1,0:T(8,128)(2,1)}) fusion(bf16[2,8,384,512]{3,2,1,0:T(8,128)(2,1)} %m1.3), kind=kLoop, calls=%fused_computation.73 | loop fusion | bytes 12582912 | tf_op jit(solution)/shard_map/slice | solution.py:121
  7.0 0.3 collective-permute-start.1
  7.5 3.3 %fusion.30 = (bf16[1,8,384,512]{3,2,1,0:T(8,128)(2,1)}, bf16[1,8,384,512]{3,2,1,0:T(8,128)(2,1)}) fusion(bf16[2,8,384,512]{3,2,1,0:T(8,128)(2,1)S(1)} %copy-done.1), kind=kLoop, calls=%fused_computation.71 | loop fusion | bytes 12582912 | tf_op jit(solution)/shard_map/slice | solution.py:133
  10.8 4.6 %copy.13 = bf16[1,8,384,512]{2,3,1,0:T(8,128)(2,1)} copy(bf16[1,8,384,512]{3,2,1,0:T(8,128)(2,1)} %get-tuple-element.14) | data formatting | bytes 6291456
  15.5 3.5 %collective-permute-start.18 = (bf16[8,384,512]{1,2,0:T(8,128)(2,1)}, bf16[8,384,512]{1,2,0:T(8,128)(2,1)}, u32[]{:S(2)}, u32[]{:S(2)}) collective-permute-start(bf16[8,384,512]{1,2,0:T(8,128)(2,1)} %bitcast.86), channel_id=1, source_target_pairs={{0,1},{1,2},{2,3},{3,4},{4,5},{5,6},{6,7},{8,9},{9,10},{10,11},{11... | collective-permute-start | bytes 9437192 | tf_op jit(solution)/shard_map/ppermute | solution.py:89
  19.0 0.6 broadcast_minimum_fusion.cnt_ref
  19.6 0.6 iota_add_fusion.src_ref
  20.2 5.3 %collective-permute-done.1.r0.r1 = bf16[2,4,384,256]{3,2,1,0:T(8,128)(2,1)} collective-permute-done((bf16[2,4,384,256]{3,2,1,0:T(8,128)(2,1)}, bf16[2,4,384,256]{3,2,1,0:T(8,128)(2,1)}, u32[]{:S(2)}, u32[]{:S(2)}) %collective-permute-start.1) | collective-permute-done | bytes 1572896 | tf_op jit(solution)/shard_map/ppermute | solution.py:83
  25.5 1.9 collective-permute-done.l0.l1
  27.4 18.2 %shard_map.77 = bf16[8,384,256]{2,1,0:T(8,128)(2,1)} custom-call(s32[2,8,2]{2,1,0:T(8,128)} %iota_add_fusion.src_ref, s32[2,8]{1,0:T(2,128)} %broadcast_minimum_fusion.cnt_ref, bf16[2,8,2,384,384]{4,3,2,1,0:T(8,128)(2,1)} %a_ref.3, bf16[2,4,384,256]{3,2,1,0:T(8,128)(2,1)} %collective-permute-done.l0.l1, bf16[2,8,384,512]{3,2,1,0:T(8,128)(2,1)} %m1.3, ...), custom_call_target="tpu_custom_call" | custom-call | flops 2415919104 | bytes 17301504 | tf_op jit(solution)/shard_map/pallas_call | solution.py:73
  45.6 2.3 dynamic-slice_bitcast_fusion.13
  47.9 0.9 collective-permute-start.2
  48.8 1.1 collective-permute-start.8
  49.9 3.1 %collective-permute-start.7 = (bf16[384,256]{1,0:T(8,128)(2,1)S(1)}, bf16[384,256]{1,0:T(8,128)(2,1)S(1)}, u32[]{:S(2)}, u32[]{:S(2)}) collective-permute-start(bf16[384,256]{1,0:T(8,128)(2,1)S(1)} %get-tuple-element.25), channel_id=1, source_target_pairs={{0,6},{1,7},{2,0},{3,1},{4,2},{5,3},{6,4},{7,5},{8,14},{9,15},{10,... | collective-permute-start | bytes 589832 | tf_op jit(solution)/shard_map/ppermute | solution.py:83
  53.1 1.8 collective-permute-start.6
  54.8 34.2 %collective-permute-done.2 = bf16[384,256]{1,0:T(8,128)(2,1)S(1)} collective-permute-done((bf16[384,256]{1,0:T(8,128)(2,1)S(1)}, bf16[384,256]{1,0:T(8,128)(2,1)S(1)}, u32[]{:S(2)}, u32[]{:S(2)}) %collective-permute-start.2) | collective-permute-done | bytes 196640 | tf_op jit(solution)/shard_map/ppermute | solution.py:83
  89.1 1.9 collective-permute-start.5
  91.0 14.8 %collective-permute-start.4 = (bf16[384,256]{1,0:T(8,128)(2,1)S(1)}, bf16[384,256]{1,0:T(8,128)(2,1)}, u32[]{:S(2)}, u32[]{:S(2)}) collective-permute-start(bf16[384,256]{1,0:T(8,128)(2,1)S(1)} %get-tuple-element.28), channel_id=1, source_target_pairs={{0,3},{1,4},{2,5},{3,6},{4,7},{5,0},{6,1},{7,2},{8,11},{9,12},{10,... | collective-permute-start | bytes 589832 | tf_op jit(solution)/shard_map/ppermute | solution.py:83
  105.7 6.1 %fusion.31 = (f32[8,384,256]{2,1,0:T(8,128)}, f32[8,384,256]{2,1,0:T(8,128)}) fusion(f32[8,384,512]{2,1,0:T(8,128)} %param.11), kind=kLoop, calls=%fused_computation.72 | loop fusion | bytes 12582912 | tf_op jit(solution)/shard_map/slice | solution.py:129
  111.9 5.3 %collective-permute-start.16 = (bf16[2,4,384,256]{3,2,1,0:T(8,128)(2,1)}, bf16[2,4,384,256]{3,2,1,0:T(8,128)(2,1)}, u32[]{:S(2)}, u32[]{:S(2)}) collective-permute-start(bf16[2,4,384,256]{3,2,1,0:T(8,128)(2,1)} %get-tuple-element.7), channel_id=1, source_target_pairs={{0,8},{8,16},{16,24},{24,32},{32,40},{40,48},{48,56},{56,64},{64,7... | collective-permute-start | bytes 4718600 | tf_op jit(solution)/shard_map/ppermute | solution.py:83
  117.2 1.7 convolution_convert_fusion.1
  118.9 4.0 %collective-permute-start.9 = (bf16[384,256]{0,1:T(8,128)(2,1)S(1)}, bf16[384,256]{0,1:T(8,128)(2,1)S(1)}, u32[]{:S(2)}, u32[]{:S(2)}) collective-permute-start(bf16[384,256]{0,1:T(8,128)(2,1)S(1)} %convolution_convert_fusion.1), channel_id=1, source_target_pairs={{0,7},{1,0},{2,1},{3,2},{4,3},{5,4},{6,5},{7,6},{8,15},{9,8},{10,9... | collective-permute-start | bytes 589832 | tf_op jit(solution)/shard_map/ppermute | solution.py:83
  122.9 4.6 %copy.14 = bf16[1,8,384,512]{2,3,1,0:T(8,128)(2,1)} copy(bf16[1,8,384,512]{3,2,1,0:T(8,128)(2,1)} %get-tuple-element.13) | data formatting | bytes 6291456
  127.5 0.5 collective-permute-done.9
  128.1 3.9 %collective-permute-start.10 = (bf16[384,256]{0,1:T(8,128)(2,1)S(1)}, bf16[384,256]{0,1:T(8,128)(2,1)S(1)}, u32[]{:S(2)}, u32[]{:S(2)}) collective-permute-start(bf16[384,256]{0,1:T(8,128)(2,1)S(1)} %convolution_convert_fusion.1), channel_id=1, source_target_pairs={{0,6},{1,7},{2,0},{3,1},{4,2},{5,3},{6,4},{7,5},{8,14},{9,15},{10,... | collective-permute-start | bytes 589832 | tf_op jit(solution)/shard_map/ppermute | solution.py:83
  131.9 0.7 bitcast_dynamic-update-slice_fusion.15
  132.6 3.2 %collective-permute-done.10 = bf16[384,256]{0,1:T(8,128)(2,1)S(1)} collective-permute-done((bf16[384,256]{0,1:T(8,128)(2,1)S(1)}, bf16[384,256]{0,1:T(8,128)(2,1)S(1)}, u32[]{:S(2)}, u32[]{:S(2)}) %collective-permute-start.10) | collective-permute-done | bytes 196640 | tf_op jit(solution)/shard_map/ppermute | solution.py:83
  135.9 5.1 %collective-permute-start.11 = (bf16[384,256]{0,1:T(8,128)(2,1)S(1)}, bf16[384,256]{0,1:T(8,128)(2,1)S(1)}, u32[]{:S(2)}, u32[]{:S(2)}) collective-permute-start(bf16[384,256]{0,1:T(8,128)(2,1)S(1)} %convolution_convert_fusion.1), channel_id=1, source_target_pairs={{0,5},{1,6},{2,7},{3,0},{4,1},{5,2},{6,3},{7,4},{8,13},{9,14},{10,... | collective-permute-start | bytes 589832 | tf_op jit(solution)/shard_map/ppermute | solution.py:83
  140.9 0.7 bitcast_dynamic-update-slice_fusion.14
  141.6 6.7 %collective-permute-done.11 = bf16[384,256]{0,1:T(8,128)(2,1)S(1)} collective-permute-done((bf16[384,256]{0,1:T(8,128)(2,1)S(1)}, bf16[384,256]{0,1:T(8,128)(2,1)S(1)}, u32[]{:S(2)}, u32[]{:S(2)}) %collective-permute-start.11) | collective-permute-done | bytes 196640 | tf_op jit(solution)/shard_map/ppermute | solution.py:83
  148.3 0.9 collective-permute-start.12
  149.3 0.7 bitcast_dynamic-update-slice_fusion.13
  150.0 4.0 %collective-permute-done.12 = bf16[384,256]{0,1:T(8,128)(2,1)S(1)} collective-permute-done((bf16[384,256]{0,1:T(8,128)(2,1)S(1)}, bf16[384,256]{0,1:T(8,128)(2,1)S(1)}, u32[]{:S(2)}, u32[]{:S(2)}) %collective-permute-start.12) | collective-permute-done | bytes 196640 | tf_op jit(solution)/shard_map/ppermute | solution.py:83
  154.0 0.7 bitcast_dynamic-update-slice_fusion.12
  154.7 8.3 %collective-permute-done.13 = bf16[384,256]{0,1:T(8,128)(2,1)S(1)} collective-permute-done((bf16[384,256]{0,1:T(8,128)(2,1)S(1)}, bf16[384,256]{0,1:T(8,128)(2,1)S(1)}, u32[]{:S(2)}, u32[]{:S(2)}) %collective-permute-start.13) | collective-permute-done | bytes 196640 | tf_op jit(solution)/shard_map/ppermute | solution.py:83
  163.0 6.5 %collective-permute-start.14 = (bf16[384,256]{0,1:T(8,128)(2,1)S(1)}, bf16[384,256]{0,1:T(8,128)(2,1)S(1)}, u32[]{:S(2)}, u32[]{:S(2)}) collective-permute-start(bf16[384,256]{0,1:T(8,128)(2,1)S(1)} %convolution_convert_fusion.1), channel_id=1, source_target_pairs={{0,2},{1,3},{2,4},{3,5},{4,6},{5,7},{6,0},{7,1},{8,10},{9,11},{10,... | collective-permute-start | bytes 589832 | tf_op jit(solution)/shard_map/ppermute | solution.py:83
  169.5 0.7 bitcast_dynamic-update-slice_fusion.11
  170.2 18.2 %shard_map.78 = bf16[8,384,256]{2,1,0:T(8,128)(2,1)} custom-call(s32[2,8,2]{2,1,0:T(8,128)} %iota_add_fusion.src_ref, s32[2,8]{1,0:T(2,128)} %broadcast_minimum_fusion.cnt_ref, bf16[2,8,2,384,384]{4,3,2,1,0:T(8,128)(2,1)} %a_ref.3, bf16[2,4,384,256]{3,2,1,0:T(8,128)(2,1)} %collective-permute-done.16.l0.l1, bf16[2,8,384,512]{3,2,1,0:T(8,128)(2,1)} %m1.3, ...), custom_call_target="tpu_custom_call" | custom-call | flops 2415919104 | bytes 17301504 | tf_op jit(solution)/shard_map/pallas_call | solution.py:73
  188.4 1.5 dynamic-slice_bitcast_fusion.6
  190.1 1.9 collective-permute-start.25
  192.0 0.7 bitcast_dynamic-update-slice_fusion.10
  192.7 1.4 collective-permute-start.24
  194.1 1.7 collective-permute-start.23
  195.8 2.4 collective-permute-start.22
  198.2 1.0 collective-permute-start.21
  199.2 3.5 %collective-permute-start.20 = (bf16[384,256]{1,0:T(8,128)(2,1)S(1)}, bf16[384,256]{1,0:T(8,128)(2,1)S(1)}, u32[]{:S(2)}, u32[]{:S(2)}) collective-permute-start(bf16[384,256]{1,0:T(8,128)(2,1)S(1)} %get-tuple-element.36), channel_id=1, source_target_pairs={{0,2},{1,3},{2,4},{3,5},{4,6},{5,7},{6,0},{7,1},{8,10},{9,11},{10,... | collective-permute-start | bytes 589832 | tf_op jit(solution)/shard_map/ppermute | solution.py:83
  202.7 0.7 bitcast_dynamic-update-slice_fusion.9
  203.4 6.1 %collective-permute-done.23 = bf16[384,256]{1,0:T(8,128)(2,1)S(1)} collective-permute-done((bf16[384,256]{1,0:T(8,128)(2,1)S(1)}, bf16[384,256]{1,0:T(8,128)(2,1)S(1)}, u32[]{:S(2)}, u32[]{:S(2)}) %collective-permute-start.23) | collective-permute-done | bytes 196640 | tf_op jit(solution)/shard_map/ppermute | solution.py:83
  209.5 5.3 %collective-permute-done.22 = bf16[384,256]{1,0:T(8,128)(2,1)S(1)} collective-permute-done((bf16[384,256]{1,0:T(8,128)(2,1)S(1)}, bf16[384,256]{1,0:T(8,128)(2,1)S(1)}, u32[]{:S(2)}, u32[]{:S(2)}) %collective-permute-start.22) | collective-permute-done | bytes 196640 | tf_op jit(solution)/shard_map/ppermute | solution.py:83
  214.9 1.5 convolution_convert_fusion
  216.5 0.7 bitcast_dynamic-update-slice_fusion.8
  217.2 2.0 collective-permute-start.32
  219.2 1.8 collective-permute-start.31
  221.0 1.3 collective-permute-start.30
  222.3 1.0 collective-permute-start.29
  223.4 6.5 %collective-permute-start.27 = (bf16[384,256]{0,1:T(8,128)(2,1)S(1)}, bf16[384,256]{0,1:T(8,128)(2,1)S(1)}, u32[]{:S(2)}, u32[]{:S(2)}) collective-permute-start(bf16[384,256]{0,1:T(8,128)(2,1)S(1)} %convolution_convert_fusion), channel_id=1, source_target_pairs={{0,6},{1,7},{2,0},{3,1},{4,2},{5,3},{6,4},{7,5},{8,14},{9,15},{10,... | collective-permute-start | bytes 589832 | tf_op jit(solution)/shard_map/ppermute | solution.py:83
  229.8 6.2 %collective-permute-done.27 = bf16[384,256]{0,1:T(8,128)(2,1)S(1)} collective-permute-done((bf16[384,256]{0,1:T(8,128)(2,1)S(1)}, bf16[384,256]{0,1:T(8,128)(2,1)S(1)}, u32[]{:S(2)}, u32[]{:S(2)}) %collective-permute-start.27) | collective-permute-done | bytes 196640 | tf_op jit(solution)/shard_map/ppermute | solution.py:83
  236.1 0.3 collective-permute-start.28
  236.4 6.2 %collective-permute-done.28 = bf16[384,256]{0,1:T(8,128)(2,1)S(1)} collective-permute-done((bf16[384,256]{0,1:T(8,128)(2,1)S(1)}, bf16[384,256]{0,1:T(8,128)(2,1)S(1)}, u32[]{:S(2)}, u32[]{:S(2)}) %collective-permute-start.28) | collective-permute-done | bytes 196640 | tf_op jit(solution)/shard_map/ppermute | solution.py:83
  242.9 2.7 %fusion = (bf16[8,384,256]{1,2,0:T(8,128)(2,1)S(1)}, bf16[8,384,256]{1,2,0:T(8,128)(2,1)S(1)}) fusion(s32[]{:T(128)S(6)} %select_n.121, bf16[8,384,256]{1,2,0:T(8,128)(2,1)S(1)} %bitcast_dynamic-update-slice_fusion, bf16[8,384,256]{1,2,0:T(8,128)(2,1)} %bitcast_dynamic-update-slice_fusion.8), kind=kLoop, calls=%fused_computation.7 | loop fusion | flops 1572864 | bytes 6291460 | tf_op jit(solution)/shard_map/jit(_roll_dynamic)/concatenate | solution.py:105
  245.6 3.9 %select_bitcast_fusion = (bf16[1,8,384,512]{2,3,1,0:T(8,128)(2,1)S(1)}, bf16[8,384,512]{1,2,0:T(8,128)(2,1)}) fusion(bf16[8,384,512]{1,2,0:T(8,128)(2,1)} %collective-permute-done.18, pred[]{:T(512)S(6)} %eq.20, bf16[8,384,256]{1,2,0:T(8,128)(2,1)S(1)} %get-tuple-element.37, bf16[8,384,256]{1,2,0:T(8,128)(2,1)S(1)} %get-tuple-element.38), kind=kLoop, calls=%fused_computation.6 | loop fusion | flops 7864320 | bytes 12582913 | tf_op jit(solution)/shard_map/broadcast_in_dim | solution.py:133
  249.5 3.4 %pad_maximum_fusion = bf16[2,8,384,512]{2,3,1,0:T(8,128)(2,1)} fusion(bf16[1,8,384,512]{2,3,1,0:T(8,128)(2,1)S(1)} %copy-done.2, bf16[1,8,384,512]{2,3,1,0:T(8,128)(2,1)S(1)} %get-tuple-element.21), kind=kLoop, calls=%fused_computation | loop fusion | flops 3145728 | bytes 12582912 | tf_op jit(solution)/shard_map/concatenate | solution.py:133
  252.9 8.6 %copy.12 = bf16[2,8,384,512]{3,2,1,0:T(8,128)(2,1)} copy(bf16[2,8,384,512]{2,3,1,0:T(8,128)(2,1)} %pad_maximum_fusion) | data formatting | bytes 12582912
  261.5 4.6 %copy.11 = bf16[8,384,512]{2,1,0:T(8,128)(2,1)} copy(bf16[8,384,512]{1,2,0:T(8,128)(2,1)} %get-tuple-element.22) | data formatting | bytes 6291456
  (47 shorter events, 1.0 us)
Async XLA Ops:
  0.6 116.6 %copy-start = (bf16[8,384,384]{2,1,0:T(8,128)(2,1)S(1)}, bf16[8,384,384]{2,1,0:T(8,128)(2,1)}, u32[]{:S(2)}) copy-start(bf16[8,384,384]{2,1,0:T(8,128)(2,1)} %param.10) | copy-start | bytes 7077892
  0.6 6.9 %copy-start.1 = (bf16[2,8,384,512]{3,2,1,0:T(8,128)(2,1)S(1)}, bf16[2,8,384,512]{3,2,1,0:T(8,128)(2,1)}, u32[]{:S(2)}) copy-start(bf16[2,8,384,512]{3,2,1,0:T(8,128)(2,1)} %m1.3) | copy-start | bytes 18874372
  7.0 18.5 %collective-permute-start.1 = (bf16[2,4,384,256]{3,2,1,0:T(8,128)(2,1)}, bf16[2,4,384,256]{3,2,1,0:T(8,128)(2,1)}, u32[]{:S(2)}, u32[]{:S(2)}) collective-permute-start(bf16[2,4,384,256]{3,2,1,0:T(8,128)(2,1)} %get-tuple-element.17), channel_id=1, source_target_pairs={{0,120},{8,0},{16,8},{24,16},{32,24},{40,32},{48,40},{56,48},{64,5... | collective-permute-start | bytes 4718600 | tf_op jit(solution)/shard_map/ppermute | solution.py:83
  7.3 20.2 %collective-permute-start = (bf16[2,4,384,256]{3,2,1,0:T(8,128)(2,1)}, bf16[2,4,384,256]{3,2,1,0:T(8,128)(2,1)}, u32[]{:S(2)}, u32[]{:S(2)}) collective-permute-start(bf16[2,4,384,256]{3,2,1,0:T(8,128)(2,1)} %get-tuple-element.20), channel_id=1, source_target_pairs={{0,8},{8,16},{16,24},{24,32},{32,40},{40,48},{48,56},{56,64},{64,7... | collective-permute-start | bytes 4718600 | tf_op jit(solution)/shard_map/ppermute | solution.py:83
  10.8 8.1 %copy-start.4 = (s32[2,8]{1,0:T(2,128)S(1)}, s32[2,8]{1,0:T(2,128)}, u32[]{:S(2)}) copy-start(s32[2,8]{1,0:T(2,128)} %param.13) | copy-start | bytes 196
  10.8 8.7 %copy-start.3 = (s32[2,8,2]{1,2,0:T(2,128)S(1)}, s32[2,8,2]{1,2,0:T(2,128)}, u32[]{:S(2)}) copy-start(s32[2,8,2]{1,2,0:T(2,128)} %param.12) | copy-start | bytes 388
  15.5 172.9 %collective-permute-start.18 = (bf16[8,384,512]{1,2,0:T(8,128)(2,1)}, bf16[8,384,512]{1,2,0:T(8,128)(2,1)}, u32[]{:S(2)}, u32[]{:S(2)}) collective-permute-start(bf16[8,384,512]{1,2,0:T(8,128)(2,1)} %bitcast.86), channel_id=1, source_target_pairs={{0,1},{1,2},{2,3},{3,4},{4,5},{5,6},{6,7},{8,9},{9,10},{10,11},{11... | collective-permute-start | bytes 9437192 | tf_op jit(solution)/shard_map/ppermute | solution.py:89
  47.9 41.2 %collective-permute-start.2 = (bf16[384,256]{1,0:T(8,128)(2,1)S(1)}, bf16[384,256]{1,0:T(8,128)(2,1)S(1)}, u32[]{:S(2)}, u32[]{:S(2)}) collective-permute-start(bf16[384,256]{1,0:T(8,128)(2,1)S(1)} %get-tuple-element.23), channel_id=1, source_target_pairs={{0,1},{1,2},{2,3},{3,4},{4,5},{5,6},{6,7},{7,0},{8,9},{9,10},{10,1... | collective-permute-start | bytes 589832 | tf_op jit(solution)/shard_map/ppermute | solution.py:83
  48.8 42.2 %collective-permute-start.8 = (bf16[384,256]{1,0:T(8,128)(2,1)S(1)}, bf16[384,256]{1,0:T(8,128)(2,1)S(1)}, u32[]{:S(2)}, u32[]{:S(2)}) collective-permute-start(bf16[384,256]{1,0:T(8,128)(2,1)S(1)} %get-tuple-element.24), channel_id=1, source_target_pairs={{0,7},{1,0},{2,1},{3,2},{4,3},{5,4},{6,5},{7,6},{8,15},{9,8},{10,9... | collective-permute-start | bytes 589832 | tf_op jit(solution)/shard_map/ppermute | solution.py:83
  49.9 55.8 %collective-permute-start.7 = (bf16[384,256]{1,0:T(8,128)(2,1)S(1)}, bf16[384,256]{1,0:T(8,128)(2,1)S(1)}, u32[]{:S(2)}, u32[]{:S(2)}) collective-permute-start(bf16[384,256]{1,0:T(8,128)(2,1)S(1)} %get-tuple-element.25), channel_id=1, source_target_pairs={{0,6},{1,7},{2,0},{3,1},{4,2},{5,3},{6,4},{7,5},{8,14},{9,15},{10,... | collective-permute-start | bytes 589832 | tf_op jit(solution)/shard_map/ppermute | solution.py:83
  53.1 58.8 %collective-permute-start.6 = (bf16[384,256]{1,0:T(8,128)(2,1)}, bf16[384,256]{1,0:T(8,128)(2,1)S(1)}, u32[]{:S(2)}, u32[]{:S(2)}) collective-permute-start(bf16[384,256]{1,0:T(8,128)(2,1)} %get-tuple-element.26), channel_id=1, source_target_pairs={{0,5},{1,6},{2,7},{3,0},{4,1},{5,2},{6,3},{7,4},{8,13},{9,14},{10,... | collective-permute-start | bytes 589832 | tf_op jit(solution)/shard_map/ppermute | solution.py:83
  89.1 28.1 %collective-permute-start.5 = (bf16[384,256]{1,0:T(8,128)(2,1)}, bf16[384,256]{1,0:T(8,128)(2,1)}, u32[]{:S(2)}, u32[]{:S(2)}) collective-permute-start(bf16[384,256]{1,0:T(8,128)(2,1)} %get-tuple-element.27), channel_id=1, source_target_pairs={{0,4},{1,5},{2,6},{3,7},{4,0},{5,1},{6,2},{7,3},{8,12},{9,13},{10,... | collective-permute-start | bytes 589832 | tf_op jit(solution)/shard_map/ppermute | solution.py:83
  91.0 26.2 %collective-permute-start.4 = (bf16[384,256]{1,0:T(8,128)(2,1)S(1)}, bf16[384,256]{1,0:T(8,128)(2,1)}, u32[]{:S(2)}, u32[]{:S(2)}) collective-permute-start(bf16[384,256]{1,0:T(8,128)(2,1)S(1)} %get-tuple-element.28), channel_id=1, source_target_pairs={{0,3},{1,4},{2,5},{3,6},{4,7},{5,0},{6,1},{7,2},{8,11},{9,12},{10,... | collective-permute-start | bytes 589832 | tf_op jit(solution)/shard_map/ppermute | solution.py:83
  105.7 11.5 %collective-permute-start.3 = (bf16[384,256]{1,0:T(8,128)(2,1)S(1)}, bf16[384,256]{1,0:T(8,128)(2,1)}, u32[]{:S(2)}, u32[]{:S(2)}) collective-permute-start(bf16[384,256]{1,0:T(8,128)(2,1)S(1)} %get-tuple-element.29), channel_id=1, source_target_pairs={{0,2},{1,3},{2,4},{3,5},{4,6},{5,7},{6,0},{7,1},{8,10},{9,11},{10,... | collective-permute-start | bytes 589832 | tf_op jit(solution)/shard_map/ppermute | solution.py:83
  111.9 58.3 %collective-permute-start.16 = (bf16[2,4,384,256]{3,2,1,0:T(8,128)(2,1)}, bf16[2,4,384,256]{3,2,1,0:T(8,128)(2,1)}, u32[]{:S(2)}, u32[]{:S(2)}) collective-permute-start(bf16[2,4,384,256]{3,2,1,0:T(8,128)(2,1)} %get-tuple-element.7), channel_id=1, source_target_pairs={{0,8},{8,16},{16,24},{24,32},{32,40},{40,48},{48,56},{56,64},{64,7... | collective-permute-start | bytes 4718600 | tf_op jit(solution)/shard_map/ppermute | solution.py:83
  117.2 53.0 %collective-permute-start.17 = (bf16[2,4,384,256]{3,2,1,0:T(8,128)(2,1)}, bf16[2,4,384,256]{3,2,1,0:T(8,128)(2,1)}, u32[]{:S(2)}, u32[]{:S(2)}) collective-permute-start(bf16[2,4,384,256]{3,2,1,0:T(8,128)(2,1)} %get-tuple-element.8), channel_id=1, source_target_pairs={{0,120},{8,0},{16,8},{24,16},{32,24},{40,32},{48,40},{56,48},{64,5... | collective-permute-start | bytes 4718600 | tf_op jit(solution)/shard_map/ppermute | solution.py:83
  118.9 9.1 %collective-permute-start.9 = (bf16[384,256]{0,1:T(8,128)(2,1)S(1)}, bf16[384,256]{0,1:T(8,128)(2,1)S(1)}, u32[]{:S(2)}, u32[]{:S(2)}) collective-permute-start(bf16[384,256]{0,1:T(8,128)(2,1)S(1)} %convolution_convert_fusion.1), channel_id=1, source_target_pairs={{0,7},{1,0},{2,1},{3,2},{4,3},{5,4},{6,5},{7,6},{8,15},{9,8},{10,9... | collective-permute-start | bytes 589832 | tf_op jit(solution)/shard_map/ppermute | solution.py:83
  127.5 68.3 %collective-permute-start.15 = (bf16[384,256]{0,1:T(8,128)(2,1)S(1)}, bf16[384,256]{0,1:T(8,128)(2,1)S(1)}, u32[]{:S(2)}, u32[]{:S(2)}) collective-permute-start(bf16[384,256]{0,1:T(8,128)(2,1)S(1)} %convolution_convert_fusion.1), channel_id=1, source_target_pairs={{0,1},{1,2},{2,3},{3,4},{4,5},{5,6},{6,7},{7,0},{8,9},{9,10},{10,1... | collective-permute-start | bytes 589832 | tf_op jit(solution)/shard_map/ppermute | solution.py:83
  128.1 7.8 %collective-permute-start.10 = (bf16[384,256]{0,1:T(8,128)(2,1)S(1)}, bf16[384,256]{0,1:T(8,128)(2,1)S(1)}, u32[]{:S(2)}, u32[]{:S(2)}) collective-permute-start(bf16[384,256]{0,1:T(8,128)(2,1)S(1)} %convolution_convert_fusion.1), channel_id=1, source_target_pairs={{0,6},{1,7},{2,0},{3,1},{4,2},{5,3},{6,4},{7,5},{8,14},{9,15},{10,... | collective-permute-start | bytes 589832 | tf_op jit(solution)/shard_map/ppermute | solution.py:83
  135.9 12.5 %collective-permute-start.11 = (bf16[384,256]{0,1:T(8,128)(2,1)S(1)}, bf16[384,256]{0,1:T(8,128)(2,1)S(1)}, u32[]{:S(2)}, u32[]{:S(2)}) collective-permute-start(bf16[384,256]{0,1:T(8,128)(2,1)S(1)} %convolution_convert_fusion.1), channel_id=1, source_target_pairs={{0,5},{1,6},{2,7},{3,0},{4,1},{5,2},{6,3},{7,4},{8,13},{9,14},{10,... | collective-permute-start | bytes 589832 | tf_op jit(solution)/shard_map/ppermute | solution.py:83
  148.3 5.7 %collective-permute-start.12 = (bf16[384,256]{0,1:T(8,128)(2,1)S(1)}, bf16[384,256]{0,1:T(8,128)(2,1)S(1)}, u32[]{:S(2)}, u32[]{:S(2)}) collective-permute-start(bf16[384,256]{0,1:T(8,128)(2,1)S(1)} %convolution_convert_fusion.1), channel_id=1, source_target_pairs={{0,4},{1,5},{2,6},{3,7},{4,0},{5,1},{6,2},{7,3},{8,12},{9,13},{10,... | collective-permute-start | bytes 589832 | tf_op jit(solution)/shard_map/ppermute | solution.py:83
  154.0 9.0 %collective-permute-start.13 = (bf16[384,256]{0,1:T(8,128)(2,1)S(1)}, bf16[384,256]{0,1:T(8,128)(2,1)S(1)}, u32[]{:S(2)}, u32[]{:S(2)}) collective-permute-start(bf16[384,256]{0,1:T(8,128)(2,1)S(1)} %convolution_convert_fusion.1), channel_id=1, source_target_pairs={{0,3},{1,4},{2,5},{3,6},{4,7},{5,0},{6,1},{7,2},{8,11},{9,12},{10,... | collective-permute-start | bytes 589832 | tf_op jit(solution)/shard_map/ppermute | solution.py:83
  163.0 29.0 %collective-permute-start.14 = (bf16[384,256]{0,1:T(8,128)(2,1)S(1)}, bf16[384,256]{0,1:T(8,128)(2,1)S(1)}, u32[]{:S(2)}, u32[]{:S(2)}) collective-permute-start(bf16[384,256]{0,1:T(8,128)(2,1)S(1)} %convolution_convert_fusion.1), channel_id=1, source_target_pairs={{0,2},{1,3},{2,4},{3,5},{4,6},{5,7},{6,0},{7,1},{8,10},{9,11},{10,... | collective-permute-start | bytes 589832 | tf_op jit(solution)/shard_map/ppermute | solution.py:83
  189.9 8.3 %collective-permute-start.19 = (bf16[384,256]{1,0:T(8,128)(2,1)S(1)}, bf16[384,256]{1,0:T(8,128)(2,1)S(1)}, u32[]{:S(2)}, u32[]{:S(2)}) collective-permute-start(bf16[384,256]{1,0:T(8,128)(2,1)S(1)} %get-tuple-element.30), channel_id=1, source_target_pairs={{0,1},{1,2},{2,3},{3,4},{4,5},{5,6},{6,7},{7,0},{8,9},{9,10},{10,1... | collective-permute-start | bytes 589832 | tf_op jit(solution)/shard_map/ppermute | solution.py:83
  190.1 9.1 %collective-permute-start.25 = (bf16[384,256]{1,0:T(8,128)(2,1)S(1)}, bf16[384,256]{1,0:T(8,128)(2,1)S(1)}, u32[]{:S(2)}, u32[]{:S(2)}) collective-permute-start(bf16[384,256]{1,0:T(8,128)(2,1)S(1)} %get-tuple-element.31), channel_id=1, source_target_pairs={{0,7},{1,0},{2,1},{3,2},{4,3},{5,4},{6,5},{7,6},{8,15},{9,8},{10,9... | collective-permute-start | bytes 589832 | tf_op jit(solution)/shard_map/ppermute | solution.py:83
  192.7 10.7 %collective-permute-start.24 = (bf16[384,256]{1,0:T(8,128)(2,1)S(1)}, bf16[384,256]{1,0:T(8,128)(2,1)S(1)}, u32[]{:S(2)}, u32[]{:S(2)}) collective-permute-start(bf16[384,256]{1,0:T(8,128)(2,1)S(1)} %get-tuple-element.32), channel_id=1, source_target_pairs={{0,6},{1,7},{2,0},{3,1},{4,2},{5,3},{6,4},{7,5},{8,14},{9,15},{10,... | collective-permute-start | bytes 589832 | tf_op jit(solution)/shard_map/ppermute | solution.py:83
  194.1 15.4 %collective-permute-start.23 = (bf16[384,256]{1,0:T(8,128)(2,1)S(1)}, bf16[384,256]{1,0:T(8,128)(2,1)S(1)}, u32[]{:S(2)}, u32[]{:S(2)}) collective-permute-start(bf16[384,256]{1,0:T(8,128)(2,1)S(1)} %get-tuple-element.33), channel_id=1, source_target_pairs={{0,5},{1,6},{2,7},{3,0},{4,1},{5,2},{6,3},{7,4},{8,13},{9,14},{10,... | collective-permute-start | bytes 589832 | tf_op jit(solution)/shard_map/ppermute | solution.py:83
  195.8 19.0 %collective-permute-start.22 = (bf16[384,256]{1,0:T(8,128)(2,1)S(1)}, bf16[384,256]{1,0:T(8,128)(2,1)S(1)}, u32[]{:S(2)}, u32[]{:S(2)}) collective-permute-start(bf16[384,256]{1,0:T(8,128)(2,1)S(1)} %get-tuple-element.34), channel_id=1, source_target_pairs={{0,4},{1,5},{2,6},{3,7},{4,0},{5,1},{6,2},{7,3},{8,12},{9,13},{10,... | collective-permute-start | bytes 589832 | tf_op jit(solution)/shard_map/ppermute | solution.py:83
  198.2 16.7 %collective-permute-start.21 = (bf16[384,256]{1,0:T(8,128)(2,1)S(1)}, bf16[384,256]{1,0:T(8,128)(2,1)S(1)}, u32[]{:S(2)}, u32[]{:S(2)}) collective-permute-start(bf16[384,256]{1,0:T(8,128)(2,1)S(1)} %get-tuple-element.35), channel_id=1, source_target_pairs={{0,3},{1,4},{2,5},{3,6},{4,7},{5,0},{6,1},{7,2},{8,11},{9,12},{10,... | collective-permute-start | bytes 589832 | tf_op jit(solution)/shard_map/ppermute | solution.py:83
  199.2 15.7 %collective-permute-start.20 = (bf16[384,256]{1,0:T(8,128)(2,1)S(1)}, bf16[384,256]{1,0:T(8,128)(2,1)S(1)}, u32[]{:S(2)}, u32[]{:S(2)}) collective-permute-start(bf16[384,256]{1,0:T(8,128)(2,1)S(1)} %get-tuple-element.36), channel_id=1, source_target_pairs={{0,2},{1,3},{2,4},{3,5},{4,6},{5,7},{6,0},{7,1},{8,10},{9,11},{10,... | collective-permute-start | bytes 589832 | tf_op jit(solution)/shard_map/ppermute | solution.py:83
  216.4 7.0 %collective-permute-start.26 = (bf16[384,256]{0,1:T(8,128)(2,1)S(1)}, bf16[384,256]{0,1:T(8,128)(2,1)S(1)}, u32[]{:S(2)}, u32[]{:S(2)}) collective-permute-start(bf16[384,256]{0,1:T(8,128)(2,1)S(1)} %convolution_convert_fusion), channel_id=1, source_target_pairs={{0,7},{1,0},{2,1},{3,2},{4,3},{5,4},{6,5},{7,6},{8,15},{9,8},{10,9... | collective-permute-start | bytes 589832 | tf_op jit(solution)/shard_map/ppermute | solution.py:83
  217.2 25.7 %collective-permute-start.32 = (bf16[384,256]{0,1:T(8,128)(2,1)S(1)}, bf16[384,256]{0,1:T(8,128)(2,1)S(1)}, u32[]{:S(2)}, u32[]{:S(2)}) collective-permute-start(bf16[384,256]{0,1:T(8,128)(2,1)S(1)} %convolution_convert_fusion), channel_id=1, source_target_pairs={{0,1},{1,2},{2,3},{3,4},{4,5},{5,6},{6,7},{7,0},{8,9},{9,10},{10,1... | collective-permute-start | bytes 589832 | tf_op jit(solution)/shard_map/ppermute | solution.py:83
  219.2 23.6 %collective-permute-start.31 = (bf16[384,256]{0,1:T(8,128)(2,1)S(1)}, bf16[384,256]{0,1:T(8,128)(2,1)S(1)}, u32[]{:S(2)}, u32[]{:S(2)}) collective-permute-start(bf16[384,256]{0,1:T(8,128)(2,1)S(1)} %convolution_convert_fusion), channel_id=1, source_target_pairs={{0,2},{1,3},{2,4},{3,5},{4,6},{5,7},{6,0},{7,1},{8,10},{9,11},{10,... | collective-permute-start | bytes 589832 | tf_op jit(solution)/shard_map/ppermute | solution.py:83
  221.0 21.7 %collective-permute-start.30 = (bf16[384,256]{0,1:T(8,128)(2,1)S(1)}, bf16[384,256]{0,1:T(8,128)(2,1)S(1)}, u32[]{:S(2)}, u32[]{:S(2)}) collective-permute-start(bf16[384,256]{0,1:T(8,128)(2,1)S(1)} %convolution_convert_fusion), channel_id=1, source_target_pairs={{0,3},{1,4},{2,5},{3,6},{4,7},{5,0},{6,1},{7,2},{8,11},{9,12},{10,... | collective-permute-start | bytes 589832 | tf_op jit(solution)/shard_map/ppermute | solution.py:83
  222.3 20.3 %collective-permute-start.29 = (bf16[384,256]{0,1:T(8,128)(2,1)S(1)}, bf16[384,256]{0,1:T(8,128)(2,1)S(1)}, u32[]{:S(2)}, u32[]{:S(2)}) collective-permute-start(bf16[384,256]{0,1:T(8,128)(2,1)S(1)} %convolution_convert_fusion), channel_id=1, source_target_pairs={{0,4},{1,5},{2,6},{3,7},{4,0},{5,1},{6,2},{7,3},{8,12},{9,13},{10,... | collective-permute-start | bytes 589832 | tf_op jit(solution)/shard_map/ppermute | solution.py:83
  223.4 12.7 %collective-permute-start.27 = (bf16[384,256]{0,1:T(8,128)(2,1)S(1)}, bf16[384,256]{0,1:T(8,128)(2,1)S(1)}, u32[]{:S(2)}, u32[]{:S(2)}) collective-permute-start(bf16[384,256]{0,1:T(8,128)(2,1)S(1)} %convolution_convert_fusion), channel_id=1, source_target_pairs={{0,6},{1,7},{2,0},{3,1},{4,2},{5,3},{6,4},{7,5},{8,14},{9,15},{10,... | collective-permute-start | bytes 589832 | tf_op jit(solution)/shard_map/ppermute | solution.py:83
  236.1 6.6 %collective-permute-start.28 = (bf16[384,256]{0,1:T(8,128)(2,1)S(1)}, bf16[384,256]{0,1:T(8,128)(2,1)S(1)}, u32[]{:S(2)}, u32[]{:S(2)}) collective-permute-start(bf16[384,256]{0,1:T(8,128)(2,1)S(1)} %convolution_convert_fusion), channel_id=1, source_target_pairs={{0,5},{1,6},{2,7},{3,0},{4,1},{5,2},{6,3},{7,4},{8,13},{9,14},{10,... | collective-permute-start | bytes 589832 | tf_op jit(solution)/shard_map/ppermute | solution.py:83
  245.6 3.9 %copy-start.2 = (bf16[1,8,384,512]{2,3,1,0:T(8,128)(2,1)S(1)}, bf16[1,8,384,512]{2,3,1,0:T(8,128)(2,1)}, u32[]{:S(2)}) copy-start(bf16[1,8,384,512]{2,3,1,0:T(8,128)(2,1)} %copy.14) | copy-start | bytes 9437188

commit v4 on v2

--- a/solution.py
+++ b/solution.py
@@ -98,19 +98,33 @@
     partial, carried = lax.optimization_barrier((partial, carried))
 
     n_lag = lax.axis_size("lag")
+    ny = n_lag // 2
     me = lax.axis_index("lag")
-    field = lax.dynamic_index_in_dim(partial, me, 0, keepdims=False).astype(jnp.float32)
-    for k in range(1, n_lag):
-        piece = lax.dynamic_index_in_dim(partial, (me + k) % n_lag, 0, keepdims=False)
-        field = field + shifted_by(piece, "lag", k).astype(jnp.float32)
+    zl, y = me // ny, me % ny
+    rows = partial.reshape((2, ny) + partial.shape[1:])
+
+    def along_y(d):
+        return [(i, (i // ny) * ny + (i % ny + d) % ny) for i in range(n_lag)]
+
+    across_z = [(i, (1 - i // ny) * ny + i % ny) for i in range(n_lag)]
+    column = lax.dynamic_index_in_dim(rows, y, 1, keepdims=False).astype(jnp.float32)
+    for d in range(1, ny):
+        piece = lax.dynamic_index_in_dim(rows, (y + d) % ny, 1, keepdims=False)
+        column = column + lax.ppermute(piece, "lag", along_y(d)).astype(jnp.float32)
+    theirs = lax.dynamic_index_in_dim(column, 1 - zl, 0, keepdims=False).astype(jnp.bfloat16)
+    field = lax.dynamic_index_in_dim(column, zl, 0, keepdims=False)
+    field = field + lax.ppermute(theirs, "lag", across_z).astype(jnp.float32)
+
     mine = lax.dynamic_index_in_dim(excitation, me, 0, keepdims=False)
     residual = (mine - field).astype(jnp.bfloat16)
     inverse = lax.dynamic_index_in_dim(self_inverse, me, 0, keepdims=False)
     block = jnp.dot(inverse, residual, preferred_element_type=jnp.float32).astype(jnp.bfloat16)
 
-    gathered = [block] + [shifted_by(block, "lag", k) for k in range(1, n_lag)]
-    ordered = jnp.stack(gathered[::-1])
-    traction = jnp.roll(ordered, me + 1, axis=0)
+    partner = lax.ppermute(block, "lag", across_z)
+    pair = jnp.where(zl == 0, jnp.stack([block, partner]), jnp.stack([partner, block]))
+    columns = [pair] + [lax.ppermute(pair, "lag", along_y(d)) for d in range(1, ny)]
+    ordered = jnp.stack(columns[::-1], axis=1)
+    traction = jnp.roll(ordered, y + 1, axis=1).reshape(partial.shape)
 
     newest = jnp.where(me == 0, traction, carried)
     shifted_history = jnp.concatenate([newest[None], history[:-1]], axis=0)

time: 224 us -> 236 us (1.054)
  starting transfers between devices: 73.6 us -> 49.3 us
  waiting for transfers between devices: 104 us -> 128 us
  local copies, waits for them, and re-layouts: 14.1 us -> 22.3 us
  other arithmetic: 8.56 us -> 11.1 us
    ppermute x0 -> x8, waiting for transfers between devices: none -> 83.2 us  [the longest x3 33.7 us: shards(): column = column + lax.ppermute(piece, 'lag', along_y(d)).astype(jnp.float32)]
    ppermute x16 -> x2, starting transfers between devices: 70.1 us -> 0.51 us  [shifted_by(): lax.ppermute(array, axis, [(i, (i + by) % count) for i in range(count)])]
    ppermute x16 -> x2, waiting for transfers between devices: 87.6 us -> 28.6 us  [shifted_by(): lax.ppermute(array, axis, [(i, (i + by) % count) for i in range(count)])]
    ppermute x0 -> x8, starting transfers between devices: none -> 45.3 us  [the longest x3 33.5 us: shards(): column = column + lax.ppermute(piece, 'lag', along_y(d)).astype(jnp.float32)]
    unnamed x28 -> x21, local copies, waits for them, and re-layouts: 1.29 us -> 8.92 us
  transfers between devices with their start and end apart: 17 -> 11, of which waited for: 8 -> 9; matrix products, arithmetic and copies ran while one was open for 2% -> 3% of each run, Pallas kernels for 9% -> 9%
where the time goes in v4:
time: 236 us; the launch traced here: 233 us
  waiting for transfers between devices  128 us (54%)
  starting transfers between devices  49.3 us (21%)
  local copies, waits for them, and re-layouts  22.3 us (9%)
  Pallas kernels  20.1 us (9%)
  other arithmetic  11.1 us (5%)
    ppermute x3, waiting for transfers between devices, shards(): column = column + lax.ppermute(piece, 'lag', along_y(d)).astype(jnp.float32)  33.7 us
    ppermute x3, starting transfers between devices, shards(): column = column + lax.ppermute(piece, 'lag', along_y(d)).astype(jnp.float32)  33.5 us
    ppermute x3, waiting for transfers between devices, shards(): lax.ppermute(pair, 'lag', along_y(d))  30.7 us
    ppermute x2, waiting for transfers between devices, shifted_by(): lax.ppermute(array, axis, [(i, (i + by) % count) for i in range(count)])  28.6 us
    pallas_call x1, Pallas kernels, lag_partial(): pl.pallas_call(term_kernel, grid_spec=grid_spec, out_shape=jax.ShapeDtype...  20.1 us
    ppermute x1, waiting for transfers between devices, passed_along(): return lax.ppermute(array, axis, pairs)  15.9 us
    ppermute x1, waiting for transfers between devices, shards(): partner = lax.ppermute(block, 'lag', across_z)  9.78 us
    ppermute x1, waiting for transfers between devices, shards(): field = field + lax.ppermute(theirs, 'lag', across_z).astype(jnp.float32)  9.01 us
  transfers between devices with their start and end apart: 11, of which 9 were waited for; matrix products, arithmetic and copies ran while one was open for 3% of the time, Pallas kernels for 9%

profile of v4, /device:TPU:14, one launch (start us, length us, event | category | flops | bytes accessed | tf_op | source)
XLA Modules:
  0.0 233.1 jit_solution(11586731062735234580)
XLA Ops:
  0.6 0.0 copy-start
  0.6 0.0 copy-start.1
  0.7 6.6 %fusion.12 = (bf16[2,4,384,512]{3,2,1,0:T(8,128)(2,1)}, bf16[2,4,384,512]{3,2,1,0:T(8,128)(2,1)}) fusion(bf16[2,8,384,512]{3,2,1,0:T(8,128)(2,1)} %m1.1), kind=kLoop, calls=%fused_computation.32 | loop fusion | bytes 12582912 | tf_op jit(solution)/shard_map/slice | solution.py:95
  7.3 0.3 collective-permute-start.1
  7.5 0.0 copy-start.5
  7.5 0.0 copy-start.6
  7.5 0.2 collective-permute-start
  7.8 0.0 copy-done.1
  7.8 3.3 %fusion.11 = (bf16[1,8,384,512]{3,2,1,0:T(8,128)(2,1)}, bf16[8,384,512]{2,1,0:T(8,128)(2,1)}) fusion(bf16[2,8,384,512]{3,2,1,0:T(8,128)(2,1)S(1)} %copy-done.1), kind=kLoop, calls=%fused_computation.31 | loop fusion | bytes 12582912 | tf_op jit(solution)/shard_map/slice | solution.py:130
  11.1 3.5 %collective-permute-start.2 = (bf16[8,384,512]{2,1,0:T(8,128)(2,1)}, bf16[8,384,512]{2,1,0:T(8,128)(2,1)}, u32[]{:S(2)}, u32[]{:S(2)}) collective-permute-start(bf16[8,384,512]{2,1,0:T(8,128)(2,1)} %get-tuple-element.7), channel_id=1, source_target_pairs={{0,1},{1,2},{2,3},{3,4},{4,5},{5,6},{6,7},{8,9},{9,10},{10,11},{11... | collective-permute-start | bytes 9437192 | tf_op jit(solution)/shard_map/ppermute | solution.py:88
  14.6 0.0 copy-done.5
  14.6 0.1 copy.8
  14.7 0.0 copy-done.6
  14.7 0.6 broadcast_minimum_fusion.cnt_ref
  15.3 0.6 iota_add_fusion.src_ref
  15.9 26.7 %collective-permute-done.1.r0.r1 = bf16[2,4,384,512]{3,2,1,0:T(8,128)(2,1)} collective-permute-done((bf16[2,4,384,512]{3,2,1,0:T(8,128)(2,1)}, bf16[2,4,384,512]{3,2,1,0:T(8,128)(2,1)}, u32[]{:S(2)}, u32[]{:S(2)}) %collective-permute-start.1) | collective-permute-done | bytes 3145760 | tf_op jit(solution)/shard_map/ppermute | solution.py:82
  42.6 1.9 collective-permute-done.l0.l1
  44.5 20.1 %shard_map.77 = bf16[8,384,512]{2,1,0:T(8,128)(2,1)} custom-call(s32[2,8,2]{2,1,0:T(8,128)} %iota_add_fusion.src_ref, s32[2,8]{1,0:T(2,128)} %broadcast_minimum_fusion.cnt_ref, bf16[2,8,2,384,384]{4,3,2,1,0:T(8,128)(2,1)} %a_ref.1, bf16[2,4,384,512]{3,2,1,0:T(8,128)(2,1)} %collective-permute-done.l0.l1, bf16[2,8,384,512]{3,2,1,0:T(8,128)(2,1)} %m1.1, ...), custom_call_target="tpu_custom_call" | custom-call | flops 4831838208 | bytes 25165824 | tf_op jit(solution)/shard_map/pallas_call | solution.py:72
  64.6 15.9 %collective-permute-done.2 = bf16[8,384,512]{2,1,0:T(8,128)(2,1)} collective-permute-done((bf16[8,384,512]{2,1,0:T(8,128)(2,1)}, bf16[8,384,512]{2,1,0:T(8,128)(2,1)}, u32[]{:S(2)}, u32[]{:S(2)}) %collective-permute-start.2) | collective-permute-done | bytes 3145760 | tf_op jit(solution)/shard_map/ppermute | solution.py:88
  80.5 3.1 %dynamic-slice_bitcast_fusion.2 = (bf16[2,384,512]{2,1,0:T(8,128)(2,1)}, bf16[2,384,512]{2,1,0:T(8,128)(2,1)}, bf16[2,384,512]{2,1,0:T(8,128)(2,1)}) fusion(bf16[2,4,384,512]{3,2,1,0:T(8,128)(2,1)} %bitcast.50, s32[]{:T(128)S(6)} %select_n.92, s32[]{:T(128)S(6)} %select_n.96, s32[]{:T(128)S(6)} %select_n.94), kind=kLoop, calls=%fused_computation.21 | loop fusion | bytes 4718604 | tf_op jit(solution)/shard_map/jit(dynamic_index_in_dim)/squeeze | solution.py:112
  83.6 1.6 collective-permute-start.3
  85.2 0.4 collective-permute-start.5
  85.6 31.5 %collective-permute-start.4 = (bf16[2,384,512]{2,1,0:T(8,128)(2,1)}, bf16[2,384,512]{2,1,0:T(8,128)(2,1)}, u32[]{:S(2)}, u32[]{:S(2)}) collective-permute-start(bf16[2,384,512]{2,1,0:T(8,128)(2,1)} %get-tuple-element.12), channel_id=1, source_target_pairs={{0,2},{1,3},{2,0},{3,1},{4,6},{5,7},{6,4},{7,5},{8,10},{9,11},{10,... | collective-permute-start | bytes 2359304 | tf_op jit(solution)/shard_map/ppermute | solution.py:113
  117.1 0.0 collective-permute-done.3
  117.1 15.1 %collective-permute-done.5 = bf16[2,384,512]{2,1,0:T(8,128)(2,1)} collective-permute-done((bf16[2,384,512]{2,1,0:T(8,128)(2,1)}, bf16[2,384,512]{2,1,0:T(8,128)(2,1)}, u32[]{:S(2)}, u32[]{:S(2)}) %collective-permute-start.5) | collective-permute-done | bytes 786464 | tf_op jit(solution)/shard_map/ppermute | solution.py:113
  132.2 18.6 %collective-permute-done.4 = bf16[2,384,512]{2,1,0:T(8,128)(2,1)} collective-permute-done((bf16[2,384,512]{2,1,0:T(8,128)(2,1)}, bf16[2,384,512]{2,1,0:T(8,128)(2,1)}, u32[]{:S(2)}, u32[]{:S(2)}) %collective-permute-start.4) | collective-permute-done | bytes 786464 | tf_op jit(solution)/shard_map/ppermute | solution.py:113
  150.8 2.0 fusion.1
  152.8 0.0 copy-start.4
  152.8 1.1 copy-done.4
  154.0 3.3 %collective-permute-start.6 = (bf16[384,512]{1,0:T(8,128)(2,1)S(1)}, bf16[384,512]{1,0:T(8,128)(2,1)S(1)}, u32[]{:S(2)}, u32[]{:S(2)}) collective-permute-start(bf16[384,512]{1,0:T(8,128)(2,1)S(1)} %fusion.4), channel_id=1, source_target_pairs={{0,4},{1,5},{2,6},{3,7},{4,0},{5,1},{6,2},{7,3},{8,12},{9,13},{10,... | collective-permute-start | bytes 1179656 | tf_op jit(solution)/shard_map/ppermute | solution.py:116
  157.3 9.0 %collective-permute-done.6 = bf16[384,512]{1,0:T(8,128)(2,1)S(1)} collective-permute-done((bf16[384,512]{1,0:T(8,128)(2,1)S(1)}, bf16[384,512]{1,0:T(8,128)(2,1)S(1)}, u32[]{:S(2)}, u32[]{:S(2)}) %collective-permute-start.6) | collective-permute-done | bytes 393248 | tf_op jit(solution)/shard_map/ppermute | solution.py:116
  166.3 0.0 copy-done
  166.3 1.8 convolution_convert_fusion
  168.1 2.4 %collective-permute-start.7 = (bf16[384,512]{1,0:T(8,128)(2,1)S(1)}, bf16[384,512]{1,0:T(8,128)(2,1)S(1)}, u32[]{:S(2)}, u32[]{:S(2)}) collective-permute-start(bf16[384,512]{1,0:T(8,128)(2,1)S(1)} %convolution_convert_fusion), channel_id=1, source_target_pairs={{0,4},{1,5},{2,6},{3,7},{4,0},{5,1},{6,2},{7,3},{8,12},{9,13},{10,... | collective-permute-start | bytes 1179656 | tf_op jit(solution)/shard_map/ppermute | solution.py:123
  170.5 9.8 %collective-permute-done.7 = bf16[384,512]{1,0:T(8,128)(2,1)S(1)} collective-permute-done((bf16[384,512]{1,0:T(8,128)(2,1)S(1)}, bf16[384,512]{1,0:T(8,128)(2,1)S(1)}, u32[]{:S(2)}, u32[]{:S(2)}) %collective-permute-start.7) | collective-permute-done | bytes 393248 | tf_op jit(solution)/shard_map/ppermute | solution.py:123
  180.3 1.0 maximum_select_fusion
  181.3 1.1 collective-permute-start.8
  182.3 2.5 %collective-permute-start.9 = (bf16[2,384,512]{2,1,0:T(8,128)(2,1)}, bf16[2,384,512]{2,1,0:T(8,128)(2,1)}, u32[]{:S(2)}, u32[]{:S(2)}) collective-permute-start(bf16[2,384,512]{2,1,0:T(8,128)(2,1)} %maximum_select_fusion), channel_id=1, source_target_pairs={{0,2},{1,3},{2,0},{3,1},{4,6},{5,7},{6,4},{7,5},{8,10},{9,11},{10,... | collective-permute-start | bytes 2359304 | tf_op jit(solution)/shard_map/ppermute | solution.py:125
  184.8 2.6 %collective-permute-start.10 = (bf16[2,384,512]{2,1,0:T(8,128)(2,1)}, bf16[2,384,512]{2,1,0:T(8,128)(2,1)}, u32[]{:S(2)}, u32[]{:S(2)}) collective-permute-start(bf16[2,384,512]{2,1,0:T(8,128)(2,1)} %maximum_select_fusion), channel_id=1, source_target_pairs={{0,1},{1,2},{2,3},{3,0},{4,5},{5,6},{6,7},{7,4},{8,9},{9,10},{10,1... | collective-permute-start | bytes 2359304 | tf_op jit(solution)/shard_map/ppermute | solution.py:125
  187.4 13.5 %collective-permute-done.8 = bf16[2,384,512]{2,1,0:T(8,128)(2,1)} collective-permute-done((bf16[2,384,512]{2,1,0:T(8,128)(2,1)}, bf16[2,384,512]{2,1,0:T(8,128)(2,1)}, u32[]{:S(2)}, u32[]{:S(2)}) %collective-permute-start.8) | collective-permute-done | bytes 786464 | tf_op jit(solution)/shard_map/ppermute | solution.py:125
  201.0 1.2 bitcast_dynamic-update-slice_fusion.2
  202.1 17.2 %collective-permute-done.9 = bf16[2,384,512]{2,1,0:T(8,128)(2,1)} collective-permute-done((bf16[2,384,512]{2,1,0:T(8,128)(2,1)}, bf16[2,384,512]{2,1,0:T(8,128)(2,1)}, u32[]{:S(2)}, u32[]{:S(2)}) %collective-permute-start.9) | collective-permute-done | bytes 786464 | tf_op jit(solution)/shard_map/ppermute | solution.py:125
  219.3 1.2 bitcast_dynamic-update-slice_fusion
  220.5 0.0 collective-permute-done.10
  220.5 1.2 bitcast_dynamic-update-slice_fusion.4
  221.7 0.1 fusion.8
  221.8 1.2 bitcast_dynamic-update-slice_fusion.3
  223.0 1.2 bitcast_dynamic-update-slice_fusion.1
  224.2 1.2 bitcast_dynamic-update-slice_fusion.5
  225.4 0.1 fusion.9
  225.6 0.3 constant_dynamic-slice_fusion
  225.9 0.0 copy-start.2
  225.9 0.0 copy-start.3
  225.9 3.4 %select_bitcast_fusion = bf16[1,8,384,512]{3,2,1,0:T(8,128)(2,1)S(1)} fusion(bf16[8,384,512]{2,1,0:T(8,128)(2,1)} %collective-permute-done.2, pred[]{:T(512)S(6)} %eq.15, bf16[2,4,384,512]{3,2,1,0:T(8,128)(2,1)S(1)} %constant_dynamic-slice_fusion), kind=kLoop, calls=%fused_computation.1 | loop fusion | flops 1572864 | bytes 9437185 | tf_op jit(solution)/shard_map/broadcast_in_dim | solution.py:130
  229.3 0.0 copy-done.2
  229.3 0.6 copy-done.3
  229.9 3.2 %pad_maximum_fusion = bf16[2,8,384,512]{3,2,1,0:T(8,128)(2,1)} fusion(bf16[1,8,384,512]{3,2,1,0:T(8,128)(2,1)S(1)} %copy-done.3, bf16[1,8,384,512]{3,2,1,0:T(8,128)(2,1)S(1)} %select_bitcast_fusion), kind=kLoop, calls=%fused_computation | loop fusion | flops 3145728 | bytes 12582912 | tf_op jit(solution)/shard_map/concatenate | solution.py:130
  (1 shorter events, 0.0 us)
Async XLA Ops:
  0.6 165.7 %copy-start = (bf16[8,384,384]{2,1,0:T(8,128)(2,1)S(1)}, bf16[8,384,384]{2,1,0:T(8,128)(2,1)}, u32[]{:S(2)}) copy-start(bf16[8,384,384]{2,1,0:T(8,128)(2,1)} %param.8) | copy-start | bytes 7077892
  0.6 7.1 %copy-start.1 = (bf16[2,8,384,512]{3,2,1,0:T(8,128)(2,1)S(1)}, bf16[2,8,384,512]{3,2,1,0:T(8,128)(2,1)}, u32[]{:S(2)}) copy-start(bf16[2,8,384,512]{3,2,1,0:T(8,128)(2,1)} %m1.1) | copy-start | bytes 18874372
  7.3 35.4 %collective-permute-start.1 = (bf16[2,4,384,512]{3,2,1,0:T(8,128)(2,1)}, bf16[2,4,384,512]{3,2,1,0:T(8,128)(2,1)}, u32[]{:S(2)}, u32[]{:S(2)}) collective-permute-start(bf16[2,4,384,512]{3,2,1,0:T(8,128)(2,1)} %get-tuple-element.8), channel_id=1, source_target_pairs={{0,120},{8,0},{16,8},{24,16},{32,24},{40,32},{48,40},{56,48},{64,5... | collective-permute-start | bytes 9437192 | tf_op jit(solution)/shard_map/ppermute | solution.py:82
  7.5 7.1 %copy-start.5 = (s32[2,8,2]{1,2,0:T(2,128)S(1)}, s32[2,8,2]{1,2,0:T(2,128)}, u32[]{:S(2)}) copy-start(s32[2,8,2]{1,2,0:T(2,128)} %param.10) | copy-start | bytes 388
  7.5 7.2 %copy-start.6 = (s32[2,8]{1,0:T(2,128)S(1)}, s32[2,8]{1,0:T(2,128)}, u32[]{:S(2)}) copy-start(s32[2,8]{1,0:T(2,128)} %param.11) | copy-start | bytes 196
  7.5 37.0 %collective-permute-start = (bf16[2,4,384,512]{3,2,1,0:T(8,128)(2,1)}, bf16[2,4,384,512]{3,2,1,0:T(8,128)(2,1)}, u32[]{:S(2)}, u32[]{:S(2)}) collective-permute-start(bf16[2,4,384,512]{3,2,1,0:T(8,128)(2,1)} %get-tuple-element.9), channel_id=1, source_target_pairs={{0,8},{8,16},{16,24},{24,32},{32,40},{40,48},{48,56},{56,64},{64,7... | collective-permute-start | bytes 9437192 | tf_op jit(solution)/shard_map/ppermute | solution.py:82
  11.1 69.5 %collective-permute-start.2 = (bf16[8,384,512]{2,1,0:T(8,128)(2,1)}, bf16[8,384,512]{2,1,0:T(8,128)(2,1)}, u32[]{:S(2)}, u32[]{:S(2)}) collective-permute-start(bf16[8,384,512]{2,1,0:T(8,128)(2,1)} %get-tuple-element.7), channel_id=1, source_target_pairs={{0,1},{1,2},{2,3},{3,4},{4,5},{5,6},{6,7},{8,9},{9,10},{10,11},{11... | collective-permute-start | bytes 9437192 | tf_op jit(solution)/shard_map/ppermute | solution.py:88
  83.6 33.5 %collective-permute-start.3 = (bf16[2,384,512]{2,1,0:T(8,128)(2,1)}, bf16[2,384,512]{2,1,0:T(8,128)(2,1)S(1)}, u32[]{:S(2)}, u32[]{:S(2)}) collective-permute-start(bf16[2,384,512]{2,1,0:T(8,128)(2,1)} %get-tuple-element.10), channel_id=1, source_target_pairs={{0,1},{1,2},{2,3},{3,0},{4,5},{5,6},{6,7},{7,4},{8,9},{9,10},{10,1... | collective-permute-start | bytes 2359304 | tf_op jit(solution)/shard_map/ppermute | solution.py:113
  85.2 47.0 %collective-permute-start.5 = (bf16[2,384,512]{2,1,0:T(8,128)(2,1)}, bf16[2,384,512]{2,1,0:T(8,128)(2,1)}, u32[]{:S(2)}, u32[]{:S(2)}) collective-permute-start(bf16[2,384,512]{2,1,0:T(8,128)(2,1)} %get-tuple-element.11), channel_id=1, source_target_pairs={{0,3},{1,0},{2,1},{3,2},{4,7},{5,4},{6,5},{7,6},{8,11},{9,8},{10,9... | collective-permute-start | bytes 2359304 | tf_op jit(solution)/shard_map/ppermute | solution.py:113
  85.6 65.2 %collective-permute-start.4 = (bf16[2,384,512]{2,1,0:T(8,128)(2,1)}, bf16[2,384,512]{2,1,0:T(8,128)(2,1)}, u32[]{:S(2)}, u32[]{:S(2)}) collective-permute-start(bf16[2,384,512]{2,1,0:T(8,128)(2,1)} %get-tuple-element.12), channel_id=1, source_target_pairs={{0,2},{1,3},{2,0},{3,1},{4,6},{5,7},{6,4},{7,5},{8,10},{9,11},{10,... | collective-permute-start | bytes 2359304 | tf_op jit(solution)/shard_map/ppermute | solution.py:113
  152.8 1.1 copy-start.4
  154.0 12.3 %collective-permute-start.6 = (bf16[384,512]{1,0:T(8,128)(2,1)S(1)}, bf16[384,512]{1,0:T(8,128)(2,1)S(1)}, u32[]{:S(2)}, u32[]{:S(2)}) collective-permute-start(bf16[384,512]{1,0:T(8,128)(2,1)S(1)} %fusion.4), channel_id=1, source_target_pairs={{0,4},{1,5},{2,6},{3,7},{4,0},{5,1},{6,2},{7,3},{8,12},{9,13},{10,... | collective-permute-start | bytes 1179656 | tf_op jit(solution)/shard_map/ppermute | solution.py:116
  168.1 12.2 %collective-permute-start.7 = (bf16[384,512]{1,0:T(8,128)(2,1)S(1)}, bf16[384,512]{1,0:T(8,128)(2,1)S(1)}, u32[]{:S(2)}, u32[]{:S(2)}) collective-permute-start(bf16[384,512]{1,0:T(8,128)(2,1)S(1)} %convolution_convert_fusion), channel_id=1, source_target_pairs={{0,4},{1,5},{2,6},{3,7},{4,0},{5,1},{6,2},{7,3},{8,12},{9,13},{10,... | collective-permute-start | bytes 1179656 | tf_op jit(solution)/shard_map/ppermute | solution.py:123
  181.3 19.7 %collective-permute-start.8 = (bf16[2,384,512]{2,1,0:T(8,128)(2,1)}, bf16[2,384,512]{2,1,0:T(8,128)(2,1)}, u32[]{:S(2)}, u32[]{:S(2)}) collective-permute-start(bf16[2,384,512]{2,1,0:T(8,128)(2,1)} %maximum_select_fusion), channel_id=1, source_target_pairs={{0,3},{1,0},{2,1},{3,2},{4,7},{5,4},{6,5},{7,6},{8,11},{9,8},{10,9... | collective-permute-start | bytes 2359304 | tf_op jit(solution)/shard_map/ppermute | solution.py:125
  182.3 37.0 %collective-permute-start.9 = (bf16[2,384,512]{2,1,0:T(8,128)(2,1)}, bf16[2,384,512]{2,1,0:T(8,128)(2,1)}, u32[]{:S(2)}, u32[]{:S(2)}) collective-permute-start(bf16[2,384,512]{2,1,0:T(8,128)(2,1)} %maximum_select_fusion), channel_id=1, source_target_pairs={{0,2},{1,3},{2,0},{3,1},{4,6},{5,7},{6,4},{7,5},{8,10},{9,11},{10,... | collective-permute-start | bytes 2359304 | tf_op jit(solution)/shard_map/ppermute | solution.py:125
  184.8 35.7 %collective-permute-start.10 = (bf16[2,384,512]{2,1,0:T(8,128)(2,1)}, bf16[2,384,512]{2,1,0:T(8,128)(2,1)}, u32[]{:S(2)}, u32[]{:S(2)}) collective-permute-start(bf16[2,384,512]{2,1,0:T(8,128)(2,1)} %maximum_select_fusion), channel_id=1, source_target_pairs={{0,1},{1,2},{2,3},{3,0},{4,5},{5,6},{6,7},{7,4},{8,9},{9,10},{10,1... | collective-permute-start | bytes 2359304 | tf_op jit(solution)/shard_map/ppermute | solution.py:125
  225.9 3.4 %copy-start.2 = (bf16[2,4,384,512]{3,2,1,0:T(8,128)(2,1)}, bf16[2,4,384,512]{3,2,1,0:T(8,128)(2,1)S(1)}, u32[]{:S(2)}) copy-start(bf16[2,4,384,512]{3,2,1,0:T(8,128)(2,1)S(1)} %constant_dynamic-slice_fusion) | copy-start | bytes 9437188
  225.9 4.0 %copy-start.3 = (bf16[1,8,384,512]{3,2,1,0:T(8,128)(2,1)S(1)}, bf16[1,8,384,512]{3,2,1,0:T(8,128)(2,1)}, u32[]{:S(2)}) copy-start(bf16[1,8,384,512]{3,2,1,0:T(8,128)(2,1)} %get-tuple-element.6) | copy-start | bytes 9437188

commit v5 on v2

--- a/solution.py
+++ b/solution.py
@@ -90,12 +90,12 @@
 
 def shards(history, lag_blocks, self_inverse, excitation, pattern, live_counts):
     blocks_here = history.shape[1]
-    carried = passed_along(history[-1], "lag", 1)
     left = shifted_by(history[:, blocks_here - EDGE:], "tile", 1)
     right = shifted_by(history[:, :EDGE], "tile", -1)
+    oldest, left, right = lax.optimization_barrier((history[-1], left, right))
+    carried = passed_along(oldest, "lag", 1)
     live = jnp.minimum(live_counts, lag_blocks.shape[2])
     partial = lag_partial(history, left, right, lag_blocks, pattern, live)
-    partial, carried = lax.optimization_barrier((partial, carried))
 
     n_lag = lax.axis_size("lag")
     me = lax.axis_index("lag")
@@ -107,6 +107,7 @@
     residual = (mine - field).astype(jnp.bfloat16)
     inverse = lax.dynamic_index_in_dim(self_inverse, me, 0, keepdims=False)
     block = jnp.dot(inverse, residual, preferred_element_type=jnp.float32).astype(jnp.bfloat16)
+    block, carried = lax.optimization_barrier((block, carried))
 
     gathered = [block] + [shifted_by(block, "lag", k) for k in range(1, n_lag)]
     ordered = jnp.stack(gathered[::-1])

time: 224 us -> 221 us (0.987)
  starting transfers between devices: 73.6 us -> 30.7 us
  waiting for transfers between devices: 104 us -> 145 us
  local copies, waits for them, and re-layouts: 14.1 us -> 11.7 us
    ppermute x16, waiting for transfers between devices: 87.6 us -> 145 us  [shifted_by(): lax.ppermute(array, axis, [(i, (i + by) % count) for i in range(count)])]
    ppermute x16, starting transfers between devices: 70.1 us -> 27.2 us  [shifted_by(): lax.ppermute(array, axis, [(i, (i + by) % count) for i in range(count)])]
    ppermute x1, waiting for transfers between devices: 16.1 us -> 0.01 us  [passed_along(): return lax.ppermute(array, axis, pairs)]
    slice x1, local copies, waits for them, and re-layouts: 6.6 us -> 3.64 us  [shards(): right = shifted_by(history[:, :EDGE], 'tile', -1)]
  transfers between devices with their start and end apart: 17 -> 17, of which waited for: 8 -> 9; matrix products, arithmetic and copies ran while one was open for 2% -> 5% of each run, Pallas kernels for 9% -> 9%
where the time goes in v5:
time: 221 us; the launch traced here: 220 us
  waiting for transfers between devices  145 us (66%)
  starting transfers between devices  30.7 us (14%)
  Pallas kernels  20.5 us (9%)
  local copies, waits for them, and re-layouts  11.7 us (5%)
  other arithmetic  8.54 us (4%)
  matrix products  2.64 us (1%)
    ppermute x16, waiting for transfers between devices, shifted_by(): lax.ppermute(array, axis, [(i, (i + by) % count) for i in range(count)])  145 us
    ppermute x16, starting transfers between devices, shifted_by(): lax.ppermute(array, axis, [(i, (i + by) % count) for i in range(count)])  27.2 us
    pallas_call x1, Pallas kernels, lag_partial(): pl.pallas_call(term_kernel, grid_spec=grid_spec, out_shape=jax.ShapeDtype...  20.5 us
  transfers between devices with their start and end apart: 17, of which 9 were waited for; matrix products, arithmetic and copies ran while one was open for 5% of the time, Pallas kernels for 9%

profile of v5, /device:TPU:14, one launch (start us, length us, event | category | flops | bytes accessed | tf_op | source)
XLA Modules:
  0.0 220.4 jit_solution(2277358778155292123)
XLA Ops:
  0.6 0.0 copy-start
  0.6 0.0 copy-start.1
  0.7 3.6 %fusion.15 = (bf16[2,4,384,512]{3,2,1,0:T(8,128)(2,1)S(1)}, bf16[2,4,384,512]{3,2,1,0:T(8,128)(2,1)S(1)}) fusion(bf16[2,8,384,512]{3,2,1,0:T(8,128)(2,1)} %m1.1), kind=kLoop, calls=%fused_computation.45 | loop fusion | bytes 12582912 | tf_op jit(solution)/shard_map/slice | solution.py:94
  4.3 0.3 collective-permute-start.1
  4.6 0.0 copy-start.5
  4.6 0.0 copy-start.6
  4.6 0.2 collective-permute-start
  4.9 0.5 copy-done.1
  5.4 3.3 %fusion.14 = (bf16[1,8,384,512]{3,2,1,0:T(8,128)(2,1)}, bf16[8,384,512]{2,1,0:T(8,128)(2,1)}) fusion(bf16[2,8,384,512]{3,2,1,0:T(8,128)(2,1)S(1)} %copy-done.1), kind=kLoop, calls=%fused_computation.44 | loop fusion | bytes 12582912 | tf_op jit(solution)/shard_map/slice | solution.py:117
  8.8 30.6 %collective-permute-done.1.r0.r1 = bf16[2,4,384,512]{3,2,1,0:T(8,128)(2,1)} collective-permute-done((bf16[2,4,384,512]{3,2,1,0:T(8,128)(2,1)S(1)}, bf16[2,4,384,512]{3,2,1,0:T(8,128)(2,1)}, u32[]{:S(2)}, u32[]{:S(2)}) %collective-permute-start.1) | collective-permute-done | bytes 3145760 | tf_op jit(solution)/shard_map/ppermute | solution.py:82
  39.4 2.0 collective-permute-done.l0.l1
  41.4 3.5 %collective-permute-start.9 = (bf16[8,384,512]{2,1,0:T(8,128)(2,1)}, bf16[8,384,512]{2,1,0:T(8,128)(2,1)}, u32[]{:S(2)}, u32[]{:S(2)}) collective-permute-start(bf16[8,384,512]{2,1,0:T(8,128)(2,1)} %get-tuple-element.9), channel_id=1, source_target_pairs={{0,1},{1,2},{2,3},{3,4},{4,5},{5,6},{6,7},{8,9},{9,10},{10,11},{11... | collective-permute-start | bytes 9437192 | tf_op jit(solution)/shard_map/ppermute | solution.py:88
  45.0 0.0 copy-done.5
  45.0 0.1 copy.8
  45.1 0.0 copy-done.6
  45.1 0.6 broadcast_minimum_fusion.cnt_ref
  45.7 0.6 iota_add_fusion.src_ref
  46.3 20.5 %shard_map.77 = bf16[8,384,512]{2,1,0:T(8,128)(2,1)} custom-call(s32[2,8,2]{2,1,0:T(8,128)} %iota_add_fusion.src_ref, s32[2,8]{1,0:T(2,128)} %broadcast_minimum_fusion.cnt_ref, bf16[2,8,2,384,384]{4,3,2,1,0:T(8,128)(2,1)} %a_ref.1, bf16[2,4,384,512]{3,2,1,0:T(8,128)(2,1)} %collective-permute-done.l0.l1, bf16[2,8,384,512]{3,2,1,0:T(8,128)(2,1)} %m1.1, ...), custom_call_target="tpu_custom_call" | custom-call | flops 4831838208 | bytes 25165824 | tf_op jit(solution)/shard_map/pallas_call | solution.py:72
  66.8 2.9 %dynamic-slice_bitcast_fusion.6 = (bf16[384,512]{1,0:T(8,128)(2,1)S(1)}, bf16[384,512]{1,0:T(8,128)(2,1)S(1)}, bf16[384,512]{1,0:T(8,128)(2,1)S(1)}, bf16[384,51...) fusion(bf16[8,384,512]{2,1,0:T(8,128)(2,1)} %shard_map.77, ...), kind=kLoop, calls=%fused_computation.36 | loop fusion | bytes 5505052 | tf_op jit(solution)/shard_map/jit(dynamic_index_in_dim)/squeeze | solution.py:104
  69.7 0.0 collective-permute-start.2
  69.8 2.0 collective-permute-start.8
  71.8 2.9 %collective-permute-start.7 = (bf16[384,512]{1,0:T(8,128)(2,1)S(1)}, bf16[384,512]{1,0:T(8,128)(2,1)S(1)}, u32[]{:S(2)}, u32[]{:S(2)}) collective-permute-start(bf16[384,512]{1,0:T(8,128)(2,1)S(1)} %get-tuple-element.20), channel_id=1, source_target_pairs={{0,6},{1,7},{2,0},{3,1},{4,2},{5,3},{6,4},{7,5},{8,14},{9,15},{10,... | collective-permute-start | bytes 1179656 | tf_op jit(solution)/shard_map/ppermute | solution.py:82
  74.6 3.7 %collective-permute-start.6 = (bf16[384,512]{1,0:T(8,128)(2,1)}, bf16[384,512]{1,0:T(8,128)(2,1)}, u32[]{:S(2)}, u32[]{:S(2)}) collective-permute-start(bf16[384,512]{1,0:T(8,128)(2,1)} %get-tuple-element.21), channel_id=1, source_target_pairs={{0,5},{1,6},{2,7},{3,0},{4,1},{5,2},{6,3},{7,4},{8,13},{9,14},{10,... | collective-permute-start | bytes 1179656 | tf_op jit(solution)/shard_map/ppermute | solution.py:82
  78.3 42.4 %collective-permute-done.2 = bf16[384,512]{1,0:T(8,128)(2,1)S(1)} collective-permute-done((bf16[384,512]{1,0:T(8,128)(2,1)S(1)}, bf16[384,512]{1,0:T(8,128)(2,1)S(1)}, u32[]{:S(2)}, u32[]{:S(2)}) %collective-permute-start.2) | collective-permute-done | bytes 393248 | tf_op jit(solution)/shard_map/ppermute | solution.py:82
  120.7 1.9 collective-permute-start.5
  122.7 0.0 collective-permute-done.8
  122.7 0.0 copy-start.3
  122.7 2.2 collective-permute-start.4
  124.8 0.0 collective-permute-done.7
  124.8 0.0 copy-done.3
  124.8 0.0 copy-start.4
  124.8 0.8 copy-done.4
  125.6 0.9 collective-permute-start.3
  126.5 20.7 %collective-permute-done.6 = bf16[384,512]{1,0:T(8,128)(2,1)} collective-permute-done((bf16[384,512]{1,0:T(8,128)(2,1)}, bf16[384,512]{1,0:T(8,128)(2,1)}, u32[]{:S(2)}, u32[]{:S(2)}) %collective-permute-start.6) | collective-permute-done | bytes 393248 | tf_op jit(solution)/shard_map/ppermute | solution.py:82
  147.2 7.7 %collective-permute-done.5 = bf16[384,512]{1,0:T(8,128)(2,1)} collective-permute-done((bf16[384,512]{1,0:T(8,128)(2,1)}, bf16[384,512]{1,0:T(8,128)(2,1)}, u32[]{:S(2)}, u32[]{:S(2)}) %collective-permute-start.5) | collective-permute-done | bytes 393248 | tf_op jit(solution)/shard_map/ppermute | solution.py:82
  154.8 0.0 collective-permute-done.4
  154.8 0.0 collective-permute-done.3
  154.8 0.0 copy-done
  154.8 2.6 %convolution_convert_fusion = bf16[384,512]{1,0:T(8,128)(2,1)S(1)} fusion(bf16[384,512]{1,0:T(8,128)(2,1)} %copy-done.3, bf16[384,512]{1,0:T(8,128)(2,1)} %copy-done.4, bf16[384,512]{1,0:T(8,128)(2,1)} %collective-permute-done.6, bf16[384,512]{1,0:T(8,128)(2,1)} %collective-permute-done.5, bf16[384,512]{1,0:T(8,128)(2,1)} %collective-permute-done.4, ...), kind=kOutput, calls=%fused_computation.3 | convolution fusion | flops 154533888 | bytes 4621312 | tf_op jit(solution)/shard_map/dot_general | solution.py:109
  157.5 0.0 collective-permute-done.9
  157.5 0.1 collective-permute-start.10
  157.6 4.6 %collective-permute-start.11 = (bf16[384,512]{1,0:T(8,128)(2,1)S(1)}, bf16[384,512]{1,0:T(8,128)(2,1)S(1)}, u32[]{:S(2)}, u32[]{:S(2)}) collective-permute-start(bf16[384,512]{1,0:T(8,128)(2,1)S(1)} %convolution_convert_fusion), channel_id=1, source_target_pairs={{0,6},{1,7},{2,0},{3,1},{4,2},{5,3},{6,4},{7,5},{8,14},{9,15},{10,... | collective-permute-start | bytes 1179656 | tf_op jit(solution)/shard_map/ppermute | solution.py:82
  162.1 0.0 collective-permute-start.16
  162.1 3.3 %collective-permute-start.15 = (bf16[384,512]{1,0:T(8,128)(2,1)S(1)}, bf16[384,512]{1,0:T(8,128)(2,1)S(1)}, u32[]{:S(2)}, u32[]{:S(2)}) collective-permute-start(bf16[384,512]{1,0:T(8,128)(2,1)S(1)} %convolution_convert_fusion), channel_id=1, source_target_pairs={{0,2},{1,3},{2,4},{3,5},{4,6},{5,7},{6,0},{7,1},{8,10},{9,11},{10,... | collective-permute-start | bytes 1179656 | tf_op jit(solution)/shard_map/ppermute | solution.py:82
  165.4 0.3 collective-permute-start.14
  165.7 2.9 %collective-permute-done.10 = bf16[384,512]{1,0:T(8,128)(2,1)S(1)} collective-permute-done((bf16[384,512]{1,0:T(8,128)(2,1)S(1)}, bf16[384,512]{1,0:T(8,128)(2,1)S(1)}, u32[]{:S(2)}, u32[]{:S(2)}) %collective-permute-start.10) | collective-permute-done | bytes 393248 | tf_op jit(solution)/shard_map/ppermute | solution.py:82
  168.7 4.0 %collective-permute-start.12 = (bf16[384,512]{1,0:T(8,128)(2,1)S(1)}, bf16[384,512]{1,0:T(8,128)(2,1)S(1)}, u32[]{:S(2)}, u32[]{:S(2)}) collective-permute-start(bf16[384,512]{1,0:T(8,128)(2,1)S(1)} %convolution_convert_fusion), channel_id=1, source_target_pairs={{0,5},{1,6},{2,7},{3,0},{4,1},{5,2},{6,3},{7,4},{8,13},{9,14},{10,... | collective-permute-start | bytes 1179656 | tf_op jit(solution)/shard_map/ppermute | solution.py:82
  172.7 7.6 %collective-permute-done.11 = bf16[384,512]{1,0:T(8,128)(2,1)S(1)} collective-permute-done((bf16[384,512]{1,0:T(8,128)(2,1)S(1)}, bf16[384,512]{1,0:T(8,128)(2,1)S(1)}, u32[]{:S(2)}, u32[]{:S(2)}) %collective-permute-start.11) | collective-permute-done | bytes 393248 | tf_op jit(solution)/shard_map/ppermute | solution.py:82
  180.3 0.9 collective-permute-start.13
  181.2 22.3 %collective-permute-done.12 = bf16[384,512]{1,0:T(8,128)(2,1)S(1)} collective-permute-done((bf16[384,512]{1,0:T(8,128)(2,1)S(1)}, bf16[384,512]{1,0:T(8,128)(2,1)S(1)}, u32[]{:S(2)}, u32[]{:S(2)}) %collective-permute-start.12) | collective-permute-done | bytes 393248 | tf_op jit(solution)/shard_map/ppermute | solution.py:82
  203.6 8.9 %collective-permute-done.13 = bf16[384,512]{1,0:T(8,128)(2,1)S(1)} collective-permute-done((bf16[384,512]{1,0:T(8,128)(2,1)S(1)}, bf16[384,512]{1,0:T(8,128)(2,1)S(1)}, u32[]{:S(2)}, u32[]{:S(2)}) %collective-permute-start.13) | collective-permute-done | bytes 393248 | tf_op jit(solution)/shard_map/ppermute | solution.py:82
  212.5 0.0 collective-permute-done.14
  212.6 0.0 collective-permute-done.15
  212.6 0.0 collective-permute-done.16
  213.0 0.0 copy-start.2
  213.0 4.1 %select_bitcast_fusion = (bf16[1,8,384,512]{3,2,1,0:T(8,128)(2,1)S(1)}, bf16[8,384,512]{2,1,0:T(8,128)(2,1)}) fusion(bf16[8,384,512]{2,1,0:T(8,128)(2,1)} %collective-permute-done.9, pred[]{:T(512)S(6)} %eq.14, bf16[16,384,512]{2,1,0:T(8,128)(2,1)S(1)} %bitcast_dynamic-update-slice_fusion.1, s32[]{:T(128)S(6)} %select_n.93), kind=kLoop, calls=%fused_computation.1 | loop fusion | flops 1572864 | bytes 12582917 | tf_op jit(solution)/shard_map/broadcast_in_dim | solution.py:117
  217.1 0.0 copy-done.2
  217.1 3.2 %pad_maximum_fusion = bf16[2,8,384,512]{3,2,1,0:T(8,128)(2,1)} fusion(bf16[1,8,384,512]{3,2,1,0:T(8,128)(2,1)S(1)} %copy-done.2, bf16[1,8,384,512]{3,2,1,0:T(8,128)(2,1)S(1)} %get-tuple-element.12), kind=kLoop, calls=%fused_computation | loop fusion | flops 3145728 | bytes 12582912 | tf_op jit(solution)/shard_map/concatenate | solution.py:117
  (16 shorter events, 0.4 us)
Async XLA Ops:
  0.6 154.2 %copy-start = (bf16[8,384,384]{2,1,0:T(8,128)(2,1)S(1)}, bf16[8,384,384]{2,1,0:T(8,128)(2,1)}, u32[]{:S(2)}) copy-start(bf16[8,384,384]{2,1,0:T(8,128)(2,1)} %param.8) | copy-start | bytes 7077892
  0.6 4.8 %copy-start.1 = (bf16[2,8,384,512]{3,2,1,0:T(8,128)(2,1)S(1)}, bf16[2,8,384,512]{3,2,1,0:T(8,128)(2,1)}, u32[]{:S(2)}) copy-start(bf16[2,8,384,512]{3,2,1,0:T(8,128)(2,1)} %m1.1) | copy-start | bytes 18874372
  4.3 35.1 %collective-permute-start.1 = (bf16[2,4,384,512]{3,2,1,0:T(8,128)(2,1)S(1)}, bf16[2,4,384,512]{3,2,1,0:T(8,128)(2,1)}, u32[]{:S(2)}, u32[]{:S(2)}) collective-permute-start(bf16[2,4,384,512]{3,2,1,0:T(8,128)(2,1)S(1)} %get-tuple-element.16), channel_id=1, source_target_pairs={{0,120},{8,0},{16,8},{24,16},{32,24},{40,32},{48,40},{56,48},{64,5... | collective-permute-start | bytes 9437192 | tf_op jit(solution)/shard_map/ppermute | solution.py:82
  4.6 40.4 %copy-start.5 = (s32[2,8,2]{1,2,0:T(2,128)S(1)}, s32[2,8,2]{1,2,0:T(2,128)}, u32[]{:S(2)}) copy-start(s32[2,8,2]{1,2,0:T(2,128)} %param.10) | copy-start | bytes 388
  4.6 40.5 %copy-start.6 = (s32[2,8]{1,0:T(2,128)S(1)}, s32[2,8]{1,0:T(2,128)}, u32[]{:S(2)}) copy-start(s32[2,8]{1,0:T(2,128)} %param.11) | copy-start | bytes 196
  4.6 36.8 %collective-permute-start = (bf16[2,4,384,512]{3,2,1,0:T(8,128)(2,1)S(1)}, bf16[2,4,384,512]{3,2,1,0:T(8,128)(2,1)}, u32[]{:S(2)}, u32[]{:S(2)}) collective-permute-start(bf16[2,4,384,512]{3,2,1,0:T(8,128)(2,1)S(1)} %get-tuple-element.17), channel_id=1, source_target_pairs={{0,8},{8,16},{16,24},{24,32},{32,40},{40,48},{48,56},{56,64},{64,7... | collective-permute-start | bytes 9437192 | tf_op jit(solution)/shard_map/ppermute | solution.py:82
  41.4 116.0 %collective-permute-start.9 = (bf16[8,384,512]{2,1,0:T(8,128)(2,1)}, bf16[8,384,512]{2,1,0:T(8,128)(2,1)}, u32[]{:S(2)}, u32[]{:S(2)}) collective-permute-start(bf16[8,384,512]{2,1,0:T(8,128)(2,1)} %get-tuple-element.9), channel_id=1, source_target_pairs={{0,1},{1,2},{2,3},{3,4},{4,5},{5,6},{6,7},{8,9},{9,10},{10,11},{11... | collective-permute-start | bytes 9437192 | tf_op jit(solution)/shard_map/ppermute | solution.py:88
  69.7 51.0 %collective-permute-start.2 = (bf16[384,512]{1,0:T(8,128)(2,1)S(1)}, bf16[384,512]{1,0:T(8,128)(2,1)S(1)}, u32[]{:S(2)}, u32[]{:S(2)}) collective-permute-start(bf16[384,512]{1,0:T(8,128)(2,1)S(1)} %get-tuple-element.18), channel_id=1, source_target_pairs={{0,1},{1,2},{2,3},{3,4},{4,5},{5,6},{6,7},{7,0},{8,9},{9,10},{10,1... | collective-permute-start | bytes 1179656 | tf_op jit(solution)/shard_map/ppermute | solution.py:82
  69.8 52.9 %collective-permute-start.8 = (bf16[384,512]{1,0:T(8,128)(2,1)S(1)}, bf16[384,512]{1,0:T(8,128)(2,1)S(1)}, u32[]{:S(2)}, u32[]{:S(2)}) collective-permute-start(bf16[384,512]{1,0:T(8,128)(2,1)S(1)} %get-tuple-element.19), channel_id=1, source_target_pairs={{0,7},{1,0},{2,1},{3,2},{4,3},{5,4},{6,5},{7,6},{8,15},{9,8},{10,9... | collective-permute-start | bytes 1179656 | tf_op jit(solution)/shard_map/ppermute | solution.py:82
  71.8 53.1 %collective-permute-start.7 = (bf16[384,512]{1,0:T(8,128)(2,1)S(1)}, bf16[384,512]{1,0:T(8,128)(2,1)S(1)}, u32[]{:S(2)}, u32[]{:S(2)}) collective-permute-start(bf16[384,512]{1,0:T(8,128)(2,1)S(1)} %get-tuple-element.20), channel_id=1, source_target_pairs={{0,6},{1,7},{2,0},{3,1},{4,2},{5,3},{6,4},{7,5},{8,14},{9,15},{10,... | collective-permute-start | bytes 1179656 | tf_op jit(solution)/shard_map/ppermute | solution.py:82
  74.6 72.5 %collective-permute-start.6 = (bf16[384,512]{1,0:T(8,128)(2,1)}, bf16[384,512]{1,0:T(8,128)(2,1)}, u32[]{:S(2)}, u32[]{:S(2)}) collective-permute-start(bf16[384,512]{1,0:T(8,128)(2,1)} %get-tuple-element.21), channel_id=1, source_target_pairs={{0,5},{1,6},{2,7},{3,0},{4,1},{5,2},{6,3},{7,4},{8,13},{9,14},{10,... | collective-permute-start | bytes 1179656 | tf_op jit(solution)/shard_map/ppermute | solution.py:82
  120.7 34.1 %collective-permute-start.5 = (bf16[384,512]{1,0:T(8,128)(2,1)}, bf16[384,512]{1,0:T(8,128)(2,1)}, u32[]{:S(2)}, u32[]{:S(2)}) collective-permute-start(bf16[384,512]{1,0:T(8,128)(2,1)} %get-tuple-element.22), channel_id=1, source_target_pairs={{0,4},{1,5},{2,6},{3,7},{4,0},{5,1},{6,2},{7,3},{8,12},{9,13},{10,... | collective-permute-start | bytes 1179656 | tf_op jit(solution)/shard_map/ppermute | solution.py:82
  122.7 2.2 copy-start.3
  122.7 32.2 %collective-permute-start.4 = (bf16[384,512]{1,0:T(8,128)(2,1)S(1)}, bf16[384,512]{1,0:T(8,128)(2,1)}, u32[]{:S(2)}, u32[]{:S(2)}) collective-permute-start(bf16[384,512]{1,0:T(8,128)(2,1)S(1)} %get-tuple-element.23), channel_id=1, source_target_pairs={{0,3},{1,4},{2,5},{3,6},{4,7},{5,0},{6,1},{7,2},{8,11},{9,12},{10,... | collective-permute-start | bytes 1179656 | tf_op jit(solution)/shard_map/ppermute | solution.py:82
  124.8 0.8 copy-start.4
  125.6 29.2 %collective-permute-start.3 = (bf16[384,512]{1,0:T(8,128)(2,1)S(1)}, bf16[384,512]{1,0:T(8,128)(2,1)}, u32[]{:S(2)}, u32[]{:S(2)}) collective-permute-start(bf16[384,512]{1,0:T(8,128)(2,1)S(1)} %get-tuple-element.24), channel_id=1, source_target_pairs={{0,2},{1,3},{2,4},{3,5},{4,6},{5,7},{6,0},{7,1},{8,10},{9,11},{10,... | collective-permute-start | bytes 1179656 | tf_op jit(solution)/shard_map/ppermute | solution.py:82
  157.5 11.2 %collective-permute-start.10 = (bf16[384,512]{1,0:T(8,128)(2,1)S(1)}, bf16[384,512]{1,0:T(8,128)(2,1)S(1)}, u32[]{:S(2)}, u32[]{:S(2)}) collective-permute-start(bf16[384,512]{1,0:T(8,128)(2,1)S(1)} %convolution_convert_fusion), channel_id=1, source_target_pairs={{0,7},{1,0},{2,1},{3,2},{4,3},{5,4},{6,5},{7,6},{8,15},{9,8},{10,9... | collective-permute-start | bytes 1179656 | tf_op jit(solution)/shard_map/ppermute | solution.py:82
  157.6 22.7 %collective-permute-start.11 = (bf16[384,512]{1,0:T(8,128)(2,1)S(1)}, bf16[384,512]{1,0:T(8,128)(2,1)S(1)}, u32[]{:S(2)}, u32[]{:S(2)}) collective-permute-start(bf16[384,512]{1,0:T(8,128)(2,1)S(1)} %convolution_convert_fusion), channel_id=1, source_target_pairs={{0,6},{1,7},{2,0},{3,1},{4,2},{5,3},{6,4},{7,5},{8,14},{9,15},{10,... | collective-permute-start | bytes 1179656 | tf_op jit(solution)/shard_map/ppermute | solution.py:82
  162.1 50.5 %collective-permute-start.16 = (bf16[384,512]{1,0:T(8,128)(2,1)S(1)}, bf16[384,512]{1,0:T(8,128)(2,1)S(1)}, u32[]{:S(2)}, u32[]{:S(2)}) collective-permute-start(bf16[384,512]{1,0:T(8,128)(2,1)S(1)} %convolution_convert_fusion), channel_id=1, source_target_pairs={{0,1},{1,2},{2,3},{3,4},{4,5},{5,6},{6,7},{7,0},{8,9},{9,10},{10,1... | collective-permute-start | bytes 1179656 | tf_op jit(solution)/shard_map/ppermute | solution.py:82
  162.1 50.5 %collective-permute-start.15 = (bf16[384,512]{1,0:T(8,128)(2,1)S(1)}, bf16[384,512]{1,0:T(8,128)(2,1)S(1)}, u32[]{:S(2)}, u32[]{:S(2)}) collective-permute-start(bf16[384,512]{1,0:T(8,128)(2,1)S(1)} %convolution_convert_fusion), channel_id=1, source_target_pairs={{0,2},{1,3},{2,4},{3,5},{4,6},{5,7},{6,0},{7,1},{8,10},{9,11},{10,... | collective-permute-start | bytes 1179656 | tf_op jit(solution)/shard_map/ppermute | solution.py:82
  165.4 47.1 %collective-permute-start.14 = (bf16[384,512]{1,0:T(8,128)(2,1)S(1)}, bf16[384,512]{1,0:T(8,128)(2,1)S(1)}, u32[]{:S(2)}, u32[]{:S(2)}) collective-permute-start(bf16[384,512]{1,0:T(8,128)(2,1)S(1)} %convolution_convert_fusion), channel_id=1, source_target_pairs={{0,3},{1,4},{2,5},{3,6},{4,7},{5,0},{6,1},{7,2},{8,11},{9,12},{10,... | collective-permute-start | bytes 1179656 | tf_op jit(solution)/shard_map/ppermute | solution.py:82
  168.7 34.9 %collective-permute-start.12 = (bf16[384,512]{1,0:T(8,128)(2,1)S(1)}, bf16[384,512]{1,0:T(8,128)(2,1)S(1)}, u32[]{:S(2)}, u32[]{:S(2)}) collective-permute-start(bf16[384,512]{1,0:T(8,128)(2,1)S(1)} %convolution_convert_fusion), channel_id=1, source_target_pairs={{0,5},{1,6},{2,7},{3,0},{4,1},{5,2},{6,3},{7,4},{8,13},{9,14},{10,... | collective-permute-start | bytes 1179656 | tf_op jit(solution)/shard_map/ppermute | solution.py:82
  180.3 32.2 %collective-permute-start.13 = (bf16[384,512]{1,0:T(8,128)(2,1)S(1)}, bf16[384,512]{1,0:T(8,128)(2,1)S(1)}, u32[]{:S(2)}, u32[]{:S(2)}) collective-permute-start(bf16[384,512]{1,0:T(8,128)(2,1)S(1)} %convolution_convert_fusion), channel_id=1, source_target_pairs={{0,4},{1,5},{2,6},{3,7},{4,0},{5,1},{6,2},{7,3},{8,12},{9,13},{10,... | collective-permute-start | bytes 1179656 | tf_op jit(solution)/shard_map/ppermute | solution.py:82
  213.0 4.1 %copy-start.2 = (bf16[1,8,384,512]{3,2,1,0:T(8,128)(2,1)S(1)}, bf16[1,8,384,512]{3,2,1,0:T(8,128)(2,1)}, u32[]{:S(2)}) copy-start(bf16[1,8,384,512]{3,2,1,0:T(8,128)(2,1)} %get-tuple-element.14) | copy-start | bytes 9437188

commit v6 on v2

--- a/solution.py
+++ b/solution.py
@@ -90,12 +90,14 @@
 
 def shards(history, lag_blocks, self_inverse, excitation, pattern, live_counts):
     blocks_here = history.shape[1]
-    carried = passed_along(history[-1], "lag", 1)
+    half = blocks_here // 2
+    early = passed_along(history[-1, :half], "lag", 1)
     left = shifted_by(history[:, blocks_here - EDGE:], "tile", 1)
     right = shifted_by(history[:, :EDGE], "tile", -1)
+    oldest, left, right, early = lax.optimization_barrier((history[-1, half:], left, right, early))
+    late = passed_along(oldest, "lag", 1)
     live = jnp.minimum(live_counts, lag_blocks.shape[2])
     partial = lag_partial(history, left, right, lag_blocks, pattern, live)
-    partial, carried = lax.optimization_barrier((partial, carried))
 
     n_lag = lax.axis_size("lag")
     me = lax.axis_index("lag")
@@ -107,6 +109,8 @@
     residual = (mine - field).astype(jnp.bfloat16)
     inverse = lax.dynamic_index_in_dim(self_inverse, me, 0, keepdims=False)
     block = jnp.dot(inverse, residual, preferred_element_type=jnp.float32).astype(jnp.bfloat16)
+    block, late = lax.optimization_barrier((block, late))
+    carried = jnp.concatenate([early, late], axis=0)
 
     gathered = [block] + [shifted_by(block, "lag", k) for k in range(1, n_lag)]
     ordered = jnp.stack(gathered[::-1])

time: 224 us -> 220 us (0.982)
  the two profiles are of different devices: /device:TPU:14 before, /device:TPU:62 now
where the time goes in v6:
time: 220 us; the launch traced here: 219 us
  starting transfers between devices  88.6 us (40%)
  waiting for transfers between devices  84.5 us (38%)
  Pallas kernels  21.5 us (10%)
  local copies, waits for them, and re-layouts  12.9 us (6%)
  other arithmetic  7.77 us (4%)
  matrix products  2.62 us (1%)
    ppermute x16, starting transfers between devices, shifted_by(): lax.ppermute(array, axis, [(i, (i + by) % count) for i in range(count)])  86 us
    ppermute x16, waiting for transfers between devices, shifted_by(): lax.ppermute(array, axis, [(i, (i + by) % count) for i in range(count)])  47.9 us
    ppermute x2, waiting for transfers between devices, passed_along(): return lax.ppermute(array, axis, pairs)  36.6 us
    pallas_call x1, Pallas kernels, lag_partial(): pl.pallas_call(term_kernel, grid_spec=grid_spec, out_shape=jax.ShapeDtype...  21.5 us
    slice x1, local copies, waits for them, and re-layouts, shards(): right = shifted_by(history[:, :EDGE], 'tile', -1)  6.6 us
  transfers between devices with their start and end apart: 18, of which 6 were waited for; matrix products, arithmetic and copies ran while one was open for 4% of the time, Pallas kernels for 10%

profile of v6, /device:TPU:62, one launch (start us, length us, event | category | flops | bytes accessed | tf_op | source)
XLA Modules:
  0.0 218.7 jit_solution(14940320144022589469)
XLA Ops:
  0.6 0.0 copy-start
  0.6 0.0 copy-start.1
  0.7 6.6 %fusion.15 = (bf16[2,4,384,512]{3,2,1,0:T(8,128)(2,1)}, bf16[2,4,384,512]{3,2,1,0:T(8,128)(2,1)}) fusion(bf16[2,8,384,512]{3,2,1,0:T(8,128)(2,1)} %m1.1), kind=kLoop, calls=%fused_computation.46 | loop fusion | bytes 12582912 | tf_op jit(solution)/shard_map/slice | solution.py:96
  7.3 0.0 copy-start.4
  7.3 0.0 copy-start.5
  7.3 0.0 collective-permute-start
  7.3 1.7 collective-permute-start.1
  9.0 0.0 copy-done.1
  9.0 2.0 slice_bitcast_fusion
  11.0 1.3 collective-permute-start.2
  12.4 0.0 copy-done.4
  12.4 0.1 copy.8
  12.5 0.0 copy-done.5
  12.5 0.5 broadcast_minimum_fusion.cnt_ref
  13.0 0.6 iota_add_fusion.src_ref
  13.6 36.6 %collective-permute-done.2 = bf16[4,384,512]{2,1,0:T(8,128)(2,1)} collective-permute-done((bf16[4,384,512]{2,1,0:T(8,128)(2,1)}, bf16[4,384,512]{2,1,0:T(8,128)(2,1)}, u32[]{:S(2)}, u32[]{:S(2)}) %collective-permute-start.2) | collective-permute-done | bytes 1572896 | tf_op jit(solution)/shard_map/ppermute | solution.py:88
  50.2 0.0 collective-permute-done.l0.l1
  50.2 0.0 collective-permute-done.1.r0.r1
  50.2 1.3 collective-permute-start.10
  51.5 21.5 %shard_map.77 = bf16[8,384,512]{2,1,0:T(8,128)(2,1)} custom-call(s32[2,8,2]{2,1,0:T(8,128)} %iota_add_fusion.src_ref, s32[2,8]{1,0:T(2,128)} %broadcast_minimum_fusion.cnt_ref, bf16[2,8,2,384,384]{4,3,2,1,0:T(8,128)(2,1)} %a_ref.1, bf16[2,4,384,512]{3,2,1,0:T(8,128)(2,1)} %collective-permute-done.l0.l1, bf16[2,8,384,512]{3,2,1,0:T(8,128)(2,1)} %m1.1, ...), custom_call_target="tpu_custom_call" | custom-call | flops 4831838208 | bytes 25165824 | tf_op jit(solution)/shard_map/pallas_call | solution.py:72
  73.0 2.9 %dynamic-slice_bitcast_fusion.6 = (bf16[384,512]{1,0:T(8,128)(2,1)S(1)}, bf16[384,512]{1,0:T(8,128)(2,1)S(1)}, bf16[384,512]{1,0:T(8,128)(2,1)S(1)}, bf16[384,51...) fusion(bf16[8,384,512]{2,1,0:T(8,128)(2,1)} %shard_map.77, ...), kind=kLoop, calls=%fused_computation.38 | loop fusion | bytes 5505052 | tf_op jit(solution)/shard_map/jit(dynamic_index_in_dim)/squeeze | solution.py:106
  75.9 2.3 %collective-permute-start.9 = (bf16[384,512]{1,0:T(8,128)(2,1)S(1)}, bf16[384,512]{1,0:T(8,128)(2,1)S(1)}, u32[]{:S(2)}, u32[]{:S(2)}) collective-permute-start(bf16[384,512]{1,0:T(8,128)(2,1)S(1)} %get-tuple-element.21), channel_id=1, source_target_pairs={{0,7},{1,0},{2,1},{3,2},{4,3},{5,4},{6,5},{7,6},{8,15},{9,8},{10,9... | collective-permute-start | bytes 1179656 | tf_op jit(solution)/shard_map/ppermute | solution.py:82
  78.2 29.7 %collective-permute-start.8 = (bf16[384,512]{1,0:T(8,128)(2,1)S(1)}, bf16[384,512]{1,0:T(8,128)(2,1)S(1)}, u32[]{:S(2)}, u32[]{:S(2)}) collective-permute-start(bf16[384,512]{1,0:T(8,128)(2,1)S(1)} %get-tuple-element.22), channel_id=1, source_target_pairs={{0,6},{1,7},{2,0},{3,1},{4,2},{5,3},{6,4},{7,5},{8,14},{9,15},{10,... | collective-permute-start | bytes 1179656 | tf_op jit(solution)/shard_map/ppermute | solution.py:82
  107.9 3.4 %collective-permute-start.7 = (bf16[384,512]{1,0:T(8,128)(2,1)S(1)}, bf16[384,512]{1,0:T(8,128)(2,1)S(1)}, u32[]{:S(2)}, u32[]{:S(2)}) collective-permute-start(bf16[384,512]{1,0:T(8,128)(2,1)S(1)} %get-tuple-element.23), channel_id=1, source_target_pairs={{0,5},{1,6},{2,7},{3,0},{4,1},{5,2},{6,3},{7,4},{8,13},{9,14},{10,... | collective-permute-start | bytes 1179656 | tf_op jit(solution)/shard_map/ppermute | solution.py:82
  111.3 0.0 collective-permute-start.6
  111.3 0.0 collective-permute-done.9
  111.3 8.7 %collective-permute-start.5 = (bf16[384,512]{1,0:T(8,128)(2,1)}, bf16[384,512]{1,0:T(8,128)(2,1)}, u32[]{:S(2)}, u32[]{:S(2)}) collective-permute-start(bf16[384,512]{1,0:T(8,128)(2,1)} %get-tuple-element.25), channel_id=1, source_target_pairs={{0,3},{1,4},{2,5},{3,6},{4,7},{5,0},{6,1},{7,2},{8,11},{9,12},{10,... | collective-permute-start | bytes 1179656 | tf_op jit(solution)/shard_map/ppermute | solution.py:82
  120.1 0.0 collective-permute-done.8
  120.1 0.0 copy-start.2
  120.1 15.1 %collective-permute-start.4 = (bf16[384,512]{1,0:T(8,128)(2,1)S(1)}, bf16[384,512]{1,0:T(8,128)(2,1)}, u32[]{:S(2)}, u32[]{:S(2)}) collective-permute-start(bf16[384,512]{1,0:T(8,128)(2,1)S(1)} %get-tuple-element.26), channel_id=1, source_target_pairs={{0,2},{1,3},{2,4},{3,5},{4,6},{5,7},{6,0},{7,1},{8,10},{9,11},{10,... | collective-permute-start | bytes 1179656 | tf_op jit(solution)/shard_map/ppermute | solution.py:82
  135.2 0.0 collective-permute-done.7
  135.2 0.0 copy-done.2
  135.2 0.0 copy-start.3
  135.2 0.8 copy-done.3
  136.0 15.1 %collective-permute-start.3 = (bf16[384,512]{1,0:T(8,128)(2,1)S(1)}, bf16[384,512]{1,0:T(8,128)(2,1)}, u32[]{:S(2)}, u32[]{:S(2)}) collective-permute-start(bf16[384,512]{1,0:T(8,128)(2,1)S(1)} %get-tuple-element.20), channel_id=1, source_target_pairs={{0,1},{1,2},{2,3},{3,4},{4,5},{5,6},{6,7},{7,0},{8,9},{9,10},{10,1... | collective-permute-start | bytes 1179656 | tf_op jit(solution)/shard_map/ppermute | solution.py:82
  151.1 0.0 collective-permute-done.6
  151.1 0.0 collective-permute-done.5
  151.1 0.0 collective-permute-done.4
  151.1 5.3 %collective-permute-done.3 = bf16[384,512]{1,0:T(8,128)(2,1)} collective-permute-done((bf16[384,512]{1,0:T(8,128)(2,1)S(1)}, bf16[384,512]{1,0:T(8,128)(2,1)}, u32[]{:S(2)}, u32[]{:S(2)}) %collective-permute-start.3) | collective-permute-done | bytes 393248 | tf_op jit(solution)/shard_map/ppermute | solution.py:82
  156.4 0.0 copy-done
  156.4 2.6 %convolution_convert_fusion = bf16[384,512]{1,0:T(8,128)(2,1)S(1)} fusion(bf16[384,512]{1,0:T(8,128)(2,1)S(1)} %collective-permute-done.9, bf16[384,512]{1,0:T(8,128)(2,1)} %copy-done.2, bf16[384,512]{1,0:T(8,128)(2,1)} %copy-done.3, bf16[384,512]{1,0:T(8,128)(2,1)} %collective-permute-done.6, bf16[384,512]{1,0:T(8,128)(2,1)} %collective-permute-done.5, ...), kind=kOutput, calls=%fused_computation.5 | convolution fusion | flops 154533888 | bytes 4621312 | tf_op jit(solution)/shard_map/dot_general | solution.py:111
  159.1 0.0 collective-permute-done.10
  159.1 1.1 collective-permute-start.11
  160.2 5.6 %collective-permute-start.12 = (bf16[384,512]{1,0:T(8,128)(2,1)S(1)}, bf16[384,512]{1,0:T(8,128)(2,1)S(1)}, u32[]{:S(2)}, u32[]{:S(2)}) collective-permute-start(bf16[384,512]{1,0:T(8,128)(2,1)S(1)} %convolution_convert_fusion), channel_id=1, source_target_pairs={{0,6},{1,7},{2,0},{3,1},{4,2},{5,3},{6,4},{7,5},{8,14},{9,15},{10,... | collective-permute-start | bytes 1179656 | tf_op jit(solution)/shard_map/ppermute | solution.py:82
  165.8 0.8 collective-permute-start.13
  166.5 0.0 collective-permute-start.14
  166.5 2.3 %collective-permute-start.15 = (bf16[384,512]{1,0:T(8,128)(2,1)S(1)}, bf16[384,512]{1,0:T(8,128)(2,1)S(1)}, u32[]{:S(2)}, u32[]{:S(2)}) collective-permute-start(bf16[384,512]{1,0:T(8,128)(2,1)S(1)} %convolution_convert_fusion), channel_id=1, source_target_pairs={{0,3},{1,4},{2,5},{3,6},{4,7},{5,0},{6,1},{7,2},{8,11},{9,12},{10,... | collective-permute-start | bytes 1179656 | tf_op jit(solution)/shard_map/ppermute | solution.py:82
  168.9 17.0 %collective-permute-done.11 = bf16[384,512]{1,0:T(8,128)(2,1)S(1)} collective-permute-done((bf16[384,512]{1,0:T(8,128)(2,1)S(1)}, bf16[384,512]{1,0:T(8,128)(2,1)S(1)}, u32[]{:S(2)}, u32[]{:S(2)}) %collective-permute-start.11) | collective-permute-done | bytes 393248 | tf_op jit(solution)/shard_map/ppermute | solution.py:82
  185.9 0.0 collective-permute-start.16
  185.9 0.0 collective-permute-done.12
  185.9 0.1 collective-permute-start.17
  186.0 2.1 collective-permute-done.13
  188.2 10.4 %collective-permute-done.14 = bf16[384,512]{1,0:T(8,128)(2,1)S(1)} collective-permute-done((bf16[384,512]{1,0:T(8,128)(2,1)S(1)}, bf16[384,512]{1,0:T(8,128)(2,1)S(1)}, u32[]{:S(2)}, u32[]{:S(2)}) %collective-permute-start.14) | collective-permute-done | bytes 393248 | tf_op jit(solution)/shard_map/ppermute | solution.py:82
  198.6 0.0 collective-permute-done.15
  198.7 13.0 %collective-permute-done.16 = bf16[384,512]{1,0:T(8,128)(2,1)S(1)} collective-permute-done((bf16[384,512]{1,0:T(8,128)(2,1)S(1)}, bf16[384,512]{1,0:T(8,128)(2,1)S(1)}, u32[]{:S(2)}, u32[]{:S(2)}) %collective-permute-start.16) | collective-permute-done | bytes 393248 | tf_op jit(solution)/shard_map/ppermute | solution.py:82
  211.7 0.0 collective-permute-done.17
  212.1 0.0 slice-start
  212.1 3.4 %fusion = (bf16[1,8,384,512]{3,2,1,0:T(8,128)(2,1)S(1)}, bf16[8,384,512]{2,1,0:T(8,128)(2,1)}) fusion(bf16[4,384,512]{2,1,0:T(8,128)(2,1)} %collective-permute-done.10, bf16[4,384,512]{2,1,0:T(8,128)(2,1)} %collective-permute-done.2, pred[]{:T(512)S(6)} %eq.14, bf16[16,384,512]{2,1,0:T(8,128)(2,1)S(1)} %bitcast_dynamic-update-slice_fusion.1, s32[]{:T(128)S(6)} %select_n.93), kind=kLoop, calls=%fused_computation.2 | loop fusion | flops 3145728 | bytes 12582917 | tf_op jit(solution)/shard_map/broadcast_in_dim | solution.py:120
  215.5 0.0 slice-done
  215.5 3.2 %pad_maximum_fusion = bf16[2,8,384,512]{3,2,1,0:T(8,128)(2,1)} fusion(bf16[1,8,384,512]{3,2,1,0:T(8,128)(2,1)S(1)} %slice-done, bf16[1,8,384,512]{3,2,1,0:T(8,128)(2,1)S(1)} %get-tuple-element.14), kind=kLoop, calls=%fused_computation | loop fusion | flops 3145728 | bytes 12582912 | tf_op jit(solution)/shard_map/concatenate | solution.py:120
  (16 shorter events, 0.4 us)
Async XLA Ops:
  0.6 155.8 %copy-start = (bf16[8,384,384]{2,1,0:T(8,128)(2,1)S(1)}, bf16[8,384,384]{2,1,0:T(8,128)(2,1)}, u32[]{:S(2)}) copy-start(bf16[8,384,384]{2,1,0:T(8,128)(2,1)} %param.8) | copy-start | bytes 7077892
  0.6 8.4 %copy-start.1 = (bf16[2,8,384,512]{3,2,1,0:T(8,128)(2,1)S(1)}, bf16[2,8,384,512]{3,2,1,0:T(8,128)(2,1)}, u32[]{:S(2)}) copy-start(bf16[2,8,384,512]{3,2,1,0:T(8,128)(2,1)} %m1.1) | copy-start | bytes 18874372
  7.3 5.2 %copy-start.4 = (s32[2,8,2]{1,2,0:T(2,128)S(1)}, s32[2,8,2]{1,2,0:T(2,128)}, u32[]{:S(2)}) copy-start(s32[2,8,2]{1,2,0:T(2,128)} %param.10) | copy-start | bytes 388
  7.3 5.3 %copy-start.5 = (s32[2,8]{1,0:T(2,128)S(1)}, s32[2,8]{1,0:T(2,128)}, u32[]{:S(2)}) copy-start(s32[2,8]{1,0:T(2,128)} %param.11) | copy-start | bytes 196
  7.3 43.0 %collective-permute-start = (bf16[2,4,384,512]{3,2,1,0:T(8,128)(2,1)}, bf16[2,4,384,512]{3,2,1,0:T(8,128)(2,1)}, u32[]{:S(2)}, u32[]{:S(2)}) collective-permute-start(bf16[2,4,384,512]{3,2,1,0:T(8,128)(2,1)} %get-tuple-element.19), channel_id=1, source_target_pairs={{0,8},{8,16},{16,24},{24,32},{32,40},{40,48},{48,56},{56,64},{64,7... | collective-permute-start | bytes 9437192 | tf_op jit(solution)/shard_map/ppermute | solution.py:82
  7.3 42.9 %collective-permute-start.1 = (bf16[2,4,384,512]{3,2,1,0:T(8,128)(2,1)}, bf16[2,4,384,512]{3,2,1,0:T(8,128)(2,1)}, u32[]{:S(2)}, u32[]{:S(2)}) collective-permute-start(bf16[2,4,384,512]{3,2,1,0:T(8,128)(2,1)} %get-tuple-element.18), channel_id=1, source_target_pairs={{0,120},{8,0},{16,8},{24,16},{32,24},{40,32},{48,40},{56,48},{64,5... | collective-permute-start | bytes 9437192 | tf_op jit(solution)/shard_map/ppermute | solution.py:82
  11.0 39.2 %collective-permute-start.2 = (bf16[4,384,512]{2,1,0:T(8,128)(2,1)}, bf16[4,384,512]{2,1,0:T(8,128)(2,1)}, u32[]{:S(2)}, u32[]{:S(2)}) collective-permute-start(bf16[4,384,512]{2,1,0:T(8,128)(2,1)} %get-tuple-element.16), channel_id=1, source_target_pairs={{0,1},{1,2},{2,3},{3,4},{4,5},{5,6},{6,7},{8,9},{9,10},{10,11},{11... | collective-permute-start | bytes 4718600 | tf_op jit(solution)/shard_map/ppermute | solution.py:88
  50.2 108.8 %collective-permute-start.10 = (bf16[4,384,512]{2,1,0:T(8,128)(2,1)}, bf16[4,384,512]{2,1,0:T(8,128)(2,1)}, u32[]{:S(2)}, u32[]{:S(2)}) collective-permute-start(bf16[4,384,512]{2,1,0:T(8,128)(2,1)} %get-tuple-element.10), channel_id=1, source_target_pairs={{0,1},{1,2},{2,3},{3,4},{4,5},{5,6},{6,7},{8,9},{9,10},{10,11},{11... | collective-permute-start | bytes 4718600 | tf_op jit(solution)/shard_map/ppermute | solution.py:88
  75.9 35.4 %collective-permute-start.9 = (bf16[384,512]{1,0:T(8,128)(2,1)S(1)}, bf16[384,512]{1,0:T(8,128)(2,1)S(1)}, u32[]{:S(2)}, u32[]{:S(2)}) collective-permute-start(bf16[384,512]{1,0:T(8,128)(2,1)S(1)} %get-tuple-element.21), channel_id=1, source_target_pairs={{0,7},{1,0},{2,1},{3,2},{4,3},{5,4},{6,5},{7,6},{8,15},{9,8},{10,9... | collective-permute-start | bytes 1179656 | tf_op jit(solution)/shard_map/ppermute | solution.py:82
  78.2 41.8 %collective-permute-start.8 = (bf16[384,512]{1,0:T(8,128)(2,1)S(1)}, bf16[384,512]{1,0:T(8,128)(2,1)S(1)}, u32[]{:S(2)}, u32[]{:S(2)}) collective-permute-start(bf16[384,512]{1,0:T(8,128)(2,1)S(1)} %get-tuple-element.22), channel_id=1, source_target_pairs={{0,6},{1,7},{2,0},{3,1},{4,2},{5,3},{6,4},{7,5},{8,14},{9,15},{10,... | collective-permute-start | bytes 1179656 | tf_op jit(solution)/shard_map/ppermute | solution.py:82
  107.9 27.3 %collective-permute-start.7 = (bf16[384,512]{1,0:T(8,128)(2,1)S(1)}, bf16[384,512]{1,0:T(8,128)(2,1)S(1)}, u32[]{:S(2)}, u32[]{:S(2)}) collective-permute-start(bf16[384,512]{1,0:T(8,128)(2,1)S(1)} %get-tuple-element.23), channel_id=1, source_target_pairs={{0,5},{1,6},{2,7},{3,0},{4,1},{5,2},{6,3},{7,4},{8,13},{9,14},{10,... | collective-permute-start | bytes 1179656 | tf_op jit(solution)/shard_map/ppermute | solution.py:82
  111.3 39.8 %collective-permute-start.6 = (bf16[384,512]{1,0:T(8,128)(2,1)}, bf16[384,512]{1,0:T(8,128)(2,1)}, u32[]{:S(2)}, u32[]{:S(2)}) collective-permute-start(bf16[384,512]{1,0:T(8,128)(2,1)} %get-tuple-element.24), channel_id=1, source_target_pairs={{0,4},{1,5},{2,6},{3,7},{4,0},{5,1},{6,2},{7,3},{8,12},{9,13},{10,... | collective-permute-start | bytes 1179656 | tf_op jit(solution)/shard_map/ppermute | solution.py:82
  111.3 39.8 %collective-permute-start.5 = (bf16[384,512]{1,0:T(8,128)(2,1)}, bf16[384,512]{1,0:T(8,128)(2,1)}, u32[]{:S(2)}, u32[]{:S(2)}) collective-permute-start(bf16[384,512]{1,0:T(8,128)(2,1)} %get-tuple-element.25), channel_id=1, source_target_pairs={{0,3},{1,4},{2,5},{3,6},{4,7},{5,0},{6,1},{7,2},{8,11},{9,12},{10,... | collective-permute-start | bytes 1179656 | tf_op jit(solution)/shard_map/ppermute | solution.py:82
  120.1 15.2 %copy-start.2 = (bf16[384,512]{1,0:T(8,128)(2,1)}, bf16[384,512]{1,0:T(8,128)(2,1)S(1)}, u32[]{:S(2)}) copy-start(bf16[384,512]{1,0:T(8,128)(2,1)S(1)} %collective-permute-done.8) | copy-start | bytes 1179652
  120.1 31.0 %collective-permute-start.4 = (bf16[384,512]{1,0:T(8,128)(2,1)S(1)}, bf16[384,512]{1,0:T(8,128)(2,1)}, u32[]{:S(2)}, u32[]{:S(2)}) collective-permute-start(bf16[384,512]{1,0:T(8,128)(2,1)S(1)} %get-tuple-element.26), channel_id=1, source_target_pairs={{0,2},{1,3},{2,4},{3,5},{4,6},{5,7},{6,0},{7,1},{8,10},{9,11},{10,... | collective-permute-start | bytes 1179656 | tf_op jit(solution)/shard_map/ppermute | solution.py:82
  135.2 0.8 copy-start.3
  136.0 20.4 %collective-permute-start.3 = (bf16[384,512]{1,0:T(8,128)(2,1)S(1)}, bf16[384,512]{1,0:T(8,128)(2,1)}, u32[]{:S(2)}, u32[]{:S(2)}) collective-permute-start(bf16[384,512]{1,0:T(8,128)(2,1)S(1)} %get-tuple-element.20), channel_id=1, source_target_pairs={{0,1},{1,2},{2,3},{3,4},{4,5},{5,6},{6,7},{7,0},{8,9},{9,10},{10,1... | collective-permute-start | bytes 1179656 | tf_op jit(solution)/shard_map/ppermute | solution.py:82
  159.1 26.8 %collective-permute-start.11 = (bf16[384,512]{1,0:T(8,128)(2,1)S(1)}, bf16[384,512]{1,0:T(8,128)(2,1)S(1)}, u32[]{:S(2)}, u32[]{:S(2)}) collective-permute-start(bf16[384,512]{1,0:T(8,128)(2,1)S(1)} %convolution_convert_fusion), channel_id=1, source_target_pairs={{0,7},{1,0},{2,1},{3,2},{4,3},{5,4},{6,5},{7,6},{8,15},{9,8},{10,9... | collective-permute-start | bytes 1179656 | tf_op jit(solution)/shard_map/ppermute | solution.py:82
  160.2 25.7 %collective-permute-start.12 = (bf16[384,512]{1,0:T(8,128)(2,1)S(1)}, bf16[384,512]{1,0:T(8,128)(2,1)S(1)}, u32[]{:S(2)}, u32[]{:S(2)}) collective-permute-start(bf16[384,512]{1,0:T(8,128)(2,1)S(1)} %convolution_convert_fusion), channel_id=1, source_target_pairs={{0,6},{1,7},{2,0},{3,1},{4,2},{5,3},{6,4},{7,5},{8,14},{9,15},{10,... | collective-permute-start | bytes 1179656 | tf_op jit(solution)/shard_map/ppermute | solution.py:82
  165.8 22.4 %collective-permute-start.13 = (bf16[384,512]{1,0:T(8,128)(2,1)S(1)}, bf16[384,512]{1,0:T(8,128)(2,1)S(1)}, u32[]{:S(2)}, u32[]{:S(2)}) collective-permute-start(bf16[384,512]{1,0:T(8,128)(2,1)S(1)} %convolution_convert_fusion), channel_id=1, source_target_pairs={{0,5},{1,6},{2,7},{3,0},{4,1},{5,2},{6,3},{7,4},{8,13},{9,14},{10,... | collective-permute-start | bytes 1179656 | tf_op jit(solution)/shard_map/ppermute | solution.py:82
  166.5 32.1 %collective-permute-start.14 = (bf16[384,512]{1,0:T(8,128)(2,1)S(1)}, bf16[384,512]{1,0:T(8,128)(2,1)S(1)}, u32[]{:S(2)}, u32[]{:S(2)}) collective-permute-start(bf16[384,512]{1,0:T(8,128)(2,1)S(1)} %convolution_convert_fusion), channel_id=1, source_target_pairs={{0,4},{1,5},{2,6},{3,7},{4,0},{5,1},{6,2},{7,3},{8,12},{9,13},{10,... | collective-permute-start | bytes 1179656 | tf_op jit(solution)/shard_map/ppermute | solution.py:82
  166.5 32.1 %collective-permute-start.15 = (bf16[384,512]{1,0:T(8,128)(2,1)S(1)}, bf16[384,512]{1,0:T(8,128)(2,1)S(1)}, u32[]{:S(2)}, u32[]{:S(2)}) collective-permute-start(bf16[384,512]{1,0:T(8,128)(2,1)S(1)} %convolution_convert_fusion), channel_id=1, source_target_pairs={{0,3},{1,4},{2,5},{3,6},{4,7},{5,0},{6,1},{7,2},{8,11},{9,12},{10,... | collective-permute-start | bytes 1179656 | tf_op jit(solution)/shard_map/ppermute | solution.py:82
  185.9 25.8 %collective-permute-start.16 = (bf16[384,512]{1,0:T(8,128)(2,1)S(1)}, bf16[384,512]{1,0:T(8,128)(2,1)S(1)}, u32[]{:S(2)}, u32[]{:S(2)}) collective-permute-start(bf16[384,512]{1,0:T(8,128)(2,1)S(1)} %convolution_convert_fusion), channel_id=1, source_target_pairs={{0,2},{1,3},{2,4},{3,5},{4,6},{5,7},{6,0},{7,1},{8,10},{9,11},{10,... | collective-permute-start | bytes 1179656 | tf_op jit(solution)/shard_map/ppermute | solution.py:82
  185.9 25.8 %collective-permute-start.17 = (bf16[384,512]{1,0:T(8,128)(2,1)S(1)}, bf16[384,512]{1,0:T(8,128)(2,1)S(1)}, u32[]{:S(2)}, u32[]{:S(2)}) collective-permute-start(bf16[384,512]{1,0:T(8,128)(2,1)S(1)} %convolution_convert_fusion), channel_id=1, source_target_pairs={{0,1},{1,2},{2,3},{3,4},{4,5},{5,6},{6,7},{7,0},{8,9},{9,10},{10,1... | collective-permute-start | bytes 1179656 | tf_op jit(solution)/shard_map/ppermute | solution.py:82
  212.1 3.4 %slice-start = ((bf16[2,8,384,512]{3,2,1,0:T(8,128)(2,1)}), bf16[1,8,384,512]{3,2,1,0:T(8,128)(2,1)S(1)}, s32[]{:S(2)}) async-start(bf16[2,8,384,512]{3,2,1,0:T(8,128)(2,1)} %m1.1), calls=%async_computation | async-start | bytes 6291456 | tf_op jit(solution)/shard_map/slice | solution.py:120

commit v7 on v6

--- a/solution.py
+++ b/solution.py
@@ -8,7 +8,7 @@
 EDGE = 4
 
 
-def term_kernel(src_ref, cnt_ref, a_ref, l0, m0, r0, l1, m1, r1, out_ref, acc_ref):
+def term_kernel(src_ref, cnt_ref, off_ref, a_ref, l0, m0, r0, l1, m1, r1, out_ref, acc_ref):
     b = pl.program_id(0)
     l = pl.program_id(1)
     blocks = pl.num_programs(0)
@@ -31,7 +31,7 @@
         out_ref[...] = acc_ref[...].astype(out_ref.dtype)
 
 
-def lag_partial(history, left, right, lag_blocks, pattern, live_counts):
+def lag_partial(history, left, right, lag_blocks, pattern, live_counts, offset):
     lags, blocks, vec, ex = history.shape
     slots = lag_blocks.shape[2]
     window = jnp.arange(blocks, dtype=jnp.int32)[None, :, None] + pattern
@@ -41,7 +41,7 @@
         return (s < cnt[l, b]) & (w >= lo) & (w < hi), w - lo
 
     def source_spec(s, lo, hi, count):
-        def index(b, l, src, cnt):
+        def index(b, l, src, cnt, off):
             on, at = used(src, cnt, l, b, s, lo, hi)
             return (jnp.where(on, l, 0), jnp.where(on, jnp.clip(at, 0, count - 1), 0), 0, 0)
         return pl.BlockSpec((None, None, vec, ex), index)
@@ -55,16 +55,16 @@
     def right_spec(s):
         return source_spec(s, EDGE + blocks, 2 * EDGE + blocks, EDGE)
 
-    in_specs = [pl.BlockSpec((None, None, slots, vec, vec), lambda b, l, src, cnt: (l, b, 0, 0, 0))]
+    in_specs = [pl.BlockSpec((None, None, slots, vec, vec), lambda b, l, src, cnt, off: (l, b, 0, 0, 0))]
     operands = [lag_blocks]
     for s in range(slots):
         in_specs += [left_spec(s), local_spec(s), right_spec(s)]
         operands += [left, history, right]
     grid_spec = pltpu.PrefetchScalarGridSpec(
-        num_scalar_prefetch=2,
+        num_scalar_prefetch=3,
         grid=(blocks, lags),
         in_specs=in_specs,
-        out_specs=pl.BlockSpec((None, vec, ex), lambda b, l, src, cnt: (b, 0, 0)),
+        out_specs=pl.BlockSpec((None, vec, ex), lambda b, l, src, cnt, off: ((b - off[0]) % blocks, 0, 0)),
         scratch_shapes=[pltpu.VMEM((vec, ex), jnp.float32)],
     )
     flops = 2 * lags * blocks * slots * vec * vec * ex
@@ -74,7 +74,7 @@
         grid_spec=grid_spec,
         out_shape=jax.ShapeDtypeStruct((blocks, vec, ex), jnp.bfloat16),
         cost_estimate=pl.CostEstimate(flops=flops, transcendentals=0, bytes_accessed=moved),
-    )(window, live_counts, *operands)
+    )(window, live_counts, offset, *operands)
 
 
 def shifted_by(array, axis, by):
@@ -97,27 +97,28 @@
     oldest, left, right, early = lax.optimization_barrier((history[-1, half:], left, right, early))
     late = passed_along(oldest, "lag", 1)
     live = jnp.minimum(live_counts, lag_blocks.shape[2])
-    partial = lag_partial(history, left, right, lag_blocks, pattern, live)
-
     n_lag = lax.axis_size("lag")
     me = lax.axis_index("lag")
-    field = lax.dynamic_index_in_dim(partial, me, 0, keepdims=False).astype(jnp.float32)
+    offset = jnp.full((1,), me, jnp.int32)
+    partial = lag_partial(history, left, right, lag_blocks, pattern, live, offset)
+
+    field = partial[0].astype(jnp.float32)
     for k in range(1, n_lag):
-        piece = lax.dynamic_index_in_dim(partial, (me + k) % n_lag, 0, keepdims=False)
-        field = field + shifted_by(piece, "lag", k).astype(jnp.float32)
+        field = field + shifted_by(partial[k], "lag", k).astype(jnp.float32)
     mine = lax.dynamic_index_in_dim(excitation, me, 0, keepdims=False)
     residual = (mine - field).astype(jnp.bfloat16)
     inverse = lax.dynamic_index_in_dim(self_inverse, me, 0, keepdims=False)
     block = jnp.dot(inverse, residual, preferred_element_type=jnp.float32).astype(jnp.bfloat16)
     block, late = lax.optimization_barrier((block, late))
     carried = jnp.concatenate([early, late], axis=0)
+    shifted_history = jnp.concatenate([carried[None], history[:-1]], axis=0)
 
     gathered = [block] + [shifted_by(block, "lag", k) for k in range(1, n_lag)]
     ordered = jnp.stack(gathered[::-1])
     traction = jnp.roll(ordered, me + 1, axis=0)
 
     newest = jnp.where(me == 0, traction, carried)
-    shifted_history = jnp.concatenate([newest[None], history[:-1]], axis=0)
+    shifted_history = lax.dynamic_update_slice(shifted_history, newest[None], (0, 0, 0, 0))
     return (traction, shifted_history)
 
 

time: 220 us -> 237 us (1.077)
  the two profiles are of different devices: /device:TPU:62 before, /device:TPU:14 now
where the time goes in v7:
time: 237 us; the launch traced here: 236 us
  waiting for transfers between devices  103 us (43%)
  starting transfers between devices  86.2 us (36%)
  Pallas kernels  21.3 us (9%)
  local copies, waits for them, and re-layouts  18 us (8%)
  other arithmetic  4.47 us (2%)
  matrix products  2.39 us (1%)
    ppermute x16, starting transfers between devices, shifted_by(): lax.ppermute(array, axis, [(i, (i + by) % count) for i in range(count)])  79.2 us
    ppermute x16, waiting for transfers between devices, shifted_by(): lax.ppermute(array, axis, [(i, (i + by) % count) for i in range(count)])  71.8 us
    ppermute x2, waiting for transfers between devices, passed_along(): return lax.ppermute(array, axis, pairs)  31 us
    pallas_call x1, Pallas kernels, lag_partial(): pl.pallas_call(term_kernel, grid_spec=grid_spec, out_shape=jax.ShapeDtype...  21.3 us
    ppermute x2, starting transfers between devices, passed_along(): return lax.ppermute(array, axis, pairs)  6.95 us
    slice x1, local copies, waits for them, and re-layouts, shards(): right = shifted_by(history[:, :EDGE], 'tile', -1)  6.6 us
    unnamed x27, local copies, waits for them, and re-layouts  4.89 us
  transfers between devices with their start and end apart: 18, of which 7 were waited for; matrix products, arithmetic and copies ran while one was open for 5% of the time, Pallas kernels for 9%

profile of v7, /device:TPU:14, one launch (start us, length us, event | category | flops | bytes accessed | tf_op | source)
XLA Modules:
  0.0 236.0 jit_solution(15862747662285593088)
XLA Ops:
  0.6 0.0 copy-start
  0.6 0.0 copy-start.1
  0.7 6.6 %fusion.12 = (bf16[2,4,384,512]{3,2,1,0:T(8,128)(2,1)}, bf16[2,4,384,512]{3,2,1,0:T(8,128)(2,1)}) fusion(bf16[2,8,384,512]{3,2,1,0:T(8,128)(2,1)} %m1.1), kind=kLoop, calls=%fused_computation.46 | loop fusion | bytes 12582912 | tf_op jit(solution)/shard_map/slice | solution.py:96
  7.3 0.0 copy-start.3
  7.3 0.0 copy-start.4
  7.3 0.3 collective-permute-start.1
  7.5 0.2 collective-permute-start
  7.8 0.0 copy-done.1
  7.8 2.0 slice_bitcast_fusion
  9.8 3.5 %collective-permute-start.2 = (bf16[4,384,512]{2,1,0:T(8,128)(2,1)}, bf16[4,384,512]{2,1,0:T(8,128)(2,1)}, u32[]{:S(2)}, u32[]{:S(2)}) collective-permute-start(bf16[4,384,512]{2,1,0:T(8,128)(2,1)} %get-tuple-element.16), channel_id=1, source_target_pairs={{0,1},{1,2},{2,3},{3,4},{4,5},{5,6},{6,7},{8,9},{9,10},{10,11},{11... | collective-permute-start | bytes 4718600 | tf_op jit(solution)/shard_map/ppermute | solution.py:88
  13.3 0.0 copy-done.3
  13.3 0.1 copy.8
  13.4 0.0 copy-done.4
  13.4 0.5 broadcast_minimum_fusion.cnt_ref
  13.9 0.6 iota_add_fusion.src_ref
  14.5 31.0 %collective-permute-done.2 = bf16[4,384,512]{2,1,0:T(8,128)(2,1)} collective-permute-done((bf16[4,384,512]{2,1,0:T(8,128)(2,1)}, bf16[4,384,512]{2,1,0:T(8,128)(2,1)}, u32[]{:S(2)}, u32[]{:S(2)}) %collective-permute-start.2) | collective-permute-done | bytes 1572896 | tf_op jit(solution)/shard_map/ppermute | solution.py:88
  45.5 0.0 collective-permute-done.1.r0.r1
  45.5 0.0 collective-permute-done.l0.l1
  45.5 3.5 %collective-permute-start.10 = (bf16[4,384,512]{2,1,0:T(8,128)(2,1)}, bf16[4,384,512]{2,1,0:T(8,128)(2,1)}, u32[]{:S(2)}, u32[]{:S(2)}) collective-permute-start(bf16[4,384,512]{2,1,0:T(8,128)(2,1)} %get-tuple-element.10), channel_id=1, source_target_pairs={{0,1},{1,2},{2,3},{3,4},{4,5},{5,6},{6,7},{8,9},{9,10},{10,11},{11... | collective-permute-start | bytes 4718600 | tf_op jit(solution)/shard_map/ppermute | solution.py:88
  49.0 21.3 %shard_map.77 = bf16[8,384,512]{2,1,0:T(8,128)(2,1)} custom-call(s32[2,8,2]{2,1,0:T(8,128)} %iota_add_fusion.src_ref, s32[2,8]{1,0:T(2,128)} %broadcast_minimum_fusion.cnt_ref, s32[1]{0:T(128)} %bitcast.2.off_ref, bf16[2,8,2,384,384]{4,3,2,1,0:T(8,128)(2,1)} %a_ref.1, bf16[2,4,384,512]{3,2,1,0:T(8,128)(2,1)} %collective-permute-done.l0.l1, ...), custom_call_target="tpu_custom_call" | custom-call | flops 4831838208 | bytes 25165824 | tf_op jit(solution)/shard_map/pallas_call | solution.py:72
  70.3 3.0 %slice_bitcast_fusion.8 = (bf16[384,512]{1,0:T(8,128)(2,1)S(1)}, bf16[384,512]{1,0:T(8,128)(2,1)S(1)}, bf16[384,512]{1,0:T(8,128)(2,1)S(1)}, bf16[384,512]{1,0:T...) fusion(bf16[8,384,512]{2,1,0:T(8,128)(2,1)} %shard_map.77), kind=kLoop, calls=%fused_computation.20 | loop fusion | bytes 5505024 | tf_op jit(solution)/shard_map/squeeze | solution.py:107
  73.3 28.9 %collective-permute-start.3 = (bf16[384,512]{1,0:T(8,128)(2,1)S(1)}, bf16[384,512]{1,0:T(8,128)(2,1)S(1)}, u32[]{:S(2)}, u32[]{:S(2)}) collective-permute-start(bf16[384,512]{1,0:T(8,128)(2,1)S(1)} %get-tuple-element.20), channel_id=1, source_target_pairs={{0,1},{1,2},{2,3},{3,4},{4,5},{5,6},{6,7},{7,0},{8,9},{9,10},{10,1... | collective-permute-start | bytes 1179656 | tf_op jit(solution)/shard_map/ppermute | solution.py:82
  102.2 0.0 collective-permute-start.9
  102.2 0.0 collective-permute-start.8
  102.2 10.9 %collective-permute-start.7 = (bf16[384,512]{1,0:T(8,128)(2,1)}, bf16[384,512]{1,0:T(8,128)(2,1)}, u32[]{:S(2)}, u32[]{:S(2)}) collective-permute-start(bf16[384,512]{1,0:T(8,128)(2,1)} %get-tuple-element.23), channel_id=1, source_target_pairs={{0,5},{1,6},{2,7},{3,0},{4,1},{5,2},{6,3},{7,4},{8,13},{9,14},{10,... | collective-permute-start | bytes 1179656 | tf_op jit(solution)/shard_map/ppermute | solution.py:82
  113.1 0.0 collective-permute-done.3
  113.1 12.0 %collective-permute-start.6 = (bf16[384,512]{1,0:T(8,128)(2,1)}, bf16[384,512]{1,0:T(8,128)(2,1)}, u32[]{:S(2)}, u32[]{:S(2)}) collective-permute-start(bf16[384,512]{1,0:T(8,128)(2,1)} %get-tuple-element.24), channel_id=1, source_target_pairs={{0,4},{1,5},{2,6},{3,7},{4,0},{5,1},{6,2},{7,3},{8,12},{9,13},{10,... | collective-permute-start | bytes 1179656 | tf_op jit(solution)/shard_map/ppermute | solution.py:82
  125.1 0.0 collective-permute-done.9
  125.1 12.3 %collective-permute-start.5 = (bf16[384,512]{1,0:T(8,128)(2,1)}, bf16[384,512]{1,0:T(8,128)(2,1)}, u32[]{:S(2)}, u32[]{:S(2)}) collective-permute-start(bf16[384,512]{1,0:T(8,128)(2,1)} %get-tuple-element.25), channel_id=1, source_target_pairs={{0,3},{1,4},{2,5},{3,6},{4,7},{5,0},{6,1},{7,2},{8,11},{9,12},{10,... | collective-permute-start | bytes 1179656 | tf_op jit(solution)/shard_map/ppermute | solution.py:82
  137.4 0.0 collective-permute-done.8
  137.4 0.0 collective-permute-start.4
  137.4 0.0 slice-start
  137.4 1.7 constant_dynamic-update-slice_fusion.1
  139.1 6.2 %collective-permute-done.7 = bf16[384,512]{1,0:T(8,128)(2,1)} collective-permute-done((bf16[384,512]{1,0:T(8,128)(2,1)}, bf16[384,512]{1,0:T(8,128)(2,1)}, u32[]{:S(2)}, u32[]{:S(2)}) %collective-permute-start.7) | collective-permute-done | bytes 393248 | tf_op jit(solution)/shard_map/ppermute | solution.py:82
  145.3 12.4 %collective-permute-done.6 = bf16[384,512]{1,0:T(8,128)(2,1)} collective-permute-done((bf16[384,512]{1,0:T(8,128)(2,1)}, bf16[384,512]{1,0:T(8,128)(2,1)}, u32[]{:S(2)}, u32[]{:S(2)}) %collective-permute-start.6) | collective-permute-done | bytes 393248 | tf_op jit(solution)/shard_map/ppermute | solution.py:82
  157.7 0.0 collective-permute-done.5
  157.7 2.1 collective-permute-done.4
  159.8 0.0 copy-done
  159.8 2.4 %convolution_convert_fusion = bf16[384,512]{1,0:T(8,128)(2,1)S(1)} fusion(bf16[384,512]{1,0:T(8,128)(2,1)S(1)} %collective-permute-done.9, bf16[384,512]{1,0:T(8,128)(2,1)S(1)} %collective-permute-done.8, bf16[384,512]{1,0:T(8,128)(2,1)} %collective-permute-done.7, bf16[384,512]{1,0:T(8,128)(2,1)} %collective-permute-done.6, ...), kind=kOutput, calls=%fused_computation.4 | convolution fusion | flops 154533888 | bytes 4621312 | tf_op jit(solution)/shard_map/dot_general | solution.py:111
  162.2 0.0 collective-permute-done.10
  162.2 0.1 collective-permute-start.17
  162.3 7.8 %collective-permute-start.16 = (bf16[384,512]{1,0:T(8,128)(2,1)S(1)}, bf16[384,512]{1,0:T(8,128)(2,1)S(1)}, u32[]{:S(2)}, u32[]{:S(2)}) collective-permute-start(bf16[384,512]{1,0:T(8,128)(2,1)S(1)} %convolution_convert_fusion), channel_id=1, source_target_pairs={{0,2},{1,3},{2,4},{3,5},{4,6},{5,7},{6,0},{7,1},{8,10},{9,11},{10,... | collective-permute-start | bytes 1179656 | tf_op jit(solution)/shard_map/ppermute | solution.py:82
  170.1 0.9 collective-permute-start.15
  171.0 1.0 collective-permute-start.12
  172.0 3.2 %collective-permute-start.11 = (bf16[384,512]{1,0:T(8,128)(2,1)S(1)}, bf16[384,512]{1,0:T(8,128)(2,1)S(1)}, u32[]{:S(2)}, u32[]{:S(2)}) collective-permute-start(bf16[384,512]{1,0:T(8,128)(2,1)S(1)} %convolution_convert_fusion), channel_id=1, source_target_pairs={{0,7},{1,0},{2,1},{3,2},{4,3},{5,4},{6,5},{7,6},{8,15},{9,8},{10,9... | collective-permute-start | bytes 1179656 | tf_op jit(solution)/shard_map/ppermute | solution.py:82
  175.1 1.5 constant_dynamic-update-slice_fusion
  176.6 0.0 slice-done
  176.6 0.6 pad_maximum_fusion
  177.2 32.9 %collective-permute-done.11 = bf16[384,512]{1,0:T(8,128)(2,1)S(1)} collective-permute-done((bf16[384,512]{1,0:T(8,128)(2,1)S(1)}, bf16[384,512]{1,0:T(8,128)(2,1)S(1)}, u32[]{:S(2)}, u32[]{:S(2)}) %collective-permute-start.11) | collective-permute-done | bytes 393248 | tf_op jit(solution)/shard_map/ppermute | solution.py:82
  210.2 0.0 collective-permute-start.13
  210.2 0.0 collective-permute-done.12
  210.2 1.7 collective-permute-start.14
  211.9 11.3 %collective-permute-done.13 = bf16[384,512]{1,0:T(8,128)(2,1)S(1)} collective-permute-done((bf16[384,512]{1,0:T(8,128)(2,1)S(1)}, bf16[384,512]{1,0:T(8,128)(2,1)S(1)}, u32[]{:S(2)}, u32[]{:S(2)}) %collective-permute-start.13) | collective-permute-done | bytes 393248 | tf_op jit(solution)/shard_map/ppermute | solution.py:82
  223.3 6.8 %collective-permute-done.14 = bf16[384,512]{1,0:T(8,128)(2,1)S(1)} collective-permute-done((bf16[384,512]{1,0:T(8,128)(2,1)S(1)}, bf16[384,512]{1,0:T(8,128)(2,1)S(1)}, u32[]{:S(2)}, u32[]{:S(2)}) %collective-permute-start.14) | collective-permute-done | bytes 393248 | tf_op jit(solution)/shard_map/ppermute | solution.py:82
  230.1 0.0 collective-permute-done.15
  230.2 0.0 collective-permute-done.16
  230.2 0.0 collective-permute-done.17
  230.6 2.8 %bitcast_dynamic-update-slice_fusion = (bf16[2,8,384,512]{3,2,1,0:T(8,128)(2,1)S(1)}, bf16[8,384,512]{2,1,0:T(8,128)(2,1)}) fusion(bf16[2,8,384,512]{3,2,1,0:T(8,128)(2,1)S(1)} %pad_maximum_fusion, bf16[8,384,512]{2,1,0:T(8,128)(2,1)S(1)} %constant_dynamic-update-slice_fusion, pred[]{:T(512)S(6)} %eq.6, ...), kind=kLoop, calls=%fused_computation.1 | loop fusion | flops 1572864 | bytes 12582917 | tf_op jit(solution)/shard_map/dynamic_update_slice | solution.py:121
  233.3 0.0 copy-start.2
  233.3 2.7 %copy-done.2 = bf16[2,8,384,512]{3,2,1,0:T(8,128)(2,1)} copy-done((bf16[2,8,384,512]{3,2,1,0:T(8,128)(2,1)}, bf16[2,8,384,512]{3,2,1,0:T(8,128)(2,1)S(1)}, u32[]{:S(2)}) %copy-start.2) | copy-done | bytes 6291480
  (16 shorter events, 0.4 us)
Async XLA Ops:
  0.6 159.2 %copy-start = (bf16[8,384,384]{2,1,0:T(8,128)(2,1)S(1)}, bf16[8,384,384]{2,1,0:T(8,128)(2,1)}, u32[]{:S(2)}) copy-start(bf16[8,384,384]{2,1,0:T(8,128)(2,1)} %param.8) | copy-start | bytes 7077892
  0.6 7.1 %copy-start.1 = (bf16[2,8,384,512]{3,2,1,0:T(8,128)(2,1)S(1)}, bf16[2,8,384,512]{3,2,1,0:T(8,128)(2,1)}, u32[]{:S(2)}) copy-start(bf16[2,8,384,512]{3,2,1,0:T(8,128)(2,1)} %m1.1) | copy-start | bytes 18874372
  7.3 6.0 %copy-start.3 = (s32[2,8,2]{1,2,0:T(2,128)S(1)}, s32[2,8,2]{1,2,0:T(2,128)}, u32[]{:S(2)}) copy-start(s32[2,8,2]{1,2,0:T(2,128)} %param.10) | copy-start | bytes 388
  7.3 6.1 %copy-start.4 = (s32[2,8]{1,0:T(2,128)S(1)}, s32[2,8]{1,0:T(2,128)}, u32[]{:S(2)}) copy-start(s32[2,8]{1,0:T(2,128)} %param.11) | copy-start | bytes 196
  7.3 38.3 %collective-permute-start.1 = (bf16[2,4,384,512]{3,2,1,0:T(8,128)(2,1)}, bf16[2,4,384,512]{3,2,1,0:T(8,128)(2,1)}, u32[]{:S(2)}, u32[]{:S(2)}) collective-permute-start(bf16[2,4,384,512]{3,2,1,0:T(8,128)(2,1)} %get-tuple-element.18), channel_id=1, source_target_pairs={{0,120},{8,0},{16,8},{24,16},{32,24},{40,32},{48,40},{56,48},{64,5... | collective-permute-start | bytes 9437192 | tf_op jit(solution)/shard_map/ppermute | solution.py:82
  7.5 38.0 %collective-permute-start = (bf16[2,4,384,512]{3,2,1,0:T(8,128)(2,1)}, bf16[2,4,384,512]{3,2,1,0:T(8,128)(2,1)}, u32[]{:S(2)}, u32[]{:S(2)}) collective-permute-start(bf16[2,4,384,512]{3,2,1,0:T(8,128)(2,1)} %get-tuple-element.19), channel_id=1, source_target_pairs={{0,8},{8,16},{16,24},{24,32},{32,40},{40,48},{48,56},{56,64},{64,7... | collective-permute-start | bytes 9437192 | tf_op jit(solution)/shard_map/ppermute | solution.py:82
  9.8 35.7 %collective-permute-start.2 = (bf16[4,384,512]{2,1,0:T(8,128)(2,1)}, bf16[4,384,512]{2,1,0:T(8,128)(2,1)}, u32[]{:S(2)}, u32[]{:S(2)}) collective-permute-start(bf16[4,384,512]{2,1,0:T(8,128)(2,1)} %get-tuple-element.16), channel_id=1, source_target_pairs={{0,1},{1,2},{2,3},{3,4},{4,5},{5,6},{6,7},{8,9},{9,10},{10,11},{11... | collective-permute-start | bytes 4718600 | tf_op jit(solution)/shard_map/ppermute | solution.py:88
  45.5 116.7 %collective-permute-start.10 = (bf16[4,384,512]{2,1,0:T(8,128)(2,1)}, bf16[4,384,512]{2,1,0:T(8,128)(2,1)}, u32[]{:S(2)}, u32[]{:S(2)}) collective-permute-start(bf16[4,384,512]{2,1,0:T(8,128)(2,1)} %get-tuple-element.10), channel_id=1, source_target_pairs={{0,1},{1,2},{2,3},{3,4},{4,5},{5,6},{6,7},{8,9},{9,10},{10,11},{11... | collective-permute-start | bytes 4718600 | tf_op jit(solution)/shard_map/ppermute | solution.py:88
  73.3 39.8 %collective-permute-start.3 = (bf16[384,512]{1,0:T(8,128)(2,1)S(1)}, bf16[384,512]{1,0:T(8,128)(2,1)S(1)}, u32[]{:S(2)}, u32[]{:S(2)}) collective-permute-start(bf16[384,512]{1,0:T(8,128)(2,1)S(1)} %get-tuple-element.20), channel_id=1, source_target_pairs={{0,1},{1,2},{2,3},{3,4},{4,5},{5,6},{6,7},{7,0},{8,9},{9,10},{10,1... | collective-permute-start | bytes 1179656 | tf_op jit(solution)/shard_map/ppermute | solution.py:82
  102.2 22.9 %collective-permute-start.9 = (bf16[384,512]{1,0:T(8,128)(2,1)S(1)}, bf16[384,512]{1,0:T(8,128)(2,1)S(1)}, u32[]{:S(2)}, u32[]{:S(2)}) collective-permute-start(bf16[384,512]{1,0:T(8,128)(2,1)S(1)} %get-tuple-element.21), channel_id=1, source_target_pairs={{0,7},{1,0},{2,1},{3,2},{4,3},{5,4},{6,5},{7,6},{8,15},{9,8},{10,9... | collective-permute-start | bytes 1179656 | tf_op jit(solution)/shard_map/ppermute | solution.py:82
  102.2 35.2 %collective-permute-start.8 = (bf16[384,512]{1,0:T(8,128)(2,1)S(1)}, bf16[384,512]{1,0:T(8,128)(2,1)S(1)}, u32[]{:S(2)}, u32[]{:S(2)}) collective-permute-start(bf16[384,512]{1,0:T(8,128)(2,1)S(1)} %get-tuple-element.22), channel_id=1, source_target_pairs={{0,6},{1,7},{2,0},{3,1},{4,2},{5,3},{6,4},{7,5},{8,14},{9,15},{10,... | collective-permute-start | bytes 1179656 | tf_op jit(solution)/shard_map/ppermute | solution.py:82
  102.2 43.0 %collective-permute-start.7 = (bf16[384,512]{1,0:T(8,128)(2,1)}, bf16[384,512]{1,0:T(8,128)(2,1)}, u32[]{:S(2)}, u32[]{:S(2)}) collective-permute-start(bf16[384,512]{1,0:T(8,128)(2,1)} %get-tuple-element.23), channel_id=1, source_target_pairs={{0,5},{1,6},{2,7},{3,0},{4,1},{5,2},{6,3},{7,4},{8,13},{9,14},{10,... | collective-permute-start | bytes 1179656 | tf_op jit(solution)/shard_map/ppermute | solution.py:82
  113.1 44.5 %collective-permute-start.6 = (bf16[384,512]{1,0:T(8,128)(2,1)}, bf16[384,512]{1,0:T(8,128)(2,1)}, u32[]{:S(2)}, u32[]{:S(2)}) collective-permute-start(bf16[384,512]{1,0:T(8,128)(2,1)} %get-tuple-element.24), channel_id=1, source_target_pairs={{0,4},{1,5},{2,6},{3,7},{4,0},{5,1},{6,2},{7,3},{8,12},{9,13},{10,... | collective-permute-start | bytes 1179656 | tf_op jit(solution)/shard_map/ppermute | solution.py:82
  125.1 32.5 %collective-permute-start.5 = (bf16[384,512]{1,0:T(8,128)(2,1)}, bf16[384,512]{1,0:T(8,128)(2,1)}, u32[]{:S(2)}, u32[]{:S(2)}) collective-permute-start(bf16[384,512]{1,0:T(8,128)(2,1)} %get-tuple-element.25), channel_id=1, source_target_pairs={{0,3},{1,4},{2,5},{3,6},{4,7},{5,0},{6,1},{7,2},{8,11},{9,12},{10,... | collective-permute-start | bytes 1179656 | tf_op jit(solution)/shard_map/ppermute | solution.py:82
  137.4 22.4 %collective-permute-start.4 = (bf16[384,512]{1,0:T(8,128)(2,1)}, bf16[384,512]{1,0:T(8,128)(2,1)}, u32[]{:S(2)}, u32[]{:S(2)}) collective-permute-start(bf16[384,512]{1,0:T(8,128)(2,1)} %get-tuple-element.26), channel_id=1, source_target_pairs={{0,2},{1,3},{2,4},{3,5},{4,6},{5,7},{6,0},{7,1},{8,10},{9,11},{10,... | collective-permute-start | bytes 1179656 | tf_op jit(solution)/shard_map/ppermute | solution.py:82
  137.4 39.2 %slice-start = ((bf16[2,8,384,512]{3,2,1,0:T(8,128)(2,1)}), bf16[1,8,384,512]{3,2,1,0:T(8,128)(2,1)S(1)}, s32[]{:S(2)}) async-start(bf16[2,8,384,512]{3,2,1,0:T(8,128)(2,1)} %m1.1), calls=%async_computation | async-start | bytes 6291456 | tf_op jit(solution)/shard_map/slice | solution.py:114
  162.2 68.0 %collective-permute-start.17 = (bf16[384,512]{1,0:T(8,128)(2,1)S(1)}, bf16[384,512]{1,0:T(8,128)(2,1)S(1)}, u32[]{:S(2)}, u32[]{:S(2)}) collective-permute-start(bf16[384,512]{1,0:T(8,128)(2,1)S(1)} %convolution_convert_fusion), channel_id=1, source_target_pairs={{0,1},{1,2},{2,3},{3,4},{4,5},{5,6},{6,7},{7,0},{8,9},{9,10},{10,1... | collective-permute-start | bytes 1179656 | tf_op jit(solution)/shard_map/ppermute | solution.py:82
  162.3 67.9 %collective-permute-start.16 = (bf16[384,512]{1,0:T(8,128)(2,1)S(1)}, bf16[384,512]{1,0:T(8,128)(2,1)S(1)}, u32[]{:S(2)}, u32[]{:S(2)}) collective-permute-start(bf16[384,512]{1,0:T(8,128)(2,1)S(1)} %convolution_convert_fusion), channel_id=1, source_target_pairs={{0,2},{1,3},{2,4},{3,5},{4,6},{5,7},{6,0},{7,1},{8,10},{9,11},{10,... | collective-permute-start | bytes 1179656 | tf_op jit(solution)/shard_map/ppermute | solution.py:82
  170.1 60.0 %collective-permute-start.15 = (bf16[384,512]{1,0:T(8,128)(2,1)S(1)}, bf16[384,512]{1,0:T(8,128)(2,1)S(1)}, u32[]{:S(2)}, u32[]{:S(2)}) collective-permute-start(bf16[384,512]{1,0:T(8,128)(2,1)S(1)} %convolution_convert_fusion), channel_id=1, source_target_pairs={{0,3},{1,4},{2,5},{3,6},{4,7},{5,0},{6,1},{7,2},{8,11},{9,12},{10,... | collective-permute-start | bytes 1179656 | tf_op jit(solution)/shard_map/ppermute | solution.py:82
  171.0 39.2 %collective-permute-start.12 = (bf16[384,512]{1,0:T(8,128)(2,1)S(1)}, bf16[384,512]{1,0:T(8,128)(2,1)S(1)}, u32[]{:S(2)}, u32[]{:S(2)}) collective-permute-start(bf16[384,512]{1,0:T(8,128)(2,1)S(1)} %convolution_convert_fusion), channel_id=1, source_target_pairs={{0,6},{1,7},{2,0},{3,1},{4,2},{5,3},{6,4},{7,5},{8,14},{9,15},{10,... | collective-permute-start | bytes 1179656 | tf_op jit(solution)/shard_map/ppermute | solution.py:82
  172.0 38.2 %collective-permute-start.11 = (bf16[384,512]{1,0:T(8,128)(2,1)S(1)}, bf16[384,512]{1,0:T(8,128)(2,1)S(1)}, u32[]{:S(2)}, u32[]{:S(2)}) collective-permute-start(bf16[384,512]{1,0:T(8,128)(2,1)S(1)} %convolution_convert_fusion), channel_id=1, source_target_pairs={{0,7},{1,0},{2,1},{3,2},{4,3},{5,4},{6,5},{7,6},{8,15},{9,8},{10,9... | collective-permute-start | bytes 1179656 | tf_op jit(solution)/shard_map/ppermute | solution.py:82
  210.2 13.1 %collective-permute-start.13 = (bf16[384,512]{1,0:T(8,128)(2,1)S(1)}, bf16[384,512]{1,0:T(8,128)(2,1)S(1)}, u32[]{:S(2)}, u32[]{:S(2)}) collective-permute-start(bf16[384,512]{1,0:T(8,128)(2,1)S(1)} %convolution_convert_fusion), channel_id=1, source_target_pairs={{0,5},{1,6},{2,7},{3,0},{4,1},{5,2},{6,3},{7,4},{8,13},{9,14},{10,... | collective-permute-start | bytes 1179656 | tf_op jit(solution)/shard_map/ppermute | solution.py:82
  210.2 19.9 %collective-permute-start.14 = (bf16[384,512]{1,0:T(8,128)(2,1)S(1)}, bf16[384,512]{1,0:T(8,128)(2,1)S(1)}, u32[]{:S(2)}, u32[]{:S(2)}) collective-permute-start(bf16[384,512]{1,0:T(8,128)(2,1)S(1)} %convolution_convert_fusion), channel_id=1, source_target_pairs={{0,4},{1,5},{2,6},{3,7},{4,0},{5,1},{6,2},{7,3},{8,12},{9,13},{10,... | collective-permute-start | bytes 1179656 | tf_op jit(solution)/shard_map/ppermute | solution.py:82
  233.3 2.7 %copy-start.2 = (bf16[2,8,384,512]{3,2,1,0:T(8,128)(2,1)}, bf16[2,8,384,512]{3,2,1,0:T(8,128)(2,1)S(1)}, u32[]{:S(2)}) copy-start(bf16[2,8,384,512]{3,2,1,0:T(8,128)(2,1)S(1)} %get-tuple-element.14) | copy-start | bytes 18874372

commit v8 on v6

--- a/solution.py
+++ b/solution.py
@@ -101,10 +101,8 @@
 
     n_lag = lax.axis_size("lag")
     me = lax.axis_index("lag")
-    field = lax.dynamic_index_in_dim(partial, me, 0, keepdims=False).astype(jnp.float32)
-    for k in range(1, n_lag):
-        piece = lax.dynamic_index_in_dim(partial, (me + k) % n_lag, 0, keepdims=False)
-        field = field + shifted_by(piece, "lag", k).astype(jnp.float32)
+    received = lax.all_to_all(partial, "lag", 0, 0, tiled=True)
+    field = jnp.sum(received.astype(jnp.float32), axis=0)
     mine = lax.dynamic_index_in_dim(excitation, me, 0, keepdims=False)
     residual = (mine - field).astype(jnp.bfloat16)
     inverse = lax.dynamic_index_in_dim(self_inverse, me, 0, keepdims=False)

time: 220 us -> 236 us (1.073)
  the two profiles are of different devices: /device:TPU:62 before, /device:TPU:6 now
where the time goes in v8:
time: 236 us; the launch traced here: 235 us
  waiting for transfers between devices  125 us (53%)
  starting transfers between devices  68.4 us (29%)
  Pallas kernels  20.4 us (9%)
  other arithmetic  10.3 us (4%)
  local copies, waits for them, and re-layouts  9.18 us (4%)
    ppermute x2, waiting for transfers between devices, passed_along(): return lax.ppermute(array, axis, pairs)  57.9 us
    all_to_all x1, starting transfers between devices, shards(): received = lax.all_to_all(partial, 'lag', 0, 0, tiled=True)  39.1 us
    all_to_all x1, waiting for transfers between devices, shards(): received = lax.all_to_all(partial, 'lag', 0, 0, tiled=True)  34 us
    ppermute x9, waiting for transfers between devices, shifted_by(): lax.ppermute(array, axis, [(i, (i + by) % count) for i in range(count)])  32.8 us
    pallas_call x1, Pallas kernels, lag_partial(): pl.pallas_call(term_kernel, grid_spec=grid_spec, out_shape=jax.ShapeDtype...  20.4 us
    ppermute x9, starting transfers between devices, shifted_by(): lax.ppermute(array, axis, [(i, (i + by) % count) for i in range(count)])  19.6 us
    ppermute x2, starting transfers between devices, passed_along(): return lax.ppermute(array, axis, pairs)  9.8 us
    slice x1, local copies, waits for them, and re-layouts, shards(): right = shifted_by(history[:, :EDGE], 'tile', -1)  6.6 us
  transfers between devices with their start and end apart: 12, of which 7 were waited for; matrix products, arithmetic and copies ran while one was open for 3% of the time, Pallas kernels for 0%

profile of v8, /device:TPU:6, one launch (start us, length us, event | category | flops | bytes accessed | tf_op | source)
XLA Modules:
  0.0 235.3 jit_solution(12642199364250917460)
XLA Ops:
  0.6 0.0 copy-start
  0.6 0.0 copy-start.1
  0.7 6.6 %fusion.7 = (bf16[2,4,384,512]{3,2,1,0:T(8,128)(2,1)}, bf16[2,4,384,512]{3,2,1,0:T(8,128)(2,1)}) fusion(bf16[2,8,384,512]{3,2,1,0:T(8,128)(2,1)} %m1.1), kind=kLoop, calls=%fused_computation.32 | loop fusion | bytes 12582912 | tf_op jit(solution)/shard_map/slice | solution.py:96
  7.3 0.0 copy-start.2
  7.3 0.0 copy-start.3
  7.3 0.0 collective-permute-start
  7.3 1.7 collective-permute-start.1
  9.0 0.0 copy-done.1
  9.0 2.0 slice_bitcast_fusion
  11.0 4.7 %collective-permute-start.2 = (bf16[4,384,512]{2,1,0:T(8,128)(2,1)}, bf16[4,384,512]{2,1,0:T(8,128)(2,1)}, u32[]{:S(2)}, u32[]{:S(2)}) collective-permute-start(bf16[4,384,512]{2,1,0:T(8,128)(2,1)} %get-tuple-element.16), channel_id=1, source_target_pairs={{0,1},{1,2},{2,3},{3,4},{4,5},{5,6},{6,7},{8,9},{9,10},{10,11},{11... | collective-permute-start | bytes 4718600 | tf_op jit(solution)/shard_map/ppermute | solution.py:88
  15.8 0.0 copy-done.2
  15.8 0.1 copy.8
  15.8 0.0 copy-done.3
  15.8 0.6 broadcast_minimum_fusion.cnt_ref
  16.4 0.6 iota_add_fusion.src_ref
  17.0 31.4 %collective-permute-done.2 = bf16[4,384,512]{2,1,0:T(8,128)(2,1)} collective-permute-done((bf16[4,384,512]{2,1,0:T(8,128)(2,1)}, bf16[4,384,512]{2,1,0:T(8,128)(2,1)}, u32[]{:S(2)}, u32[]{:S(2)}) %collective-permute-start.2) | collective-permute-done | bytes 1572896 | tf_op jit(solution)/shard_map/ppermute | solution.py:88
  48.4 0.0 collective-permute-done.l0.l1
  48.4 0.0 collective-permute-done.1.r0.r1
  48.4 20.4 %shard_map.77 = bf16[8,384,512]{2,1,0:T(8,128)(2,1)} custom-call(s32[2,8,2]{2,1,0:T(8,128)} %iota_add_fusion.src_ref, s32[2,8]{1,0:T(2,128)} %broadcast_minimum_fusion.cnt_ref, bf16[2,8,2,384,384]{4,3,2,1,0:T(8,128)(2,1)} %a_ref.1, bf16[2,4,384,512]{3,2,1,0:T(8,128)(2,1)} %collective-permute-done.l0.l1, bf16[2,8,384,512]{3,2,1,0:T(8,128)(2,1)} %m1.1, ...), custom_call_target="tpu_custom_call" | custom-call | flops 4831838208 | bytes 25165824 | tf_op jit(solution)/shard_map/pallas_call | solution.py:72
  68.8 39.1 %all-to-all-start = ((bf16[8,384,512]{2,1,0:T(8,128)(2,1)}), bf16[8,384,512]{2,1,0:T(8,128)(2,1)}, u32[]{:S(2)}, u32[]{:S(2)}) async-start(bf16[8,384,512]{2,1,0:T(8,128)(2,1)} %shard_map.77), calls=%async_computation | async-start | bytes 6291456 | tf_op jit(solution)/shard_map/all_to_all | solution.py:104
  107.9 5.1 %collective-permute-start.3 = (bf16[4,384,512]{2,1,0:T(8,128)(2,1)}, bf16[4,384,512]{2,1,0:T(8,128)(2,1)}, u32[]{:S(2)}, u32[]{:S(2)}) collective-permute-start(bf16[4,384,512]{2,1,0:T(8,128)(2,1)} %get-tuple-element.10), channel_id=1, source_target_pairs={{0,1},{1,2},{2,3},{3,4},{4,5},{5,6},{6,7},{8,9},{9,10},{10,11},{11... | collective-permute-start | bytes 4718600 | tf_op jit(solution)/shard_map/ppermute | solution.py:88
  113.0 34.0 %all-to-all-done = bf16[8,384,512]{2,1,0:T(8,128)(2,1)} async-done(((bf16[8,384,512]{2,1,0:T(8,128)(2,1)}), bf16[8,384,512]{2,1,0:T(8,128)(2,1)}, u32[]{:S(2)}, u32[]{:S(2)}) %all-to-all-start) | async-done | bytes 3145760 | tf_op jit(solution)/shard_map/all_to_all | solution.py:104
  147.0 2.4 %convert_reduce_fusion = f32[384,512]{1,0:T(8,128)S(1)} fusion(bf16[8,384,512]{2,1,0:T(8,128)(2,1)} %all-to-all-done), kind=kLoop, calls=%fused_computation.1 | loop fusion | flops 2949120 | bytes 3932160 | tf_op jit(solution)/shard_map/reduce_sum | solution.py:105
  149.4 0.0 copy-done
  149.4 1.6 convolution_convert_fusion
  151.0 26.5 %collective-permute-done.3 = bf16[4,384,512]{2,1,0:T(8,128)(2,1)} collective-permute-done((bf16[4,384,512]{2,1,0:T(8,128)(2,1)}, bf16[4,384,512]{2,1,0:T(8,128)(2,1)}, u32[]{:S(2)}, u32[]{:S(2)}) %collective-permute-start.3) | collective-permute-done | bytes 1572896 | tf_op jit(solution)/shard_map/ppermute | solution.py:88
  177.5 8.5 %collective-permute-start.4 = (bf16[384,512]{1,0:T(8,128)(2,1)S(1)}, bf16[384,512]{1,0:T(8,128)(2,1)S(1)}, u32[]{:S(2)}, u32[]{:S(2)}) collective-permute-start(bf16[384,512]{1,0:T(8,128)(2,1)S(1)} %convolution_convert_fusion), channel_id=1, source_target_pairs={{0,7},{1,0},{2,1},{3,2},{4,3},{5,4},{6,5},{7,6},{8,15},{9,8},{10,9... | collective-permute-start | bytes 1179656 | tf_op jit(solution)/shard_map/ppermute | solution.py:82
  185.9 0.0 collective-permute-start.5
  185.9 0.8 collective-permute-start.6
  186.7 1.5 collective-permute-start.7
  188.2 1.4 collective-permute-start.8
  189.7 17.8 %collective-permute-done.4 = bf16[384,512]{1,0:T(8,128)(2,1)S(1)} collective-permute-done((bf16[384,512]{1,0:T(8,128)(2,1)S(1)}, bf16[384,512]{1,0:T(8,128)(2,1)S(1)}, u32[]{:S(2)}, u32[]{:S(2)}) %collective-permute-start.4) | collective-permute-done | bytes 393248 | tf_op jit(solution)/shard_map/ppermute | solution.py:82
  207.5 0.0 collective-permute-start.9
  207.5 0.0 collective-permute-done.5
  207.5 5.6 %collective-permute-start.10 = (bf16[384,512]{1,0:T(8,128)(2,1)S(1)}, bf16[384,512]{1,0:T(8,128)(2,1)S(1)}, u32[]{:S(2)}, u32[]{:S(2)}) collective-permute-start(bf16[384,512]{1,0:T(8,128)(2,1)S(1)} %convolution_convert_fusion), channel_id=1, source_target_pairs={{0,1},{1,2},{2,3},{3,4},{4,5},{5,6},{6,7},{7,0},{8,9},{9,10},{10,1... | collective-permute-start | bytes 1179656 | tf_op jit(solution)/shard_map/ppermute | solution.py:82
  213.2 0.0 collective-permute-done.6
  213.2 0.0 collective-permute-done.7
  213.3 9.6 %collective-permute-done.8 = bf16[384,512]{1,0:T(8,128)(2,1)S(1)} collective-permute-done((bf16[384,512]{1,0:T(8,128)(2,1)S(1)}, bf16[384,512]{1,0:T(8,128)(2,1)S(1)}, u32[]{:S(2)}, u32[]{:S(2)}) %collective-permute-start.8) | collective-permute-done | bytes 393248 | tf_op jit(solution)/shard_map/ppermute | solution.py:82
  222.9 0.8 collective-permute-done.9
  223.8 4.5 %collective-permute-done.10 = bf16[384,512]{1,0:T(8,128)(2,1)S(1)} collective-permute-done((bf16[384,512]{1,0:T(8,128)(2,1)S(1)}, bf16[384,512]{1,0:T(8,128)(2,1)S(1)}, u32[]{:S(2)}, u32[]{:S(2)}) %collective-permute-start.10) | collective-permute-done | bytes 393248 | tf_op jit(solution)/shard_map/ppermute | solution.py:82
  228.6 0.0 slice-start
  228.6 3.4 %fusion = (bf16[1,8,384,512]{3,2,1,0:T(8,128)(2,1)S(1)}, bf16[8,384,512]{2,1,0:T(8,128)(2,1)}) fusion(bf16[4,384,512]{2,1,0:T(8,128)(2,1)} %collective-permute-done.3, bf16[4,384,512]{2,1,0:T(8,128)(2,1)} %collective-permute-done.2, pred[]{:T(512)S(6)} %eq.6, bf16[16,384,512]{2,1,0:T(8,128)(2,1)S(1)} %bitcast_dynamic-update-slice_fusion.1, s32[]{:T(128)S(6)} %select_n.29), kind=kLoop, calls=%fused_computation.3 | loop fusion | flops 3145728 | bytes 12582917 | tf_op jit(solution)/shard_map/broadcast_in_dim | solution.py:118
  232.0 0.0 slice-done
  232.0 3.2 %pad_maximum_fusion = bf16[2,8,384,512]{3,2,1,0:T(8,128)(2,1)} fusion(bf16[1,8,384,512]{3,2,1,0:T(8,128)(2,1)S(1)} %slice-done, bf16[1,8,384,512]{3,2,1,0:T(8,128)(2,1)S(1)} %get-tuple-element.14), kind=kLoop, calls=%fused_computation | loop fusion | flops 3145728 | bytes 12582912 | tf_op jit(solution)/shard_map/concatenate | solution.py:118
  (16 shorter events, 0.4 us)
Async XLA Ops:
  0.6 148.8 %copy-start = (bf16[8,384,384]{2,1,0:T(8,128)(2,1)S(1)}, bf16[8,384,384]{2,1,0:T(8,128)(2,1)}, u32[]{:S(2)}) copy-start(bf16[8,384,384]{2,1,0:T(8,128)(2,1)} %param.8) | copy-start | bytes 7077892
  0.6 8.4 %copy-start.1 = (bf16[2,8,384,512]{3,2,1,0:T(8,128)(2,1)S(1)}, bf16[2,8,384,512]{3,2,1,0:T(8,128)(2,1)}, u32[]{:S(2)}) copy-start(bf16[2,8,384,512]{3,2,1,0:T(8,128)(2,1)} %m1.1) | copy-start | bytes 18874372
  7.3 8.5 %copy-start.2 = (s32[2,8,2]{1,2,0:T(2,128)S(1)}, s32[2,8,2]{1,2,0:T(2,128)}, u32[]{:S(2)}) copy-start(s32[2,8,2]{1,2,0:T(2,128)} %param.10) | copy-start | bytes 388
  7.3 8.6 %copy-start.3 = (s32[2,8]{1,0:T(2,128)S(1)}, s32[2,8]{1,0:T(2,128)}, u32[]{:S(2)}) copy-start(s32[2,8]{1,0:T(2,128)} %param.11) | copy-start | bytes 196
  7.3 41.1 %collective-permute-start = (bf16[2,4,384,512]{3,2,1,0:T(8,128)(2,1)}, bf16[2,4,384,512]{3,2,1,0:T(8,128)(2,1)}, u32[]{:S(2)}, u32[]{:S(2)}) collective-permute-start(bf16[2,4,384,512]{3,2,1,0:T(8,128)(2,1)} %get-tuple-element.19), channel_id=1, source_target_pairs={{0,8},{8,16},{16,24},{24,32},{32,40},{40,48},{48,56},{56,64},{64,7... | collective-permute-start | bytes 9437192 | tf_op jit(solution)/shard_map/ppermute | solution.py:82
  7.3 41.1 %collective-permute-start.1 = (bf16[2,4,384,512]{3,2,1,0:T(8,128)(2,1)}, bf16[2,4,384,512]{3,2,1,0:T(8,128)(2,1)}, u32[]{:S(2)}, u32[]{:S(2)}) collective-permute-start(bf16[2,4,384,512]{3,2,1,0:T(8,128)(2,1)} %get-tuple-element.18), channel_id=1, source_target_pairs={{0,120},{8,0},{16,8},{24,16},{32,24},{40,32},{48,40},{56,48},{64,5... | collective-permute-start | bytes 9437192 | tf_op jit(solution)/shard_map/ppermute | solution.py:82
  11.0 37.4 %collective-permute-start.2 = (bf16[4,384,512]{2,1,0:T(8,128)(2,1)}, bf16[4,384,512]{2,1,0:T(8,128)(2,1)}, u32[]{:S(2)}, u32[]{:S(2)}) collective-permute-start(bf16[4,384,512]{2,1,0:T(8,128)(2,1)} %get-tuple-element.16), channel_id=1, source_target_pairs={{0,1},{1,2},{2,3},{3,4},{4,5},{5,6},{6,7},{8,9},{9,10},{10,11},{11... | collective-permute-start | bytes 4718600 | tf_op jit(solution)/shard_map/ppermute | solution.py:88
  68.8 78.2 %all-to-all-start = ((bf16[8,384,512]{2,1,0:T(8,128)(2,1)}), bf16[8,384,512]{2,1,0:T(8,128)(2,1)}, u32[]{:S(2)}, u32[]{:S(2)}) async-start(bf16[8,384,512]{2,1,0:T(8,128)(2,1)} %shard_map.77), calls=%async_computation | async-start | bytes 6291456 | tf_op jit(solution)/shard_map/all_to_all | solution.py:104
  107.9 69.6 %collective-permute-start.3 = (bf16[4,384,512]{2,1,0:T(8,128)(2,1)}, bf16[4,384,512]{2,1,0:T(8,128)(2,1)}, u32[]{:S(2)}, u32[]{:S(2)}) collective-permute-start(bf16[4,384,512]{2,1,0:T(8,128)(2,1)} %get-tuple-element.10), channel_id=1, source_target_pairs={{0,1},{1,2},{2,3},{3,4},{4,5},{5,6},{6,7},{8,9},{9,10},{10,11},{11... | collective-permute-start | bytes 4718600 | tf_op jit(solution)/shard_map/ppermute | solution.py:88
  177.5 30.0 %collective-permute-start.4 = (bf16[384,512]{1,0:T(8,128)(2,1)S(1)}, bf16[384,512]{1,0:T(8,128)(2,1)S(1)}, u32[]{:S(2)}, u32[]{:S(2)}) collective-permute-start(bf16[384,512]{1,0:T(8,128)(2,1)S(1)} %convolution_convert_fusion), channel_id=1, source_target_pairs={{0,7},{1,0},{2,1},{3,2},{4,3},{5,4},{6,5},{7,6},{8,15},{9,8},{10,9... | collective-permute-start | bytes 1179656 | tf_op jit(solution)/shard_map/ppermute | solution.py:82
  185.9 21.6 %collective-permute-start.5 = (bf16[384,512]{1,0:T(8,128)(2,1)S(1)}, bf16[384,512]{1,0:T(8,128)(2,1)S(1)}, u32[]{:S(2)}, u32[]{:S(2)}) collective-permute-start(bf16[384,512]{1,0:T(8,128)(2,1)S(1)} %convolution_convert_fusion), channel_id=1, source_target_pairs={{0,6},{1,7},{2,0},{3,1},{4,2},{5,3},{6,4},{7,5},{8,14},{9,15},{10,... | collective-permute-start | bytes 1179656 | tf_op jit(solution)/shard_map/ppermute | solution.py:82
  185.9 27.2 %collective-permute-start.6 = (bf16[384,512]{1,0:T(8,128)(2,1)S(1)}, bf16[384,512]{1,0:T(8,128)(2,1)S(1)}, u32[]{:S(2)}, u32[]{:S(2)}) collective-permute-start(bf16[384,512]{1,0:T(8,128)(2,1)S(1)} %convolution_convert_fusion), channel_id=1, source_target_pairs={{0,5},{1,6},{2,7},{3,0},{4,1},{5,2},{6,3},{7,4},{8,13},{9,14},{10,... | collective-permute-start | bytes 1179656 | tf_op jit(solution)/shard_map/ppermute | solution.py:82
  186.7 26.5 %collective-permute-start.7 = (bf16[384,512]{1,0:T(8,128)(2,1)S(1)}, bf16[384,512]{1,0:T(8,128)(2,1)S(1)}, u32[]{:S(2)}, u32[]{:S(2)}) collective-permute-start(bf16[384,512]{1,0:T(8,128)(2,1)S(1)} %convolution_convert_fusion), channel_id=1, source_target_pairs={{0,4},{1,5},{2,6},{3,7},{4,0},{5,1},{6,2},{7,3},{8,12},{9,13},{10,... | collective-permute-start | bytes 1179656 | tf_op jit(solution)/shard_map/ppermute | solution.py:82
  188.2 34.6 %collective-permute-start.8 = (bf16[384,512]{1,0:T(8,128)(2,1)S(1)}, bf16[384,512]{1,0:T(8,128)(2,1)S(1)}, u32[]{:S(2)}, u32[]{:S(2)}) collective-permute-start(bf16[384,512]{1,0:T(8,128)(2,1)S(1)} %convolution_convert_fusion), channel_id=1, source_target_pairs={{0,3},{1,4},{2,5},{3,6},{4,7},{5,0},{6,1},{7,2},{8,11},{9,12},{10,... | collective-permute-start | bytes 1179656 | tf_op jit(solution)/shard_map/ppermute | solution.py:82
  207.5 16.2 %collective-permute-start.9 = (bf16[384,512]{1,0:T(8,128)(2,1)S(1)}, bf16[384,512]{1,0:T(8,128)(2,1)S(1)}, u32[]{:S(2)}, u32[]{:S(2)}) collective-permute-start(bf16[384,512]{1,0:T(8,128)(2,1)S(1)} %convolution_convert_fusion), channel_id=1, source_target_pairs={{0,2},{1,3},{2,4},{3,5},{4,6},{5,7},{6,0},{7,1},{8,10},{9,11},{10,... | collective-permute-start | bytes 1179656 | tf_op jit(solution)/shard_map/ppermute | solution.py:82
  207.5 20.7 %collective-permute-start.10 = (bf16[384,512]{1,0:T(8,128)(2,1)S(1)}, bf16[384,512]{1,0:T(8,128)(2,1)S(1)}, u32[]{:S(2)}, u32[]{:S(2)}) collective-permute-start(bf16[384,512]{1,0:T(8,128)(2,1)S(1)} %convolution_convert_fusion), channel_id=1, source_target_pairs={{0,1},{1,2},{2,3},{3,4},{4,5},{5,6},{6,7},{7,0},{8,9},{9,10},{10,1... | collective-permute-start | bytes 1179656 | tf_op jit(solution)/shard_map/ppermute | solution.py:82
  228.6 3.4 %slice-start = ((bf16[2,8,384,512]{3,2,1,0:T(8,128)(2,1)}), bf16[1,8,384,512]{3,2,1,0:T(8,128)(2,1)S(1)}, s32[]{:S(2)}) async-start(bf16[2,8,384,512]{3,2,1,0:T(8,128)(2,1)} %m1.1), calls=%async_computation.1 | async-start | bytes 6291456 | tf_op jit(solution)/shard_map/slice | solution.py:118

commit v9 on v6

--- a/solution.py
+++ b/solution.py
@@ -98,6 +98,7 @@
     late = passed_along(oldest, "lag", 1)
     live = jnp.minimum(live_counts, lag_blocks.shape[2])
     partial = lag_partial(history, left, right, lag_blocks, pattern, live)
+    partial, late = lax.optimization_barrier((partial, late))
 
     n_lag = lax.axis_size("lag")
     me = lax.axis_index("lag")
@@ -109,7 +110,6 @@
     residual = (mine - field).astype(jnp.bfloat16)
     inverse = lax.dynamic_index_in_dim(self_inverse, me, 0, keepdims=False)
     block = jnp.dot(inverse, residual, preferred_element_type=jnp.float32).astype(jnp.bfloat16)
-    block, late = lax.optimization_barrier((block, late))
     carried = jnp.concatenate([early, late], axis=0)
 
     gathered = [block] + [shifted_by(block, "lag", k) for k in range(1, n_lag)]

time: 220 us -> 227 us (1.032)
  the two profiles are of different devices: /device:TPU:62 before, /device:TPU:14 now
where the time goes in v9:
time: 227 us; the launch traced here: 224 us
  waiting for transfers between devices  94.4 us (42%)
  starting transfers between devices  88.3 us (39%)
  Pallas kernels  20 us (9%)
  local copies, waits for them, and re-layouts  10.5 us (5%)
  other arithmetic  7.52 us (3%)
  matrix products  2.63 us (1%)
    ppermute x16, starting transfers between devices, shifted_by(): lax.ppermute(array, axis, [(i, (i + by) % count) for i in range(count)])  81.4 us
    ppermute x2, waiting for transfers between devices, passed_along(): return lax.ppermute(array, axis, pairs)  47.3 us
    ppermute x16, waiting for transfers between devices, shifted_by(): lax.ppermute(array, axis, [(i, (i + by) % count) for i in range(count)])  47.1 us
    pallas_call x1, Pallas kernels, lag_partial(): pl.pallas_call(term_kernel, grid_spec=grid_spec, out_shape=jax.ShapeDtype...  20 us
    ppermute x2, starting transfers between devices, passed_along(): return lax.ppermute(array, axis, pairs)  6.95 us
  transfers between devices with their start and end apart: 18, of which 8 were waited for; matrix products, arithmetic and copies ran while one was open for 1% of the time, Pallas kernels for 9%

profile of v9, /device:TPU:14, one launch (start us, length us, event | category | flops | bytes accessed | tf_op | source)
XLA Modules:
  0.0 224.4 jit_solution(9002646291247008986)
XLA Ops:
  0.6 0.0 copy-start
  0.6 0.0 copy-start.1
  0.7 3.6 %fusion.15 = (bf16[2,4,384,512]{3,2,1,0:T(8,128)(2,1)S(1)}, bf16[2,4,384,512]{3,2,1,0:T(8,128)(2,1)S(1)}) fusion(bf16[2,8,384,512]{3,2,1,0:T(8,128)(2,1)} %m1.1), kind=kLoop, calls=%fused_computation.46 | loop fusion | bytes 12582912 | tf_op jit(solution)/shard_map/slice | solution.py:96
  4.3 0.0 copy-start.5
  4.3 0.0 copy-start.6
  4.3 0.1 collective-permute-start
  4.4 1.7 collective-permute-start.1
  6.1 0.0 copy-done.1
  6.1 1.4 slice_bitcast_fusion
  7.6 3.5 %collective-permute-start.2 = (bf16[4,384,512]{2,1,0:T(8,128)(2,1)S(1)}, bf16[4,384,512]{2,1,0:T(8,128)(2,1)S(1)}, u32[]{:S(2)}, u32[]{:S(2)}) collective-permute-start(bf16[4,384,512]{2,1,0:T(8,128)(2,1)S(1)} %get-tuple-element.16), channel_id=1, source_target_pairs={{0,1},{1,2},{2,3},{3,4},{4,5},{5,6},{6,7},{8,9},{9,10},{10,11},{11... | collective-permute-start | bytes 4718600 | tf_op jit(solution)/shard_map/ppermute | solution.py:88
  11.1 34.5 %collective-permute-done.2 = bf16[4,384,512]{2,1,0:T(8,128)(2,1)S(1)} collective-permute-done((bf16[4,384,512]{2,1,0:T(8,128)(2,1)S(1)}, bf16[4,384,512]{2,1,0:T(8,128)(2,1)S(1)}, u32[]{:S(2)}, u32[]{:S(2)}) %collective-permute-start.2) | collective-permute-done | bytes 1572896 | tf_op jit(solution)/shard_map/ppermute | solution.py:88
  45.5 0.0 copy-start.2
  45.5 0.0 collective-permute-done.l0.l1
  45.5 0.0 collective-permute-done.1.r0.r1
  45.6 1.2 copy-done.2
  46.8 3.5 %collective-permute-start.3 = (bf16[4,384,512]{2,1,0:T(8,128)(2,1)}, bf16[4,384,512]{2,1,0:T(8,128)(2,1)}, u32[]{:S(2)}, u32[]{:S(2)}) collective-permute-start(bf16[4,384,512]{2,1,0:T(8,128)(2,1)} %get-tuple-element.10), channel_id=1, source_target_pairs={{0,1},{1,2},{2,3},{3,4},{4,5},{5,6},{6,7},{8,9},{9,10},{10,11},{11... | collective-permute-start | bytes 4718600 | tf_op jit(solution)/shard_map/ppermute | solution.py:88
  50.4 0.0 copy-done.5
  50.4 0.1 copy.8
  50.4 0.0 copy-done.6
  50.5 0.5 broadcast_minimum_fusion.cnt_ref
  51.0 0.6 iota_add_fusion.src_ref
  51.6 20.0 %shard_map.77 = bf16[8,384,512]{2,1,0:T(8,128)(2,1)} custom-call(s32[2,8,2]{2,1,0:T(8,128)} %iota_add_fusion.src_ref, s32[2,8]{1,0:T(2,128)} %broadcast_minimum_fusion.cnt_ref, bf16[2,8,2,384,384]{4,3,2,1,0:T(8,128)(2,1)} %a_ref.1, bf16[2,4,384,512]{3,2,1,0:T(8,128)(2,1)} %collective-permute-done.l0.l1, bf16[2,8,384,512]{3,2,1,0:T(8,128)(2,1)} %m1.1, ...), custom_call_target="tpu_custom_call" | custom-call | flops 4831838208 | bytes 25165824 | tf_op jit(solution)/shard_map/pallas_call | solution.py:72
  71.6 12.8 %collective-permute-done.3 = bf16[4,384,512]{2,1,0:T(8,128)(2,1)} collective-permute-done((bf16[4,384,512]{2,1,0:T(8,128)(2,1)}, bf16[4,384,512]{2,1,0:T(8,128)(2,1)}, u32[]{:S(2)}, u32[]{:S(2)}) %collective-permute-start.3) | collective-permute-done | bytes 1572896 | tf_op jit(solution)/shard_map/ppermute | solution.py:88
  84.4 2.9 %dynamic-slice_bitcast_fusion.6 = (bf16[384,512]{1,0:T(8,128)(2,1)S(1)}, bf16[384,512]{1,0:T(8,128)(2,1)S(1)}, bf16[384,512]{1,0:T(8,128)(2,1)S(1)}, bf16[384,51...) fusion(bf16[8,384,512]{2,1,0:T(8,128)(2,1)} %shard_map.77, ...), kind=kLoop, calls=%fused_computation.38 | loop fusion | bytes 5505052 | tf_op jit(solution)/shard_map/jit(dynamic_index_in_dim)/squeeze | solution.py:107
  87.2 0.0 collective-permute-start.10
  87.2 6.3 %collective-permute-start.9 = (bf16[384,512]{1,0:T(8,128)(2,1)S(1)}, bf16[384,512]{1,0:T(8,128)(2,1)S(1)}, u32[]{:S(2)}, u32[]{:S(2)}) collective-permute-start(bf16[384,512]{1,0:T(8,128)(2,1)S(1)} %get-tuple-element.22), channel_id=1, source_target_pairs={{0,6},{1,7},{2,0},{3,1},{4,2},{5,3},{6,4},{7,5},{8,14},{9,15},{10,... | collective-permute-start | bytes 1179656 | tf_op jit(solution)/shard_map/ppermute | solution.py:82
  93.6 33.2 %collective-permute-start.8 = (bf16[384,512]{1,0:T(8,128)(2,1)}, bf16[384,512]{1,0:T(8,128)(2,1)}, u32[]{:S(2)}, u32[]{:S(2)}) collective-permute-start(bf16[384,512]{1,0:T(8,128)(2,1)} %get-tuple-element.23), channel_id=1, source_target_pairs={{0,5},{1,6},{2,7},{3,0},{4,1},{5,2},{6,3},{7,4},{8,13},{9,14},{10,... | collective-permute-start | bytes 1179656 | tf_op jit(solution)/shard_map/ppermute | solution.py:82
  126.8 0.0 collective-permute-start.7
  126.8 2.0 collective-permute-start.6
  128.8 0.0 collective-permute-done.10
  128.8 22.1 %collective-permute-start.5 = (bf16[384,512]{1,0:T(8,128)(2,1)S(1)}, bf16[384,512]{1,0:T(8,128)(2,1)}, u32[]{:S(2)}, u32[]{:S(2)}) collective-permute-start(bf16[384,512]{1,0:T(8,128)(2,1)S(1)} %get-tuple-element.26), channel_id=1, source_target_pairs={{0,2},{1,3},{2,4},{3,5},{4,6},{5,7},{6,0},{7,1},{8,10},{9,11},{10,... | collective-permute-start | bytes 1179656 | tf_op jit(solution)/shard_map/ppermute | solution.py:82
  150.9 0.0 collective-permute-done.9
  150.9 0.0 copy-start.4
  150.9 0.8 copy-done.4
  151.6 0.0 collective-permute-start.4
  151.6 0.0 collective-permute-done.8
  151.6 10.4 %collective-permute-done.7 = bf16[384,512]{1,0:T(8,128)(2,1)} collective-permute-done((bf16[384,512]{1,0:T(8,128)(2,1)}, bf16[384,512]{1,0:T(8,128)(2,1)}, u32[]{:S(2)}, u32[]{:S(2)}) %collective-permute-start.7) | collective-permute-done | bytes 393248 | tf_op jit(solution)/shard_map/ppermute | solution.py:82
  162.1 0.0 collective-permute-done.6
  162.1 0.0 collective-permute-done.5
  162.1 0.0 collective-permute-done.4
  162.1 0.0 copy-done
  162.1 2.6 %convolution_convert_fusion = bf16[384,512]{1,0:T(8,128)(2,1)S(1)} fusion(bf16[384,512]{1,0:T(8,128)(2,1)S(1)} %collective-permute-done.10, bf16[384,512]{1,0:T(8,128)(2,1)} %copy-done.4, bf16[384,512]{1,0:T(8,128)(2,1)} %collective-permute-done.8, bf16[384,512]{1,0:T(8,128)(2,1)} %collective-permute-done.7, bf16[384,512]{1,0:T(8,128)(2,1)} %collective-permute-done.6, ...), kind=kOutput, calls=%fused_computation.5 | convolution fusion | flops 154533888 | bytes 4621312 | tf_op jit(solution)/shard_map/dot_general | solution.py:112
  164.7 8.3 %collective-permute-start.11 = (bf16[384,512]{1,0:T(8,128)(2,1)S(1)}, bf16[384,512]{1,0:T(8,128)(2,1)S(1)}, u32[]{:S(2)}, u32[]{:S(2)}) collective-permute-start(bf16[384,512]{1,0:T(8,128)(2,1)S(1)} %convolution_convert_fusion), channel_id=1, source_target_pairs={{0,7},{1,0},{2,1},{3,2},{4,3},{5,4},{6,5},{7,6},{8,15},{9,8},{10,9... | collective-permute-start | bytes 1179656 | tf_op jit(solution)/shard_map/ppermute | solution.py:82
  173.0 2.9 %collective-permute-start.12 = (bf16[384,512]{1,0:T(8,128)(2,1)S(1)}, bf16[384,512]{1,0:T(8,128)(2,1)S(1)}, u32[]{:S(2)}, u32[]{:S(2)}) collective-permute-start(bf16[384,512]{1,0:T(8,128)(2,1)S(1)} %convolution_convert_fusion), channel_id=1, source_target_pairs={{0,6},{1,7},{2,0},{3,1},{4,2},{5,3},{6,4},{7,5},{8,14},{9,15},{10,... | collective-permute-start | bytes 1179656 | tf_op jit(solution)/shard_map/ppermute | solution.py:82
  175.9 0.0 copy-start.3
  175.9 0.0 collective-permute-start.13
  175.9 4.0 %collective-permute-start.14 = (bf16[384,512]{1,0:T(8,128)(2,1)S(1)}, bf16[384,512]{1,0:T(8,128)(2,1)S(1)}, u32[]{:S(2)}, u32[]{:S(2)}) collective-permute-start(bf16[384,512]{1,0:T(8,128)(2,1)S(1)} %convolution_convert_fusion), channel_id=1, source_target_pairs={{0,4},{1,5},{2,6},{3,7},{4,0},{5,1},{6,2},{7,3},{8,12},{9,13},{10,... | collective-permute-start | bytes 1179656 | tf_op jit(solution)/shard_map/ppermute | solution.py:82
  179.9 0.0 collective-permute-start.15
  179.9 2.6 %collective-permute-done.11 = bf16[384,512]{1,0:T(8,128)(2,1)S(1)} collective-permute-done((bf16[384,512]{1,0:T(8,128)(2,1)S(1)}, bf16[384,512]{1,0:T(8,128)(2,1)S(1)}, u32[]{:S(2)}, u32[]{:S(2)}) %collective-permute-start.11) | collective-permute-done | bytes 393248 | tf_op jit(solution)/shard_map/ppermute | solution.py:82
  182.5 0.8 collective-permute-start.16
  183.3 9.9 %collective-permute-done.12 = bf16[384,512]{1,0:T(8,128)(2,1)S(1)} collective-permute-done((bf16[384,512]{1,0:T(8,128)(2,1)S(1)}, bf16[384,512]{1,0:T(8,128)(2,1)S(1)}, u32[]{:S(2)}, u32[]{:S(2)}) %collective-permute-start.12) | collective-permute-done | bytes 393248 | tf_op jit(solution)/shard_map/ppermute | solution.py:82
  193.3 0.0 collective-permute-start.17
  193.3 6.4 %collective-permute-done.13 = bf16[384,512]{1,0:T(8,128)(2,1)S(1)} collective-permute-done((bf16[384,512]{1,0:T(8,128)(2,1)S(1)}, bf16[384,512]{1,0:T(8,128)(2,1)S(1)}, u32[]{:S(2)}, u32[]{:S(2)}) %collective-permute-start.13) | collective-permute-done | bytes 393248 | tf_op jit(solution)/shard_map/ppermute | solution.py:82
  199.8 11.5 %collective-permute-done.14 = bf16[384,512]{1,0:T(8,128)(2,1)S(1)} collective-permute-done((bf16[384,512]{1,0:T(8,128)(2,1)S(1)}, bf16[384,512]{1,0:T(8,128)(2,1)S(1)}, u32[]{:S(2)}, u32[]{:S(2)}) %collective-permute-start.14) | collective-permute-done | bytes 393248 | tf_op jit(solution)/shard_map/ppermute | solution.py:82
  211.2 0.0 collective-permute-done.15
  211.3 6.2 %collective-permute-done.16 = bf16[384,512]{1,0:T(8,128)(2,1)S(1)} collective-permute-done((bf16[384,512]{1,0:T(8,128)(2,1)S(1)}, bf16[384,512]{1,0:T(8,128)(2,1)S(1)}, u32[]{:S(2)}, u32[]{:S(2)}) %collective-permute-start.16) | collective-permute-done | bytes 393248 | tf_op jit(solution)/shard_map/ppermute | solution.py:82
  217.6 0.0 collective-permute-done.17
  217.9 0.0 copy-done.3
  217.9 0.0 slice-start
  217.9 3.2 %fusion = (bf16[1,8,384,512]{3,2,1,0:T(8,128)(2,1)S(1)}, bf16[8,384,512]{2,1,0:T(8,128)(2,1)}) fusion(bf16[4,384,512]{2,1,0:T(8,128)(2,1)} %collective-permute-done.3, bf16[4,384,512]{2,1,0:T(8,128)(2,1)S(1)} %copy-done.3, pred[]{:T(512)S(6)} %eq.14, bf16[16,384,512]{2,1,0:T(8,128)(2,1)S(1)} %bitcast_dynamic-update-slice_fusion.1, s32[]{:T(128)S(6)} %select_n.93), kind=kLoop, calls=%fused_computation.2 | loop fusion | flops 3145728 | bytes 12582917 | tf_op jit(solution)/shard_map/broadcast_in_dim | solution.py:120
  221.1 0.0 slice-done
  221.1 3.2 %pad_maximum_fusion = bf16[2,8,384,512]{3,2,1,0:T(8,128)(2,1)} fusion(bf16[1,8,384,512]{3,2,1,0:T(8,128)(2,1)S(1)} %slice-done, bf16[1,8,384,512]{3,2,1,0:T(8,128)(2,1)S(1)} %get-tuple-element.14), kind=kLoop, calls=%fused_computation | loop fusion | flops 3145728 | bytes 12582912 | tf_op jit(solution)/shard_map/concatenate | solution.py:120
  (16 shorter events, 0.4 us)
Async XLA Ops:
  0.6 161.5 %copy-start = (bf16[8,384,384]{2,1,0:T(8,128)(2,1)S(1)}, bf16[8,384,384]{2,1,0:T(8,128)(2,1)}, u32[]{:S(2)}) copy-start(bf16[8,384,384]{2,1,0:T(8,128)(2,1)} %param.8) | copy-start | bytes 7077892
  0.6 5.5 %copy-start.1 = (bf16[2,8,384,512]{3,2,1,0:T(8,128)(2,1)S(1)}, bf16[2,8,384,512]{3,2,1,0:T(8,128)(2,1)}, u32[]{:S(2)}) copy-start(bf16[2,8,384,512]{3,2,1,0:T(8,128)(2,1)} %m1.1) | copy-start | bytes 18874372
  4.3 46.0 %copy-start.5 = (s32[2,8,2]{1,2,0:T(2,128)S(1)}, s32[2,8,2]{1,2,0:T(2,128)}, u32[]{:S(2)}) copy-start(s32[2,8,2]{1,2,0:T(2,128)} %param.10) | copy-start | bytes 388
  4.3 46.1 %copy-start.6 = (s32[2,8]{1,0:T(2,128)S(1)}, s32[2,8]{1,0:T(2,128)}, u32[]{:S(2)}) copy-start(s32[2,8]{1,0:T(2,128)} %param.11) | copy-start | bytes 196
  4.3 41.2 %collective-permute-start = (bf16[2,4,384,512]{3,2,1,0:T(8,128)(2,1)S(1)}, bf16[2,4,384,512]{3,2,1,0:T(8,128)(2,1)}, u32[]{:S(2)}, u32[]{:S(2)}) collective-permute-start(bf16[2,4,384,512]{3,2,1,0:T(8,128)(2,1)S(1)} %get-tuple-element.19), channel_id=1, source_target_pairs={{0,8},{8,16},{16,24},{24,32},{32,40},{40,48},{48,56},{56,64},{64,7... | collective-permute-start | bytes 9437192 | tf_op jit(solution)/shard_map/ppermute | solution.py:82
  4.4 41.1 %collective-permute-start.1 = (bf16[2,4,384,512]{3,2,1,0:T(8,128)(2,1)S(1)}, bf16[2,4,384,512]{3,2,1,0:T(8,128)(2,1)}, u32[]{:S(2)}, u32[]{:S(2)}) collective-permute-start(bf16[2,4,384,512]{3,2,1,0:T(8,128)(2,1)S(1)} %get-tuple-element.18), channel_id=1, source_target_pairs={{0,120},{8,0},{16,8},{24,16},{32,24},{40,32},{48,40},{56,48},{64,5... | collective-permute-start | bytes 9437192 | tf_op jit(solution)/shard_map/ppermute | solution.py:82
  7.6 38.0 %collective-permute-start.2 = (bf16[4,384,512]{2,1,0:T(8,128)(2,1)S(1)}, bf16[4,384,512]{2,1,0:T(8,128)(2,1)S(1)}, u32[]{:S(2)}, u32[]{:S(2)}) collective-permute-start(bf16[4,384,512]{2,1,0:T(8,128)(2,1)S(1)} %get-tuple-element.16), channel_id=1, source_target_pairs={{0,1},{1,2},{2,3},{3,4},{4,5},{5,6},{6,7},{8,9},{9,10},{10,11},{11... | collective-permute-start | bytes 4718600 | tf_op jit(solution)/shard_map/ppermute | solution.py:88
  45.5 1.2 copy-start.2
  46.8 37.6 %collective-permute-start.3 = (bf16[4,384,512]{2,1,0:T(8,128)(2,1)}, bf16[4,384,512]{2,1,0:T(8,128)(2,1)}, u32[]{:S(2)}, u32[]{:S(2)}) collective-permute-start(bf16[4,384,512]{2,1,0:T(8,128)(2,1)} %get-tuple-element.10), channel_id=1, source_target_pairs={{0,1},{1,2},{2,3},{3,4},{4,5},{5,6},{6,7},{8,9},{9,10},{10,11},{11... | collective-permute-start | bytes 4718600 | tf_op jit(solution)/shard_map/ppermute | solution.py:88
  87.2 41.6 %collective-permute-start.10 = (bf16[384,512]{1,0:T(8,128)(2,1)S(1)}, bf16[384,512]{1,0:T(8,128)(2,1)S(1)}, u32[]{:S(2)}, u32[]{:S(2)}) collective-permute-start(bf16[384,512]{1,0:T(8,128)(2,1)S(1)} %get-tuple-element.21), channel_id=1, source_target_pairs={{0,7},{1,0},{2,1},{3,2},{4,3},{5,4},{6,5},{7,6},{8,15},{9,8},{10,9... | collective-permute-start | bytes 1179656 | tf_op jit(solution)/shard_map/ppermute | solution.py:82
  87.2 63.6 %collective-permute-start.9 = (bf16[384,512]{1,0:T(8,128)(2,1)S(1)}, bf16[384,512]{1,0:T(8,128)(2,1)S(1)}, u32[]{:S(2)}, u32[]{:S(2)}) collective-permute-start(bf16[384,512]{1,0:T(8,128)(2,1)S(1)} %get-tuple-element.22), channel_id=1, source_target_pairs={{0,6},{1,7},{2,0},{3,1},{4,2},{5,3},{6,4},{7,5},{8,14},{9,15},{10,... | collective-permute-start | bytes 1179656 | tf_op jit(solution)/shard_map/ppermute | solution.py:82
  93.6 58.1 %collective-permute-start.8 = (bf16[384,512]{1,0:T(8,128)(2,1)}, bf16[384,512]{1,0:T(8,128)(2,1)}, u32[]{:S(2)}, u32[]{:S(2)}) collective-permute-start(bf16[384,512]{1,0:T(8,128)(2,1)} %get-tuple-element.23), channel_id=1, source_target_pairs={{0,5},{1,6},{2,7},{3,0},{4,1},{5,2},{6,3},{7,4},{8,13},{9,14},{10,... | collective-permute-start | bytes 1179656 | tf_op jit(solution)/shard_map/ppermute | solution.py:82
  126.8 35.3 %collective-permute-start.7 = (bf16[384,512]{1,0:T(8,128)(2,1)}, bf16[384,512]{1,0:T(8,128)(2,1)}, u32[]{:S(2)}, u32[]{:S(2)}) collective-permute-start(bf16[384,512]{1,0:T(8,128)(2,1)} %get-tuple-element.24), channel_id=1, source_target_pairs={{0,4},{1,5},{2,6},{3,7},{4,0},{5,1},{6,2},{7,3},{8,12},{9,13},{10,... | collective-permute-start | bytes 1179656 | tf_op jit(solution)/shard_map/ppermute | solution.py:82
  126.8 35.3 %collective-permute-start.6 = (bf16[384,512]{1,0:T(8,128)(2,1)}, bf16[384,512]{1,0:T(8,128)(2,1)}, u32[]{:S(2)}, u32[]{:S(2)}) collective-permute-start(bf16[384,512]{1,0:T(8,128)(2,1)} %get-tuple-element.25), channel_id=1, source_target_pairs={{0,3},{1,4},{2,5},{3,6},{4,7},{5,0},{6,1},{7,2},{8,11},{9,12},{10,... | collective-permute-start | bytes 1179656 | tf_op jit(solution)/shard_map/ppermute | solution.py:82
  128.8 33.3 %collective-permute-start.5 = (bf16[384,512]{1,0:T(8,128)(2,1)S(1)}, bf16[384,512]{1,0:T(8,128)(2,1)}, u32[]{:S(2)}, u32[]{:S(2)}) collective-permute-start(bf16[384,512]{1,0:T(8,128)(2,1)S(1)} %get-tuple-element.26), channel_id=1, source_target_pairs={{0,2},{1,3},{2,4},{3,5},{4,6},{5,7},{6,0},{7,1},{8,10},{9,11},{10,... | collective-permute-start | bytes 1179656 | tf_op jit(solution)/shard_map/ppermute | solution.py:82
  150.9 0.8 copy-start.4
  151.6 10.5 %collective-permute-start.4 = (bf16[384,512]{1,0:T(8,128)(2,1)S(1)}, bf16[384,512]{1,0:T(8,128)(2,1)}, u32[]{:S(2)}, u32[]{:S(2)}) collective-permute-start(bf16[384,512]{1,0:T(8,128)(2,1)S(1)} %get-tuple-element.20), channel_id=1, source_target_pairs={{0,1},{1,2},{2,3},{3,4},{4,5},{5,6},{6,7},{7,0},{8,9},{9,10},{10,1... | collective-permute-start | bytes 1179656 | tf_op jit(solution)/shard_map/ppermute | solution.py:82
  164.7 17.8 %collective-permute-start.11 = (bf16[384,512]{1,0:T(8,128)(2,1)S(1)}, bf16[384,512]{1,0:T(8,128)(2,1)S(1)}, u32[]{:S(2)}, u32[]{:S(2)}) collective-permute-start(bf16[384,512]{1,0:T(8,128)(2,1)S(1)} %convolution_convert_fusion), channel_id=1, source_target_pairs={{0,7},{1,0},{2,1},{3,2},{4,3},{5,4},{6,5},{7,6},{8,15},{9,8},{10,9... | collective-permute-start | bytes 1179656 | tf_op jit(solution)/shard_map/ppermute | solution.py:82
  173.0 20.3 %collective-permute-start.12 = (bf16[384,512]{1,0:T(8,128)(2,1)S(1)}, bf16[384,512]{1,0:T(8,128)(2,1)S(1)}, u32[]{:S(2)}, u32[]{:S(2)}) collective-permute-start(bf16[384,512]{1,0:T(8,128)(2,1)S(1)} %convolution_convert_fusion), channel_id=1, source_target_pairs={{0,6},{1,7},{2,0},{3,1},{4,2},{5,3},{6,4},{7,5},{8,14},{9,15},{10,... | collective-permute-start | bytes 1179656 | tf_op jit(solution)/shard_map/ppermute | solution.py:82
  175.9 42.1 %copy-start.3 = (bf16[4,384,512]{2,1,0:T(8,128)(2,1)S(1)}, bf16[4,384,512]{2,1,0:T(8,128)(2,1)}, u32[]{:S(2)}) copy-start(bf16[4,384,512]{2,1,0:T(8,128)(2,1)} %copy-done.2) | copy-start | bytes 4718596
  175.9 23.9 %collective-permute-start.13 = (bf16[384,512]{1,0:T(8,128)(2,1)S(1)}, bf16[384,512]{1,0:T(8,128)(2,1)S(1)}, u32[]{:S(2)}, u32[]{:S(2)}) collective-permute-start(bf16[384,512]{1,0:T(8,128)(2,1)S(1)} %convolution_convert_fusion), channel_id=1, source_target_pairs={{0,5},{1,6},{2,7},{3,0},{4,1},{5,2},{6,3},{7,4},{8,13},{9,14},{10,... | collective-permute-start | bytes 1179656 | tf_op jit(solution)/shard_map/ppermute | solution.py:82
  175.9 35.3 %collective-permute-start.14 = (bf16[384,512]{1,0:T(8,128)(2,1)S(1)}, bf16[384,512]{1,0:T(8,128)(2,1)S(1)}, u32[]{:S(2)}, u32[]{:S(2)}) collective-permute-start(bf16[384,512]{1,0:T(8,128)(2,1)S(1)} %convolution_convert_fusion), channel_id=1, source_target_pairs={{0,4},{1,5},{2,6},{3,7},{4,0},{5,1},{6,2},{7,3},{8,12},{9,13},{10,... | collective-permute-start | bytes 1179656 | tf_op jit(solution)/shard_map/ppermute | solution.py:82
  179.9 31.4 %collective-permute-start.15 = (bf16[384,512]{1,0:T(8,128)(2,1)S(1)}, bf16[384,512]{1,0:T(8,128)(2,1)S(1)}, u32[]{:S(2)}, u32[]{:S(2)}) collective-permute-start(bf16[384,512]{1,0:T(8,128)(2,1)S(1)} %convolution_convert_fusion), channel_id=1, source_target_pairs={{0,3},{1,4},{2,5},{3,6},{4,7},{5,0},{6,1},{7,2},{8,11},{9,12},{10,... | collective-permute-start | bytes 1179656 | tf_op jit(solution)/shard_map/ppermute | solution.py:82
  182.5 35.0 %collective-permute-start.16 = (bf16[384,512]{1,0:T(8,128)(2,1)S(1)}, bf16[384,512]{1,0:T(8,128)(2,1)S(1)}, u32[]{:S(2)}, u32[]{:S(2)}) collective-permute-start(bf16[384,512]{1,0:T(8,128)(2,1)S(1)} %convolution_convert_fusion), channel_id=1, source_target_pairs={{0,2},{1,3},{2,4},{3,5},{4,6},{5,7},{6,0},{7,1},{8,10},{9,11},{10,... | collective-permute-start | bytes 1179656 | tf_op jit(solution)/shard_map/ppermute | solution.py:82
  193.3 24.3 %collective-permute-start.17 = (bf16[384,512]{1,0:T(8,128)(2,1)S(1)}, bf16[384,512]{1,0:T(8,128)(2,1)S(1)}, u32[]{:S(2)}, u32[]{:S(2)}) collective-permute-start(bf16[384,512]{1,0:T(8,128)(2,1)S(1)} %convolution_convert_fusion), channel_id=1, source_target_pairs={{0,1},{1,2},{2,3},{3,4},{4,5},{5,6},{6,7},{7,0},{8,9},{9,10},{10,1... | collective-permute-start | bytes 1179656 | tf_op jit(solution)/shard_map/ppermute | solution.py:82
  217.9 3.2 %slice-start = ((bf16[2,8,384,512]{3,2,1,0:T(8,128)(2,1)}), bf16[1,8,384,512]{3,2,1,0:T(8,128)(2,1)S(1)}, s32[]{:S(2)}) async-start(bf16[2,8,384,512]{3,2,1,0:T(8,128)(2,1)} %m1.1), calls=%async_computation | async-start | bytes 6291456 | tf_op jit(solution)/shard_map/slice | solution.py:120

commit v10 on v7

--- a/solution.py
+++ b/solution.py
@@ -111,14 +111,13 @@
     block = jnp.dot(inverse, residual, preferred_element_type=jnp.float32).astype(jnp.bfloat16)
     block, late = lax.optimization_barrier((block, late))
     carried = jnp.concatenate([early, late], axis=0)
-    shifted_history = jnp.concatenate([carried[None], history[:-1]], axis=0)
 
     gathered = [block] + [shifted_by(block, "lag", k) for k in range(1, n_lag)]
     ordered = jnp.stack(gathered[::-1])
     traction = jnp.roll(ordered, me + 1, axis=0)
 
     newest = jnp.where(me == 0, traction, carried)
-    shifted_history = lax.dynamic_update_slice(shifted_history, newest[None], (0, 0, 0, 0))
+    shifted_history = jnp.concatenate([newest[None], history[:-1]], axis=0)
     return (traction, shifted_history)
 
 

time: 237 us -> 229 us (0.966)
  the two profiles are of different devices: /device:TPU:14 before, /device:TPU:62 now
where the time goes in v10:
time: 229 us; the launch traced here: 228 us
  waiting for transfers between devices  96.7 us (42%)
  starting transfers between devices  86.3 us (38%)
  Pallas kernels  21.7 us (9%)
  local copies, waits for them, and re-layouts  12.3 us (5%)
  other arithmetic  7.78 us (3%)
  matrix products  2.5 us (1%)
    ppermute x16, starting transfers between devices, shifted_by(): lax.ppermute(array, axis, [(i, (i + by) % count) for i in range(count)])  83.8 us
    ppermute x16, waiting for transfers between devices, shifted_by(): lax.ppermute(array, axis, [(i, (i + by) % count) for i in range(count)])  60 us
    ppermute x2, waiting for transfers between devices, passed_along(): return lax.ppermute(array, axis, pairs)  36.7 us
    pallas_call x1, Pallas kernels, lag_partial(): pl.pallas_call(term_kernel, grid_spec=grid_spec, out_shape=jax.ShapeDtype...  21.7 us
    slice x1, local copies, waits for them, and re-layouts, shards(): right = shifted_by(history[:, :EDGE], 'tile', -1)  6.6 us
  transfers between devices with their start and end apart: 18, of which 9 were waited for; matrix products, arithmetic and copies ran while one was open for 4% of the time, Pallas kernels for 10%

profile of v10, /device:TPU:62, one launch (start us, length us, event | category | flops | bytes accessed | tf_op | source)
XLA Modules:
  0.0 228.2 jit_solution(17901405206103457469)
XLA Ops:
  0.6 0.0 copy-start
  0.6 0.0 copy-start.1
  0.7 6.6 %fusion.13 = (bf16[2,4,384,512]{3,2,1,0:T(8,128)(2,1)}, bf16[2,4,384,512]{3,2,1,0:T(8,128)(2,1)}) fusion(bf16[2,8,384,512]{3,2,1,0:T(8,128)(2,1)} %m1.1), kind=kLoop, calls=%fused_computation.45 | loop fusion | bytes 12582912 | tf_op jit(solution)/shard_map/slice | solution.py:96
  7.3 0.0 copy-start.3
  7.3 0.0 copy-start.4
  7.3 0.0 collective-permute-start
  7.3 1.7 collective-permute-start.1
  9.0 0.0 copy-done.1
  9.0 2.1 slice_bitcast_fusion
  11.1 1.3 collective-permute-start.2
  12.4 0.0 copy-done.3
  12.4 0.1 copy.8
  12.5 0.0 copy-done.4
  12.5 0.5 broadcast_minimum_fusion.cnt_ref
  13.1 0.6 iota_add_fusion.src_ref
  13.7 36.7 %collective-permute-done.2 = bf16[4,384,512]{2,1,0:T(8,128)(2,1)} collective-permute-done((bf16[4,384,512]{2,1,0:T(8,128)(2,1)}, bf16[4,384,512]{2,1,0:T(8,128)(2,1)}, u32[]{:S(2)}, u32[]{:S(2)}) %collective-permute-start.2) | collective-permute-done | bytes 1572896 | tf_op jit(solution)/shard_map/ppermute | solution.py:88
  50.3 0.0 collective-permute-done.l0.l1
  50.3 0.0 collective-permute-done.1.r0.r1
  50.3 1.3 collective-permute-start.10
  51.6 21.7 %shard_map.77 = bf16[8,384,512]{2,1,0:T(8,128)(2,1)} custom-call(s32[2,8,2]{2,1,0:T(8,128)} %iota_add_fusion.src_ref, s32[2,8]{1,0:T(2,128)} %broadcast_minimum_fusion.cnt_ref, s32[1]{0:T(128)} %bitcast.2.off_ref, bf16[2,8,2,384,384]{4,3,2,1,0:T(8,128)(2,1)} %a_ref.1, bf16[2,4,384,512]{3,2,1,0:T(8,128)(2,1)} %collective-permute-done.l0.l1, ...), custom_call_target="tpu_custom_call" | custom-call | flops 4831838208 | bytes 25165824 | tf_op jit(solution)/shard_map/pallas_call | solution.py:72
  73.4 3.0 %slice_bitcast_fusion.8 = (bf16[384,512]{1,0:T(8,128)(2,1)S(1)}, bf16[384,512]{1,0:T(8,128)(2,1)}, bf16[384,512]{1,0:T(8,128)(2,1)}, bf16[384,512]{1,0:T(8,128)(...) fusion(bf16[8,384,512]{2,1,0:T(8,128)(2,1)} %shard_map.77), kind=kLoop, calls=%fused_computation.21 | loop fusion | bytes 5505024 | tf_op jit(solution)/shard_map/squeeze | solution.py:107
  76.4 1.1 collective-permute-start.3
  77.5 31.2 %collective-permute-start.4 = (bf16[384,512]{1,0:T(8,128)(2,1)S(1)}, bf16[384,512]{1,0:T(8,128)(2,1)S(1)}, u32[]{:S(2)}, u32[]{:S(2)}) collective-permute-start(bf16[384,512]{1,0:T(8,128)(2,1)S(1)} %get-tuple-element.26), channel_id=1, source_target_pairs={{0,2},{1,3},{2,4},{3,5},{4,6},{5,7},{6,0},{7,1},{8,10},{9,11},{10,... | collective-permute-start | bytes 1179656 | tf_op jit(solution)/shard_map/ppermute | solution.py:82
  108.7 3.0 %collective-permute-start.5 = (bf16[384,512]{1,0:T(8,128)(2,1)S(1)}, bf16[384,512]{1,0:T(8,128)(2,1)S(1)}, u32[]{:S(2)}, u32[]{:S(2)}) collective-permute-start(bf16[384,512]{1,0:T(8,128)(2,1)S(1)} %get-tuple-element.25), channel_id=1, source_target_pairs={{0,3},{1,4},{2,5},{3,6},{4,7},{5,0},{6,1},{7,2},{8,11},{9,12},{10,... | collective-permute-start | bytes 1179656 | tf_op jit(solution)/shard_map/ppermute | solution.py:82
  111.6 0.0 collective-permute-start.6
  111.6 0.0 collective-permute-done.3
  111.6 36.5 %collective-permute-start.7 = (bf16[384,512]{1,0:T(8,128)(2,1)}, bf16[384,512]{1,0:T(8,128)(2,1)}, u32[]{:S(2)}, u32[]{:S(2)}) collective-permute-start(bf16[384,512]{1,0:T(8,128)(2,1)} %get-tuple-element.23), channel_id=1, source_target_pairs={{0,5},{1,6},{2,7},{3,0},{4,1},{5,2},{6,3},{7,4},{8,13},{9,14},{10,... | collective-permute-start | bytes 1179656 | tf_op jit(solution)/shard_map/ppermute | solution.py:82
  148.2 0.0 collective-permute-done.4
  148.2 0.0 collective-permute-start.8
  148.2 0.0 collective-permute-done.5
  148.2 0.0 copy-start.2
  148.2 0.8 collective-permute-start.9
  149.0 0.0 collective-permute-done.6
  149.0 7.1 %collective-permute-done.7 = bf16[384,512]{1,0:T(8,128)(2,1)} collective-permute-done((bf16[384,512]{1,0:T(8,128)(2,1)}, bf16[384,512]{1,0:T(8,128)(2,1)}, u32[]{:S(2)}, u32[]{:S(2)}) %collective-permute-start.7) | collective-permute-done | bytes 393248 | tf_op jit(solution)/shard_map/ppermute | solution.py:82
  156.1 6.7 %collective-permute-done.8 = bf16[384,512]{1,0:T(8,128)(2,1)} collective-permute-done((bf16[384,512]{1,0:T(8,128)(2,1)}, bf16[384,512]{1,0:T(8,128)(2,1)}, u32[]{:S(2)}, u32[]{:S(2)}) %collective-permute-start.8) | collective-permute-done | bytes 393248 | tf_op jit(solution)/shard_map/ppermute | solution.py:82
  162.9 0.0 copy-done.2
  162.9 6.1 %collective-permute-done.9 = bf16[384,512]{1,0:T(8,128)(2,1)} collective-permute-done((bf16[384,512]{1,0:T(8,128)(2,1)}, bf16[384,512]{1,0:T(8,128)(2,1)}, u32[]{:S(2)}, u32[]{:S(2)}) %collective-permute-start.9) | collective-permute-done | bytes 393248 | tf_op jit(solution)/shard_map/ppermute | solution.py:82
  169.0 0.0 copy-done
  169.0 2.5 %convolution_convert_fusion = bf16[384,512]{1,0:T(8,128)(2,1)S(1)} fusion(bf16[384,512]{1,0:T(8,128)(2,1)} %collective-permute-done.9, bf16[384,512]{1,0:T(8,128)(2,1)} %collective-permute-done.8, bf16[384,512]{1,0:T(8,128)(2,1)} %collective-permute-done.7, bf16[384,512]{1,0:T(8,128)(2,1)} %collective-permute-done.6, bf16[384,512]{1,0:T(8,128)(2,1)} %copy-done.2, ...), kind=kOutput, calls=%fused_computation.5 | convolution fusion | flops 154533888 | bytes 4621312 | tf_op jit(solution)/shard_map/dot_general | solution.py:111
  171.5 0.0 collective-permute-done.10
  171.5 1.3 collective-permute-start.11
  172.8 4.6 %collective-permute-start.12 = (bf16[384,512]{1,0:T(8,128)(2,1)S(1)}, bf16[384,512]{1,0:T(8,128)(2,1)S(1)}, u32[]{:S(2)}, u32[]{:S(2)}) collective-permute-start(bf16[384,512]{1,0:T(8,128)(2,1)S(1)} %convolution_convert_fusion), channel_id=1, source_target_pairs={{0,6},{1,7},{2,0},{3,1},{4,2},{5,3},{6,4},{7,5},{8,14},{9,15},{10,... | collective-permute-start | bytes 1179656 | tf_op jit(solution)/shard_map/ppermute | solution.py:82
  177.4 1.1 collective-permute-start.13
  178.5 0.0 collective-permute-start.14
  178.5 2.3 %collective-permute-start.15 = (bf16[384,512]{1,0:T(8,128)(2,1)S(1)}, bf16[384,512]{1,0:T(8,128)(2,1)S(1)}, u32[]{:S(2)}, u32[]{:S(2)}) collective-permute-start(bf16[384,512]{1,0:T(8,128)(2,1)S(1)} %convolution_convert_fusion), channel_id=1, source_target_pairs={{0,3},{1,4},{2,5},{3,6},{4,7},{5,0},{6,1},{7,2},{8,11},{9,12},{10,... | collective-permute-start | bytes 1179656 | tf_op jit(solution)/shard_map/ppermute | solution.py:82
  180.8 18.1 %collective-permute-done.11 = bf16[384,512]{1,0:T(8,128)(2,1)S(1)} collective-permute-done((bf16[384,512]{1,0:T(8,128)(2,1)S(1)}, bf16[384,512]{1,0:T(8,128)(2,1)S(1)}, u32[]{:S(2)}, u32[]{:S(2)}) %collective-permute-start.11) | collective-permute-done | bytes 393248 | tf_op jit(solution)/shard_map/ppermute | solution.py:82
  199.0 0.0 collective-permute-start.16
  199.0 0.0 collective-permute-done.12
  199.0 0.1 collective-permute-start.17
  199.1 3.2 %collective-permute-done.13 = bf16[384,512]{1,0:T(8,128)(2,1)S(1)} collective-permute-done((bf16[384,512]{1,0:T(8,128)(2,1)S(1)}, bf16[384,512]{1,0:T(8,128)(2,1)S(1)}, u32[]{:S(2)}, u32[]{:S(2)}) %collective-permute-start.13) | collective-permute-done | bytes 393248 | tf_op jit(solution)/shard_map/ppermute | solution.py:82
  202.3 9.4 %collective-permute-done.14 = bf16[384,512]{1,0:T(8,128)(2,1)S(1)} collective-permute-done((bf16[384,512]{1,0:T(8,128)(2,1)S(1)}, bf16[384,512]{1,0:T(8,128)(2,1)S(1)}, u32[]{:S(2)}, u32[]{:S(2)}) %collective-permute-start.14) | collective-permute-done | bytes 393248 | tf_op jit(solution)/shard_map/ppermute | solution.py:82
  211.7 4.6 %collective-permute-done.15 = bf16[384,512]{1,0:T(8,128)(2,1)S(1)} collective-permute-done((bf16[384,512]{1,0:T(8,128)(2,1)S(1)}, bf16[384,512]{1,0:T(8,128)(2,1)S(1)}, u32[]{:S(2)}, u32[]{:S(2)}) %collective-permute-start.15) | collective-permute-done | bytes 393248 | tf_op jit(solution)/shard_map/ppermute | solution.py:82
  216.4 0.0 collective-permute-done.16
  216.4 4.8 %collective-permute-done.17 = bf16[384,512]{1,0:T(8,128)(2,1)S(1)} collective-permute-done((bf16[384,512]{1,0:T(8,128)(2,1)S(1)}, bf16[384,512]{1,0:T(8,128)(2,1)S(1)}, u32[]{:S(2)}, u32[]{:S(2)}) %collective-permute-start.17) | collective-permute-done | bytes 393248 | tf_op jit(solution)/shard_map/ppermute | solution.py:82
  221.6 0.0 slice-start
  221.6 3.4 %fusion = (bf16[1,8,384,512]{3,2,1,0:T(8,128)(2,1)S(1)}, bf16[8,384,512]{2,1,0:T(8,128)(2,1)}) fusion(bf16[4,384,512]{2,1,0:T(8,128)(2,1)} %collective-permute-done.10, bf16[4,384,512]{2,1,0:T(8,128)(2,1)} %collective-permute-done.2, pred[]{:T(512)S(6)} %eq.6, bf16[16,384,512]{2,1,0:T(8,128)(2,1)S(1)} %bitcast_dynamic-update-slice_fusion.1, s32[]{:T(128)S(6)} %select_n.29), kind=kLoop, calls=%fused_computation.2 | loop fusion | flops 3145728 | bytes 12582917 | tf_op jit(solution)/shard_map/broadcast_in_dim | solution.py:120
  225.0 0.0 slice-done
  225.0 3.2 %pad_maximum_fusion = bf16[2,8,384,512]{3,2,1,0:T(8,128)(2,1)} fusion(bf16[1,8,384,512]{3,2,1,0:T(8,128)(2,1)S(1)} %slice-done, bf16[1,8,384,512]{3,2,1,0:T(8,128)(2,1)S(1)} %get-tuple-element.14), kind=kLoop, calls=%fused_computation | loop fusion | flops 3145728 | bytes 12582912 | tf_op jit(solution)/shard_map/concatenate | solution.py:120
  (16 shorter events, 0.4 us)
Async XLA Ops:
  0.6 168.3 %copy-start = (bf16[8,384,384]{2,1,0:T(8,128)(2,1)S(1)}, bf16[8,384,384]{2,1,0:T(8,128)(2,1)}, u32[]{:S(2)}) copy-start(bf16[8,384,384]{2,1,0:T(8,128)(2,1)} %param.8) | copy-start | bytes 7077892
  0.6 8.4 %copy-start.1 = (bf16[2,8,384,512]{3,2,1,0:T(8,128)(2,1)S(1)}, bf16[2,8,384,512]{3,2,1,0:T(8,128)(2,1)}, u32[]{:S(2)}) copy-start(bf16[2,8,384,512]{3,2,1,0:T(8,128)(2,1)} %m1.1) | copy-start | bytes 18874372
  7.3 5.2 %copy-start.3 = (s32[2,8,2]{1,2,0:T(2,128)S(1)}, s32[2,8,2]{1,2,0:T(2,128)}, u32[]{:S(2)}) copy-start(s32[2,8,2]{1,2,0:T(2,128)} %param.10) | copy-start | bytes 388
  7.3 5.3 %copy-start.4 = (s32[2,8]{1,0:T(2,128)S(1)}, s32[2,8]{1,0:T(2,128)}, u32[]{:S(2)}) copy-start(s32[2,8]{1,0:T(2,128)} %param.11) | copy-start | bytes 196
  7.3 43.1 %collective-permute-start = (bf16[2,4,384,512]{3,2,1,0:T(8,128)(2,1)}, bf16[2,4,384,512]{3,2,1,0:T(8,128)(2,1)}, u32[]{:S(2)}, u32[]{:S(2)}) collective-permute-start(bf16[2,4,384,512]{3,2,1,0:T(8,128)(2,1)} %get-tuple-element.19), channel_id=1, source_target_pairs={{0,8},{8,16},{16,24},{24,32},{32,40},{40,48},{48,56},{56,64},{64,7... | collective-permute-start | bytes 9437192 | tf_op jit(solution)/shard_map/ppermute | solution.py:82
  7.3 43.1 %collective-permute-start.1 = (bf16[2,4,384,512]{3,2,1,0:T(8,128)(2,1)}, bf16[2,4,384,512]{3,2,1,0:T(8,128)(2,1)}, u32[]{:S(2)}, u32[]{:S(2)}) collective-permute-start(bf16[2,4,384,512]{3,2,1,0:T(8,128)(2,1)} %get-tuple-element.18), channel_id=1, source_target_pairs={{0,120},{8,0},{16,8},{24,16},{32,24},{40,32},{48,40},{56,48},{64,5... | collective-permute-start | bytes 9437192 | tf_op jit(solution)/shard_map/ppermute | solution.py:82
  11.1 39.2 %collective-permute-start.2 = (bf16[4,384,512]{2,1,0:T(8,128)(2,1)}, bf16[4,384,512]{2,1,0:T(8,128)(2,1)}, u32[]{:S(2)}, u32[]{:S(2)}) collective-permute-start(bf16[4,384,512]{2,1,0:T(8,128)(2,1)} %get-tuple-element.16), channel_id=1, source_target_pairs={{0,1},{1,2},{2,3},{3,4},{4,5},{5,6},{6,7},{8,9},{9,10},{10,11},{11... | collective-permute-start | bytes 4718600 | tf_op jit(solution)/shard_map/ppermute | solution.py:88
  50.3 121.1 %collective-permute-start.10 = (bf16[4,384,512]{2,1,0:T(8,128)(2,1)}, bf16[4,384,512]{2,1,0:T(8,128)(2,1)}, u32[]{:S(2)}, u32[]{:S(2)}) collective-permute-start(bf16[4,384,512]{2,1,0:T(8,128)(2,1)} %get-tuple-element.10), channel_id=1, source_target_pairs={{0,1},{1,2},{2,3},{3,4},{4,5},{5,6},{6,7},{8,9},{9,10},{10,11},{11... | collective-permute-start | bytes 4718600 | tf_op jit(solution)/shard_map/ppermute | solution.py:88
  76.4 35.2 %collective-permute-start.3 = (bf16[384,512]{1,0:T(8,128)(2,1)S(1)}, bf16[384,512]{1,0:T(8,128)(2,1)S(1)}, u32[]{:S(2)}, u32[]{:S(2)}) collective-permute-start(bf16[384,512]{1,0:T(8,128)(2,1)S(1)} %get-tuple-element.20), channel_id=1, source_target_pairs={{0,1},{1,2},{2,3},{3,4},{4,5},{5,6},{6,7},{7,0},{8,9},{9,10},{10,1... | collective-permute-start | bytes 1179656 | tf_op jit(solution)/shard_map/ppermute | solution.py:82
  77.5 70.7 %collective-permute-start.4 = (bf16[384,512]{1,0:T(8,128)(2,1)S(1)}, bf16[384,512]{1,0:T(8,128)(2,1)S(1)}, u32[]{:S(2)}, u32[]{:S(2)}) collective-permute-start(bf16[384,512]{1,0:T(8,128)(2,1)S(1)} %get-tuple-element.26), channel_id=1, source_target_pairs={{0,2},{1,3},{2,4},{3,5},{4,6},{5,7},{6,0},{7,1},{8,10},{9,11},{10,... | collective-permute-start | bytes 1179656 | tf_op jit(solution)/shard_map/ppermute | solution.py:82
  108.7 39.5 %collective-permute-start.5 = (bf16[384,512]{1,0:T(8,128)(2,1)S(1)}, bf16[384,512]{1,0:T(8,128)(2,1)S(1)}, u32[]{:S(2)}, u32[]{:S(2)}) collective-permute-start(bf16[384,512]{1,0:T(8,128)(2,1)S(1)} %get-tuple-element.25), channel_id=1, source_target_pairs={{0,3},{1,4},{2,5},{3,6},{4,7},{5,0},{6,1},{7,2},{8,11},{9,12},{10,... | collective-permute-start | bytes 1179656 | tf_op jit(solution)/shard_map/ppermute | solution.py:82
  111.6 37.4 %collective-permute-start.6 = (bf16[384,512]{1,0:T(8,128)(2,1)}, bf16[384,512]{1,0:T(8,128)(2,1)}, u32[]{:S(2)}, u32[]{:S(2)}) collective-permute-start(bf16[384,512]{1,0:T(8,128)(2,1)} %get-tuple-element.24), channel_id=1, source_target_pairs={{0,4},{1,5},{2,6},{3,7},{4,0},{5,1},{6,2},{7,3},{8,12},{9,13},{10,... | collective-permute-start | bytes 1179656 | tf_op jit(solution)/shard_map/ppermute | solution.py:82
  111.6 44.5 %collective-permute-start.7 = (bf16[384,512]{1,0:T(8,128)(2,1)}, bf16[384,512]{1,0:T(8,128)(2,1)}, u32[]{:S(2)}, u32[]{:S(2)}) collective-permute-start(bf16[384,512]{1,0:T(8,128)(2,1)} %get-tuple-element.23), channel_id=1, source_target_pairs={{0,5},{1,6},{2,7},{3,0},{4,1},{5,2},{6,3},{7,4},{8,13},{9,14},{10,... | collective-permute-start | bytes 1179656 | tf_op jit(solution)/shard_map/ppermute | solution.py:82
  148.2 14.7 %collective-permute-start.8 = (bf16[384,512]{1,0:T(8,128)(2,1)}, bf16[384,512]{1,0:T(8,128)(2,1)}, u32[]{:S(2)}, u32[]{:S(2)}) collective-permute-start(bf16[384,512]{1,0:T(8,128)(2,1)} %get-tuple-element.22), channel_id=1, source_target_pairs={{0,6},{1,7},{2,0},{3,1},{4,2},{5,3},{6,4},{7,5},{8,14},{9,15},{10,... | collective-permute-start | bytes 1179656 | tf_op jit(solution)/shard_map/ppermute | solution.py:82
  148.2 14.7 %copy-start.2 = (bf16[384,512]{1,0:T(8,128)(2,1)}, bf16[384,512]{1,0:T(8,128)(2,1)S(1)}, u32[]{:S(2)}) copy-start(bf16[384,512]{1,0:T(8,128)(2,1)S(1)} %collective-permute-done.5) | copy-start | bytes 1179652
  148.2 20.8 %collective-permute-start.9 = (bf16[384,512]{1,0:T(8,128)(2,1)}, bf16[384,512]{1,0:T(8,128)(2,1)}, u32[]{:S(2)}, u32[]{:S(2)}) collective-permute-start(bf16[384,512]{1,0:T(8,128)(2,1)} %get-tuple-element.21), channel_id=1, source_target_pairs={{0,7},{1,0},{2,1},{3,2},{4,3},{5,4},{6,5},{7,6},{8,15},{9,8},{10,9... | collective-permute-start | bytes 1179656 | tf_op jit(solution)/shard_map/ppermute | solution.py:82
  171.5 27.5 %collective-permute-start.11 = (bf16[384,512]{1,0:T(8,128)(2,1)S(1)}, bf16[384,512]{1,0:T(8,128)(2,1)S(1)}, u32[]{:S(2)}, u32[]{:S(2)}) collective-permute-start(bf16[384,512]{1,0:T(8,128)(2,1)S(1)} %convolution_convert_fusion), channel_id=1, source_target_pairs={{0,7},{1,0},{2,1},{3,2},{4,3},{5,4},{6,5},{7,6},{8,15},{9,8},{10,9... | collective-permute-start | bytes 1179656 | tf_op jit(solution)/shard_map/ppermute | solution.py:82
  172.8 26.2 %collective-permute-start.12 = (bf16[384,512]{1,0:T(8,128)(2,1)S(1)}, bf16[384,512]{1,0:T(8,128)(2,1)S(1)}, u32[]{:S(2)}, u32[]{:S(2)}) collective-permute-start(bf16[384,512]{1,0:T(8,128)(2,1)S(1)} %convolution_convert_fusion), channel_id=1, source_target_pairs={{0,6},{1,7},{2,0},{3,1},{4,2},{5,3},{6,4},{7,5},{8,14},{9,15},{10,... | collective-permute-start | bytes 1179656 | tf_op jit(solution)/shard_map/ppermute | solution.py:82
  177.4 24.9 %collective-permute-start.13 = (bf16[384,512]{1,0:T(8,128)(2,1)S(1)}, bf16[384,512]{1,0:T(8,128)(2,1)S(1)}, u32[]{:S(2)}, u32[]{:S(2)}) collective-permute-start(bf16[384,512]{1,0:T(8,128)(2,1)S(1)} %convolution_convert_fusion), channel_id=1, source_target_pairs={{0,5},{1,6},{2,7},{3,0},{4,1},{5,2},{6,3},{7,4},{8,13},{9,14},{10,... | collective-permute-start | bytes 1179656 | tf_op jit(solution)/shard_map/ppermute | solution.py:82
  178.5 33.2 %collective-permute-start.14 = (bf16[384,512]{1,0:T(8,128)(2,1)S(1)}, bf16[384,512]{1,0:T(8,128)(2,1)S(1)}, u32[]{:S(2)}, u32[]{:S(2)}) collective-permute-start(bf16[384,512]{1,0:T(8,128)(2,1)S(1)} %convolution_convert_fusion), channel_id=1, source_target_pairs={{0,4},{1,5},{2,6},{3,7},{4,0},{5,1},{6,2},{7,3},{8,12},{9,13},{10,... | collective-permute-start | bytes 1179656 | tf_op jit(solution)/shard_map/ppermute | solution.py:82
  178.5 37.8 %collective-permute-start.15 = (bf16[384,512]{1,0:T(8,128)(2,1)S(1)}, bf16[384,512]{1,0:T(8,128)(2,1)S(1)}, u32[]{:S(2)}, u32[]{:S(2)}) collective-permute-start(bf16[384,512]{1,0:T(8,128)(2,1)S(1)} %convolution_convert_fusion), channel_id=1, source_target_pairs={{0,3},{1,4},{2,5},{3,6},{4,7},{5,0},{6,1},{7,2},{8,11},{9,12},{10,... | collective-permute-start | bytes 1179656 | tf_op jit(solution)/shard_map/ppermute | solution.py:82
  199.0 17.4 %collective-permute-start.16 = (bf16[384,512]{1,0:T(8,128)(2,1)S(1)}, bf16[384,512]{1,0:T(8,128)(2,1)S(1)}, u32[]{:S(2)}, u32[]{:S(2)}) collective-permute-start(bf16[384,512]{1,0:T(8,128)(2,1)S(1)} %convolution_convert_fusion), channel_id=1, source_target_pairs={{0,2},{1,3},{2,4},{3,5},{4,6},{5,7},{6,0},{7,1},{8,10},{9,11},{10,... | collective-permute-start | bytes 1179656 | tf_op jit(solution)/shard_map/ppermute | solution.py:82
  199.0 22.2 %collective-permute-start.17 = (bf16[384,512]{1,0:T(8,128)(2,1)S(1)}, bf16[384,512]{1,0:T(8,128)(2,1)S(1)}, u32[]{:S(2)}, u32[]{:S(2)}) collective-permute-start(bf16[384,512]{1,0:T(8,128)(2,1)S(1)} %convolution_convert_fusion), channel_id=1, source_target_pairs={{0,1},{1,2},{2,3},{3,4},{4,5},{5,6},{6,7},{7,0},{8,9},{9,10},{10,1... | collective-permute-start | bytes 1179656 | tf_op jit(solution)/shard_map/ppermute | solution.py:82
  221.6 3.4 %slice-start = ((bf16[2,8,384,512]{3,2,1,0:T(8,128)(2,1)}), bf16[1,8,384,512]{3,2,1,0:T(8,128)(2,1)S(1)}, s32[]{:S(2)}) async-start(bf16[2,8,384,512]{3,2,1,0:T(8,128)(2,1)} %m1.1), calls=%async_computation | async-start | bytes 6291456 | tf_op jit(solution)/shard_map/slice | solution.py:120

commit v11 on v6

--- a/solution.py
+++ b/solution.py
@@ -94,8 +94,8 @@
     early = passed_along(history[-1, :half], "lag", 1)
     left = shifted_by(history[:, blocks_here - EDGE:], "tile", 1)
     right = shifted_by(history[:, :EDGE], "tile", -1)
-    oldest, left, right, early = lax.optimization_barrier((history[-1, half:], left, right, early))
-    late = passed_along(oldest, "lag", 1)
+    after, left, right, early = lax.optimization_barrier((history, left, right, early))
+    late = passed_along(after[-1, half:], "lag", 1)
     live = jnp.minimum(live_counts, lag_blocks.shape[2])
     partial = lag_partial(history, left, right, lag_blocks, pattern, live)
 

time: 220 us -> 223 us (1.014)
  starting transfers between devices: 88.6 us -> 82.4 us
  waiting for transfers between devices: 84.5 us -> 90.6 us
    ppermute x16, starting transfers between devices: 86 us -> 79.8 us  [shifted_by(): lax.ppermute(array, axis, [(i, (i + by) % count) for i in range(count)])]
    ppermute x16, waiting for transfers between devices: 47.9 us -> 54 us  [shifted_by(): lax.ppermute(array, axis, [(i, (i + by) % count) for i in range(count)])]
    squeeze x0 -> x1, local copies, waits for them, and re-layouts: none -> 2.65 us  [shards(): late = passed_along(after[-1, half:], 'lag', 1)]
  transfers between devices with their start and end apart: 18 -> 18, of which waited for: 6 -> 8; matrix products, arithmetic and copies ran while one was open for 4% -> 4% of each run, Pallas kernels for 10% -> 10%
where the time goes in v11:
time: 223 us; the launch traced here: 222 us
  waiting for transfers between devices  90.6 us (41%)
  starting transfers between devices  82.4 us (37%)
  Pallas kernels  22.4 us (10%)
  local copies, waits for them, and re-layouts  14.9 us (7%)
  other arithmetic  7.83 us (4%)
  matrix products  2.62 us (1%)
    ppermute x16, starting transfers between devices, shifted_by(): lax.ppermute(array, axis, [(i, (i + by) % count) for i in range(count)])  79.8 us
    ppermute x16, waiting for transfers between devices, shifted_by(): lax.ppermute(array, axis, [(i, (i + by) % count) for i in range(count)])  54 us
    ppermute x2, waiting for transfers between devices, passed_along(): return lax.ppermute(array, axis, pairs)  36.5 us
    pallas_call x1, Pallas kernels, lag_partial(): pl.pallas_call(term_kernel, grid_spec=grid_spec, out_shape=jax.ShapeDtype...  22.4 us
    slice x1, local copies, waits for them, and re-layouts, shards(): right = shifted_by(history[:, :EDGE], 'tile', -1)  6.62 us
  transfers between devices with their start and end apart: 18, of which 8 were waited for; matrix products, arithmetic and copies ran while one was open for 4% of the time, Pallas kernels for 10%

profile of v11, /device:TPU:62, one launch (start us, length us, event | category | flops | bytes accessed | tf_op | source)
XLA Modules:
  0.0 221.5 jit_solution(2504359006817295428)
XLA Ops:
  0.6 0.0 copy-start
  0.6 0.0 copy-start.1
  0.7 0.0 copy-start.4
  0.7 0.0 copy-start.5
  0.7 6.6 %fusion.15 = (bf16[2,4,384,512]{3,2,1,0:T(8,128)(2,1)}, bf16[2,4,384,512]{3,2,1,0:T(8,128)(2,1)}) fusion(bf16[2,8,384,512]{3,2,1,0:T(8,128)(2,1)} %m1.1), kind=kLoop, calls=%fused_computation.46 | loop fusion | bytes 12582912 | tf_op jit(solution)/shard_map/slice | solution.py:96
  7.3 0.0 collective-permute-start
  7.3 1.7 collective-permute-start.1
  9.0 0.0 copy-done.1
  9.0 1.4 slice_bitcast_fusion.1
  10.4 1.3 collective-permute-start.2
  11.8 0.0 copy-done.4
  11.8 0.1 copy.8
  11.9 0.0 copy-done.5
  11.9 0.6 broadcast_minimum_fusion.cnt_ref
  12.5 0.6 iota_add_fusion.src_ref
  13.1 36.5 %collective-permute-done.2 = bf16[4,384,512]{2,1,0:T(8,128)(2,1)} collective-permute-done((bf16[4,384,512]{2,1,0:T(8,128)(2,1)}, bf16[4,384,512]{2,1,0:T(8,128)(2,1)}, u32[]{:S(2)}, u32[]{:S(2)}) %collective-permute-start.2) | collective-permute-done | bytes 1572896 | tf_op jit(solution)/shard_map/ppermute | solution.py:88
  49.6 0.0 collective-permute-done.l0.l1
  49.6 0.0 collective-permute-done.1.r0.r1
  49.6 2.7 %slice_bitcast_fusion = bf16[4,384,512]{2,1,0:T(8,128)(2,1)} fusion(bf16[2,8,384,512]{3,2,1,0:T(8,128)(2,1)} %m1.1), kind=kLoop, calls=%fused_computation.3 | loop fusion | bytes 3145728 | tf_op jit(solution)/shard_map/squeeze | solution.py:98
  52.2 1.3 collective-permute-start.10
  53.5 22.4 %shard_map.77 = bf16[8,384,512]{2,1,0:T(8,128)(2,1)} custom-call(s32[2,8,2]{2,1,0:T(8,128)} %iota_add_fusion.src_ref, s32[2,8]{1,0:T(2,128)} %broadcast_minimum_fusion.cnt_ref, bf16[2,8,2,384,384]{4,3,2,1,0:T(8,128)(2,1)} %a_ref.1, bf16[2,4,384,512]{3,2,1,0:T(8,128)(2,1)} %collective-permute-done.l0.l1, bf16[2,8,384,512]{3,2,1,0:T(8,128)(2,1)} %m1.1, ...), custom_call_target="tpu_custom_call" | custom-call | flops 4831838208 | bytes 25165824 | tf_op jit(solution)/shard_map/pallas_call | solution.py:72
  75.9 2.9 %dynamic-slice_bitcast_fusion.6 = (bf16[384,512]{1,0:T(8,128)(2,1)S(1)}, bf16[384,512]{1,0:T(8,128)(2,1)S(1)}, bf16[384,512]{1,0:T(8,128)(2,1)S(1)}, bf16[384,51...) fusion(bf16[8,384,512]{2,1,0:T(8,128)(2,1)} %shard_map.77, ...), kind=kLoop, calls=%fused_computation.38 | loop fusion | bytes 5505052 | tf_op jit(solution)/shard_map/jit(dynamic_index_in_dim)/squeeze | solution.py:106
  78.8 0.3 collective-permute-start.9
  79.1 32.4 %collective-permute-start.8 = (bf16[384,512]{1,0:T(8,128)(2,1)S(1)}, bf16[384,512]{1,0:T(8,128)(2,1)S(1)}, u32[]{:S(2)}, u32[]{:S(2)}) collective-permute-start(bf16[384,512]{1,0:T(8,128)(2,1)S(1)} %get-tuple-element.20), channel_id=1, source_target_pairs={{0,6},{1,7},{2,0},{3,1},{4,2},{5,3},{6,4},{7,5},{8,14},{9,15},{10,... | collective-permute-start | bytes 1179656 | tf_op jit(solution)/shard_map/ppermute | solution.py:82
  111.5 1.8 collective-permute-start.7
  113.4 0.0 collective-permute-start.6
  113.4 0.0 collective-permute-done.9
  113.4 8.7 %collective-permute-start.5 = (bf16[384,512]{1,0:T(8,128)(2,1)}, bf16[384,512]{1,0:T(8,128)(2,1)}, u32[]{:S(2)}, u32[]{:S(2)}) collective-permute-start(bf16[384,512]{1,0:T(8,128)(2,1)} %get-tuple-element.23), channel_id=1, source_target_pairs={{0,3},{1,4},{2,5},{3,6},{4,7},{5,0},{6,1},{7,2},{8,11},{9,12},{10,... | collective-permute-start | bytes 1179656 | tf_op jit(solution)/shard_map/ppermute | solution.py:82
  122.1 0.0 collective-permute-done.8
  122.1 0.0 copy-start.2
  122.1 15.1 %collective-permute-start.4 = (bf16[384,512]{1,0:T(8,128)(2,1)S(1)}, bf16[384,512]{1,0:T(8,128)(2,1)}, u32[]{:S(2)}, u32[]{:S(2)}) collective-permute-start(bf16[384,512]{1,0:T(8,128)(2,1)S(1)} %get-tuple-element.24), channel_id=1, source_target_pairs={{0,2},{1,3},{2,4},{3,5},{4,6},{5,7},{6,0},{7,1},{8,10},{9,11},{10,... | collective-permute-start | bytes 1179656 | tf_op jit(solution)/shard_map/ppermute | solution.py:82
  137.2 0.0 collective-permute-done.7
  137.2 0.0 copy-done.2
  137.2 0.0 copy-start.3
  137.2 0.7 copy-done.3
  138.0 10.1 %collective-permute-start.3 = (bf16[384,512]{1,0:T(8,128)(2,1)S(1)}, bf16[384,512]{1,0:T(8,128)(2,1)}, u32[]{:S(2)}, u32[]{:S(2)}) collective-permute-start(bf16[384,512]{1,0:T(8,128)(2,1)S(1)} %get-tuple-element.18), channel_id=1, source_target_pairs={{0,1},{1,2},{2,3},{3,4},{4,5},{5,6},{6,7},{7,0},{8,9},{9,10},{10,1... | collective-permute-start | bytes 1179656 | tf_op jit(solution)/shard_map/ppermute | solution.py:82
  148.0 0.0 collective-permute-done.6
  148.0 4.2 %collective-permute-done.5 = bf16[384,512]{1,0:T(8,128)(2,1)} collective-permute-done((bf16[384,512]{1,0:T(8,128)(2,1)}, bf16[384,512]{1,0:T(8,128)(2,1)}, u32[]{:S(2)}, u32[]{:S(2)}) %collective-permute-start.5) | collective-permute-done | bytes 393248 | tf_op jit(solution)/shard_map/ppermute | solution.py:82
  152.3 0.0 collective-permute-done.4
  152.3 5.9 %collective-permute-done.3 = bf16[384,512]{1,0:T(8,128)(2,1)} collective-permute-done((bf16[384,512]{1,0:T(8,128)(2,1)S(1)}, bf16[384,512]{1,0:T(8,128)(2,1)}, u32[]{:S(2)}, u32[]{:S(2)}) %collective-permute-start.3) | collective-permute-done | bytes 393248 | tf_op jit(solution)/shard_map/ppermute | solution.py:82
  158.2 0.0 copy-done
  158.2 2.6 %convolution_convert_fusion = bf16[384,512]{1,0:T(8,128)(2,1)S(1)} fusion(bf16[384,512]{1,0:T(8,128)(2,1)S(1)} %collective-permute-done.9, bf16[384,512]{1,0:T(8,128)(2,1)} %copy-done.2, bf16[384,512]{1,0:T(8,128)(2,1)} %copy-done.3, bf16[384,512]{1,0:T(8,128)(2,1)} %collective-permute-done.6, bf16[384,512]{1,0:T(8,128)(2,1)} %collective-permute-done.5, ...), kind=kOutput, calls=%fused_computation.5 | convolution fusion | flops 154533888 | bytes 4621312 | tf_op jit(solution)/shard_map/dot_general | solution.py:111
  160.8 0.0 collective-permute-done.10
  160.8 2.5 %collective-permute-start.11 = (bf16[384,512]{1,0:T(8,128)(2,1)S(1)}, bf16[384,512]{1,0:T(8,128)(2,1)S(1)}, u32[]{:S(2)}, u32[]{:S(2)}) collective-permute-start(bf16[384,512]{1,0:T(8,128)(2,1)S(1)} %convolution_convert_fusion), channel_id=1, source_target_pairs={{0,7},{1,0},{2,1},{3,2},{4,3},{5,4},{6,5},{7,6},{8,15},{9,8},{10,9... | collective-permute-start | bytes 1179656 | tf_op jit(solution)/shard_map/ppermute | solution.py:82
  163.3 4.2 %collective-permute-start.12 = (bf16[384,512]{1,0:T(8,128)(2,1)S(1)}, bf16[384,512]{1,0:T(8,128)(2,1)S(1)}, u32[]{:S(2)}, u32[]{:S(2)}) collective-permute-start(bf16[384,512]{1,0:T(8,128)(2,1)S(1)} %convolution_convert_fusion), channel_id=1, source_target_pairs={{0,6},{1,7},{2,0},{3,1},{4,2},{5,3},{6,4},{7,5},{8,14},{9,15},{10,... | collective-permute-start | bytes 1179656 | tf_op jit(solution)/shard_map/ppermute | solution.py:82
  167.5 0.0 collective-permute-start.13
  167.5 1.1 collective-permute-start.14
  168.6 1.9 collective-permute-start.15
  170.4 6.1 %collective-permute-done.11 = bf16[384,512]{1,0:T(8,128)(2,1)S(1)} collective-permute-done((bf16[384,512]{1,0:T(8,128)(2,1)S(1)}, bf16[384,512]{1,0:T(8,128)(2,1)S(1)}, u32[]{:S(2)}, u32[]{:S(2)}) %collective-permute-start.11) | collective-permute-done | bytes 393248 | tf_op jit(solution)/shard_map/ppermute | solution.py:82
  176.5 0.0 collective-permute-start.16
  176.6 11.0 %collective-permute-done.12 = bf16[384,512]{1,0:T(8,128)(2,1)S(1)} collective-permute-done((bf16[384,512]{1,0:T(8,128)(2,1)S(1)}, bf16[384,512]{1,0:T(8,128)(2,1)S(1)}, u32[]{:S(2)}, u32[]{:S(2)}) %collective-permute-start.12) | collective-permute-done | bytes 393248 | tf_op jit(solution)/shard_map/ppermute | solution.py:82
  187.5 0.0 collective-permute-start.17
  187.6 3.0 %collective-permute-done.13 = bf16[384,512]{1,0:T(8,128)(2,1)S(1)} collective-permute-done((bf16[384,512]{1,0:T(8,128)(2,1)S(1)}, bf16[384,512]{1,0:T(8,128)(2,1)S(1)}, u32[]{:S(2)}, u32[]{:S(2)}) %collective-permute-start.13) | collective-permute-done | bytes 393248 | tf_op jit(solution)/shard_map/ppermute | solution.py:82
  190.5 9.1 %collective-permute-done.14 = bf16[384,512]{1,0:T(8,128)(2,1)S(1)} collective-permute-done((bf16[384,512]{1,0:T(8,128)(2,1)S(1)}, bf16[384,512]{1,0:T(8,128)(2,1)S(1)}, u32[]{:S(2)}, u32[]{:S(2)}) %collective-permute-start.14) | collective-permute-done | bytes 393248 | tf_op jit(solution)/shard_map/ppermute | solution.py:82
  199.7 0.0 collective-permute-done.15
  199.7 14.8 %collective-permute-done.16 = bf16[384,512]{1,0:T(8,128)(2,1)S(1)} collective-permute-done((bf16[384,512]{1,0:T(8,128)(2,1)S(1)}, bf16[384,512]{1,0:T(8,128)(2,1)S(1)}, u32[]{:S(2)}, u32[]{:S(2)}) %collective-permute-start.16) | collective-permute-done | bytes 393248 | tf_op jit(solution)/shard_map/ppermute | solution.py:82
  214.5 0.0 collective-permute-done.17
  214.9 0.0 slice-start
  214.9 3.4 %fusion = (bf16[1,8,384,512]{3,2,1,0:T(8,128)(2,1)S(1)}, bf16[8,384,512]{2,1,0:T(8,128)(2,1)}) fusion(bf16[4,384,512]{2,1,0:T(8,128)(2,1)} %collective-permute-done.10, bf16[4,384,512]{2,1,0:T(8,128)(2,1)} %collective-permute-done.2, pred[]{:T(512)S(6)} %eq.14, bf16[16,384,512]{2,1,0:T(8,128)(2,1)S(1)} %bitcast_dynamic-update-slice_fusion.1, s32[]{:T(128)S(6)} %select_n.93), kind=kLoop, calls=%fused_computation.2 | loop fusion | flops 3145728 | bytes 12582917 | tf_op jit(solution)/shard_map/broadcast_in_dim | solution.py:120
  218.3 0.0 slice-done
  218.3 3.2 %pad_maximum_fusion = bf16[2,8,384,512]{3,2,1,0:T(8,128)(2,1)} fusion(bf16[1,8,384,512]{3,2,1,0:T(8,128)(2,1)S(1)} %slice-done, bf16[1,8,384,512]{3,2,1,0:T(8,128)(2,1)S(1)} %get-tuple-element.14), kind=kLoop, calls=%fused_computation | loop fusion | flops 3145728 | bytes 12582912 | tf_op jit(solution)/shard_map/concatenate | solution.py:120
  (16 shorter events, 0.4 us)
Async XLA Ops:
  0.6 157.6 %copy-start = (bf16[8,384,384]{2,1,0:T(8,128)(2,1)S(1)}, bf16[8,384,384]{2,1,0:T(8,128)(2,1)}, u32[]{:S(2)}) copy-start(bf16[8,384,384]{2,1,0:T(8,128)(2,1)} %param.8) | copy-start | bytes 7077892
  0.6 8.4 %copy-start.1 = (bf16[2,8,384,512]{3,2,1,0:T(8,128)(2,1)S(1)}, bf16[2,8,384,512]{3,2,1,0:T(8,128)(2,1)}, u32[]{:S(2)}) copy-start(bf16[2,8,384,512]{3,2,1,0:T(8,128)(2,1)} %m1.1) | copy-start | bytes 18874372
  0.7 11.1 %copy-start.4 = (s32[2,8,2]{1,2,0:T(2,128)S(1)}, s32[2,8,2]{1,2,0:T(2,128)}, u32[]{:S(2)}) copy-start(s32[2,8,2]{1,2,0:T(2,128)} %param.10) | copy-start | bytes 388
  0.7 11.2 %copy-start.5 = (s32[2,8]{1,0:T(2,128)S(1)}, s32[2,8]{1,0:T(2,128)}, u32[]{:S(2)}) copy-start(s32[2,8]{1,0:T(2,128)} %param.11) | copy-start | bytes 196
  7.3 42.3 %collective-permute-start = (bf16[2,4,384,512]{3,2,1,0:T(8,128)(2,1)}, bf16[2,4,384,512]{3,2,1,0:T(8,128)(2,1)}, u32[]{:S(2)}, u32[]{:S(2)}) collective-permute-start(bf16[2,4,384,512]{3,2,1,0:T(8,128)(2,1)} %get-tuple-element.17), channel_id=1, source_target_pairs={{0,8},{8,16},{16,24},{24,32},{32,40},{40,48},{48,56},{56,64},{64,7... | collective-permute-start | bytes 9437192 | tf_op jit(solution)/shard_map/ppermute | solution.py:82
  7.3 42.3 %collective-permute-start.1 = (bf16[2,4,384,512]{3,2,1,0:T(8,128)(2,1)}, bf16[2,4,384,512]{3,2,1,0:T(8,128)(2,1)}, u32[]{:S(2)}, u32[]{:S(2)}) collective-permute-start(bf16[2,4,384,512]{3,2,1,0:T(8,128)(2,1)} %get-tuple-element.16), channel_id=1, source_target_pairs={{0,120},{8,0},{16,8},{24,16},{32,24},{40,32},{48,40},{56,48},{64,5... | collective-permute-start | bytes 9437192 | tf_op jit(solution)/shard_map/ppermute | solution.py:82
  10.4 39.2 %collective-permute-start.2 = (bf16[4,384,512]{2,1,0:T(8,128)(2,1)}, bf16[4,384,512]{2,1,0:T(8,128)(2,1)}, u32[]{:S(2)}, u32[]{:S(2)}) collective-permute-start(bf16[4,384,512]{2,1,0:T(8,128)(2,1)} %slice_bitcast_fusion.1), channel_id=1, source_target_pairs={{0,1},{1,2},{2,3},{3,4},{4,5},{5,6},{6,7},{8,9},{9,10},{10,11},{11... | collective-permute-start | bytes 4718600 | tf_op jit(solution)/shard_map/ppermute | solution.py:88
  52.2 108.6 %collective-permute-start.10 = (bf16[4,384,512]{2,1,0:T(8,128)(2,1)}, bf16[4,384,512]{2,1,0:T(8,128)(2,1)}, u32[]{:S(2)}, u32[]{:S(2)}) collective-permute-start(bf16[4,384,512]{2,1,0:T(8,128)(2,1)} %slice_bitcast_fusion), channel_id=1, source_target_pairs={{0,1},{1,2},{2,3},{3,4},{4,5},{5,6},{6,7},{8,9},{9,10},{10,11},{11... | collective-permute-start | bytes 4718600 | tf_op jit(solution)/shard_map/ppermute | solution.py:88
  78.8 34.6 %collective-permute-start.9 = (bf16[384,512]{1,0:T(8,128)(2,1)S(1)}, bf16[384,512]{1,0:T(8,128)(2,1)S(1)}, u32[]{:S(2)}, u32[]{:S(2)}) collective-permute-start(bf16[384,512]{1,0:T(8,128)(2,1)S(1)} %get-tuple-element.19), channel_id=1, source_target_pairs={{0,7},{1,0},{2,1},{3,2},{4,3},{5,4},{6,5},{7,6},{8,15},{9,8},{10,9... | collective-permute-start | bytes 1179656 | tf_op jit(solution)/shard_map/ppermute | solution.py:82
  79.1 43.0 %collective-permute-start.8 = (bf16[384,512]{1,0:T(8,128)(2,1)S(1)}, bf16[384,512]{1,0:T(8,128)(2,1)S(1)}, u32[]{:S(2)}, u32[]{:S(2)}) collective-permute-start(bf16[384,512]{1,0:T(8,128)(2,1)S(1)} %get-tuple-element.20), channel_id=1, source_target_pairs={{0,6},{1,7},{2,0},{3,1},{4,2},{5,3},{6,4},{7,5},{8,14},{9,15},{10,... | collective-permute-start | bytes 1179656 | tf_op jit(solution)/shard_map/ppermute | solution.py:82
  111.5 25.7 %collective-permute-start.7 = (bf16[384,512]{1,0:T(8,128)(2,1)S(1)}, bf16[384,512]{1,0:T(8,128)(2,1)S(1)}, u32[]{:S(2)}, u32[]{:S(2)}) collective-permute-start(bf16[384,512]{1,0:T(8,128)(2,1)S(1)} %get-tuple-element.21), channel_id=1, source_target_pairs={{0,5},{1,6},{2,7},{3,0},{4,1},{5,2},{6,3},{7,4},{8,13},{9,14},{10,... | collective-permute-start | bytes 1179656 | tf_op jit(solution)/shard_map/ppermute | solution.py:82
  113.4 34.7 %collective-permute-start.6 = (bf16[384,512]{1,0:T(8,128)(2,1)}, bf16[384,512]{1,0:T(8,128)(2,1)}, u32[]{:S(2)}, u32[]{:S(2)}) collective-permute-start(bf16[384,512]{1,0:T(8,128)(2,1)} %get-tuple-element.22), channel_id=1, source_target_pairs={{0,4},{1,5},{2,6},{3,7},{4,0},{5,1},{6,2},{7,3},{8,12},{9,13},{10,... | collective-permute-start | bytes 1179656 | tf_op jit(solution)/shard_map/ppermute | solution.py:82
  113.4 38.9 %collective-permute-start.5 = (bf16[384,512]{1,0:T(8,128)(2,1)}, bf16[384,512]{1,0:T(8,128)(2,1)}, u32[]{:S(2)}, u32[]{:S(2)}) collective-permute-start(bf16[384,512]{1,0:T(8,128)(2,1)} %get-tuple-element.23), channel_id=1, source_target_pairs={{0,3},{1,4},{2,5},{3,6},{4,7},{5,0},{6,1},{7,2},{8,11},{9,12},{10,... | collective-permute-start | bytes 1179656 | tf_op jit(solution)/shard_map/ppermute | solution.py:82
  122.1 15.1 %copy-start.2 = (bf16[384,512]{1,0:T(8,128)(2,1)}, bf16[384,512]{1,0:T(8,128)(2,1)S(1)}, u32[]{:S(2)}) copy-start(bf16[384,512]{1,0:T(8,128)(2,1)S(1)} %collective-permute-done.8) | copy-start | bytes 1179652
  122.1 30.1 %collective-permute-start.4 = (bf16[384,512]{1,0:T(8,128)(2,1)S(1)}, bf16[384,512]{1,0:T(8,128)(2,1)}, u32[]{:S(2)}, u32[]{:S(2)}) collective-permute-start(bf16[384,512]{1,0:T(8,128)(2,1)S(1)} %get-tuple-element.24), channel_id=1, source_target_pairs={{0,2},{1,3},{2,4},{3,5},{4,6},{5,7},{6,0},{7,1},{8,10},{9,11},{10,... | collective-permute-start | bytes 1179656 | tf_op jit(solution)/shard_map/ppermute | solution.py:82
  137.2 0.7 copy-start.3
  138.0 20.2 %collective-permute-start.3 = (bf16[384,512]{1,0:T(8,128)(2,1)S(1)}, bf16[384,512]{1,0:T(8,128)(2,1)}, u32[]{:S(2)}, u32[]{:S(2)}) collective-permute-start(bf16[384,512]{1,0:T(8,128)(2,1)S(1)} %get-tuple-element.18), channel_id=1, source_target_pairs={{0,1},{1,2},{2,3},{3,4},{4,5},{5,6},{6,7},{7,0},{8,9},{9,10},{10,1... | collective-permute-start | bytes 1179656 | tf_op jit(solution)/shard_map/ppermute | solution.py:82
  160.8 15.7 %collective-permute-start.11 = (bf16[384,512]{1,0:T(8,128)(2,1)S(1)}, bf16[384,512]{1,0:T(8,128)(2,1)S(1)}, u32[]{:S(2)}, u32[]{:S(2)}) collective-permute-start(bf16[384,512]{1,0:T(8,128)(2,1)S(1)} %convolution_convert_fusion), channel_id=1, source_target_pairs={{0,7},{1,0},{2,1},{3,2},{4,3},{5,4},{6,5},{7,6},{8,15},{9,8},{10,9... | collective-permute-start | bytes 1179656 | tf_op jit(solution)/shard_map/ppermute | solution.py:82
  163.3 24.3 %collective-permute-start.12 = (bf16[384,512]{1,0:T(8,128)(2,1)S(1)}, bf16[384,512]{1,0:T(8,128)(2,1)S(1)}, u32[]{:S(2)}, u32[]{:S(2)}) collective-permute-start(bf16[384,512]{1,0:T(8,128)(2,1)S(1)} %convolution_convert_fusion), channel_id=1, source_target_pairs={{0,6},{1,7},{2,0},{3,1},{4,2},{5,3},{6,4},{7,5},{8,14},{9,15},{10,... | collective-permute-start | bytes 1179656 | tf_op jit(solution)/shard_map/ppermute | solution.py:82
  167.5 23.0 %collective-permute-start.13 = (bf16[384,512]{1,0:T(8,128)(2,1)S(1)}, bf16[384,512]{1,0:T(8,128)(2,1)S(1)}, u32[]{:S(2)}, u32[]{:S(2)}) collective-permute-start(bf16[384,512]{1,0:T(8,128)(2,1)S(1)} %convolution_convert_fusion), channel_id=1, source_target_pairs={{0,5},{1,6},{2,7},{3,0},{4,1},{5,2},{6,3},{7,4},{8,13},{9,14},{10,... | collective-permute-start | bytes 1179656 | tf_op jit(solution)/shard_map/ppermute | solution.py:82
  167.5 32.1 %collective-permute-start.14 = (bf16[384,512]{1,0:T(8,128)(2,1)S(1)}, bf16[384,512]{1,0:T(8,128)(2,1)S(1)}, u32[]{:S(2)}, u32[]{:S(2)}) collective-permute-start(bf16[384,512]{1,0:T(8,128)(2,1)S(1)} %convolution_convert_fusion), channel_id=1, source_target_pairs={{0,4},{1,5},{2,6},{3,7},{4,0},{5,1},{6,2},{7,3},{8,12},{9,13},{10,... | collective-permute-start | bytes 1179656 | tf_op jit(solution)/shard_map/ppermute | solution.py:82
  168.6 31.1 %collective-permute-start.15 = (bf16[384,512]{1,0:T(8,128)(2,1)S(1)}, bf16[384,512]{1,0:T(8,128)(2,1)S(1)}, u32[]{:S(2)}, u32[]{:S(2)}) collective-permute-start(bf16[384,512]{1,0:T(8,128)(2,1)S(1)} %convolution_convert_fusion), channel_id=1, source_target_pairs={{0,3},{1,4},{2,5},{3,6},{4,7},{5,0},{6,1},{7,2},{8,11},{9,12},{10,... | collective-permute-start | bytes 1179656 | tf_op jit(solution)/shard_map/ppermute | solution.py:82
  176.5 38.0 %collective-permute-start.16 = (bf16[384,512]{1,0:T(8,128)(2,1)S(1)}, bf16[384,512]{1,0:T(8,128)(2,1)S(1)}, u32[]{:S(2)}, u32[]{:S(2)}) collective-permute-start(bf16[384,512]{1,0:T(8,128)(2,1)S(1)} %convolution_convert_fusion), channel_id=1, source_target_pairs={{0,2},{1,3},{2,4},{3,5},{4,6},{5,7},{6,0},{7,1},{8,10},{9,11},{10,... | collective-permute-start | bytes 1179656 | tf_op jit(solution)/shard_map/ppermute | solution.py:82
  187.5 27.0 %collective-permute-start.17 = (bf16[384,512]{1,0:T(8,128)(2,1)S(1)}, bf16[384,512]{1,0:T(8,128)(2,1)S(1)}, u32[]{:S(2)}, u32[]{:S(2)}) collective-permute-start(bf16[384,512]{1,0:T(8,128)(2,1)S(1)} %convolution_convert_fusion), channel_id=1, source_target_pairs={{0,1},{1,2},{2,3},{3,4},{4,5},{5,6},{6,7},{7,0},{8,9},{9,10},{10,1... | collective-permute-start | bytes 1179656 | tf_op jit(solution)/shard_map/ppermute | solution.py:82
  214.9 3.4 %slice-start = ((bf16[2,8,384,512]{3,2,1,0:T(8,128)(2,1)}), bf16[1,8,384,512]{3,2,1,0:T(8,128)(2,1)S(1)}, s32[]{:S(2)}) async-start(bf16[2,8,384,512]{3,2,1,0:T(8,128)(2,1)} %m1.1), calls=%async_computation | async-start | bytes 6291456 | tf_op jit(solution)/shard_map/slice | solution.py:120

commit v12 on v6

--- a/solution.py
+++ b/solution.py
@@ -8,27 +8,23 @@
 EDGE = 4
 
 
-def term_kernel(src_ref, cnt_ref, a_ref, l0, m0, r0, l1, m1, r1, out_ref, acc_ref):
+def term_kernel(src_ref, cnt_ref, a_ref, *refs):
+    *sources, out_ref, acc_ref = refs
     b = pl.program_id(0)
-    l = pl.program_id(1)
     blocks = pl.num_programs(0)
-
-    @pl.when(l == 0)
-    def _():
-        acc_ref[...] = jnp.zeros_like(acc_ref)
-
-    cnt = cnt_ref[l, b]
-    for s, (lf, md, rt) in enumerate(((l0, m0, r0), (l1, m1, r1))):
-        w = src_ref[l, b, s]
-        live = s < cnt
-        for ref, cond in ((lf, w < EDGE), (md, (w >= EDGE) & (w < EDGE + blocks)), (rt, w >= EDGE + blocks)):
-            @pl.when(live & cond)
-            def _():
-                acc_ref[...] += jnp.dot(a_ref[s], ref[...], preferred_element_type=jnp.float32)
-
-    @pl.when(l == pl.num_programs(1) - 1)
-    def _():
-        out_ref[...] = acc_ref[...].astype(out_ref.dtype)
+    lags, slots = a_ref.shape[0], a_ref.shape[1]
+    acc_ref[...] = jnp.zeros_like(acc_ref)
+    for l in range(lags):
+        cnt = cnt_ref[l, b]
+        for s in range(slots):
+            lf, md, rt = sources[3 * (l * slots + s):3 * (l * slots + s) + 3]
+            w = src_ref[l, b, s]
+            live = s < cnt
+            for ref, cond in ((lf, w < EDGE), (md, (w >= EDGE) & (w < EDGE + blocks)), (rt, w >= EDGE + blocks)):
+                @pl.when(live & cond)
+                def _():
+                    acc_ref[...] += jnp.dot(a_ref[l, s], ref[...], preferred_element_type=jnp.float32)
+    out_ref[...] = acc_ref[...].astype(out_ref.dtype)
 
 
 def lag_partial(history, left, right, lag_blocks, pattern, live_counts):
@@ -36,35 +32,28 @@
     slots = lag_blocks.shape[2]
     window = jnp.arange(blocks, dtype=jnp.int32)[None, :, None] + pattern
 
-    def used(src, cnt, l, b, s, lo, hi):
-        w = src[l, b, s]
-        return (s < cnt[l, b]) & (w >= lo) & (w < hi), w - lo
-
-    def source_spec(s, lo, hi, count):
-        def index(b, l, src, cnt):
-            on, at = used(src, cnt, l, b, s, lo, hi)
-            return (jnp.where(on, l, 0), jnp.where(on, jnp.clip(at, 0, count - 1), 0), 0, 0)
+    def source_spec(l, s, lo, hi, count):
+        def index(b, src, cnt):
+            w = src[l, b, s]
+            on = (s < cnt[l, b]) & (w >= lo) & (w < hi)
+            return (jnp.where(on, l, 0), jnp.where(on, jnp.clip(w - lo, 0, count - 1), 0), 0, 0)
         return pl.BlockSpec((None, None, vec, ex), index)
 
-    def local_spec(s):
-        return source_spec(s, EDGE, EDGE + blocks, blocks)
-
-    def left_spec(s):
-        return source_spec(s, 0, EDGE, EDGE)
-
-    def right_spec(s):
-        return source_spec(s, EDGE + blocks, 2 * EDGE + blocks, EDGE)
-
-    in_specs = [pl.BlockSpec((None, None, slots, vec, vec), lambda b, l, src, cnt: (l, b, 0, 0, 0))]
+    in_specs = [pl.BlockSpec((lags, None, slots, vec, vec), lambda b, src, cnt: (0, b, 0, 0, 0))]
     operands = [lag_blocks]
-    for s in range(slots):
-        in_specs += [left_spec(s), local_spec(s), right_spec(s)]
-        operands += [left, history, right]
+    for l in range(lags):
+        for s in range(slots):
+            in_specs += [
+                source_spec(l, s, 0, EDGE, EDGE),
+                source_spec(l, s, EDGE, EDGE + blocks, blocks),
+                source_spec(l, s, EDGE + blocks, 2 * EDGE + blocks, EDGE),
+            ]
+            operands += [left, history, right]
     grid_spec = pltpu.PrefetchScalarGridSpec(
         num_scalar_prefetch=2,
-        grid=(blocks, lags),
+        grid=(blocks,),
         in_specs=in_specs,
-        out_specs=pl.BlockSpec((None, vec, ex), lambda b, l, src, cnt: (b, 0, 0)),
+        out_specs=pl.BlockSpec((None, vec, ex), lambda b, src, cnt: (b, 0, 0)),
         scratch_shapes=[pltpu.VMEM((vec, ex), jnp.float32)],
     )
     flops = 2 * lags * blocks * slots * vec * vec * ex

time: 220 us -> 220 us (level)
  the two profiles are of different devices: /device:TPU:62 before, /device:TPU:14 now
where the time goes in v12:
time: 220 us; the launch traced here: 219 us
  waiting for transfers between devices  93.4 us (42%)
  starting transfers between devices  82.6 us (38%)
  Pallas kernels  18.4 us (8%)
  local copies, waits for them, and re-layouts  12.9 us (6%)
  other arithmetic  7.77 us (4%)
  matrix products  2.62 us (1%)
    ppermute x16, starting transfers between devices, shifted_by(): lax.ppermute(array, axis, [(i, (i + by) % count) for i in range(count)])  75.7 us
    ppermute x16, waiting for transfers between devices, shifted_by(): lax.ppermute(array, axis, [(i, (i + by) % count) for i in range(count)])  59.9 us
    ppermute x2, waiting for transfers between devices, passed_along(): return lax.ppermute(array, axis, pairs)  33.5 us
    pallas_call x1, Pallas kernels, lag_partial(): pl.pallas_call(term_kernel, grid_spec=grid_spec, out_shape=jax.ShapeDtype...  18.4 us
    ppermute x2, starting transfers between devices, passed_along(): return lax.ppermute(array, axis, pairs)  6.95 us
    slice x1, local copies, waits for them, and re-layouts, shards(): right = shifted_by(history[:, :EDGE], 'tile', -1)  6.6 us
  transfers between devices with their start and end apart: 18, of which 9 were waited for; matrix products, arithmetic and copies ran while one was open for 4% of the time, Pallas kernels for 8%

profile of v12, /device:TPU:14, one launch (start us, length us, event | category | flops | bytes accessed | tf_op | source)
XLA Modules:
  0.0 218.6 jit_solution(12490572688852085142)
XLA Ops:
  0.6 0.0 copy-start
  0.6 0.0 copy-start.1
  0.7 6.6 %fusion.15 = (bf16[2,4,384,512]{3,2,1,0:T(8,128)(2,1)}, bf16[2,4,384,512]{3,2,1,0:T(8,128)(2,1)}) fusion(bf16[2,8,384,512]{3,2,1,0:T(8,128)(2,1)} %refs_10_.1), kind=kLoop, calls=%fused_computation.46 | loop fusion | bytes 12582912 | tf_op jit(solution)/shard_map/slice | solution.py:85
  7.3 0.0 copy-start.4
  7.3 0.0 copy-start.5
  7.3 0.0 collective-permute-start
  7.3 1.7 collective-permute-start.1
  9.0 0.0 copy-done.1
  9.0 2.0 slice_bitcast_fusion
  11.0 3.5 %collective-permute-start.2 = (bf16[4,384,512]{2,1,0:T(8,128)(2,1)}, bf16[4,384,512]{2,1,0:T(8,128)(2,1)}, u32[]{:S(2)}, u32[]{:S(2)}) collective-permute-start(bf16[4,384,512]{2,1,0:T(8,128)(2,1)} %get-tuple-element.16), channel_id=1, source_target_pairs={{0,1},{1,2},{2,3},{3,4},{4,5},{5,6},{6,7},{8,9},{9,10},{10,11},{11... | collective-permute-start | bytes 4718600 | tf_op jit(solution)/shard_map/ppermute | solution.py:77
  14.6 0.0 copy-done.4
  14.6 0.1 copy.8
  14.7 0.0 copy-done.5
  14.7 0.5 broadcast_minimum_fusion.cnt_ref
  15.2 0.6 iota_add_fusion.src_ref
  15.8 33.5 %collective-permute-done.2 = bf16[4,384,512]{2,1,0:T(8,128)(2,1)} collective-permute-done((bf16[4,384,512]{2,1,0:T(8,128)(2,1)}, bf16[4,384,512]{2,1,0:T(8,128)(2,1)}, u32[]{:S(2)}, u32[]{:S(2)}) %collective-permute-start.2) | collective-permute-done | bytes 1572896 | tf_op jit(solution)/shard_map/ppermute | solution.py:77
  49.3 0.0 collective-permute-done.refs_0_.refs_3_.refs_6_.refs_9_
  49.3 0.0 collective-permute-done.1.refs_2_.refs_5_.refs_8_.refs_11_
  49.3 3.5 %collective-permute-start.10 = (bf16[4,384,512]{2,1,0:T(8,128)(2,1)}, bf16[4,384,512]{2,1,0:T(8,128)(2,1)}, u32[]{:S(2)}, u32[]{:S(2)}) collective-permute-start(bf16[4,384,512]{2,1,0:T(8,128)(2,1)} %get-tuple-element.10), channel_id=1, source_target_pairs={{0,1},{1,2},{2,3},{3,4},{4,5},{5,6},{6,7},{8,9},{9,10},{10,11},{11... | collective-permute-start | bytes 4718600 | tf_op jit(solution)/shard_map/ppermute | solution.py:77
  52.8 18.4 %shard_map.77 = bf16[8,384,512]{2,1,0:T(8,128)(2,1)} custom-call(s32[2,8,2]{2,1,0:T(8,128)} %iota_add_fusion.src_ref, s32[2,8]{1,0:T(2,128)} %broadcast_minimum_fusion.cnt_ref, bf16[2,8,2,384,384]{4,3,2,1,0:T(8,128)(2,1)} %a_ref.1, bf16[2,4,384,512]{3,2,1,0:T(8,128)(2,1)} %collective-permute-done.refs_0_.refs_3_.refs_6_.refs_9_, ...), custom_call_target="tpu_custom_call" | custom-call | flops 4831838208 | bytes 25165824 | tf_op jit(solution)/shard_map/pallas_call | solution.py:61
  71.2 2.9 %dynamic-slice_bitcast_fusion.6 = (bf16[384,512]{1,0:T(8,128)(2,1)S(1)}, bf16[384,512]{1,0:T(8,128)(2,1)S(1)}, bf16[384,512]{1,0:T(8,128)(2,1)S(1)}, bf16[384,51...) fusion(bf16[8,384,512]{2,1,0:T(8,128)(2,1)} %shard_map.77, ...), kind=kLoop, calls=%fused_computation.38 | loop fusion | bytes 5505052 | tf_op jit(solution)/shard_map/jit(dynamic_index_in_dim)/squeeze | solution.py:95
  74.2 2.8 %collective-permute-start.9 = (bf16[384,512]{1,0:T(8,128)(2,1)S(1)}, bf16[384,512]{1,0:T(8,128)(2,1)S(1)}, u32[]{:S(2)}, u32[]{:S(2)}) collective-permute-start(bf16[384,512]{1,0:T(8,128)(2,1)S(1)} %get-tuple-element.21), channel_id=1, source_target_pairs={{0,7},{1,0},{2,1},{3,2},{4,3},{5,4},{6,5},{7,6},{8,15},{9,8},{10,9... | collective-permute-start | bytes 1179656 | tf_op jit(solution)/shard_map/ppermute | solution.py:71
  76.9 1.5 collective-permute-start.8
  78.4 35.3 %collective-permute-start.7 = (bf16[384,512]{1,0:T(8,128)(2,1)S(1)}, bf16[384,512]{1,0:T(8,128)(2,1)S(1)}, u32[]{:S(2)}, u32[]{:S(2)}) collective-permute-start(bf16[384,512]{1,0:T(8,128)(2,1)S(1)} %get-tuple-element.23), channel_id=1, source_target_pairs={{0,5},{1,6},{2,7},{3,0},{4,1},{5,2},{6,3},{7,4},{8,13},{9,14},{10,... | collective-permute-start | bytes 1179656 | tf_op jit(solution)/shard_map/ppermute | solution.py:71
  113.7 0.0 collective-permute-start.6
  113.7 0.1 collective-permute-done.9
  113.8 19.6 %collective-permute-start.5 = (bf16[384,512]{1,0:T(8,128)(2,1)}, bf16[384,512]{1,0:T(8,128)(2,1)}, u32[]{:S(2)}, u32[]{:S(2)}) collective-permute-start(bf16[384,512]{1,0:T(8,128)(2,1)} %get-tuple-element.25), channel_id=1, source_target_pairs={{0,3},{1,4},{2,5},{3,6},{4,7},{5,0},{6,1},{7,2},{8,11},{9,12},{10,... | collective-permute-start | bytes 1179656 | tf_op jit(solution)/shard_map/ppermute | solution.py:71
  133.4 0.0 collective-permute-done.8
  133.4 0.0 copy-start.2
  133.4 3.7 %collective-permute-start.4 = (bf16[384,512]{1,0:T(8,128)(2,1)S(1)}, bf16[384,512]{1,0:T(8,128)(2,1)}, u32[]{:S(2)}, u32[]{:S(2)}) collective-permute-start(bf16[384,512]{1,0:T(8,128)(2,1)S(1)} %get-tuple-element.26), channel_id=1, source_target_pairs={{0,2},{1,3},{2,4},{3,5},{4,6},{5,7},{6,0},{7,1},{8,10},{9,11},{10,... | collective-permute-start | bytes 1179656 | tf_op jit(solution)/shard_map/ppermute | solution.py:71
  137.1 12.1 %collective-permute-done.7 = bf16[384,512]{1,0:T(8,128)(2,1)S(1)} collective-permute-done((bf16[384,512]{1,0:T(8,128)(2,1)S(1)}, bf16[384,512]{1,0:T(8,128)(2,1)S(1)}, u32[]{:S(2)}, u32[]{:S(2)}) %collective-permute-start.7) | collective-permute-done | bytes 393248 | tf_op jit(solution)/shard_map/ppermute | solution.py:71
  149.2 0.0 copy-done.2
  149.2 0.0 copy-start.3
  149.2 0.8 copy-done.3
  150.0 0.0 collective-permute-start.3
  150.0 0.0 collective-permute-done.6
  150.0 0.0 collective-permute-done.5
  150.0 0.0 collective-permute-done.4
  150.0 10.1 %collective-permute-done.3 = bf16[384,512]{1,0:T(8,128)(2,1)} collective-permute-done((bf16[384,512]{1,0:T(8,128)(2,1)S(1)}, bf16[384,512]{1,0:T(8,128)(2,1)}, u32[]{:S(2)}, u32[]{:S(2)}) %collective-permute-start.3) | collective-permute-done | bytes 393248 | tf_op jit(solution)/shard_map/ppermute | solution.py:71
  160.1 0.0 copy-done
  160.1 2.6 %convolution_convert_fusion = bf16[384,512]{1,0:T(8,128)(2,1)S(1)} fusion(bf16[384,512]{1,0:T(8,128)(2,1)S(1)} %collective-permute-done.9, bf16[384,512]{1,0:T(8,128)(2,1)} %copy-done.2, bf16[384,512]{1,0:T(8,128)(2,1)} %copy-done.3, bf16[384,512]{1,0:T(8,128)(2,1)} %collective-permute-done.6, bf16[384,512]{1,0:T(8,128)(2,1)} %collective-permute-done.5, ...), kind=kOutput, calls=%fused_computation.5 | convolution fusion | flops 154533888 | bytes 4621312 | tf_op jit(solution)/shard_map/dot_general | solution.py:100
  162.7 0.0 collective-permute-done.10
  162.7 0.1 collective-permute-start.11
  162.8 0.6 collective-permute-start.12
  163.4 7.0 %collective-permute-start.13 = (bf16[384,512]{1,0:T(8,128)(2,1)S(1)}, bf16[384,512]{1,0:T(8,128)(2,1)S(1)}, u32[]{:S(2)}, u32[]{:S(2)}) collective-permute-start(bf16[384,512]{1,0:T(8,128)(2,1)S(1)} %convolution_convert_fusion), channel_id=1, source_target_pairs={{0,5},{1,6},{2,7},{3,0},{4,1},{5,2},{6,3},{7,4},{8,13},{9,14},{10,... | collective-permute-start | bytes 1179656 | tf_op jit(solution)/shard_map/ppermute | solution.py:71
  170.3 0.0 collective-permute-start.14
  170.3 3.5 %collective-permute-start.15 = (bf16[384,512]{1,0:T(8,128)(2,1)S(1)}, bf16[384,512]{1,0:T(8,128)(2,1)S(1)}, u32[]{:S(2)}, u32[]{:S(2)}) collective-permute-start(bf16[384,512]{1,0:T(8,128)(2,1)S(1)} %convolution_convert_fusion), channel_id=1, source_target_pairs={{0,3},{1,4},{2,5},{3,6},{4,7},{5,0},{6,1},{7,2},{8,11},{9,12},{10,... | collective-permute-start | bytes 1179656 | tf_op jit(solution)/shard_map/ppermute | solution.py:71
  173.9 5.2 %collective-permute-done.11 = bf16[384,512]{1,0:T(8,128)(2,1)S(1)} collective-permute-done((bf16[384,512]{1,0:T(8,128)(2,1)S(1)}, bf16[384,512]{1,0:T(8,128)(2,1)S(1)}, u32[]{:S(2)}, u32[]{:S(2)}) %collective-permute-start.11) | collective-permute-done | bytes 393248 | tf_op jit(solution)/shard_map/ppermute | solution.py:71
  179.1 0.0 collective-permute-start.16
  179.1 4.7 %collective-permute-done.12 = bf16[384,512]{1,0:T(8,128)(2,1)S(1)} collective-permute-done((bf16[384,512]{1,0:T(8,128)(2,1)S(1)}, bf16[384,512]{1,0:T(8,128)(2,1)S(1)}, u32[]{:S(2)}, u32[]{:S(2)}) %collective-permute-start.12) | collective-permute-done | bytes 393248 | tf_op jit(solution)/shard_map/ppermute | solution.py:71
  183.9 0.0 collective-permute-start.17
  183.9 10.1 %collective-permute-done.13 = bf16[384,512]{1,0:T(8,128)(2,1)S(1)} collective-permute-done((bf16[384,512]{1,0:T(8,128)(2,1)S(1)}, bf16[384,512]{1,0:T(8,128)(2,1)S(1)}, u32[]{:S(2)}, u32[]{:S(2)}) %collective-permute-start.13) | collective-permute-done | bytes 393248 | tf_op jit(solution)/shard_map/ppermute | solution.py:71
  194.0 11.6 %collective-permute-done.14 = bf16[384,512]{1,0:T(8,128)(2,1)S(1)} collective-permute-done((bf16[384,512]{1,0:T(8,128)(2,1)S(1)}, bf16[384,512]{1,0:T(8,128)(2,1)S(1)}, u32[]{:S(2)}, u32[]{:S(2)}) %collective-permute-start.14) | collective-permute-done | bytes 393248 | tf_op jit(solution)/shard_map/ppermute | solution.py:71
  205.7 0.0 collective-permute-done.15
  205.7 0.0 collective-permute-done.16
  205.8 5.9 %collective-permute-done.17 = bf16[384,512]{1,0:T(8,128)(2,1)S(1)} collective-permute-done((bf16[384,512]{1,0:T(8,128)(2,1)S(1)}, bf16[384,512]{1,0:T(8,128)(2,1)S(1)}, u32[]{:S(2)}, u32[]{:S(2)}) %collective-permute-start.17) | collective-permute-done | bytes 393248 | tf_op jit(solution)/shard_map/ppermute | solution.py:71
  212.0 0.0 slice-start
  212.0 3.4 %fusion = (bf16[1,8,384,512]{3,2,1,0:T(8,128)(2,1)S(1)}, bf16[8,384,512]{2,1,0:T(8,128)(2,1)}) fusion(bf16[4,384,512]{2,1,0:T(8,128)(2,1)} %collective-permute-done.10, bf16[4,384,512]{2,1,0:T(8,128)(2,1)} %collective-permute-done.2, pred[]{:T(512)S(6)} %eq.14, bf16[16,384,512]{2,1,0:T(8,128)(2,1)S(1)} %bitcast_dynamic-update-slice_fusion.1, s32[]{:T(128)S(6)} %select_n.93), kind=kLoop, calls=%fused_computation.2 | loop fusion | flops 3145728 | bytes 12582917 | tf_op jit(solution)/shard_map/broadcast_in_dim | solution.py:109
  215.4 0.0 slice-done
  215.4 3.2 %pad_maximum_fusion = bf16[2,8,384,512]{3,2,1,0:T(8,128)(2,1)} fusion(bf16[1,8,384,512]{3,2,1,0:T(8,128)(2,1)S(1)} %slice-done, bf16[1,8,384,512]{3,2,1,0:T(8,128)(2,1)S(1)} %get-tuple-element.14), kind=kLoop, calls=%fused_computation | loop fusion | flops 3145728 | bytes 12582912 | tf_op jit(solution)/shard_map/concatenate | solution.py:109
  (16 shorter events, 0.4 us)
Async XLA Ops:
  0.6 159.4 %copy-start = (bf16[8,384,384]{2,1,0:T(8,128)(2,1)S(1)}, bf16[8,384,384]{2,1,0:T(8,128)(2,1)}, u32[]{:S(2)}) copy-start(bf16[8,384,384]{2,1,0:T(8,128)(2,1)} %param.8) | copy-start | bytes 7077892
  0.6 8.4 %copy-start.1 = (bf16[2,8,384,512]{3,2,1,0:T(8,128)(2,1)S(1)}, bf16[2,8,384,512]{3,2,1,0:T(8,128)(2,1)}, u32[]{:S(2)}) copy-start(bf16[2,8,384,512]{3,2,1,0:T(8,128)(2,1)} %refs_10_.1) | copy-start | bytes 18874372
  7.3 7.4 %copy-start.4 = (s32[2,8,2]{1,2,0:T(2,128)S(1)}, s32[2,8,2]{1,2,0:T(2,128)}, u32[]{:S(2)}) copy-start(s32[2,8,2]{1,2,0:T(2,128)} %param.10) | copy-start | bytes 388
  7.3 7.4 %copy-start.5 = (s32[2,8]{1,0:T(2,128)S(1)}, s32[2,8]{1,0:T(2,128)}, u32[]{:S(2)}) copy-start(s32[2,8]{1,0:T(2,128)} %param.11) | copy-start | bytes 196
  7.3 42.1 %collective-permute-start = (bf16[2,4,384,512]{3,2,1,0:T(8,128)(2,1)}, bf16[2,4,384,512]{3,2,1,0:T(8,128)(2,1)}, u32[]{:S(2)}, u32[]{:S(2)}) collective-permute-start(bf16[2,4,384,512]{3,2,1,0:T(8,128)(2,1)} %get-tuple-element.19), channel_id=1, source_target_pairs={{0,8},{8,16},{16,24},{24,32},{32,40},{40,48},{48,56},{56,64},{64,7... | collective-permute-start | bytes 9437192 | tf_op jit(solution)/shard_map/ppermute | solution.py:71
  7.3 42.0 %collective-permute-start.1 = (bf16[2,4,384,512]{3,2,1,0:T(8,128)(2,1)}, bf16[2,4,384,512]{3,2,1,0:T(8,128)(2,1)}, u32[]{:S(2)}, u32[]{:S(2)}) collective-permute-start(bf16[2,4,384,512]{3,2,1,0:T(8,128)(2,1)} %get-tuple-element.18), channel_id=1, source_target_pairs={{0,120},{8,0},{16,8},{24,16},{32,24},{40,32},{48,40},{56,48},{64,5... | collective-permute-start | bytes 9437192 | tf_op jit(solution)/shard_map/ppermute | solution.py:71
  11.0 38.3 %collective-permute-start.2 = (bf16[4,384,512]{2,1,0:T(8,128)(2,1)}, bf16[4,384,512]{2,1,0:T(8,128)(2,1)}, u32[]{:S(2)}, u32[]{:S(2)}) collective-permute-start(bf16[4,384,512]{2,1,0:T(8,128)(2,1)} %get-tuple-element.16), channel_id=1, source_target_pairs={{0,1},{1,2},{2,3},{3,4},{4,5},{5,6},{6,7},{8,9},{9,10},{10,11},{11... | collective-permute-start | bytes 4718600 | tf_op jit(solution)/shard_map/ppermute | solution.py:77
  49.3 113.4 %collective-permute-start.10 = (bf16[4,384,512]{2,1,0:T(8,128)(2,1)}, bf16[4,384,512]{2,1,0:T(8,128)(2,1)}, u32[]{:S(2)}, u32[]{:S(2)}) collective-permute-start(bf16[4,384,512]{2,1,0:T(8,128)(2,1)} %get-tuple-element.10), channel_id=1, source_target_pairs={{0,1},{1,2},{2,3},{3,4},{4,5},{5,6},{6,7},{8,9},{9,10},{10,11},{11... | collective-permute-start | bytes 4718600 | tf_op jit(solution)/shard_map/ppermute | solution.py:77
  74.2 39.6 %collective-permute-start.9 = (bf16[384,512]{1,0:T(8,128)(2,1)S(1)}, bf16[384,512]{1,0:T(8,128)(2,1)S(1)}, u32[]{:S(2)}, u32[]{:S(2)}) collective-permute-start(bf16[384,512]{1,0:T(8,128)(2,1)S(1)} %get-tuple-element.21), channel_id=1, source_target_pairs={{0,7},{1,0},{2,1},{3,2},{4,3},{5,4},{6,5},{7,6},{8,15},{9,8},{10,9... | collective-permute-start | bytes 1179656 | tf_op jit(solution)/shard_map/ppermute | solution.py:71
  76.9 56.4 %collective-permute-start.8 = (bf16[384,512]{1,0:T(8,128)(2,1)S(1)}, bf16[384,512]{1,0:T(8,128)(2,1)S(1)}, u32[]{:S(2)}, u32[]{:S(2)}) collective-permute-start(bf16[384,512]{1,0:T(8,128)(2,1)S(1)} %get-tuple-element.22), channel_id=1, source_target_pairs={{0,6},{1,7},{2,0},{3,1},{4,2},{5,3},{6,4},{7,5},{8,14},{9,15},{10,... | collective-permute-start | bytes 1179656 | tf_op jit(solution)/shard_map/ppermute | solution.py:71
  78.4 70.8 %collective-permute-start.7 = (bf16[384,512]{1,0:T(8,128)(2,1)S(1)}, bf16[384,512]{1,0:T(8,128)(2,1)S(1)}, u32[]{:S(2)}, u32[]{:S(2)}) collective-permute-start(bf16[384,512]{1,0:T(8,128)(2,1)S(1)} %get-tuple-element.23), channel_id=1, source_target_pairs={{0,5},{1,6},{2,7},{3,0},{4,1},{5,2},{6,3},{7,4},{8,13},{9,14},{10,... | collective-permute-start | bytes 1179656 | tf_op jit(solution)/shard_map/ppermute | solution.py:71
  113.7 36.3 %collective-permute-start.6 = (bf16[384,512]{1,0:T(8,128)(2,1)}, bf16[384,512]{1,0:T(8,128)(2,1)}, u32[]{:S(2)}, u32[]{:S(2)}) collective-permute-start(bf16[384,512]{1,0:T(8,128)(2,1)} %get-tuple-element.24), channel_id=1, source_target_pairs={{0,4},{1,5},{2,6},{3,7},{4,0},{5,1},{6,2},{7,3},{8,12},{9,13},{10,... | collective-permute-start | bytes 1179656 | tf_op jit(solution)/shard_map/ppermute | solution.py:71
  113.8 36.2 %collective-permute-start.5 = (bf16[384,512]{1,0:T(8,128)(2,1)}, bf16[384,512]{1,0:T(8,128)(2,1)}, u32[]{:S(2)}, u32[]{:S(2)}) collective-permute-start(bf16[384,512]{1,0:T(8,128)(2,1)} %get-tuple-element.25), channel_id=1, source_target_pairs={{0,3},{1,4},{2,5},{3,6},{4,7},{5,0},{6,1},{7,2},{8,11},{9,12},{10,... | collective-permute-start | bytes 1179656 | tf_op jit(solution)/shard_map/ppermute | solution.py:71
  133.4 15.9 %copy-start.2 = (bf16[384,512]{1,0:T(8,128)(2,1)}, bf16[384,512]{1,0:T(8,128)(2,1)S(1)}, u32[]{:S(2)}) copy-start(bf16[384,512]{1,0:T(8,128)(2,1)S(1)} %collective-permute-done.8) | copy-start | bytes 1179652
  133.4 16.6 %collective-permute-start.4 = (bf16[384,512]{1,0:T(8,128)(2,1)S(1)}, bf16[384,512]{1,0:T(8,128)(2,1)}, u32[]{:S(2)}, u32[]{:S(2)}) collective-permute-start(bf16[384,512]{1,0:T(8,128)(2,1)S(1)} %get-tuple-element.26), channel_id=1, source_target_pairs={{0,2},{1,3},{2,4},{3,5},{4,6},{5,7},{6,0},{7,1},{8,10},{9,11},{10,... | collective-permute-start | bytes 1179656 | tf_op jit(solution)/shard_map/ppermute | solution.py:71
  149.2 0.8 copy-start.3
  150.0 10.1 %collective-permute-start.3 = (bf16[384,512]{1,0:T(8,128)(2,1)S(1)}, bf16[384,512]{1,0:T(8,128)(2,1)}, u32[]{:S(2)}, u32[]{:S(2)}) collective-permute-start(bf16[384,512]{1,0:T(8,128)(2,1)S(1)} %get-tuple-element.20), channel_id=1, source_target_pairs={{0,1},{1,2},{2,3},{3,4},{4,5},{5,6},{6,7},{7,0},{8,9},{9,10},{10,1... | collective-permute-start | bytes 1179656 | tf_op jit(solution)/shard_map/ppermute | solution.py:71
  162.7 16.4 %collective-permute-start.11 = (bf16[384,512]{1,0:T(8,128)(2,1)S(1)}, bf16[384,512]{1,0:T(8,128)(2,1)S(1)}, u32[]{:S(2)}, u32[]{:S(2)}) collective-permute-start(bf16[384,512]{1,0:T(8,128)(2,1)S(1)} %convolution_convert_fusion), channel_id=1, source_target_pairs={{0,7},{1,0},{2,1},{3,2},{4,3},{5,4},{6,5},{7,6},{8,15},{9,8},{10,9... | collective-permute-start | bytes 1179656 | tf_op jit(solution)/shard_map/ppermute | solution.py:71
  162.8 21.1 %collective-permute-start.12 = (bf16[384,512]{1,0:T(8,128)(2,1)S(1)}, bf16[384,512]{1,0:T(8,128)(2,1)S(1)}, u32[]{:S(2)}, u32[]{:S(2)}) collective-permute-start(bf16[384,512]{1,0:T(8,128)(2,1)S(1)} %convolution_convert_fusion), channel_id=1, source_target_pairs={{0,6},{1,7},{2,0},{3,1},{4,2},{5,3},{6,4},{7,5},{8,14},{9,15},{10,... | collective-permute-start | bytes 1179656 | tf_op jit(solution)/shard_map/ppermute | solution.py:71
  163.4 30.6 %collective-permute-start.13 = (bf16[384,512]{1,0:T(8,128)(2,1)S(1)}, bf16[384,512]{1,0:T(8,128)(2,1)S(1)}, u32[]{:S(2)}, u32[]{:S(2)}) collective-permute-start(bf16[384,512]{1,0:T(8,128)(2,1)S(1)} %convolution_convert_fusion), channel_id=1, source_target_pairs={{0,5},{1,6},{2,7},{3,0},{4,1},{5,2},{6,3},{7,4},{8,13},{9,14},{10,... | collective-permute-start | bytes 1179656 | tf_op jit(solution)/shard_map/ppermute | solution.py:71
  170.3 35.3 %collective-permute-start.14 = (bf16[384,512]{1,0:T(8,128)(2,1)S(1)}, bf16[384,512]{1,0:T(8,128)(2,1)S(1)}, u32[]{:S(2)}, u32[]{:S(2)}) collective-permute-start(bf16[384,512]{1,0:T(8,128)(2,1)S(1)} %convolution_convert_fusion), channel_id=1, source_target_pairs={{0,4},{1,5},{2,6},{3,7},{4,0},{5,1},{6,2},{7,3},{8,12},{9,13},{10,... | collective-permute-start | bytes 1179656 | tf_op jit(solution)/shard_map/ppermute | solution.py:71
  170.3 35.3 %collective-permute-start.15 = (bf16[384,512]{1,0:T(8,128)(2,1)S(1)}, bf16[384,512]{1,0:T(8,128)(2,1)S(1)}, u32[]{:S(2)}, u32[]{:S(2)}) collective-permute-start(bf16[384,512]{1,0:T(8,128)(2,1)S(1)} %convolution_convert_fusion), channel_id=1, source_target_pairs={{0,3},{1,4},{2,5},{3,6},{4,7},{5,0},{6,1},{7,2},{8,11},{9,12},{10,... | collective-permute-start | bytes 1179656 | tf_op jit(solution)/shard_map/ppermute | solution.py:71
  179.1 26.6 %collective-permute-start.16 = (bf16[384,512]{1,0:T(8,128)(2,1)S(1)}, bf16[384,512]{1,0:T(8,128)(2,1)S(1)}, u32[]{:S(2)}, u32[]{:S(2)}) collective-permute-start(bf16[384,512]{1,0:T(8,128)(2,1)S(1)} %convolution_convert_fusion), channel_id=1, source_target_pairs={{0,2},{1,3},{2,4},{3,5},{4,6},{5,7},{6,0},{7,1},{8,10},{9,11},{10,... | collective-permute-start | bytes 1179656 | tf_op jit(solution)/shard_map/ppermute | solution.py:71
  183.9 27.7 %collective-permute-start.17 = (bf16[384,512]{1,0:T(8,128)(2,1)S(1)}, bf16[384,512]{1,0:T(8,128)(2,1)S(1)}, u32[]{:S(2)}, u32[]{:S(2)}) collective-permute-start(bf16[384,512]{1,0:T(8,128)(2,1)S(1)} %convolution_convert_fusion), channel_id=1, source_target_pairs={{0,1},{1,2},{2,3},{3,4},{4,5},{5,6},{6,7},{7,0},{8,9},{9,10},{10,1... | collective-permute-start | bytes 1179656 | tf_op jit(solution)/shard_map/ppermute | solution.py:71
  212.0 3.4 %slice-start = ((bf16[2,8,384,512]{3,2,1,0:T(8,128)(2,1)}), bf16[1,8,384,512]{3,2,1,0:T(8,128)(2,1)S(1)}, s32[]{:S(2)}) async-start(bf16[2,8,384,512]{3,2,1,0:T(8,128)(2,1)} %refs_10_.1), calls=%async_computation | async-start | bytes 6291456 | tf_op jit(solution)/shard_map/slice | solution.py:109

commit v13 on v12

--- a/solution.py
+++ b/solution.py
@@ -8,22 +8,25 @@
 EDGE = 4
 
 
-def term_kernel(src_ref, cnt_ref, a_ref, *refs):
-    *sources, out_ref, acc_ref = refs
+def term_kernel(src_ref, cnt_ref, a_ref, left_ref, hist_ref, right_ref, out_ref, acc_ref):
     b = pl.program_id(0)
-    blocks = pl.num_programs(0)
     lags, slots = a_ref.shape[0], a_ref.shape[1]
+    blocks = hist_ref.shape[1]
     acc_ref[...] = jnp.zeros_like(acc_ref)
     for l in range(lags):
         cnt = cnt_ref[l, b]
         for s in range(slots):
-            lf, md, rt = sources[3 * (l * slots + s):3 * (l * slots + s) + 3]
             w = src_ref[l, b, s]
             live = s < cnt
-            for ref, cond in ((lf, w < EDGE), (md, (w >= EDGE) & (w < EDGE + blocks)), (rt, w >= EDGE + blocks)):
+            picks = (
+                (left_ref, w < EDGE, jnp.clip(w, 0, EDGE - 1)),
+                (hist_ref, (w >= EDGE) & (w < EDGE + blocks), jnp.clip(w - EDGE, 0, blocks - 1)),
+                (right_ref, w >= EDGE + blocks, jnp.clip(w - EDGE - blocks, 0, EDGE - 1)),
+            )
+            for ref, cond, at in picks:
                 @pl.when(live & cond)
                 def _():
-                    acc_ref[...] += jnp.dot(a_ref[l, s], ref[...], preferred_element_type=jnp.float32)
+                    acc_ref[...] += jnp.dot(a_ref[l, s], ref[l, at], preferred_element_type=jnp.float32)
     out_ref[...] = acc_ref[...].astype(out_ref.dtype)
 
 
@@ -32,23 +35,15 @@
     slots = lag_blocks.shape[2]
     window = jnp.arange(blocks, dtype=jnp.int32)[None, :, None] + pattern
 
-    def source_spec(l, s, lo, hi, count):
-        def index(b, src, cnt):
-            w = src[l, b, s]
-            on = (s < cnt[l, b]) & (w >= lo) & (w < hi)
-            return (jnp.where(on, l, 0), jnp.where(on, jnp.clip(w - lo, 0, count - 1), 0), 0, 0)
-        return pl.BlockSpec((None, None, vec, ex), index)
+    def whole(array):
+        return pl.BlockSpec(array.shape, lambda b, src, cnt: (0,) * array.ndim)
 
-    in_specs = [pl.BlockSpec((lags, None, slots, vec, vec), lambda b, src, cnt: (0, b, 0, 0, 0))]
-    operands = [lag_blocks]
-    for l in range(lags):
-        for s in range(slots):
-            in_specs += [
-                source_spec(l, s, 0, EDGE, EDGE),
-                source_spec(l, s, EDGE, EDGE + blocks, blocks),
-                source_spec(l, s, EDGE + blocks, 2 * EDGE + blocks, EDGE),
-            ]
-            operands += [left, history, right]
+    in_specs = [
+        pl.BlockSpec((lags, None, slots, vec, vec), lambda b, src, cnt: (0, b, 0, 0, 0)),
+        whole(left),
+        whole(history),
+        whole(right),
+    ]
     grid_spec = pltpu.PrefetchScalarGridSpec(
         num_scalar_prefetch=2,
         grid=(blocks,),
@@ -57,13 +52,13 @@
         scratch_shapes=[pltpu.VMEM((vec, ex), jnp.float32)],
     )
     flops = 2 * lags * blocks * slots * vec * vec * ex
-    moved = 2 * (lag_blocks.size + slots * history.size + blocks * vec * ex)
+    moved = 2 * (lag_blocks.size + history.size + left.size + right.size + blocks * vec * ex)
     return pl.pallas_call(
         term_kernel,
         grid_spec=grid_spec,
         out_shape=jax.ShapeDtypeStruct((blocks, vec, ex), jnp.bfloat16),
         cost_estimate=pl.CostEstimate(flops=flops, transcendentals=0, bytes_accessed=moved),
-    )(window, live_counts, *operands)
+    )(window, live_counts, lag_blocks, left, history, right)
 
 
 def shifted_by(array, axis, by):

time: 220 us -> 221 us (level)
  waiting for transfers between devices: 93.4 us -> 95.7 us
    ppermute x16, waiting for transfers between devices: 59.9 us -> 62.3 us  [shifted_by(): lax.ppermute(array, axis, [(i, (i + by) % count) for i in range(count)])]
where the time goes in v13:
time: 221 us; the launch traced here: 218 us
  waiting for transfers between devices  95.7 us (43%)
  starting transfers between devices  81 us (37%)
  Pallas kernels  17.1 us (8%)
  local copies, waits for them, and re-layouts  12.9 us (6%)
  other arithmetic  7.77 us (4%)
  matrix products  2.62 us (1%)
    ppermute x16, starting transfers between devices, shifted_by(): lax.ppermute(array, axis, [(i, (i + by) % count) for i in range(count)])  74 us
    ppermute x16, waiting for transfers between devices, shifted_by(): lax.ppermute(array, axis, [(i, (i + by) % count) for i in range(count)])  62.3 us
    ppermute x2, waiting for transfers between devices, passed_along(): return lax.ppermute(array, axis, pairs)  33.5 us
    pallas_call x1, Pallas kernels, lag_partial(): pl.pallas_call(term_kernel, grid_spec=grid_spec, out_shape=jax.ShapeDtype...  17.1 us
    ppermute x2, starting transfers between devices, passed_along(): return lax.ppermute(array, axis, pairs)  6.95 us
    slice x1, local copies, waits for them, and re-layouts, shards(): right = shifted_by(history[:, :EDGE], 'tile', -1)  6.6 us
  transfers between devices with their start and end apart: 18, of which 9 were waited for; matrix products, arithmetic and copies ran while one was open for 4% of the time, Pallas kernels for 8%

profile of v13, /device:TPU:14, one launch (start us, length us, event | category | flops | bytes accessed | tf_op | source)
XLA Modules:
  0.0 218.0 jit_solution(11024750807922814737)
XLA Ops:
  0.6 0.0 copy-start
  0.6 0.0 copy-start.1
  0.7 6.6 %fusion.15 = (bf16[2,4,384,512]{3,2,1,0:T(8,128)(2,1)}, bf16[2,4,384,512]{3,2,1,0:T(8,128)(2,1)}) fusion(bf16[2,8,384,512]{3,2,1,0:T(8,128)(2,1)} %hist_ref.1), kind=kLoop, calls=%fused_computation.46 | loop fusion | bytes 12582912 | tf_op jit(solution)/shard_map/slice | solution.py:80
  7.3 0.0 copy-start.4
  7.3 0.0 copy-start.5
  7.3 0.0 collective-permute-start
  7.3 1.7 collective-permute-start.1
  9.0 0.0 copy-done.1
  9.0 2.0 slice_bitcast_fusion
  11.0 3.5 %collective-permute-start.2 = (bf16[4,384,512]{2,1,0:T(8,128)(2,1)}, bf16[4,384,512]{2,1,0:T(8,128)(2,1)}, u32[]{:S(2)}, u32[]{:S(2)}) collective-permute-start(bf16[4,384,512]{2,1,0:T(8,128)(2,1)} %get-tuple-element.16), channel_id=1, source_target_pairs={{0,1},{1,2},{2,3},{3,4},{4,5},{5,6},{6,7},{8,9},{9,10},{10,11},{11... | collective-permute-start | bytes 4718600 | tf_op jit(solution)/shard_map/ppermute | solution.py:72
  14.6 0.0 copy-done.4
  14.6 0.1 copy.8
  14.7 0.0 copy-done.5
  14.7 0.5 broadcast_minimum_fusion.cnt_ref
  15.2 0.6 iota_add_fusion.src_ref
  15.8 33.5 %collective-permute-done.2 = bf16[4,384,512]{2,1,0:T(8,128)(2,1)} collective-permute-done((bf16[4,384,512]{2,1,0:T(8,128)(2,1)}, bf16[4,384,512]{2,1,0:T(8,128)(2,1)}, u32[]{:S(2)}, u32[]{:S(2)}) %collective-permute-start.2) | collective-permute-done | bytes 1572896 | tf_op jit(solution)/shard_map/ppermute | solution.py:72
  49.3 0.0 collective-permute-done.left_ref
  49.3 0.0 collective-permute-done.1.right_ref
  49.3 3.5 %collective-permute-start.10 = (bf16[4,384,512]{2,1,0:T(8,128)(2,1)}, bf16[4,384,512]{2,1,0:T(8,128)(2,1)}, u32[]{:S(2)}, u32[]{:S(2)}) collective-permute-start(bf16[4,384,512]{2,1,0:T(8,128)(2,1)} %get-tuple-element.10), channel_id=1, source_target_pairs={{0,1},{1,2},{2,3},{3,4},{4,5},{5,6},{6,7},{8,9},{9,10},{10,11},{11... | collective-permute-start | bytes 4718600 | tf_op jit(solution)/shard_map/ppermute | solution.py:72
  52.8 17.1 %shard_map.77 = bf16[8,384,512]{2,1,0:T(8,128)(2,1)} custom-call(s32[2,8,2]{2,1,0:T(8,128)} %iota_add_fusion.src_ref, s32[2,8]{1,0:T(2,128)} %broadcast_minimum_fusion.cnt_ref, bf16[2,8,2,384,384]{4,3,2,1,0:T(8,128)(2,1)} %a_ref.1, bf16[2,4,384,512]{3,2,1,0:T(8,128)(2,1)} %collective-permute-done.left_ref, bf16[2,8,384,512]{3,2,1,0:T(8,128)(2,1)} %hist_ref.1, ...), custom_call_target="tpu_custom_call" | custom-call | flops 4831838208 | bytes 25165824 | tf_op jit(solution)/shard_map/pallas_call | solution.py:56
  69.9 2.9 %dynamic-slice_bitcast_fusion.6 = (bf16[384,512]{1,0:T(8,128)(2,1)S(1)}, bf16[384,512]{1,0:T(8,128)(2,1)S(1)}, bf16[384,512]{1,0:T(8,128)(2,1)S(1)}, bf16[384,51...) fusion(bf16[8,384,512]{2,1,0:T(8,128)(2,1)} %shard_map.77, ...), kind=kLoop, calls=%fused_computation.38 | loop fusion | bytes 5505052 | tf_op jit(solution)/shard_map/jit(dynamic_index_in_dim)/squeeze | solution.py:90
  72.8 2.3 %collective-permute-start.9 = (bf16[384,512]{1,0:T(8,128)(2,1)S(1)}, bf16[384,512]{1,0:T(8,128)(2,1)S(1)}, u32[]{:S(2)}, u32[]{:S(2)}) collective-permute-start(bf16[384,512]{1,0:T(8,128)(2,1)S(1)} %get-tuple-element.21), channel_id=1, source_target_pairs={{0,7},{1,0},{2,1},{3,2},{4,3},{5,4},{6,5},{7,6},{8,15},{9,8},{10,9... | collective-permute-start | bytes 1179656 | tf_op jit(solution)/shard_map/ppermute | solution.py:66
  75.2 2.9 %collective-permute-start.8 = (bf16[384,512]{1,0:T(8,128)(2,1)S(1)}, bf16[384,512]{1,0:T(8,128)(2,1)S(1)}, u32[]{:S(2)}, u32[]{:S(2)}) collective-permute-start(bf16[384,512]{1,0:T(8,128)(2,1)S(1)} %get-tuple-element.22), channel_id=1, source_target_pairs={{0,6},{1,7},{2,0},{3,1},{4,2},{5,3},{6,4},{7,5},{8,14},{9,15},{10,... | collective-permute-start | bytes 1179656 | tf_op jit(solution)/shard_map/ppermute | solution.py:66
  78.1 34.0 %collective-permute-start.7 = (bf16[384,512]{1,0:T(8,128)(2,1)S(1)}, bf16[384,512]{1,0:T(8,128)(2,1)S(1)}, u32[]{:S(2)}, u32[]{:S(2)}) collective-permute-start(bf16[384,512]{1,0:T(8,128)(2,1)S(1)} %get-tuple-element.23), channel_id=1, source_target_pairs={{0,5},{1,6},{2,7},{3,0},{4,1},{5,2},{6,3},{7,4},{8,13},{9,14},{10,... | collective-permute-start | bytes 1179656 | tf_op jit(solution)/shard_map/ppermute | solution.py:66
  112.1 0.0 collective-permute-start.6
  112.1 1.1 collective-permute-done.9
  113.2 18.6 %collective-permute-start.5 = (bf16[384,512]{1,0:T(8,128)(2,1)}, bf16[384,512]{1,0:T(8,128)(2,1)}, u32[]{:S(2)}, u32[]{:S(2)}) collective-permute-start(bf16[384,512]{1,0:T(8,128)(2,1)} %get-tuple-element.25), channel_id=1, source_target_pairs={{0,3},{1,4},{2,5},{3,6},{4,7},{5,0},{6,1},{7,2},{8,11},{9,12},{10,... | collective-permute-start | bytes 1179656 | tf_op jit(solution)/shard_map/ppermute | solution.py:66
  131.8 0.0 collective-permute-done.8
  131.8 0.0 copy-start.2
  131.8 3.9 %collective-permute-start.4 = (bf16[384,512]{1,0:T(8,128)(2,1)S(1)}, bf16[384,512]{1,0:T(8,128)(2,1)}, u32[]{:S(2)}, u32[]{:S(2)}) collective-permute-start(bf16[384,512]{1,0:T(8,128)(2,1)S(1)} %get-tuple-element.26), channel_id=1, source_target_pairs={{0,2},{1,3},{2,4},{3,5},{4,6},{5,7},{6,0},{7,1},{8,10},{9,11},{10,... | collective-permute-start | bytes 1179656 | tf_op jit(solution)/shard_map/ppermute | solution.py:66
  135.6 14.5 %collective-permute-done.7 = bf16[384,512]{1,0:T(8,128)(2,1)S(1)} collective-permute-done((bf16[384,512]{1,0:T(8,128)(2,1)S(1)}, bf16[384,512]{1,0:T(8,128)(2,1)S(1)}, u32[]{:S(2)}, u32[]{:S(2)}) %collective-permute-start.7) | collective-permute-done | bytes 393248 | tf_op jit(solution)/shard_map/ppermute | solution.py:66
  150.1 0.0 copy-done.2
  150.2 0.0 copy-start.3
  150.2 0.8 copy-done.3
  150.9 0.0 collective-permute-start.3
  150.9 0.0 collective-permute-done.6
  150.9 0.0 collective-permute-done.5
  150.9 0.0 collective-permute-done.4
  150.9 10.3 %collective-permute-done.3 = bf16[384,512]{1,0:T(8,128)(2,1)} collective-permute-done((bf16[384,512]{1,0:T(8,128)(2,1)S(1)}, bf16[384,512]{1,0:T(8,128)(2,1)}, u32[]{:S(2)}, u32[]{:S(2)}) %collective-permute-start.3) | collective-permute-done | bytes 393248 | tf_op jit(solution)/shard_map/ppermute | solution.py:66
  161.3 0.0 copy-done
  161.3 2.6 %convolution_convert_fusion = bf16[384,512]{1,0:T(8,128)(2,1)S(1)} fusion(bf16[384,512]{1,0:T(8,128)(2,1)S(1)} %collective-permute-done.9, bf16[384,512]{1,0:T(8,128)(2,1)} %copy-done.2, bf16[384,512]{1,0:T(8,128)(2,1)} %copy-done.3, bf16[384,512]{1,0:T(8,128)(2,1)} %collective-permute-done.6, bf16[384,512]{1,0:T(8,128)(2,1)} %collective-permute-done.5, ...), kind=kOutput, calls=%fused_computation.5 | convolution fusion | flops 154533888 | bytes 4621312 | tf_op jit(solution)/shard_map/dot_general | solution.py:95
  163.9 0.0 collective-permute-done.10
  163.9 0.1 collective-permute-start.11
  164.0 0.1 collective-permute-start.12
  164.1 6.9 %collective-permute-start.13 = (bf16[384,512]{1,0:T(8,128)(2,1)S(1)}, bf16[384,512]{1,0:T(8,128)(2,1)S(1)}, u32[]{:S(2)}, u32[]{:S(2)}) collective-permute-start(bf16[384,512]{1,0:T(8,128)(2,1)S(1)} %convolution_convert_fusion), channel_id=1, source_target_pairs={{0,5},{1,6},{2,7},{3,0},{4,1},{5,2},{6,3},{7,4},{8,13},{9,14},{10,... | collective-permute-start | bytes 1179656 | tf_op jit(solution)/shard_map/ppermute | solution.py:66
  171.0 0.0 collective-permute-start.14
  171.0 3.5 %collective-permute-start.15 = (bf16[384,512]{1,0:T(8,128)(2,1)S(1)}, bf16[384,512]{1,0:T(8,128)(2,1)S(1)}, u32[]{:S(2)}, u32[]{:S(2)}) collective-permute-start(bf16[384,512]{1,0:T(8,128)(2,1)S(1)} %convolution_convert_fusion), channel_id=1, source_target_pairs={{0,3},{1,4},{2,5},{3,6},{4,7},{5,0},{6,1},{7,2},{8,11},{9,12},{10,... | collective-permute-start | bytes 1179656 | tf_op jit(solution)/shard_map/ppermute | solution.py:66
  174.5 6.9 %collective-permute-done.11 = bf16[384,512]{1,0:T(8,128)(2,1)S(1)} collective-permute-done((bf16[384,512]{1,0:T(8,128)(2,1)S(1)}, bf16[384,512]{1,0:T(8,128)(2,1)S(1)}, u32[]{:S(2)}, u32[]{:S(2)}) %collective-permute-start.11) | collective-permute-done | bytes 393248 | tf_op jit(solution)/shard_map/ppermute | solution.py:66
  181.4 0.0 collective-permute-start.16
  181.4 3.2 %collective-permute-done.12 = bf16[384,512]{1,0:T(8,128)(2,1)S(1)} collective-permute-done((bf16[384,512]{1,0:T(8,128)(2,1)S(1)}, bf16[384,512]{1,0:T(8,128)(2,1)S(1)}, u32[]{:S(2)}, u32[]{:S(2)}) %collective-permute-start.12) | collective-permute-done | bytes 393248 | tf_op jit(solution)/shard_map/ppermute | solution.py:66
  184.6 0.0 collective-permute-start.17
  184.6 15.7 %collective-permute-done.13 = bf16[384,512]{1,0:T(8,128)(2,1)S(1)} collective-permute-done((bf16[384,512]{1,0:T(8,128)(2,1)S(1)}, bf16[384,512]{1,0:T(8,128)(2,1)S(1)}, u32[]{:S(2)}, u32[]{:S(2)}) %collective-permute-start.13) | collective-permute-done | bytes 393248 | tf_op jit(solution)/shard_map/ppermute | solution.py:66
  200.4 5.9 %collective-permute-done.14 = bf16[384,512]{1,0:T(8,128)(2,1)S(1)} collective-permute-done((bf16[384,512]{1,0:T(8,128)(2,1)S(1)}, bf16[384,512]{1,0:T(8,128)(2,1)S(1)}, u32[]{:S(2)}, u32[]{:S(2)}) %collective-permute-start.14) | collective-permute-done | bytes 393248 | tf_op jit(solution)/shard_map/ppermute | solution.py:66
  206.3 0.0 collective-permute-done.15
  206.4 0.0 collective-permute-done.16
  206.4 4.6 %collective-permute-done.17 = bf16[384,512]{1,0:T(8,128)(2,1)S(1)} collective-permute-done((bf16[384,512]{1,0:T(8,128)(2,1)S(1)}, bf16[384,512]{1,0:T(8,128)(2,1)S(1)}, u32[]{:S(2)}, u32[]{:S(2)}) %collective-permute-start.17) | collective-permute-done | bytes 393248 | tf_op jit(solution)/shard_map/ppermute | solution.py:66
  211.4 0.0 slice-start
  211.4 3.4 %fusion = (bf16[1,8,384,512]{3,2,1,0:T(8,128)(2,1)S(1)}, bf16[8,384,512]{2,1,0:T(8,128)(2,1)}) fusion(bf16[4,384,512]{2,1,0:T(8,128)(2,1)} %collective-permute-done.10, bf16[4,384,512]{2,1,0:T(8,128)(2,1)} %collective-permute-done.2, pred[]{:T(512)S(6)} %eq.14, bf16[16,384,512]{2,1,0:T(8,128)(2,1)S(1)} %bitcast_dynamic-update-slice_fusion.1, s32[]{:T(128)S(6)} %select_n.93), kind=kLoop, calls=%fused_computation.2 | loop fusion | flops 3145728 | bytes 12582917 | tf_op jit(solution)/shard_map/broadcast_in_dim | solution.py:104
  214.8 0.0 slice-done
  214.8 3.2 %pad_maximum_fusion = bf16[2,8,384,512]{3,2,1,0:T(8,128)(2,1)} fusion(bf16[1,8,384,512]{3,2,1,0:T(8,128)(2,1)S(1)} %slice-done, bf16[1,8,384,512]{3,2,1,0:T(8,128)(2,1)S(1)} %get-tuple-element.14), kind=kLoop, calls=%fused_computation | loop fusion | flops 3145728 | bytes 12582912 | tf_op jit(solution)/shard_map/concatenate | solution.py:104
  (16 shorter events, 0.4 us)
Async XLA Ops:
  0.6 160.7 %copy-start = (bf16[8,384,384]{2,1,0:T(8,128)(2,1)S(1)}, bf16[8,384,384]{2,1,0:T(8,128)(2,1)}, u32[]{:S(2)}) copy-start(bf16[8,384,384]{2,1,0:T(8,128)(2,1)} %param.8) | copy-start | bytes 7077892
  0.6 8.4 %copy-start.1 = (bf16[2,8,384,512]{3,2,1,0:T(8,128)(2,1)S(1)}, bf16[2,8,384,512]{3,2,1,0:T(8,128)(2,1)}, u32[]{:S(2)}) copy-start(bf16[2,8,384,512]{3,2,1,0:T(8,128)(2,1)} %hist_ref.1) | copy-start | bytes 18874372
  7.3 7.4 %copy-start.4 = (s32[2,8,2]{1,2,0:T(2,128)S(1)}, s32[2,8,2]{1,2,0:T(2,128)}, u32[]{:S(2)}) copy-start(s32[2,8,2]{1,2,0:T(2,128)} %param.10) | copy-start | bytes 388
  7.3 7.4 %copy-start.5 = (s32[2,8]{1,0:T(2,128)S(1)}, s32[2,8]{1,0:T(2,128)}, u32[]{:S(2)}) copy-start(s32[2,8]{1,0:T(2,128)} %param.11) | copy-start | bytes 196
  7.3 42.1 %collective-permute-start = (bf16[2,4,384,512]{3,2,1,0:T(8,128)(2,1)}, bf16[2,4,384,512]{3,2,1,0:T(8,128)(2,1)}, u32[]{:S(2)}, u32[]{:S(2)}) collective-permute-start(bf16[2,4,384,512]{3,2,1,0:T(8,128)(2,1)} %get-tuple-element.19), channel_id=1, source_target_pairs={{0,8},{8,16},{16,24},{24,32},{32,40},{40,48},{48,56},{56,64},{64,7... | collective-permute-start | bytes 9437192 | tf_op jit(solution)/shard_map/ppermute | solution.py:66
  7.3 42.0 %collective-permute-start.1 = (bf16[2,4,384,512]{3,2,1,0:T(8,128)(2,1)}, bf16[2,4,384,512]{3,2,1,0:T(8,128)(2,1)}, u32[]{:S(2)}, u32[]{:S(2)}) collective-permute-start(bf16[2,4,384,512]{3,2,1,0:T(8,128)(2,1)} %get-tuple-element.18), channel_id=1, source_target_pairs={{0,120},{8,0},{16,8},{24,16},{32,24},{40,32},{48,40},{56,48},{64,5... | collective-permute-start | bytes 9437192 | tf_op jit(solution)/shard_map/ppermute | solution.py:66
  11.0 38.3 %collective-permute-start.2 = (bf16[4,384,512]{2,1,0:T(8,128)(2,1)}, bf16[4,384,512]{2,1,0:T(8,128)(2,1)}, u32[]{:S(2)}, u32[]{:S(2)}) collective-permute-start(bf16[4,384,512]{2,1,0:T(8,128)(2,1)} %get-tuple-element.16), channel_id=1, source_target_pairs={{0,1},{1,2},{2,3},{3,4},{4,5},{5,6},{6,7},{8,9},{9,10},{10,11},{11... | collective-permute-start | bytes 4718600 | tf_op jit(solution)/shard_map/ppermute | solution.py:72
  49.3 114.6 %collective-permute-start.10 = (bf16[4,384,512]{2,1,0:T(8,128)(2,1)}, bf16[4,384,512]{2,1,0:T(8,128)(2,1)}, u32[]{:S(2)}, u32[]{:S(2)}) collective-permute-start(bf16[4,384,512]{2,1,0:T(8,128)(2,1)} %get-tuple-element.10), channel_id=1, source_target_pairs={{0,1},{1,2},{2,3},{3,4},{4,5},{5,6},{6,7},{8,9},{9,10},{10,11},{11... | collective-permute-start | bytes 4718600 | tf_op jit(solution)/shard_map/ppermute | solution.py:72
  72.8 40.4 %collective-permute-start.9 = (bf16[384,512]{1,0:T(8,128)(2,1)S(1)}, bf16[384,512]{1,0:T(8,128)(2,1)S(1)}, u32[]{:S(2)}, u32[]{:S(2)}) collective-permute-start(bf16[384,512]{1,0:T(8,128)(2,1)S(1)} %get-tuple-element.21), channel_id=1, source_target_pairs={{0,7},{1,0},{2,1},{3,2},{4,3},{5,4},{6,5},{7,6},{8,15},{9,8},{10,9... | collective-permute-start | bytes 1179656 | tf_op jit(solution)/shard_map/ppermute | solution.py:66
  75.2 56.6 %collective-permute-start.8 = (bf16[384,512]{1,0:T(8,128)(2,1)S(1)}, bf16[384,512]{1,0:T(8,128)(2,1)S(1)}, u32[]{:S(2)}, u32[]{:S(2)}) collective-permute-start(bf16[384,512]{1,0:T(8,128)(2,1)S(1)} %get-tuple-element.22), channel_id=1, source_target_pairs={{0,6},{1,7},{2,0},{3,1},{4,2},{5,3},{6,4},{7,5},{8,14},{9,15},{10,... | collective-permute-start | bytes 1179656 | tf_op jit(solution)/shard_map/ppermute | solution.py:66
  78.1 72.1 %collective-permute-start.7 = (bf16[384,512]{1,0:T(8,128)(2,1)S(1)}, bf16[384,512]{1,0:T(8,128)(2,1)S(1)}, u32[]{:S(2)}, u32[]{:S(2)}) collective-permute-start(bf16[384,512]{1,0:T(8,128)(2,1)S(1)} %get-tuple-element.23), channel_id=1, source_target_pairs={{0,5},{1,6},{2,7},{3,0},{4,1},{5,2},{6,3},{7,4},{8,13},{9,14},{10,... | collective-permute-start | bytes 1179656 | tf_op jit(solution)/shard_map/ppermute | solution.py:66
  112.1 38.9 %collective-permute-start.6 = (bf16[384,512]{1,0:T(8,128)(2,1)}, bf16[384,512]{1,0:T(8,128)(2,1)}, u32[]{:S(2)}, u32[]{:S(2)}) collective-permute-start(bf16[384,512]{1,0:T(8,128)(2,1)} %get-tuple-element.24), channel_id=1, source_target_pairs={{0,4},{1,5},{2,6},{3,7},{4,0},{5,1},{6,2},{7,3},{8,12},{9,13},{10,... | collective-permute-start | bytes 1179656 | tf_op jit(solution)/shard_map/ppermute | solution.py:66
  113.2 37.7 %collective-permute-start.5 = (bf16[384,512]{1,0:T(8,128)(2,1)}, bf16[384,512]{1,0:T(8,128)(2,1)}, u32[]{:S(2)}, u32[]{:S(2)}) collective-permute-start(bf16[384,512]{1,0:T(8,128)(2,1)} %get-tuple-element.25), channel_id=1, source_target_pairs={{0,3},{1,4},{2,5},{3,6},{4,7},{5,0},{6,1},{7,2},{8,11},{9,12},{10,... | collective-permute-start | bytes 1179656 | tf_op jit(solution)/shard_map/ppermute | solution.py:66
  131.8 18.4 %copy-start.2 = (bf16[384,512]{1,0:T(8,128)(2,1)}, bf16[384,512]{1,0:T(8,128)(2,1)S(1)}, u32[]{:S(2)}) copy-start(bf16[384,512]{1,0:T(8,128)(2,1)S(1)} %collective-permute-done.8) | copy-start | bytes 1179652
  131.8 19.1 %collective-permute-start.4 = (bf16[384,512]{1,0:T(8,128)(2,1)S(1)}, bf16[384,512]{1,0:T(8,128)(2,1)}, u32[]{:S(2)}, u32[]{:S(2)}) collective-permute-start(bf16[384,512]{1,0:T(8,128)(2,1)S(1)} %get-tuple-element.26), channel_id=1, source_target_pairs={{0,2},{1,3},{2,4},{3,5},{4,6},{5,7},{6,0},{7,1},{8,10},{9,11},{10,... | collective-permute-start | bytes 1179656 | tf_op jit(solution)/shard_map/ppermute | solution.py:66
  150.2 0.8 copy-start.3
  150.9 10.4 %collective-permute-start.3 = (bf16[384,512]{1,0:T(8,128)(2,1)S(1)}, bf16[384,512]{1,0:T(8,128)(2,1)}, u32[]{:S(2)}, u32[]{:S(2)}) collective-permute-start(bf16[384,512]{1,0:T(8,128)(2,1)S(1)} %get-tuple-element.20), channel_id=1, source_target_pairs={{0,1},{1,2},{2,3},{3,4},{4,5},{5,6},{6,7},{7,0},{8,9},{9,10},{10,1... | collective-permute-start | bytes 1179656 | tf_op jit(solution)/shard_map/ppermute | solution.py:66
  163.9 17.5 %collective-permute-start.11 = (bf16[384,512]{1,0:T(8,128)(2,1)S(1)}, bf16[384,512]{1,0:T(8,128)(2,1)S(1)}, u32[]{:S(2)}, u32[]{:S(2)}) collective-permute-start(bf16[384,512]{1,0:T(8,128)(2,1)S(1)} %convolution_convert_fusion), channel_id=1, source_target_pairs={{0,7},{1,0},{2,1},{3,2},{4,3},{5,4},{6,5},{7,6},{8,15},{9,8},{10,9... | collective-permute-start | bytes 1179656 | tf_op jit(solution)/shard_map/ppermute | solution.py:66
  164.0 20.6 %collective-permute-start.12 = (bf16[384,512]{1,0:T(8,128)(2,1)S(1)}, bf16[384,512]{1,0:T(8,128)(2,1)S(1)}, u32[]{:S(2)}, u32[]{:S(2)}) collective-permute-start(bf16[384,512]{1,0:T(8,128)(2,1)S(1)} %convolution_convert_fusion), channel_id=1, source_target_pairs={{0,6},{1,7},{2,0},{3,1},{4,2},{5,3},{6,4},{7,5},{8,14},{9,15},{10,... | collective-permute-start | bytes 1179656 | tf_op jit(solution)/shard_map/ppermute | solution.py:66
  164.1 36.3 %collective-permute-start.13 = (bf16[384,512]{1,0:T(8,128)(2,1)S(1)}, bf16[384,512]{1,0:T(8,128)(2,1)S(1)}, u32[]{:S(2)}, u32[]{:S(2)}) collective-permute-start(bf16[384,512]{1,0:T(8,128)(2,1)S(1)} %convolution_convert_fusion), channel_id=1, source_target_pairs={{0,5},{1,6},{2,7},{3,0},{4,1},{5,2},{6,3},{7,4},{8,13},{9,14},{10,... | collective-permute-start | bytes 1179656 | tf_op jit(solution)/shard_map/ppermute | solution.py:66
  171.0 35.3 %collective-permute-start.14 = (bf16[384,512]{1,0:T(8,128)(2,1)S(1)}, bf16[384,512]{1,0:T(8,128)(2,1)S(1)}, u32[]{:S(2)}, u32[]{:S(2)}) collective-permute-start(bf16[384,512]{1,0:T(8,128)(2,1)S(1)} %convolution_convert_fusion), channel_id=1, source_target_pairs={{0,4},{1,5},{2,6},{3,7},{4,0},{5,1},{6,2},{7,3},{8,12},{9,13},{10,... | collective-permute-start | bytes 1179656 | tf_op jit(solution)/shard_map/ppermute | solution.py:66
  171.0 35.3 %collective-permute-start.15 = (bf16[384,512]{1,0:T(8,128)(2,1)S(1)}, bf16[384,512]{1,0:T(8,128)(2,1)S(1)}, u32[]{:S(2)}, u32[]{:S(2)}) collective-permute-start(bf16[384,512]{1,0:T(8,128)(2,1)S(1)} %convolution_convert_fusion), channel_id=1, source_target_pairs={{0,3},{1,4},{2,5},{3,6},{4,7},{5,0},{6,1},{7,2},{8,11},{9,12},{10,... | collective-permute-start | bytes 1179656 | tf_op jit(solution)/shard_map/ppermute | solution.py:66
  181.4 25.0 %collective-permute-start.16 = (bf16[384,512]{1,0:T(8,128)(2,1)S(1)}, bf16[384,512]{1,0:T(8,128)(2,1)S(1)}, u32[]{:S(2)}, u32[]{:S(2)}) collective-permute-start(bf16[384,512]{1,0:T(8,128)(2,1)S(1)} %convolution_convert_fusion), channel_id=1, source_target_pairs={{0,2},{1,3},{2,4},{3,5},{4,6},{5,7},{6,0},{7,1},{8,10},{9,11},{10,... | collective-permute-start | bytes 1179656 | tf_op jit(solution)/shard_map/ppermute | solution.py:66
  184.6 26.4 %collective-permute-start.17 = (bf16[384,512]{1,0:T(8,128)(2,1)S(1)}, bf16[384,512]{1,0:T(8,128)(2,1)S(1)}, u32[]{:S(2)}, u32[]{:S(2)}) collective-permute-start(bf16[384,512]{1,0:T(8,128)(2,1)S(1)} %convolution_convert_fusion), channel_id=1, source_target_pairs={{0,1},{1,2},{2,3},{3,4},{4,5},{5,6},{6,7},{7,0},{8,9},{9,10},{10,1... | collective-permute-start | bytes 1179656 | tf_op jit(solution)/shard_map/ppermute | solution.py:66
  211.4 3.4 %slice-start = ((bf16[2,8,384,512]{3,2,1,0:T(8,128)(2,1)}), bf16[1,8,384,512]{3,2,1,0:T(8,128)(2,1)S(1)}, s32[]{:S(2)}) async-start(bf16[2,8,384,512]{3,2,1,0:T(8,128)(2,1)} %hist_ref.1), calls=%async_computation | async-start | bytes 6291456 | tf_op jit(solution)/shard_map/slice | solution.py:104

commit v14 on v12

--- a/solution.py
+++ b/solution.py
@@ -100,13 +100,14 @@
     block = jnp.dot(inverse, residual, preferred_element_type=jnp.float32).astype(jnp.bfloat16)
     block, late = lax.optimization_barrier((block, late))
     carried = jnp.concatenate([early, late], axis=0)
+    shifted_history = jnp.concatenate([carried[None], history[:-1]], axis=0)
 
     gathered = [block] + [shifted_by(block, "lag", k) for k in range(1, n_lag)]
     ordered = jnp.stack(gathered[::-1])
     traction = jnp.roll(ordered, me + 1, axis=0)
 
     newest = jnp.where(me == 0, traction, carried)
-    shifted_history = jnp.concatenate([newest[None], history[:-1]], axis=0)
+    shifted_history = lax.dynamic_update_slice(shifted_history, newest[None], (0, 0, 0, 0))
     return (traction, shifted_history)
 
 

time: 220 us -> 232 us (1.055)
  starting transfers between devices: 82.6 us -> 92.6 us
  local copies, waits for them, and re-layouts: 12.9 us -> 18.7 us
  other arithmetic: 7.77 us -> 4.49 us
    ppermute x16, starting transfers between devices: 75.7 us -> 85.6 us  [shifted_by(): lax.ppermute(array, axis, [(i, (i + by) % count) for i in range(count)])]
    ppermute x16, waiting for transfers between devices: 59.9 us -> 64.5 us  [shifted_by(): lax.ppermute(array, axis, [(i, (i + by) % count) for i in range(count)])]
    unnamed x28 -> x31, local copies, waits for them, and re-layouts: 1.28 us -> 5.65 us
    broadcast_in_dim x1 -> x0, other arithmetic: 3.41 us -> none  [shards(): shifted_history = jnp.concatenate([newest[None], history[:-1]], axis=0)]
    dynamic_update_slice x0 -> x1, other arithmetic: none -> 2.77 us  [shards(): lax.dynamic_update_slice(shifted_history, newest[None], (0, 0, 0, 0))]
    concatenate x1, other arithmetic: 3.24 us -> 0.58 us  [shards(): shifted_history = jnp.concatenate([carried[None], history[:-1]], axis=0)]
    ppermute x2, waiting for transfers between devices: 33.5 us -> 30.9 us  [passed_along(): return lax.ppermute(array, axis, pairs)]
  transfers between devices with their start and end apart: 18 -> 18, of which waited for: 9 -> 6; matrix products, arithmetic and copies ran while one was open for 4% -> 5% of each run, Pallas kernels for 8% -> 7%
where the time goes in v14:
time: 232 us
  waiting for transfers between devices  95.5 us (41%)
  starting transfers between devices  92.6 us (40%)
  local copies, waits for them, and re-layouts  18.7 us (8%)
  Pallas kernels  17.1 us (7%)
  other arithmetic  4.49 us (2%)
  matrix products  2.63 us (1%)
    ppermute x16, starting transfers between devices, shifted_by(): lax.ppermute(array, axis, [(i, (i + by) % count) for i in range(count)])  85.6 us
    ppermute x16, waiting for transfers between devices, shifted_by(): lax.ppermute(array, axis, [(i, (i + by) % count) for i in range(count)])  64.5 us
    ppermute x2, waiting for transfers between devices, passed_along(): return lax.ppermute(array, axis, pairs)  30.9 us
    pallas_call x1, Pallas kernels, lag_partial(): pl.pallas_call(term_kernel, grid_spec=grid_spec, out_shape=jax.ShapeDtype...  17.1 us
    ppermute x2, starting transfers between devices, passed_along(): return lax.ppermute(array, axis, pairs)  6.95 us
    slice x1, local copies, waits for them, and re-layouts, shards(): right = shifted_by(history[:, :EDGE], 'tile', -1)  6.6 us
    unnamed x31, local copies, waits for them, and re-layouts  5.65 us
  transfers between devices with their start and end apart: 18, of which 6 were waited for; matrix products, arithmetic and copies ran while one was open for 5% of the time, Pallas kernels for 7%

profile of v14, /device:TPU:14, one launch (start us, length us, event | category | flops | bytes accessed | tf_op | source)
XLA Modules:
  0.0 231.9 jit_solution(326910180469106277)
XLA Ops:
  0.6 0.0 copy-start
  0.6 0.0 copy-start.1
  0.7 6.6 %fusion.14 = (bf16[2,4,384,512]{3,2,1,0:T(8,128)(2,1)}, bf16[2,4,384,512]{3,2,1,0:T(8,128)(2,1)}) fusion(bf16[2,8,384,512]{3,2,1,0:T(8,128)(2,1)} %refs_10_.1), kind=kLoop, calls=%fused_computation.47 | loop fusion | bytes 12582912 | tf_op jit(solution)/shard_map/slice | solution.py:85
  7.3 0.0 copy-start.5
  7.3 0.0 copy-start.6
  7.3 0.3 collective-permute-start.1
  7.5 0.2 collective-permute-start
  7.8 0.0 copy-done.1
  7.8 2.0 slice_bitcast_fusion
  9.8 3.5 %collective-permute-start.2 = (bf16[4,384,512]{2,1,0:T(8,128)(2,1)}, bf16[4,384,512]{2,1,0:T(8,128)(2,1)}, u32[]{:S(2)}, u32[]{:S(2)}) collective-permute-start(bf16[4,384,512]{2,1,0:T(8,128)(2,1)} %get-tuple-element.16), channel_id=1, source_target_pairs={{0,1},{1,2},{2,3},{3,4},{4,5},{5,6},{6,7},{8,9},{9,10},{10,11},{11... | collective-permute-start | bytes 4718600 | tf_op jit(solution)/shard_map/ppermute | solution.py:77
  13.4 0.0 copy-done.5
  13.4 0.1 copy.8
  13.5 0.0 copy-done.6
  13.5 0.5 broadcast_minimum_fusion.cnt_ref
  14.0 0.6 iota_add_fusion.src_ref
  14.6 30.9 %collective-permute-done.2 = bf16[4,384,512]{2,1,0:T(8,128)(2,1)} collective-permute-done((bf16[4,384,512]{2,1,0:T(8,128)(2,1)}, bf16[4,384,512]{2,1,0:T(8,128)(2,1)}, u32[]{:S(2)}, u32[]{:S(2)}) %collective-permute-start.2) | collective-permute-done | bytes 1572896 | tf_op jit(solution)/shard_map/ppermute | solution.py:77
  45.5 0.0 collective-permute-done.1.refs_2_.refs_5_.refs_8_.refs_11_
  45.5 0.0 collective-permute-done.refs_0_.refs_3_.refs_6_.refs_9_
  45.5 3.5 %collective-permute-start.10 = (bf16[4,384,512]{2,1,0:T(8,128)(2,1)}, bf16[4,384,512]{2,1,0:T(8,128)(2,1)}, u32[]{:S(2)}, u32[]{:S(2)}) collective-permute-start(bf16[4,384,512]{2,1,0:T(8,128)(2,1)} %get-tuple-element.10), channel_id=1, source_target_pairs={{0,1},{1,2},{2,3},{3,4},{4,5},{5,6},{6,7},{8,9},{9,10},{10,11},{11... | collective-permute-start | bytes 4718600 | tf_op jit(solution)/shard_map/ppermute | solution.py:77
  49.0 17.1 %shard_map.77 = bf16[8,384,512]{2,1,0:T(8,128)(2,1)} custom-call(s32[2,8,2]{2,1,0:T(8,128)} %iota_add_fusion.src_ref, s32[2,8]{1,0:T(2,128)} %broadcast_minimum_fusion.cnt_ref, bf16[2,8,2,384,384]{4,3,2,1,0:T(8,128)(2,1)} %a_ref.1, bf16[2,4,384,512]{3,2,1,0:T(8,128)(2,1)} %collective-permute-done.refs_0_.refs_3_.refs_6_.refs_9_, ...), custom_call_target="tpu_custom_call" | custom-call | flops 4831838208 | bytes 25165824 | tf_op jit(solution)/shard_map/pallas_call | solution.py:61
  66.1 2.9 %dynamic-slice_bitcast_fusion.6 = (bf16[384,512]{1,0:T(8,128)(2,1)S(1)}, bf16[384,512]{1,0:T(8,128)(2,1)S(1)}, bf16[384,512]{1,0:T(8,128)(2,1)S(1)}, bf16[384,51...) fusion(bf16[8,384,512]{2,1,0:T(8,128)(2,1)} %shard_map.77, ...), kind=kLoop, calls=%fused_computation.37 | loop fusion | bytes 5505052 | tf_op jit(solution)/shard_map/jit(dynamic_index_in_dim)/squeeze | solution.py:95
  69.0 30.6 %collective-permute-start.3 = (bf16[384,512]{1,0:T(8,128)(2,1)S(1)}, bf16[384,512]{1,0:T(8,128)(2,1)S(1)}, u32[]{:S(2)}, u32[]{:S(2)}) collective-permute-start(bf16[384,512]{1,0:T(8,128)(2,1)S(1)} %get-tuple-element.20), channel_id=1, source_target_pairs={{0,1},{1,2},{2,3},{3,4},{4,5},{5,6},{6,7},{7,0},{8,9},{9,10},{10,1... | collective-permute-start | bytes 1179656 | tf_op jit(solution)/shard_map/ppermute | solution.py:71
  99.6 0.0 collective-permute-start.9
  99.6 0.0 collective-permute-start.8
  99.7 10.3 %collective-permute-start.7 = (bf16[384,512]{1,0:T(8,128)(2,1)}, bf16[384,512]{1,0:T(8,128)(2,1)}, u32[]{:S(2)}, u32[]{:S(2)}) collective-permute-start(bf16[384,512]{1,0:T(8,128)(2,1)} %get-tuple-element.23), channel_id=1, source_target_pairs={{0,5},{1,6},{2,7},{3,0},{4,1},{5,2},{6,3},{7,4},{8,13},{9,14},{10,... | collective-permute-start | bytes 1179656 | tf_op jit(solution)/shard_map/ppermute | solution.py:71
  110.0 0.0 collective-permute-done.3
  110.0 15.1 %collective-permute-start.6 = (bf16[384,512]{1,0:T(8,128)(2,1)}, bf16[384,512]{1,0:T(8,128)(2,1)}, u32[]{:S(2)}, u32[]{:S(2)}) collective-permute-start(bf16[384,512]{1,0:T(8,128)(2,1)} %get-tuple-element.24), channel_id=1, source_target_pairs={{0,4},{1,5},{2,6},{3,7},{4,0},{5,1},{6,2},{7,3},{8,12},{9,13},{10,... | collective-permute-start | bytes 1179656 | tf_op jit(solution)/shard_map/ppermute | solution.py:71
  125.1 0.0 collective-permute-done.9
  125.2 0.0 copy-start.3
  125.2 11.6 %collective-permute-start.5 = (bf16[384,512]{1,0:T(8,128)(2,1)S(1)}, bf16[384,512]{1,0:T(8,128)(2,1)}, u32[]{:S(2)}, u32[]{:S(2)}) collective-permute-start(bf16[384,512]{1,0:T(8,128)(2,1)S(1)} %get-tuple-element.25), channel_id=1, source_target_pairs={{0,3},{1,4},{2,5},{3,6},{4,7},{5,0},{6,1},{7,2},{8,11},{9,12},{10,... | collective-permute-start | bytes 1179656 | tf_op jit(solution)/shard_map/ppermute | solution.py:71
  136.7 0.0 collective-permute-done.8
  136.7 0.0 copy-done.3
  136.7 0.0 copy-start.4
  136.7 0.8 copy-done.4
  137.5 0.0 collective-permute-start.4
  137.5 0.0 slice-start
  137.5 1.7 constant_dynamic-update-slice_fusion.1
  139.2 5.9 %collective-permute-done.7 = bf16[384,512]{1,0:T(8,128)(2,1)} collective-permute-done((bf16[384,512]{1,0:T(8,128)(2,1)}, bf16[384,512]{1,0:T(8,128)(2,1)}, u32[]{:S(2)}, u32[]{:S(2)}) %collective-permute-start.7) | collective-permute-done | bytes 393248 | tf_op jit(solution)/shard_map/ppermute | solution.py:71
  145.0 12.8 %collective-permute-done.6 = bf16[384,512]{1,0:T(8,128)(2,1)} collective-permute-done((bf16[384,512]{1,0:T(8,128)(2,1)}, bf16[384,512]{1,0:T(8,128)(2,1)}, u32[]{:S(2)}, u32[]{:S(2)}) %collective-permute-start.6) | collective-permute-done | bytes 393248 | tf_op jit(solution)/shard_map/ppermute | solution.py:71
  157.9 0.0 collective-permute-done.5
  157.9 0.0 collective-permute-done.4
  157.9 0.0 copy-done
  157.9 2.6 %convolution_convert_fusion = bf16[384,512]{1,0:T(8,128)(2,1)S(1)} fusion(bf16[384,512]{1,0:T(8,128)(2,1)} %copy-done.3, bf16[384,512]{1,0:T(8,128)(2,1)} %copy-done.4, bf16[384,512]{1,0:T(8,128)(2,1)} %collective-permute-done.7, bf16[384,512]{1,0:T(8,128)(2,1)} %collective-permute-done.6, bf16[384,512]{1,0:T(8,128)(2,1)} %collective-permute-done.5, ...), kind=kOutput, calls=%fused_computation.4 | convolution fusion | flops 154533888 | bytes 4621312 | tf_op jit(solution)/shard_map/dot_general | solution.py:100
  160.5 0.0 collective-permute-done.10
  160.6 0.1 collective-permute-start.17
  160.6 9.7 %collective-permute-start.16 = (bf16[384,512]{1,0:T(8,128)(2,1)S(1)}, bf16[384,512]{1,0:T(8,128)(2,1)S(1)}, u32[]{:S(2)}, u32[]{:S(2)}) collective-permute-start(bf16[384,512]{1,0:T(8,128)(2,1)S(1)} %convolution_convert_fusion), channel_id=1, source_target_pairs={{0,2},{1,3},{2,4},{3,5},{4,6},{5,7},{6,0},{7,1},{8,10},{9,11},{10,... | collective-permute-start | bytes 1179656 | tf_op jit(solution)/shard_map/ppermute | solution.py:71
  170.4 0.0 collective-permute-start.15
  170.4 1.8 collective-permute-start.12
  172.2 3.2 %collective-permute-start.11 = (bf16[384,512]{1,0:T(8,128)(2,1)S(1)}, bf16[384,512]{1,0:T(8,128)(2,1)S(1)}, u32[]{:S(2)}, u32[]{:S(2)}) collective-permute-start(bf16[384,512]{1,0:T(8,128)(2,1)S(1)} %convolution_convert_fusion), channel_id=1, source_target_pairs={{0,7},{1,0},{2,1},{3,2},{4,3},{5,4},{6,5},{7,6},{8,15},{9,8},{10,9... | collective-permute-start | bytes 1179656 | tf_op jit(solution)/shard_map/ppermute | solution.py:71
  175.4 1.5 constant_dynamic-update-slice_fusion
  176.9 0.0 slice-done
  176.9 0.6 pad_maximum_fusion
  177.5 28.6 %collective-permute-done.11 = bf16[384,512]{1,0:T(8,128)(2,1)S(1)} collective-permute-done((bf16[384,512]{1,0:T(8,128)(2,1)S(1)}, bf16[384,512]{1,0:T(8,128)(2,1)S(1)}, u32[]{:S(2)}, u32[]{:S(2)}) %collective-permute-start.11) | collective-permute-done | bytes 393248 | tf_op jit(solution)/shard_map/ppermute | solution.py:71
  206.1 0.0 collective-permute-start.13
  206.1 0.0 collective-permute-done.12
  206.1 2.6 %collective-permute-start.14 = (bf16[384,512]{1,0:T(8,128)(2,1)S(1)}, bf16[384,512]{1,0:T(8,128)(2,1)S(1)}, u32[]{:S(2)}, u32[]{:S(2)}) collective-permute-start(bf16[384,512]{1,0:T(8,128)(2,1)S(1)} %convolution_convert_fusion), channel_id=1, source_target_pairs={{0,4},{1,5},{2,6},{3,7},{4,0},{5,1},{6,2},{7,3},{8,12},{9,13},{10,... | collective-permute-start | bytes 1179656 | tf_op jit(solution)/shard_map/ppermute | solution.py:71
  208.8 10.7 %collective-permute-done.13 = bf16[384,512]{1,0:T(8,128)(2,1)S(1)} collective-permute-done((bf16[384,512]{1,0:T(8,128)(2,1)S(1)}, bf16[384,512]{1,0:T(8,128)(2,1)S(1)}, u32[]{:S(2)}, u32[]{:S(2)}) %collective-permute-start.13) | collective-permute-done | bytes 393248 | tf_op jit(solution)/shard_map/ppermute | solution.py:71
  219.5 6.5 %collective-permute-done.14 = bf16[384,512]{1,0:T(8,128)(2,1)S(1)} collective-permute-done((bf16[384,512]{1,0:T(8,128)(2,1)S(1)}, bf16[384,512]{1,0:T(8,128)(2,1)S(1)}, u32[]{:S(2)}, u32[]{:S(2)}) %collective-permute-start.14) | collective-permute-done | bytes 393248 | tf_op jit(solution)/shard_map/ppermute | solution.py:71
  226.0 0.0 collective-permute-done.15
  226.0 0.0 collective-permute-done.16
  226.1 0.0 collective-permute-done.17
  226.5 2.8 %bitcast_dynamic-update-slice_fusion = (bf16[2,8,384,512]{3,2,1,0:T(8,128)(2,1)S(1)}, bf16[8,384,512]{2,1,0:T(8,128)(2,1)}) fusion(bf16[2,8,384,512]{3,2,1,0:T(8,128)(2,1)S(1)} %pad_maximum_fusion, bf16[8,384,512]{2,1,0:T(8,128)(2,1)S(1)} %constant_dynamic-update-slice_fusion, pred[]{:T(512)S(6)} %eq.14, ...), kind=kLoop, calls=%fused_computation.1 | loop fusion | flops 1572864 | bytes 12582917 | tf_op jit(solution)/shard_map/dynamic_update_slice | solution.py:110
  229.2 0.0 copy-start.2
  229.2 2.7 %copy-done.2 = bf16[2,8,384,512]{3,2,1,0:T(8,128)(2,1)} copy-done((bf16[2,8,384,512]{3,2,1,0:T(8,128)(2,1)}, bf16[2,8,384,512]{3,2,1,0:T(8,128)(2,1)S(1)}, u32[]{:S(2)}) %copy-start.2) | copy-done | bytes 6291480
  (16 shorter events, 0.4 us)
Async XLA Ops:
  0.6 157.3 %copy-start = (bf16[8,384,384]{2,1,0:T(8,128)(2,1)S(1)}, bf16[8,384,384]{2,1,0:T(8,128)(2,1)}, u32[]{:S(2)}) copy-start(bf16[8,384,384]{2,1,0:T(8,128)(2,1)} %param.8) | copy-start | bytes 7077892
  0.6 7.1 %copy-start.1 = (bf16[2,8,384,512]{3,2,1,0:T(8,128)(2,1)S(1)}, bf16[2,8,384,512]{3,2,1,0:T(8,128)(2,1)}, u32[]{:S(2)}) copy-start(bf16[2,8,384,512]{3,2,1,0:T(8,128)(2,1)} %refs_10_.1) | copy-start | bytes 18874372
  7.3 6.1 %copy-start.5 = (s32[2,8,2]{1,2,0:T(2,128)S(1)}, s32[2,8,2]{1,2,0:T(2,128)}, u32[]{:S(2)}) copy-start(s32[2,8,2]{1,2,0:T(2,128)} %param.10) | copy-start | bytes 388
  7.3 6.2 %copy-start.6 = (s32[2,8]{1,0:T(2,128)S(1)}, s32[2,8]{1,0:T(2,128)}, u32[]{:S(2)}) copy-start(s32[2,8]{1,0:T(2,128)} %param.11) | copy-start | bytes 196
  7.3 38.3 %collective-permute-start.1 = (bf16[2,4,384,512]{3,2,1,0:T(8,128)(2,1)}, bf16[2,4,384,512]{3,2,1,0:T(8,128)(2,1)}, u32[]{:S(2)}, u32[]{:S(2)}) collective-permute-start(bf16[2,4,384,512]{3,2,1,0:T(8,128)(2,1)} %get-tuple-element.18), channel_id=1, source_target_pairs={{0,120},{8,0},{16,8},{24,16},{32,24},{40,32},{48,40},{56,48},{64,5... | collective-permute-start | bytes 9437192 | tf_op jit(solution)/shard_map/ppermute | solution.py:71
  7.5 38.0 %collective-permute-start = (bf16[2,4,384,512]{3,2,1,0:T(8,128)(2,1)}, bf16[2,4,384,512]{3,2,1,0:T(8,128)(2,1)}, u32[]{:S(2)}, u32[]{:S(2)}) collective-permute-start(bf16[2,4,384,512]{3,2,1,0:T(8,128)(2,1)} %get-tuple-element.19), channel_id=1, source_target_pairs={{0,8},{8,16},{16,24},{24,32},{32,40},{40,48},{48,56},{56,64},{64,7... | collective-permute-start | bytes 9437192 | tf_op jit(solution)/shard_map/ppermute | solution.py:71
  9.8 35.7 %collective-permute-start.2 = (bf16[4,384,512]{2,1,0:T(8,128)(2,1)}, bf16[4,384,512]{2,1,0:T(8,128)(2,1)}, u32[]{:S(2)}, u32[]{:S(2)}) collective-permute-start(bf16[4,384,512]{2,1,0:T(8,128)(2,1)} %get-tuple-element.16), channel_id=1, source_target_pairs={{0,1},{1,2},{2,3},{3,4},{4,5},{5,6},{6,7},{8,9},{9,10},{10,11},{11... | collective-permute-start | bytes 4718600 | tf_op jit(solution)/shard_map/ppermute | solution.py:77
  45.5 115.0 %collective-permute-start.10 = (bf16[4,384,512]{2,1,0:T(8,128)(2,1)}, bf16[4,384,512]{2,1,0:T(8,128)(2,1)}, u32[]{:S(2)}, u32[]{:S(2)}) collective-permute-start(bf16[4,384,512]{2,1,0:T(8,128)(2,1)} %get-tuple-element.10), channel_id=1, source_target_pairs={{0,1},{1,2},{2,3},{3,4},{4,5},{5,6},{6,7},{8,9},{9,10},{10,11},{11... | collective-permute-start | bytes 4718600 | tf_op jit(solution)/shard_map/ppermute | solution.py:77
  69.0 41.0 %collective-permute-start.3 = (bf16[384,512]{1,0:T(8,128)(2,1)S(1)}, bf16[384,512]{1,0:T(8,128)(2,1)S(1)}, u32[]{:S(2)}, u32[]{:S(2)}) collective-permute-start(bf16[384,512]{1,0:T(8,128)(2,1)S(1)} %get-tuple-element.20), channel_id=1, source_target_pairs={{0,1},{1,2},{2,3},{3,4},{4,5},{5,6},{6,7},{7,0},{8,9},{9,10},{10,1... | collective-permute-start | bytes 1179656 | tf_op jit(solution)/shard_map/ppermute | solution.py:71
  99.6 25.5 %collective-permute-start.9 = (bf16[384,512]{1,0:T(8,128)(2,1)S(1)}, bf16[384,512]{1,0:T(8,128)(2,1)S(1)}, u32[]{:S(2)}, u32[]{:S(2)}) collective-permute-start(bf16[384,512]{1,0:T(8,128)(2,1)S(1)} %get-tuple-element.21), channel_id=1, source_target_pairs={{0,7},{1,0},{2,1},{3,2},{4,3},{5,4},{6,5},{7,6},{8,15},{9,8},{10,9... | collective-permute-start | bytes 1179656 | tf_op jit(solution)/shard_map/ppermute | solution.py:71
  99.6 37.1 %collective-permute-start.8 = (bf16[384,512]{1,0:T(8,128)(2,1)S(1)}, bf16[384,512]{1,0:T(8,128)(2,1)S(1)}, u32[]{:S(2)}, u32[]{:S(2)}) collective-permute-start(bf16[384,512]{1,0:T(8,128)(2,1)S(1)} %get-tuple-element.22), channel_id=1, source_target_pairs={{0,6},{1,7},{2,0},{3,1},{4,2},{5,3},{6,4},{7,5},{8,14},{9,15},{10,... | collective-permute-start | bytes 1179656 | tf_op jit(solution)/shard_map/ppermute | solution.py:71
  99.7 45.4 %collective-permute-start.7 = (bf16[384,512]{1,0:T(8,128)(2,1)}, bf16[384,512]{1,0:T(8,128)(2,1)}, u32[]{:S(2)}, u32[]{:S(2)}) collective-permute-start(bf16[384,512]{1,0:T(8,128)(2,1)} %get-tuple-element.23), channel_id=1, source_target_pairs={{0,5},{1,6},{2,7},{3,0},{4,1},{5,2},{6,3},{7,4},{8,13},{9,14},{10,... | collective-permute-start | bytes 1179656 | tf_op jit(solution)/shard_map/ppermute | solution.py:71
  110.0 47.9 %collective-permute-start.6 = (bf16[384,512]{1,0:T(8,128)(2,1)}, bf16[384,512]{1,0:T(8,128)(2,1)}, u32[]{:S(2)}, u32[]{:S(2)}) collective-permute-start(bf16[384,512]{1,0:T(8,128)(2,1)} %get-tuple-element.24), channel_id=1, source_target_pairs={{0,4},{1,5},{2,6},{3,7},{4,0},{5,1},{6,2},{7,3},{8,12},{9,13},{10,... | collective-permute-start | bytes 1179656 | tf_op jit(solution)/shard_map/ppermute | solution.py:71
  125.2 11.6 %copy-start.3 = (bf16[384,512]{1,0:T(8,128)(2,1)}, bf16[384,512]{1,0:T(8,128)(2,1)S(1)}, u32[]{:S(2)}) copy-start(bf16[384,512]{1,0:T(8,128)(2,1)S(1)} %collective-permute-done.9) | copy-start | bytes 1179652
  125.2 32.7 %collective-permute-start.5 = (bf16[384,512]{1,0:T(8,128)(2,1)S(1)}, bf16[384,512]{1,0:T(8,128)(2,1)}, u32[]{:S(2)}, u32[]{:S(2)}) collective-permute-start(bf16[384,512]{1,0:T(8,128)(2,1)S(1)} %get-tuple-element.25), channel_id=1, source_target_pairs={{0,3},{1,4},{2,5},{3,6},{4,7},{5,0},{6,1},{7,2},{8,11},{9,12},{10,... | collective-permute-start | bytes 1179656 | tf_op jit(solution)/shard_map/ppermute | solution.py:71
  136.7 0.8 copy-start.4
  137.5 20.4 %collective-permute-start.4 = (bf16[384,512]{1,0:T(8,128)(2,1)S(1)}, bf16[384,512]{1,0:T(8,128)(2,1)}, u32[]{:S(2)}, u32[]{:S(2)}) collective-permute-start(bf16[384,512]{1,0:T(8,128)(2,1)S(1)} %get-tuple-element.26), channel_id=1, source_target_pairs={{0,2},{1,3},{2,4},{3,5},{4,6},{5,7},{6,0},{7,1},{8,10},{9,11},{10,... | collective-permute-start | bytes 1179656 | tf_op jit(solution)/shard_map/ppermute | solution.py:71
  137.5 39.4 %slice-start = ((bf16[2,8,384,512]{3,2,1,0:T(8,128)(2,1)}), bf16[1,8,384,512]{3,2,1,0:T(8,128)(2,1)S(1)}, s32[]{:S(2)}) async-start(bf16[2,8,384,512]{3,2,1,0:T(8,128)(2,1)} %refs_10_.1), calls=%async_computation | async-start | bytes 6291456 | tf_op jit(solution)/shard_map/slice | solution.py:103
  160.6 65.5 %collective-permute-start.17 = (bf16[384,512]{1,0:T(8,128)(2,1)S(1)}, bf16[384,512]{1,0:T(8,128)(2,1)S(1)}, u32[]{:S(2)}, u32[]{:S(2)}) collective-permute-start(bf16[384,512]{1,0:T(8,128)(2,1)S(1)} %convolution_convert_fusion), channel_id=1, source_target_pairs={{0,1},{1,2},{2,3},{3,4},{4,5},{5,6},{6,7},{7,0},{8,9},{9,10},{10,1... | collective-permute-start | bytes 1179656 | tf_op jit(solution)/shard_map/ppermute | solution.py:71
  160.6 65.4 %collective-permute-start.16 = (bf16[384,512]{1,0:T(8,128)(2,1)S(1)}, bf16[384,512]{1,0:T(8,128)(2,1)S(1)}, u32[]{:S(2)}, u32[]{:S(2)}) collective-permute-start(bf16[384,512]{1,0:T(8,128)(2,1)S(1)} %convolution_convert_fusion), channel_id=1, source_target_pairs={{0,2},{1,3},{2,4},{3,5},{4,6},{5,7},{6,0},{7,1},{8,10},{9,11},{10,... | collective-permute-start | bytes 1179656 | tf_op jit(solution)/shard_map/ppermute | solution.py:71
  170.4 55.6 %collective-permute-start.15 = (bf16[384,512]{1,0:T(8,128)(2,1)S(1)}, bf16[384,512]{1,0:T(8,128)(2,1)S(1)}, u32[]{:S(2)}, u32[]{:S(2)}) collective-permute-start(bf16[384,512]{1,0:T(8,128)(2,1)S(1)} %convolution_convert_fusion), channel_id=1, source_target_pairs={{0,3},{1,4},{2,5},{3,6},{4,7},{5,0},{6,1},{7,2},{8,11},{9,12},{10,... | collective-permute-start | bytes 1179656 | tf_op jit(solution)/shard_map/ppermute | solution.py:71
  170.4 35.7 %collective-permute-start.12 = (bf16[384,512]{1,0:T(8,128)(2,1)S(1)}, bf16[384,512]{1,0:T(8,128)(2,1)S(1)}, u32[]{:S(2)}, u32[]{:S(2)}) collective-permute-start(bf16[384,512]{1,0:T(8,128)(2,1)S(1)} %convolution_convert_fusion), channel_id=1, source_target_pairs={{0,6},{1,7},{2,0},{3,1},{4,2},{5,3},{6,4},{7,5},{8,14},{9,15},{10,... | collective-permute-start | bytes 1179656 | tf_op jit(solution)/shard_map/ppermute | solution.py:71
  172.2 33.9 %collective-permute-start.11 = (bf16[384,512]{1,0:T(8,128)(2,1)S(1)}, bf16[384,512]{1,0:T(8,128)(2,1)S(1)}, u32[]{:S(2)}, u32[]{:S(2)}) collective-permute-start(bf16[384,512]{1,0:T(8,128)(2,1)S(1)} %convolution_convert_fusion), channel_id=1, source_target_pairs={{0,7},{1,0},{2,1},{3,2},{4,3},{5,4},{6,5},{7,6},{8,15},{9,8},{10,9... | collective-permute-start | bytes 1179656 | tf_op jit(solution)/shard_map/ppermute | solution.py:71
  206.1 13.3 %collective-permute-start.13 = (bf16[384,512]{1,0:T(8,128)(2,1)S(1)}, bf16[384,512]{1,0:T(8,128)(2,1)S(1)}, u32[]{:S(2)}, u32[]{:S(2)}) collective-permute-start(bf16[384,512]{1,0:T(8,128)(2,1)S(1)} %convolution_convert_fusion), channel_id=1, source_target_pairs={{0,5},{1,6},{2,7},{3,0},{4,1},{5,2},{6,3},{7,4},{8,13},{9,14},{10,... | collective-permute-start | bytes 1179656 | tf_op jit(solution)/shard_map/ppermute | solution.py:71
  206.1 19.8 %collective-permute-start.14 = (bf16[384,512]{1,0:T(8,128)(2,1)S(1)}, bf16[384,512]{1,0:T(8,128)(2,1)S(1)}, u32[]{:S(2)}, u32[]{:S(2)}) collective-permute-start(bf16[384,512]{1,0:T(8,128)(2,1)S(1)} %convolution_convert_fusion), channel_id=1, source_target_pairs={{0,4},{1,5},{2,6},{3,7},{4,0},{5,1},{6,2},{7,3},{8,12},{9,13},{10,... | collective-permute-start | bytes 1179656 | tf_op jit(solution)/shard_map/ppermute | solution.py:71
  229.2 2.7 %copy-start.2 = (bf16[2,8,384,512]{3,2,1,0:T(8,128)(2,1)}, bf16[2,8,384,512]{3,2,1,0:T(8,128)(2,1)S(1)}, u32[]{:S(2)}) copy-start(bf16[2,8,384,512]{3,2,1,0:T(8,128)(2,1)S(1)} %get-tuple-element.14) | copy-start | bytes 18874372

commit v15 on v12

--- a/solution.py
+++ b/solution.py
@@ -79,11 +79,9 @@
 
 def shards(history, lag_blocks, self_inverse, excitation, pattern, live_counts):
     blocks_here = history.shape[1]
-    half = blocks_here // 2
-    early = passed_along(history[-1, :half], "lag", 1)
     left = shifted_by(history[:, blocks_here - EDGE:], "tile", 1)
     right = shifted_by(history[:, :EDGE], "tile", -1)
-    oldest, left, right, early = lax.optimization_barrier((history[-1, half:], left, right, early))
+    oldest, left, right = lax.optimization_barrier((history[-1], left, right))
     late = passed_along(oldest, "lag", 1)
     live = jnp.minimum(live_counts, lag_blocks.shape[2])
     partial = lag_partial(history, left, right, lag_blocks, pattern, live)
@@ -99,7 +97,7 @@
     inverse = lax.dynamic_index_in_dim(self_inverse, me, 0, keepdims=False)
     block = jnp.dot(inverse, residual, preferred_element_type=jnp.float32).astype(jnp.bfloat16)
     block, late = lax.optimization_barrier((block, late))
-    carried = jnp.concatenate([early, late], axis=0)
+    carried = late
 
     gathered = [block] + [shifted_by(block, "lag", k) for k in range(1, n_lag)]
     ordered = jnp.stack(gathered[::-1])

time: 220 us -> 221 us (level)
  waiting for transfers between devices: 93.4 us -> 149 us
  starting transfers between devices: 82.6 us -> 29.2 us
    ppermute x16, waiting for transfers between devices: 59.9 us -> 149 us  [shifted_by(): lax.ppermute(array, axis, [(i, (i + by) % count) for i in range(count)])]
    ppermute x16, starting transfers between devices: 75.7 us -> 25.7 us  [shifted_by(): lax.ppermute(array, axis, [(i, (i + by) % count) for i in range(count)])]
    ppermute x2 -> x1, waiting for transfers between devices: 33.5 us -> 0.01 us  [passed_along(): return lax.ppermute(array, axis, pairs)]
    ppermute x2 -> x1, starting transfers between devices: 6.95 us -> 3.47 us  [passed_along(): return lax.ppermute(array, axis, pairs)]
    slice x2 -> x1, local copies, waits for them, and re-layouts: 0.01 us -> 3.34 us  [shards(): shifted_history = jnp.concatenate([newest[None], history[:-1]], axis=0)]
    slice x1, local copies, waits for them, and re-layouts: 6.6 us -> 3.64 us  [shards(): right = shifted_by(history[:, :EDGE], 'tile', -1)]
  transfers between devices with their start and end apart: 18 -> 17, of which waited for: 9 -> 9; matrix products, arithmetic and copies ran while one was open for 4% -> 5% of each run, Pallas kernels for 8% -> 8%
where the time goes in v15:
time: 221 us; the launch traced here: 220 us
  waiting for transfers between devices  149 us (67%)
  starting transfers between devices  29.2 us (13%)
  Pallas kernels  18.6 us (8%)
  local copies, waits for them, and re-layouts  11.8 us (5%)
  other arithmetic  8.54 us (4%)
  matrix products  2.64 us (1%)
    ppermute x16, waiting for transfers between devices, shifted_by(): lax.ppermute(array, axis, [(i, (i + by) % count) for i in range(count)])  149 us
    ppermute x16, starting transfers between devices, shifted_by(): lax.ppermute(array, axis, [(i, (i + by) % count) for i in range(count)])  25.7 us
    pallas_call x1, Pallas kernels, lag_partial(): pl.pallas_call(term_kernel, grid_spec=grid_spec, out_shape=jax.ShapeDtype...  18.6 us
  transfers between devices with their start and end apart: 17, of which 9 were waited for; matrix products, arithmetic and copies ran while one was open for 5% of the time, Pallas kernels for 8%

profile of v15, /device:TPU:14, one launch (start us, length us, event | category | flops | bytes accessed | tf_op | source)
XLA Modules:
  0.0 220.4 jit_solution(6213385129848792135)
XLA Ops:
  0.6 0.0 copy-start
  0.6 0.0 copy-start.1
  0.7 3.6 %fusion.15 = (bf16[2,4,384,512]{3,2,1,0:T(8,128)(2,1)S(1)}, bf16[2,4,384,512]{3,2,1,0:T(8,128)(2,1)S(1)}) fusion(bf16[2,8,384,512]{3,2,1,0:T(8,128)(2,1)} %refs_10_.1), kind=kLoop, calls=%fused_computation.45 | loop fusion | bytes 12582912 | tf_op jit(solution)/shard_map/slice | solution.py:83
  4.3 0.3 collective-permute-start.1
  4.6 0.0 copy-start.5
  4.6 0.0 copy-start.6
  4.6 0.2 collective-permute-start
  4.9 0.5 copy-done.1
  5.4 3.3 %fusion.14 = (bf16[1,8,384,512]{3,2,1,0:T(8,128)(2,1)}, bf16[8,384,512]{2,1,0:T(8,128)(2,1)}) fusion(bf16[2,8,384,512]{3,2,1,0:T(8,128)(2,1)S(1)} %copy-done.1), kind=kLoop, calls=%fused_computation.44 | loop fusion | bytes 12582912 | tf_op jit(solution)/shard_map/slice | solution.py:107
  8.8 30.6 %collective-permute-done.1.refs_2_.refs_5_.refs_8_.refs_11_ = bf16[2,4,384,512]{3,2,1,0:T(8,128)(2,1)} collective-permute-done((bf16[2,4,384,512]{3,2,1,0:T(8,128)(2,1)S(1)}, bf16[2,4,384,512]{3,2,1,0:T(8,128)(2,1)}, u32[]{:S(2)}, u32[]{:S(2)}) %collective-permute-start.1) | collective-permute-done | bytes 3145760 | tf_op jit(solution)/shard_map/ppermute | solution.py:71
  39.4 2.0 collective-permute-done.refs_0_.refs_3_.refs_6_.refs_9_
  41.4 3.5 %collective-permute-start.9 = (bf16[8,384,512]{2,1,0:T(8,128)(2,1)}, bf16[8,384,512]{2,1,0:T(8,128)(2,1)}, u32[]{:S(2)}, u32[]{:S(2)}) collective-permute-start(bf16[8,384,512]{2,1,0:T(8,128)(2,1)} %get-tuple-element.9), channel_id=1, source_target_pairs={{0,1},{1,2},{2,3},{3,4},{4,5},{5,6},{6,7},{8,9},{9,10},{10,11},{11... | collective-permute-start | bytes 9437192 | tf_op jit(solution)/shard_map/ppermute | solution.py:77
  45.0 0.0 copy-done.5
  45.0 0.1 copy.8
  45.1 0.0 copy-done.6
  45.1 0.6 broadcast_minimum_fusion.cnt_ref
  45.7 0.6 iota_add_fusion.src_ref
  46.3 18.6 %shard_map.77 = bf16[8,384,512]{2,1,0:T(8,128)(2,1)} custom-call(s32[2,8,2]{2,1,0:T(8,128)} %iota_add_fusion.src_ref, s32[2,8]{1,0:T(2,128)} %broadcast_minimum_fusion.cnt_ref, bf16[2,8,2,384,384]{4,3,2,1,0:T(8,128)(2,1)} %a_ref.1, bf16[2,4,384,512]{3,2,1,0:T(8,128)(2,1)} %collective-permute-done.refs_0_.refs_3_.refs_6_.refs_9_, ...), custom_call_target="tpu_custom_call" | custom-call | flops 4831838208 | bytes 25165824 | tf_op jit(solution)/shard_map/pallas_call | solution.py:61
  64.9 2.9 %dynamic-slice_bitcast_fusion.6 = (bf16[384,512]{1,0:T(8,128)(2,1)S(1)}, bf16[384,512]{1,0:T(8,128)(2,1)S(1)}, bf16[384,512]{1,0:T(8,128)(2,1)S(1)}, bf16[384,51...) fusion(bf16[8,384,512]{2,1,0:T(8,128)(2,1)} %shard_map.77, ...), kind=kLoop, calls=%fused_computation.36 | loop fusion | bytes 5505052 | tf_op jit(solution)/shard_map/jit(dynamic_index_in_dim)/squeeze | solution.py:93
  67.8 1.9 collective-permute-start.2
  69.7 0.1 collective-permute-start.8
  69.9 2.4 %collective-permute-start.7 = (bf16[384,512]{1,0:T(8,128)(2,1)S(1)}, bf16[384,512]{1,0:T(8,128)(2,1)S(1)}, u32[]{:S(2)}, u32[]{:S(2)}) collective-permute-start(bf16[384,512]{1,0:T(8,128)(2,1)S(1)} %get-tuple-element.20), channel_id=1, source_target_pairs={{0,6},{1,7},{2,0},{3,1},{4,2},{5,3},{6,4},{7,5},{8,14},{9,15},{10,... | collective-permute-start | bytes 1179656 | tf_op jit(solution)/shard_map/ppermute | solution.py:71
  72.3 2.7 %collective-permute-start.6 = (bf16[384,512]{1,0:T(8,128)(2,1)}, bf16[384,512]{1,0:T(8,128)(2,1)}, u32[]{:S(2)}, u32[]{:S(2)}) collective-permute-start(bf16[384,512]{1,0:T(8,128)(2,1)} %get-tuple-element.21), channel_id=1, source_target_pairs={{0,5},{1,6},{2,7},{3,0},{4,1},{5,2},{6,3},{7,4},{8,13},{9,14},{10,... | collective-permute-start | bytes 1179656 | tf_op jit(solution)/shard_map/ppermute | solution.py:71
  74.9 45.8 %collective-permute-done.2 = bf16[384,512]{1,0:T(8,128)(2,1)S(1)} collective-permute-done((bf16[384,512]{1,0:T(8,128)(2,1)S(1)}, bf16[384,512]{1,0:T(8,128)(2,1)S(1)}, u32[]{:S(2)}, u32[]{:S(2)}) %collective-permute-start.2) | collective-permute-done | bytes 393248 | tf_op jit(solution)/shard_map/ppermute | solution.py:71
  120.7 1.9 collective-permute-start.5
  122.7 0.0 collective-permute-done.8
  122.7 0.0 copy-start.3
  122.7 2.2 collective-permute-start.4
  124.8 0.0 collective-permute-done.7
  124.8 0.0 copy-done.3
  124.8 0.0 copy-start.4
  124.8 0.8 copy-done.4
  125.6 0.9 collective-permute-start.3
  126.5 20.7 %collective-permute-done.6 = bf16[384,512]{1,0:T(8,128)(2,1)} collective-permute-done((bf16[384,512]{1,0:T(8,128)(2,1)}, bf16[384,512]{1,0:T(8,128)(2,1)}, u32[]{:S(2)}, u32[]{:S(2)}) %collective-permute-start.6) | collective-permute-done | bytes 393248 | tf_op jit(solution)/shard_map/ppermute | solution.py:71
  147.2 7.7 %collective-permute-done.5 = bf16[384,512]{1,0:T(8,128)(2,1)} collective-permute-done((bf16[384,512]{1,0:T(8,128)(2,1)}, bf16[384,512]{1,0:T(8,128)(2,1)}, u32[]{:S(2)}, u32[]{:S(2)}) %collective-permute-start.5) | collective-permute-done | bytes 393248 | tf_op jit(solution)/shard_map/ppermute | solution.py:71
  154.8 0.0 collective-permute-done.4
  154.8 0.0 collective-permute-done.3
  154.8 0.0 copy-done
  154.8 2.6 %convolution_convert_fusion = bf16[384,512]{1,0:T(8,128)(2,1)S(1)} fusion(bf16[384,512]{1,0:T(8,128)(2,1)} %copy-done.3, bf16[384,512]{1,0:T(8,128)(2,1)} %copy-done.4, bf16[384,512]{1,0:T(8,128)(2,1)} %collective-permute-done.6, bf16[384,512]{1,0:T(8,128)(2,1)} %collective-permute-done.5, bf16[384,512]{1,0:T(8,128)(2,1)} %collective-permute-done.4, ...), kind=kOutput, calls=%fused_computation.3 | convolution fusion | flops 154533888 | bytes 4621312 | tf_op jit(solution)/shard_map/dot_general | solution.py:98
  157.5 0.0 collective-permute-done.9
  157.5 0.1 collective-permute-start.10
  157.6 4.6 %collective-permute-start.11 = (bf16[384,512]{1,0:T(8,128)(2,1)S(1)}, bf16[384,512]{1,0:T(8,128)(2,1)S(1)}, u32[]{:S(2)}, u32[]{:S(2)}) collective-permute-start(bf16[384,512]{1,0:T(8,128)(2,1)S(1)} %convolution_convert_fusion), channel_id=1, source_target_pairs={{0,6},{1,7},{2,0},{3,1},{4,2},{5,3},{6,4},{7,5},{8,14},{9,15},{10,... | collective-permute-start | bytes 1179656 | tf_op jit(solution)/shard_map/ppermute | solution.py:71
  162.1 0.0 collective-permute-start.16
  162.1 3.3 %collective-permute-start.15 = (bf16[384,512]{1,0:T(8,128)(2,1)S(1)}, bf16[384,512]{1,0:T(8,128)(2,1)S(1)}, u32[]{:S(2)}, u32[]{:S(2)}) collective-permute-start(bf16[384,512]{1,0:T(8,128)(2,1)S(1)} %convolution_convert_fusion), channel_id=1, source_target_pairs={{0,2},{1,3},{2,4},{3,5},{4,6},{5,7},{6,0},{7,1},{8,10},{9,11},{10,... | collective-permute-start | bytes 1179656 | tf_op jit(solution)/shard_map/ppermute | solution.py:71
  165.4 0.3 collective-permute-start.14
  165.7 2.9 %collective-permute-done.10 = bf16[384,512]{1,0:T(8,128)(2,1)S(1)} collective-permute-done((bf16[384,512]{1,0:T(8,128)(2,1)S(1)}, bf16[384,512]{1,0:T(8,128)(2,1)S(1)}, u32[]{:S(2)}, u32[]{:S(2)}) %collective-permute-start.10) | collective-permute-done | bytes 393248 | tf_op jit(solution)/shard_map/ppermute | solution.py:71
  168.7 4.0 %collective-permute-start.12 = (bf16[384,512]{1,0:T(8,128)(2,1)S(1)}, bf16[384,512]{1,0:T(8,128)(2,1)S(1)}, u32[]{:S(2)}, u32[]{:S(2)}) collective-permute-start(bf16[384,512]{1,0:T(8,128)(2,1)S(1)} %convolution_convert_fusion), channel_id=1, source_target_pairs={{0,5},{1,6},{2,7},{3,0},{4,1},{5,2},{6,3},{7,4},{8,13},{9,14},{10,... | collective-permute-start | bytes 1179656 | tf_op jit(solution)/shard_map/ppermute | solution.py:71
  172.7 7.6 %collective-permute-done.11 = bf16[384,512]{1,0:T(8,128)(2,1)S(1)} collective-permute-done((bf16[384,512]{1,0:T(8,128)(2,1)S(1)}, bf16[384,512]{1,0:T(8,128)(2,1)S(1)}, u32[]{:S(2)}, u32[]{:S(2)}) %collective-permute-start.11) | collective-permute-done | bytes 393248 | tf_op jit(solution)/shard_map/ppermute | solution.py:71
  180.3 0.9 collective-permute-start.13
  181.2 22.3 %collective-permute-done.12 = bf16[384,512]{1,0:T(8,128)(2,1)S(1)} collective-permute-done((bf16[384,512]{1,0:T(8,128)(2,1)S(1)}, bf16[384,512]{1,0:T(8,128)(2,1)S(1)}, u32[]{:S(2)}, u32[]{:S(2)}) %collective-permute-start.12) | collective-permute-done | bytes 393248 | tf_op jit(solution)/shard_map/ppermute | solution.py:71
  203.6 8.9 %collective-permute-done.13 = bf16[384,512]{1,0:T(8,128)(2,1)S(1)} collective-permute-done((bf16[384,512]{1,0:T(8,128)(2,1)S(1)}, bf16[384,512]{1,0:T(8,128)(2,1)S(1)}, u32[]{:S(2)}, u32[]{:S(2)}) %collective-permute-start.13) | collective-permute-done | bytes 393248 | tf_op jit(solution)/shard_map/ppermute | solution.py:71
  212.5 0.0 collective-permute-done.14
  212.6 0.0 collective-permute-done.15
  212.6 0.0 collective-permute-done.16
  213.0 0.0 copy-start.2
  213.0 4.1 %select_bitcast_fusion = (bf16[1,8,384,512]{3,2,1,0:T(8,128)(2,1)S(1)}, bf16[8,384,512]{2,1,0:T(8,128)(2,1)}) fusion(bf16[8,384,512]{2,1,0:T(8,128)(2,1)} %collective-permute-done.9, pred[]{:T(512)S(6)} %eq.14, bf16[16,384,512]{2,1,0:T(8,128)(2,1)S(1)} %bitcast_dynamic-update-slice_fusion.1, s32[]{:T(128)S(6)} %select_n.93), kind=kLoop, calls=%fused_computation.1 | loop fusion | flops 1572864 | bytes 12582917 | tf_op jit(solution)/shard_map/broadcast_in_dim | solution.py:107
  217.1 0.0 copy-done.2
  217.1 3.2 %pad_maximum_fusion = bf16[2,8,384,512]{3,2,1,0:T(8,128)(2,1)} fusion(bf16[1,8,384,512]{3,2,1,0:T(8,128)(2,1)S(1)} %copy-done.2, bf16[1,8,384,512]{3,2,1,0:T(8,128)(2,1)S(1)} %get-tuple-element.12), kind=kLoop, calls=%fused_computation | loop fusion | flops 3145728 | bytes 12582912 | tf_op jit(solution)/shard_map/concatenate | solution.py:107
  (16 shorter events, 0.4 us)
Async XLA Ops:
  0.6 154.2 %copy-start = (bf16[8,384,384]{2,1,0:T(8,128)(2,1)S(1)}, bf16[8,384,384]{2,1,0:T(8,128)(2,1)}, u32[]{:S(2)}) copy-start(bf16[8,384,384]{2,1,0:T(8,128)(2,1)} %param.8) | copy-start | bytes 7077892
  0.6 4.8 %copy-start.1 = (bf16[2,8,384,512]{3,2,1,0:T(8,128)(2,1)S(1)}, bf16[2,8,384,512]{3,2,1,0:T(8,128)(2,1)}, u32[]{:S(2)}) copy-start(bf16[2,8,384,512]{3,2,1,0:T(8,128)(2,1)} %refs_10_.1) | copy-start | bytes 18874372
  4.3 35.1 %collective-permute-start.1 = (bf16[2,4,384,512]{3,2,1,0:T(8,128)(2,1)S(1)}, bf16[2,4,384,512]{3,2,1,0:T(8,128)(2,1)}, u32[]{:S(2)}, u32[]{:S(2)}) collective-permute-start(bf16[2,4,384,512]{3,2,1,0:T(8,128)(2,1)S(1)} %get-tuple-element.16), channel_id=1, source_target_pairs={{0,120},{8,0},{16,8},{24,16},{32,24},{40,32},{48,40},{56,48},{64,5... | collective-permute-start | bytes 9437192 | tf_op jit(solution)/shard_map/ppermute | solution.py:71
  4.6 40.4 %copy-start.5 = (s32[2,8,2]{1,2,0:T(2,128)S(1)}, s32[2,8,2]{1,2,0:T(2,128)}, u32[]{:S(2)}) copy-start(s32[2,8,2]{1,2,0:T(2,128)} %param.10) | copy-start | bytes 388
  4.6 40.5 %copy-start.6 = (s32[2,8]{1,0:T(2,128)S(1)}, s32[2,8]{1,0:T(2,128)}, u32[]{:S(2)}) copy-start(s32[2,8]{1,0:T(2,128)} %param.11) | copy-start | bytes 196
  4.6 36.8 %collective-permute-start = (bf16[2,4,384,512]{3,2,1,0:T(8,128)(2,1)S(1)}, bf16[2,4,384,512]{3,2,1,0:T(8,128)(2,1)}, u32[]{:S(2)}, u32[]{:S(2)}) collective-permute-start(bf16[2,4,384,512]{3,2,1,0:T(8,128)(2,1)S(1)} %get-tuple-element.17), channel_id=1, source_target_pairs={{0,8},{8,16},{16,24},{24,32},{32,40},{40,48},{48,56},{56,64},{64,7... | collective-permute-start | bytes 9437192 | tf_op jit(solution)/shard_map/ppermute | solution.py:71
  41.4 116.0 %collective-permute-start.9 = (bf16[8,384,512]{2,1,0:T(8,128)(2,1)}, bf16[8,384,512]{2,1,0:T(8,128)(2,1)}, u32[]{:S(2)}, u32[]{:S(2)}) collective-permute-start(bf16[8,384,512]{2,1,0:T(8,128)(2,1)} %get-tuple-element.9), channel_id=1, source_target_pairs={{0,1},{1,2},{2,3},{3,4},{4,5},{5,6},{6,7},{8,9},{9,10},{10,11},{11... | collective-permute-start | bytes 9437192 | tf_op jit(solution)/shard_map/ppermute | solution.py:77
  67.8 52.9 %collective-permute-start.2 = (bf16[384,512]{1,0:T(8,128)(2,1)S(1)}, bf16[384,512]{1,0:T(8,128)(2,1)S(1)}, u32[]{:S(2)}, u32[]{:S(2)}) collective-permute-start(bf16[384,512]{1,0:T(8,128)(2,1)S(1)} %get-tuple-element.18), channel_id=1, source_target_pairs={{0,1},{1,2},{2,3},{3,4},{4,5},{5,6},{6,7},{7,0},{8,9},{9,10},{10,1... | collective-permute-start | bytes 1179656 | tf_op jit(solution)/shard_map/ppermute | solution.py:71
  69.7 52.9 %collective-permute-start.8 = (bf16[384,512]{1,0:T(8,128)(2,1)S(1)}, bf16[384,512]{1,0:T(8,128)(2,1)S(1)}, u32[]{:S(2)}, u32[]{:S(2)}) collective-permute-start(bf16[384,512]{1,0:T(8,128)(2,1)S(1)} %get-tuple-element.19), channel_id=1, source_target_pairs={{0,7},{1,0},{2,1},{3,2},{4,3},{5,4},{6,5},{7,6},{8,15},{9,8},{10,9... | collective-permute-start | bytes 1179656 | tf_op jit(solution)/shard_map/ppermute | solution.py:71
  69.9 55.0 %collective-permute-start.7 = (bf16[384,512]{1,0:T(8,128)(2,1)S(1)}, bf16[384,512]{1,0:T(8,128)(2,1)S(1)}, u32[]{:S(2)}, u32[]{:S(2)}) collective-permute-start(bf16[384,512]{1,0:T(8,128)(2,1)S(1)} %get-tuple-element.20), channel_id=1, source_target_pairs={{0,6},{1,7},{2,0},{3,1},{4,2},{5,3},{6,4},{7,5},{8,14},{9,15},{10,... | collective-permute-start | bytes 1179656 | tf_op jit(solution)/shard_map/ppermute | solution.py:71
  72.3 74.9 %collective-permute-start.6 = (bf16[384,512]{1,0:T(8,128)(2,1)}, bf16[384,512]{1,0:T(8,128)(2,1)}, u32[]{:S(2)}, u32[]{:S(2)}) collective-permute-start(bf16[384,512]{1,0:T(8,128)(2,1)} %get-tuple-element.21), channel_id=1, source_target_pairs={{0,5},{1,6},{2,7},{3,0},{4,1},{5,2},{6,3},{7,4},{8,13},{9,14},{10,... | collective-permute-start | bytes 1179656 | tf_op jit(solution)/shard_map/ppermute | solution.py:71
  120.7 34.1 %collective-permute-start.5 = (bf16[384,512]{1,0:T(8,128)(2,1)}, bf16[384,512]{1,0:T(8,128)(2,1)}, u32[]{:S(2)}, u32[]{:S(2)}) collective-permute-start(bf16[384,512]{1,0:T(8,128)(2,1)} %get-tuple-element.22), channel_id=1, source_target_pairs={{0,4},{1,5},{2,6},{3,7},{4,0},{5,1},{6,2},{7,3},{8,12},{9,13},{10,... | collective-permute-start | bytes 1179656 | tf_op jit(solution)/shard_map/ppermute | solution.py:71
  122.7 2.2 copy-start.3
  122.7 32.2 %collective-permute-start.4 = (bf16[384,512]{1,0:T(8,128)(2,1)S(1)}, bf16[384,512]{1,0:T(8,128)(2,1)}, u32[]{:S(2)}, u32[]{:S(2)}) collective-permute-start(bf16[384,512]{1,0:T(8,128)(2,1)S(1)} %get-tuple-element.23), channel_id=1, source_target_pairs={{0,3},{1,4},{2,5},{3,6},{4,7},{5,0},{6,1},{7,2},{8,11},{9,12},{10,... | collective-permute-start | bytes 1179656 | tf_op jit(solution)/shard_map/ppermute | solution.py:71
  124.8 0.8 copy-start.4
  125.6 29.2 %collective-permute-start.3 = (bf16[384,512]{1,0:T(8,128)(2,1)S(1)}, bf16[384,512]{1,0:T(8,128)(2,1)}, u32[]{:S(2)}, u32[]{:S(2)}) collective-permute-start(bf16[384,512]{1,0:T(8,128)(2,1)S(1)} %get-tuple-element.24), channel_id=1, source_target_pairs={{0,2},{1,3},{2,4},{3,5},{4,6},{5,7},{6,0},{7,1},{8,10},{9,11},{10,... | collective-permute-start | bytes 1179656 | tf_op jit(solution)/shard_map/ppermute | solution.py:71
  157.5 11.2 %collective-permute-start.10 = (bf16[384,512]{1,0:T(8,128)(2,1)S(1)}, bf16[384,512]{1,0:T(8,128)(2,1)S(1)}, u32[]{:S(2)}, u32[]{:S(2)}) collective-permute-start(bf16[384,512]{1,0:T(8,128)(2,1)S(1)} %convolution_convert_fusion), channel_id=1, source_target_pairs={{0,7},{1,0},{2,1},{3,2},{4,3},{5,4},{6,5},{7,6},{8,15},{9,8},{10,9... | collective-permute-start | bytes 1179656 | tf_op jit(solution)/shard_map/ppermute | solution.py:71
  157.6 22.7 %collective-permute-start.11 = (bf16[384,512]{1,0:T(8,128)(2,1)S(1)}, bf16[384,512]{1,0:T(8,128)(2,1)S(1)}, u32[]{:S(2)}, u32[]{:S(2)}) collective-permute-start(bf16[384,512]{1,0:T(8,128)(2,1)S(1)} %convolution_convert_fusion), channel_id=1, source_target_pairs={{0,6},{1,7},{2,0},{3,1},{4,2},{5,3},{6,4},{7,5},{8,14},{9,15},{10,... | collective-permute-start | bytes 1179656 | tf_op jit(solution)/shard_map/ppermute | solution.py:71
  162.1 50.5 %collective-permute-start.16 = (bf16[384,512]{1,0:T(8,128)(2,1)S(1)}, bf16[384,512]{1,0:T(8,128)(2,1)S(1)}, u32[]{:S(2)}, u32[]{:S(2)}) collective-permute-start(bf16[384,512]{1,0:T(8,128)(2,1)S(1)} %convolution_convert_fusion), channel_id=1, source_target_pairs={{0,1},{1,2},{2,3},{3,4},{4,5},{5,6},{6,7},{7,0},{8,9},{9,10},{10,1... | collective-permute-start | bytes 1179656 | tf_op jit(solution)/shard_map/ppermute | solution.py:71
  162.1 50.5 %collective-permute-start.15 = (bf16[384,512]{1,0:T(8,128)(2,1)S(1)}, bf16[384,512]{1,0:T(8,128)(2,1)S(1)}, u32[]{:S(2)}, u32[]{:S(2)}) collective-permute-start(bf16[384,512]{1,0:T(8,128)(2,1)S(1)} %convolution_convert_fusion), channel_id=1, source_target_pairs={{0,2},{1,3},{2,4},{3,5},{4,6},{5,7},{6,0},{7,1},{8,10},{9,11},{10,... | collective-permute-start | bytes 1179656 | tf_op jit(solution)/shard_map/ppermute | solution.py:71
  165.4 47.1 %collective-permute-start.14 = (bf16[384,512]{1,0:T(8,128)(2,1)S(1)}, bf16[384,512]{1,0:T(8,128)(2,1)S(1)}, u32[]{:S(2)}, u32[]{:S(2)}) collective-permute-start(bf16[384,512]{1,0:T(8,128)(2,1)S(1)} %convolution_convert_fusion), channel_id=1, source_target_pairs={{0,3},{1,4},{2,5},{3,6},{4,7},{5,0},{6,1},{7,2},{8,11},{9,12},{10,... | collective-permute-start | bytes 1179656 | tf_op jit(solution)/shard_map/ppermute | solution.py:71
  168.7 34.9 %collective-permute-start.12 = (bf16[384,512]{1,0:T(8,128)(2,1)S(1)}, bf16[384,512]{1,0:T(8,128)(2,1)S(1)}, u32[]{:S(2)}, u32[]{:S(2)}) collective-permute-start(bf16[384,512]{1,0:T(8,128)(2,1)S(1)} %convolution_convert_fusion), channel_id=1, source_target_pairs={{0,5},{1,6},{2,7},{3,0},{4,1},{5,2},{6,3},{7,4},{8,13},{9,14},{10,... | collective-permute-start | bytes 1179656 | tf_op jit(solution)/shard_map/ppermute | solution.py:71
  180.3 32.2 %collective-permute-start.13 = (bf16[384,512]{1,0:T(8,128)(2,1)S(1)}, bf16[384,512]{1,0:T(8,128)(2,1)S(1)}, u32[]{:S(2)}, u32[]{:S(2)}) collective-permute-start(bf16[384,512]{1,0:T(8,128)(2,1)S(1)} %convolution_convert_fusion), channel_id=1, source_target_pairs={{0,4},{1,5},{2,6},{3,7},{4,0},{5,1},{6,2},{7,3},{8,12},{9,13},{10,... | collective-permute-start | bytes 1179656 | tf_op jit(solution)/shard_map/ppermute | solution.py:71
  213.0 4.1 %copy-start.2 = (bf16[1,8,384,512]{3,2,1,0:T(8,128)(2,1)S(1)}, bf16[1,8,384,512]{3,2,1,0:T(8,128)(2,1)}, u32[]{:S(2)}) copy-start(bf16[1,8,384,512]{3,2,1,0:T(8,128)(2,1)} %get-tuple-element.14) | copy-start | bytes 9437188
